TPU v7x, 32 devices: a whole 2x2x4 slice. The times are simulated.
32 devices in a mesh: gx: 8 (over z, core), gy: 4 (over y, x).
Axes of the slice: x: 2, y: 2, z: 4, core: 2. Of those that a mesh axis runs over, the one named last changes fastest.
Arguments:
- gap: float32 [8, 4, 896, 128], P('gx', 'gy'), may hold values from -6 to 6
- own_rows: float32 [8, 4, 640, 896], P('gx', 'gy')
- spill_rows: float32 [8, 4, 2, 128, 896], P('gx', 'gy')
- tile_plan: int32 [8, 4, 2], P('gx', 'gy'), may hold values from -1 to 6, as said below
- orders: int32 [8, 4], P('gx', 'gy'), may hold values from 384 to 896, as said below
- slot_rows: int32 [8, 4, 896], P('gx', 'gy'), may hold values from 0 to 895, each once within a row
Outputs:
- solution: float32 [8, 4, 896, 128], P('gx', 'gy')
- residual: float32 [8, 4, 896, 128], P('gx', 'gy')
Inputs may be any that keep to these rules, and one draw needn't show every extreme that they name: `orders`: the largest order, 896, is taken by some subdomain in every draw. `tile_plan`: for subdomain (i, j) and slot s, the index of the row tile of its operator stored in slot s of spill_rows on subdomain ((i + (s + 1) * 2) mod 8, j), or -1. Every tile from 5 on that holds rows under the subdomain's order sits in exactly one slot, and no other tile does. `slot_rows`: for each subdomain a permutation of its operator rows over its slots.
All inputs are finite; a program needn't handle non-finite values.
Results may differ from a plain program's by a relative error of at most 0.0003.
Values sent between devices are 32-bit elements; how exact they have to be, the bound alone decides.
No kernel may reach another device: no remote copies, remote signals or barrier semaphores. Data moves between devices by JAX's collectives and lax.ppermute only.
A program may use at most 64 MiB of HBM per device.

v0:
```python
import jax
import jax.numpy as jnp
from jax import lax
from jax.sharding import PartitionSpec as P

ITERS = 4


low_bound = 0.5
high_bound = 7.0


def shifted(block, axis, distance):
    devices = range(lax.axis_size(axis))
    route = [(i - distance, i) for i in devices if i - distance in devices]
    return lax.ppermute(block, axis, route)


def from_behind(value, axis, steps):
    count = lax.axis_size(axis)
    pairs = [(source, (source + steps) % count) for source in range(count)]
    return lax.ppermute(value, axis, pairs)


def multiply_pair(operands):
    return jnp.dot(
        operands[0],
        operands[1],
        precision=lax.Precision.HIGHEST,
        preferred_element_type=jnp.float32,
    )


def empty_pair(operands):
    return jnp.zeros((operands[0].shape[0], operands[1].shape[1]), jnp.float32)


def tile_product(row_block, multipliers, active):
    return lax.cond(active, multiply_pair, empty_pair, (row_block, multipliers))


def along_x(part, offset):
    return shifted(part, "gx", offset)


def along_y(part, offset):
    return shifted(part, "gy", offset)


def face_sum(local):
    width = local.shape[0] // 4
    low_x = local[0:width]
    high_x = local[width : 2 * width]
    low_y = local[2 * width : 3 * width]
    high_y = local[3 * width : 4 * width]
    return jnp.concatenate(
        [
            low_x + along_x(high_x, 1),
            high_x + along_x(low_x, -1),
            low_y + along_y(high_y, 1),
            high_y + along_y(low_y, -1),
        ],
        axis=0,
    )


def body(gap, own_rows, spill_rows, tile_plan, orders, slot_rows):
    order_max = gap.shape[2]
    tile_rows = spill_rows.shape[3]
    own_tiles = own_rows.shape[2] // tile_rows
    hop_span = lax.axis_size("gx") // 4
    own_block = own_rows[0, 0]
    spill_block = spill_rows[0, 0]
    plan_row = tile_plan[0, 0]
    order_now = orders[0, 0]
    slot_map = slot_rows[0, 0]
    row_ids = jnp.arange(order_max, dtype=jnp.int32)
    face_sign = jnp.where(row_ids // (order_max // 4) % 2 == 0, -1.0, 1.0).astype(jnp.float32)
    slot_of_row = jnp.zeros((order_max,), jnp.int32).at[slot_map].set(row_ids)
    live_rows = (row_ids < order_now).astype(jnp.float32)[:, None]
    row_sign = face_sign[slot_of_row][:, None] * live_rows
    homed = [
        from_behind(spill_block[slot_id], "gx", -(slot_id + 1) * hop_span) for slot_id in range(2)
    ]
    extra_rows = []
    for extra_id in range(2):
        gathered = jnp.zeros_like(homed[0])
        for slot_id in range(2):
            gathered = gathered + jnp.where(
                plan_row[slot_id] == own_tiles + extra_id, homed[slot_id], 0.0
            )
        extra_rows.append(gathered)
    load = face_sum(gap[0, 0])
    centre = (high_bound + low_bound) / 2.0
    half_width = (high_bound - low_bound) / 2.0
    sigma_value = centre / half_width
    rho_value = 1.0 / sigma_value
    solution = jnp.zeros_like(load)
    residual = load
    direction = residual / centre
    for step_id in range(ITERS):
        solution = solution + direction
        multipliers = direction[slot_of_row] * row_sign
        pieces = [
            tile_product(
                own_block[tile_id * tile_rows : (tile_id + 1) * tile_rows],
                multipliers,
                tile_id * tile_rows < order_now,
            )
            for tile_id in range(own_tiles)
        ]
        for apply_extra_id in range(2):
            pieces.append(
                tile_product(
                    extra_rows[apply_extra_id],
                    multipliers,
                    (own_tiles + apply_extra_id) * tile_rows < order_now,
                )
            )
        result = jnp.concatenate(pieces, axis=0) * live_rows
        residual = residual - face_sum(result[slot_map] * face_sign[:, None])
        if step_id + 1 < ITERS:
            rho_next = 1.0 / (2.0 * sigma_value - rho_value)
            direction = rho_next * rho_value * direction + 2.0 * rho_next / half_width * residual
            rho_value = rho_next
    return (solution[None, None], residual[None, None])


def solution(mesh):
    in_specs = (
        P("gx", "gy", None, None),
        P("gx", "gy", None, None),
        P("gx", "gy", None, None, None),
        P("gx", "gy", None),
        P("gx", "gy"),
        P("gx", "gy", None),
    )
    out_specs = (P("gx", "gy", None, None), P("gx", "gy", None, None))
    return jax.shard_map(body, mesh=mesh, in_specs=in_specs, out_specs=out_specs, check_vma=False)
```

profile of v0, /device:TPU:0, one launch (start us, length us, event | category | flops | bytes accessed | tf_op | source)
XLA Modules:
  0.0 194.7 jit_solution(7582297773425951439)
XLA Ops:
  1.7 2.4 %collective-permute-start = (f32[224,128]{1,0:T(8,128)S(1)}, f32[224,128]{1,0:T(8,128)S(1)}, u32[]{:S(2)}, u32[]{:S(2)}) collective-permute-start(f32[224,128]{1,0:T(8,128)S(1)} %get-tuple-element.299), channel_id=1, source_target_pairs={{0,4},{4,8},{8,12},{12,16},{16,20},{20,24},{24,28},{1,5},{5,9},{9,... | collective-permute-start | bytes 344072 | tf_op jit(solution)/shard_map/ppermute | solution.py:16
  4.1 1.3 collective-permute-start.1
  5.4 4.9 %collective-permute-start.2 = (f32[224,128]{1,0:T(8,128)S(1)}, f32[224,128]{1,0:T(8,128)}, u32[]{:S(2)}, u32[]{:S(2)}) collective-permute-start(f32[224,128]{1,0:T(8,128)S(1)} %get-tuple-element.301), channel_id=1, source_target_pairs={{0,1},{1,2},{2,3},{4,5},{5,6},{6,7},{8,9},{9,10},{10,11},{12,13},{... | collective-permute-start | bytes 344072 | tf_op jit(solution)/shard_map/ppermute | solution.py:16
  11.6 2.1 %slice_bitcast_fusion.1 = (f32[128,896]{1,0:T(8,128)}, f32[128,896]{1,0:T(8,128)}) fusion(f32[1,1,2,128,896]{4,3,2,1,0:T(8,128)} %param.64), kind=kLoop, calls=%fused_computation.27 | loop fusion | bytes 1835008 | tf_op jit(solution)/shard_map/squeeze | solution.py:83
  13.7 6.1 %collective-permute-start.4 = (f32[128,896]{1,0:T(8,128)}, f32[128,896]{1,0:T(8,128)}, u32[]{:S(2)}, u32[]{:S(2)}) collective-permute-start(f32[128,896]{1,0:T(8,128)} %get-tuple-element.261), channel_id=1, source_target_pairs={{0,24},{4,28},{8,0},{12,4},{16,8},{20,12},{24,16},{28,20},{1,25},{... | collective-permute-start | bytes 1376264 | tf_op jit(solution)/shard_map/ppermute | solution.py:22
  20.6 5.3 %scatter_custom_fusion = s32[896]{0:T(1024)S(1)} fusion(s32[896]{0:T(1024)S(1)} %fusion.10, s32[896]{0:T(1024)S(1)} %iota.21, s32[]{:T(128)} %constant.63.clone.1), kind=kCustom, calls=%fused_computation.103 | custom fusion | bytes 3588 | tf_op jit(solution)/shard_map/scatter | solution.py:79
  25.9 1.7 slice_bitcast_fusion.2
  27.6 3.7 %gather_fusion.1 = f32[896]{0:T(1024)S(1)} fusion(f32[896]{0:T(1024)S(1)} %fusion.9, s32[1024]{0:T(1024)S(1)} %get-tuple-element.306), kind=kCustom, calls=%fused_computation.1 | custom fusion | bytes 10752 | tf_op jit(solution)/shard_map/gather | solution.py:81
  35.5 2.8 %gather_fusion = f32[896,128]{1,0:T(8,128)} fusion(f32[896,128]{1,0:T(8,128)S(1)} %broadcast_multiply_fusion.12, s32[1024]{0:T(1024)S(1)} %get-tuple-element.306), kind=kCustom, calls=%fused_computation | custom fusion | bytes 921088 | tf_op jit(solution)/shard_map/gather | solution.py:103
  45.2 9.9 %collective-permute-done.5 = f32[128,896]{1,0:T(8,128)} collective-permute-done((f32[128,896]{1,0:T(8,128)}, f32[128,896]{1,0:T(8,128)}, u32[]{:S(2)}, u32[]{:S(2)}) %collective-permute-start.5) | collective-permute-done | bytes 458784 | tf_op jit(solution)/shard_map/ppermute | solution.py:22
  55.1 2.2 %select_add_fusion = (f32[128,896]{1,0:T(8,128)}, f32[128,896]{1,0:T(8,128)}) fusion(f32[128,896]{1,0:T(8,128)} %collective-permute-done.5, f32[128,896]{1,0:T(8,128)} %collective-permute-done.4, pred[]{:T(512)} %bitcast.20, pred[]{:T(512)} %bitcast.19, pred[]{:T(512)} %bitcast.17, pred[]{:T(512)} %bitcast.15), kind=kLoop, calls=%fused_computation.24 | loop fusion | flops 688128 | bytes 1835012 | tf_op jit(solution)/shard_map/add | solution.py:89
  59.8 2.8 %gather_fusion.2 = f32[896,128]{1,0:T(8,128)} fusion(f32[896,128]{1,0:T(8,128)S(1)} %broadcast_multiply_fusion.7, s32[1024]{0:T(1024)S(1)} %get-tuple-element.305), kind=kCustom, calls=%fused_computation.2 | custom fusion | bytes 921088 | tf_op jit(solution)/shard_map/gather | solution.py:121
  63.8 5.1 %collective-permute-start.6 = (f32[224,128]{1,0:T(8,128)S(1)}, f32[224,128]{1,0:T(8,128)S(1)}, u32[]{:S(2)}, u32[]{:S(2)}) collective-permute-start(f32[224,128]{1,0:T(8,128)S(1)} %get-tuple-element.291), channel_id=1, source_target_pairs={{0,4},{4,8},{8,12},{12,16},{16,20},{20,24},{24,28},{1,5},{5,9},{9,... | collective-permute-start | bytes 344072 | tf_op jit(solution)/shard_map/ppermute | solution.py:16
  68.9 1.3 collective-permute-start.8
  70.2 1.3 collective-permute-start.9
  71.5 1.3 collective-permute-start.7
  73.1 7.4 %collective-permute-done.9 = f32[224,128]{1,0:T(8,128)S(1)} collective-permute-done((f32[224,128]{1,0:T(8,128)S(1)}, f32[224,128]{1,0:T(8,128)S(1)}, u32[]{:S(2)}, u32[]{:S(2)}) %collective-permute-start.9) | collective-permute-done | bytes 114720 | tf_op jit(solution)/shard_map/ppermute | solution.py:16
  81.3 2.8 %gather_fusion.3 = f32[896,128]{1,0:T(8,128)} fusion(f32[896,128]{1,0:T(8,128)S(1)} %multiply_add_fusion.1, s32[1024]{0:T(1024)S(1)} %get-tuple-element.306), kind=kCustom, calls=%fused_computation.3 | custom fusion | bytes 921088 | tf_op jit(solution)/shard_map/gather | solution.py:103
  92.1 1.5 constant_dynamic-update-slice_fusion.11
  93.6 1.5 constant_dynamic-update-slice_fusion.10
  95.0 1.5 constant_dynamic-update-slice_fusion.9
  96.5 1.5 constant_dynamic-update-slice_fusion.8
  98.0 1.5 constant_dynamic-update-slice_fusion.7
  100.6 2.8 %gather_fusion.4 = f32[896,128]{1,0:T(8,128)} fusion(f32[896,128]{1,0:T(8,128)S(1)} %broadcast_multiply_fusion.6, s32[1024]{0:T(1024)S(1)} %get-tuple-element.305), kind=kCustom, calls=%fused_computation.4 | custom fusion | bytes 921088 | tf_op jit(solution)/shard_map/gather | solution.py:121
  104.8 5.2 %collective-permute-start.10 = (f32[224,128]{1,0:T(8,128)S(1)}, f32[224,128]{1,0:T(8,128)S(1)}, u32[]{:S(2)}, u32[]{:S(2)}) collective-permute-start(f32[224,128]{1,0:T(8,128)S(1)} %get-tuple-element.283), channel_id=1, source_target_pairs={{0,4},{4,8},{8,12},{12,16},{16,20},{20,24},{24,28},{1,5},{5,9},{9,... | collective-permute-start | bytes 344072 | tf_op jit(solution)/shard_map/ppermute | solution.py:16
  110.0 1.4 collective-permute-start.12
  111.5 1.3 collective-permute-start.13
  112.8 1.3 collective-permute-start.11
  114.4 8.4 %collective-permute-done.13 = f32[224,128]{1,0:T(8,128)S(1)} collective-permute-done((f32[224,128]{1,0:T(8,128)S(1)}, f32[224,128]{1,0:T(8,128)S(1)}, u32[]{:S(2)}, u32[]{:S(2)}) %collective-permute-start.13) | collective-permute-done | bytes 114720 | tf_op jit(solution)/shard_map/ppermute | solution.py:16
  123.8 2.8 %gather_fusion.5 = f32[896,128]{1,0:T(8,128)} fusion(f32[896,128]{1,0:T(8,128)S(1)} %multiply_add_fusion, s32[1024]{0:T(1024)S(1)} %get-tuple-element.306), kind=kCustom, calls=%fused_computation.5 | custom fusion | bytes 921088 | tf_op jit(solution)/shard_map/gather | solution.py:103
  134.5 1.5 constant_dynamic-update-slice_fusion.18
  136.0 1.5 constant_dynamic-update-slice_fusion.17
  137.5 1.5 constant_dynamic-update-slice_fusion.16
  138.9 1.5 constant_dynamic-update-slice_fusion.15
  140.4 1.5 constant_dynamic-update-slice_fusion.14
  143.1 2.8 %gather_fusion.6 = f32[896,128]{1,0:T(8,128)} fusion(f32[896,128]{1,0:T(8,128)S(1)} %broadcast_multiply_fusion.5, s32[1024]{0:T(1024)S(1)} %get-tuple-element.305), kind=kCustom, calls=%fused_computation.6 | custom fusion | bytes 921088 | tf_op jit(solution)/shard_map/gather | solution.py:121
  146.0 1.3 broadcast_multiply_fusion.1
  147.3 5.2 %collective-permute-start.14 = (f32[224,128]{1,0:T(8,128)S(1)}, f32[224,128]{1,0:T(8,128)S(1)}, u32[]{:S(2)}, u32[]{:S(2)}) collective-permute-start(f32[224,128]{1,0:T(8,128)S(1)} %get-tuple-element.275), channel_id=1, source_target_pairs={{0,4},{4,8},{8,12},{12,16},{16,20},{20,24},{24,28},{1,5},{5,9},{9,... | collective-permute-start | bytes 344072 | tf_op jit(solution)/shard_map/ppermute | solution.py:16
  152.6 1.4 collective-permute-start.16
  154.0 1.3 collective-permute-start.17
  157.1 8.2 %collective-permute-done.17 = f32[224,128]{1,0:T(8,128)S(1)} collective-permute-done((f32[224,128]{1,0:T(8,128)S(1)}, f32[224,128]{1,0:T(8,128)S(1)}, u32[]{:S(2)}, u32[]{:S(2)}) %collective-permute-start.17) | collective-permute-done | bytes 114720 | tf_op jit(solution)/shard_map/ppermute | solution.py:16
  166.4 2.8 %gather_fusion.7 = f32[896,128]{1,0:T(8,128)} fusion(f32[896,128]{1,0:T(8,128)S(1)} %fusion.1, s32[1024]{0:T(1024)S(1)} %get-tuple-element.306), kind=kCustom, calls=%fused_computation.7 | custom fusion | bytes 921088 | tf_op jit(solution)/shard_map/gather | solution.py:103
  173.6 1.9 gather_fusion.8
  175.7 5.8 %collective-permute-start.18 = (f32[224,128]{1,0:T(8,128)S(1)}, f32[224,128]{1,0:T(8,128)S(1)}, u32[]{:S(2)}, u32[]{:S(2)}) collective-permute-start(f32[224,128]{1,0:T(8,128)S(1)} %get-tuple-element.267), channel_id=1, source_target_pairs={{0,4},{4,8},{8,12},{12,16},{16,20},{20,24},{24,28},{1,5},{5,9},{9,... | collective-permute-start | bytes 344072 | tf_op jit(solution)/shard_map/ppermute | solution.py:16
  181.5 1.3 collective-permute-start.20
  182.8 1.3 collective-permute-start.21
  184.1 1.3 collective-permute-start.19
  186.6 7.1 %collective-permute-done.21 = f32[224,128]{1,0:T(8,128)S(1)} collective-permute-done((f32[224,128]{1,0:T(8,128)S(1)}, f32[224,128]{1,0:T(8,128)S(1)}, u32[]{:S(2)}, u32[]{:S(2)}) %collective-permute-start.21) | collective-permute-done | bytes 114720 | tf_op jit(solution)/shard_map/ppermute | solution.py:16
  (223 shorter events, 61.1 us)
Async XLA Ops:
  0.6 19.9 %copy-start.45 = (s32[1,1,896]{2,1,0:T(1,128)S(1)}, s32[1,1,896]{2,1,0:T(1,128)}, u32[]{:S(2)}) copy-start(s32[1,1,896]{2,1,0:T(1,128)} %param.67) | copy-start | bytes 10756
  1.7 32.6 %collective-permute-start = (f32[224,128]{1,0:T(8,128)S(1)}, f32[224,128]{1,0:T(8,128)S(1)}, u32[]{:S(2)}, u32[]{:S(2)}) collective-permute-start(f32[224,128]{1,0:T(8,128)S(1)} %get-tuple-element.299), channel_id=1, source_target_pairs={{0,4},{4,8},{8,12},{12,16},{16,20},{20,24},{24,28},{1,5},{5,9},{9,... | collective-permute-start | bytes 344072 | tf_op jit(solution)/shard_map/ppermute | solution.py:16
  4.1 30.3 %collective-permute-start.1 = (f32[224,128]{1,0:T(8,128)S(1)}, f32[224,128]{1,0:T(8,128)S(1)}, u32[]{:S(2)}, u32[]{:S(2)}) collective-permute-start(f32[224,128]{1,0:T(8,128)S(1)} %get-tuple-element.300), channel_id=1, source_target_pairs={{4,0},{8,4},{12,8},{16,12},{20,16},{24,20},{28,24},{5,1},{9,5},{13... | collective-permute-start | bytes 344072 | tf_op jit(solution)/shard_map/ppermute | solution.py:16
  5.4 29.0 %collective-permute-start.2 = (f32[224,128]{1,0:T(8,128)S(1)}, f32[224,128]{1,0:T(8,128)}, u32[]{:S(2)}, u32[]{:S(2)}) collective-permute-start(f32[224,128]{1,0:T(8,128)S(1)} %get-tuple-element.301), channel_id=1, source_target_pairs={{0,1},{1,2},{2,3},{4,5},{5,6},{6,7},{8,9},{9,10},{10,11},{12,13},{... | collective-permute-start | bytes 344072 | tf_op jit(solution)/shard_map/ppermute | solution.py:16
  10.3 24.1 %collective-permute-start.3 = (f32[224,128]{1,0:T(8,128)S(1)}, f32[224,128]{1,0:T(8,128)}, u32[]{:S(2)}, u32[]{:S(2)}) collective-permute-start(f32[224,128]{1,0:T(8,128)S(1)} %get-tuple-element.302), channel_id=1, source_target_pairs={{1,0},{2,1},{3,2},{5,4},{6,5},{7,6},{9,8},{10,9},{11,10},{13,12},{... | collective-permute-start | bytes 344072 | tf_op jit(solution)/shard_map/ppermute | solution.py:16
  13.7 31.4 %collective-permute-start.4 = (f32[128,896]{1,0:T(8,128)}, f32[128,896]{1,0:T(8,128)}, u32[]{:S(2)}, u32[]{:S(2)}) collective-permute-start(f32[128,896]{1,0:T(8,128)} %get-tuple-element.261), channel_id=1, source_target_pairs={{0,24},{4,28},{8,0},{12,4},{16,8},{20,12},{24,16},{28,20},{1,25},{... | collective-permute-start | bytes 1376264 | tf_op jit(solution)/shard_map/ppermute | solution.py:22
  34.3 20.8 %collective-permute-start.5 = (f32[128,896]{1,0:T(8,128)}, f32[128,896]{1,0:T(8,128)}, u32[]{:S(2)}, u32[]{:S(2)}) collective-permute-start(f32[128,896]{1,0:T(8,128)} %get-tuple-element.262), channel_id=1, source_target_pairs={{0,16},{4,20},{8,24},{12,28},{16,0},{20,4},{24,8},{28,12},{1,17},{... | collective-permute-start | bytes 1376264 | tf_op jit(solution)/shard_map/ppermute | solution.py:22
  35.5 45.1 %copy-start = (f32[224,128]{1,0:T(8,128)}, f32[224,128]{1,0:T(8,128)S(1)}, u32[]{:S(2)}) copy-start(f32[224,128]{1,0:T(8,128)S(1)} %get-tuple-element.297) | copy-start | bytes 344068
  35.5 45.1 %copy-start.4 = (f32[224,128]{1,0:T(8,128)}, f32[224,128]{1,0:T(8,128)S(1)}, u32[]{:S(2)}) copy-start(f32[224,128]{1,0:T(8,128)S(1)} %get-tuple-element.298) | copy-start | bytes 344068
  63.8 9.0 %collective-permute-start.6 = (f32[224,128]{1,0:T(8,128)S(1)}, f32[224,128]{1,0:T(8,128)S(1)}, u32[]{:S(2)}, u32[]{:S(2)}) collective-permute-start(f32[224,128]{1,0:T(8,128)S(1)} %get-tuple-element.291), channel_id=1, source_target_pairs={{0,4},{4,8},{8,12},{12,16},{16,20},{20,24},{24,28},{1,5},{5,9},{9,... | collective-permute-start | bytes 344072 | tf_op jit(solution)/shard_map/ppermute | solution.py:16
  68.9 4.1 %collective-permute-start.8 = (f32[224,128]{1,0:T(8,128)S(1)}, f32[224,128]{1,0:T(8,128)S(1)}, u32[]{:S(2)}, u32[]{:S(2)}) collective-permute-start(f32[224,128]{1,0:T(8,128)S(1)} %get-tuple-element.292), channel_id=1, source_target_pairs={{0,1},{1,2},{2,3},{4,5},{5,6},{6,7},{8,9},{9,10},{10,11},{12,13},{... | collective-permute-start | bytes 344072 | tf_op jit(solution)/shard_map/ppermute | solution.py:16
  70.2 10.2 %collective-permute-start.9 = (f32[224,128]{1,0:T(8,128)S(1)}, f32[224,128]{1,0:T(8,128)S(1)}, u32[]{:S(2)}, u32[]{:S(2)}) collective-permute-start(f32[224,128]{1,0:T(8,128)S(1)} %get-tuple-element.293), channel_id=1, source_target_pairs={{1,0},{2,1},{3,2},{5,4},{6,5},{7,6},{9,8},{10,9},{11,10},{13,12},{... | collective-permute-start | bytes 344072 | tf_op jit(solution)/shard_map/ppermute | solution.py:16
  71.5 8.9 %collective-permute-start.7 = (f32[224,128]{1,0:T(8,128)S(1)}, f32[224,128]{1,0:T(8,128)S(1)}, u32[]{:S(2)}, u32[]{:S(2)}) collective-permute-start(f32[224,128]{1,0:T(8,128)S(1)} %get-tuple-element.294), channel_id=1, source_target_pairs={{4,0},{8,4},{12,8},{16,12},{20,16},{24,20},{28,24},{5,1},{9,5},{13... | collective-permute-start | bytes 344072 | tf_op jit(solution)/shard_map/ppermute | solution.py:16
  103.4 20.2 %copy-start.1 = (f32[224,128]{1,0:T(8,128)S(1)}, f32[224,128]{1,0:T(8,128)}, u32[]{:S(2)}) copy-start(f32[224,128]{1,0:T(8,128)} %copy-done) | copy-start | bytes 344068
  103.5 20.2 %copy-start.5 = (f32[224,128]{1,0:T(8,128)S(1)}, f32[224,128]{1,0:T(8,128)}, u32[]{:S(2)}) copy-start(f32[224,128]{1,0:T(8,128)} %copy-done.4) | copy-start | bytes 344068
  103.5 20.2 %copy-start.9 = (f32[224,128]{1,0:T(8,128)S(1)}, f32[224,128]{1,0:T(8,128)}, u32[]{:S(2)}) copy-start(f32[224,128]{1,0:T(8,128)} %copy-done.8) | copy-start | bytes 344068
  103.5 20.2 %copy-start.13 = (f32[224,128]{1,0:T(8,128)S(1)}, f32[224,128]{1,0:T(8,128)}, u32[]{:S(2)}) copy-start(f32[224,128]{1,0:T(8,128)} %copy-done.12) | copy-start | bytes 344068
  103.5 20.2 %copy-start.17 = (f32[224,128]{1,0:T(8,128)S(1)}, f32[224,128]{1,0:T(8,128)}, u32[]{:S(2)}) copy-start(f32[224,128]{1,0:T(8,128)} %copy-done.16) | copy-start | bytes 344068
  103.5 20.2 %copy-start.21 = (f32[224,128]{1,0:T(8,128)S(1)}, f32[224,128]{1,0:T(8,128)}, u32[]{:S(2)}) copy-start(f32[224,128]{1,0:T(8,128)} %copy-done.20) | copy-start | bytes 344068
  104.8 9.3 %collective-permute-start.10 = (f32[224,128]{1,0:T(8,128)S(1)}, f32[224,128]{1,0:T(8,128)S(1)}, u32[]{:S(2)}, u32[]{:S(2)}) collective-permute-start(f32[224,128]{1,0:T(8,128)S(1)} %get-tuple-element.283), channel_id=1, source_target_pairs={{0,4},{4,8},{8,12},{12,16},{16,20},{20,24},{24,28},{1,5},{5,9},{9,... | collective-permute-start | bytes 344072 | tf_op jit(solution)/shard_map/ppermute | solution.py:16
  110.0 4.3 %collective-permute-start.12 = (f32[224,128]{1,0:T(8,128)S(1)}, f32[224,128]{1,0:T(8,128)S(1)}, u32[]{:S(2)}, u32[]{:S(2)}) collective-permute-start(f32[224,128]{1,0:T(8,128)S(1)} %get-tuple-element.284), channel_id=1, source_target_pairs={{0,1},{1,2},{2,3},{4,5},{5,6},{6,7},{8,9},{9,10},{10,11},{12,13},{... | collective-permute-start | bytes 344072 | tf_op jit(solution)/shard_map/ppermute | solution.py:16
  111.5 11.3 %collective-permute-start.13 = (f32[224,128]{1,0:T(8,128)S(1)}, f32[224,128]{1,0:T(8,128)S(1)}, u32[]{:S(2)}, u32[]{:S(2)}) collective-permute-start(f32[224,128]{1,0:T(8,128)S(1)} %get-tuple-element.285), channel_id=1, source_target_pairs={{1,0},{2,1},{3,2},{5,4},{6,5},{7,6},{9,8},{10,9},{11,10},{13,12},{... | collective-permute-start | bytes 344072 | tf_op jit(solution)/shard_map/ppermute | solution.py:16
  112.8 10.0 %collective-permute-start.11 = (f32[224,128]{1,0:T(8,128)S(1)}, f32[224,128]{1,0:T(8,128)S(1)}, u32[]{:S(2)}, u32[]{:S(2)}) collective-permute-start(f32[224,128]{1,0:T(8,128)S(1)} %get-tuple-element.286), channel_id=1, source_target_pairs={{4,0},{8,4},{12,8},{16,12},{20,16},{24,20},{28,24},{5,1},{9,5},{13... | collective-permute-start | bytes 344072 | tf_op jit(solution)/shard_map/ppermute | solution.py:16
  145.9 20.3 %copy-start.2 = (f32[224,128]{1,0:T(8,128)S(1)}, f32[224,128]{1,0:T(8,128)}, u32[]{:S(2)}) copy-start(f32[224,128]{1,0:T(8,128)} %copy-done) | copy-start | bytes 344068
  145.9 20.3 %copy-start.6 = (f32[224,128]{1,0:T(8,128)S(1)}, f32[224,128]{1,0:T(8,128)}, u32[]{:S(2)}) copy-start(f32[224,128]{1,0:T(8,128)} %copy-done.4) | copy-start | bytes 344068
  145.9 20.3 %copy-start.10 = (f32[224,128]{1,0:T(8,128)S(1)}, f32[224,128]{1,0:T(8,128)}, u32[]{:S(2)}) copy-start(f32[224,128]{1,0:T(8,128)} %copy-done.8) | copy-start | bytes 344068
  145.9 20.3 %copy-start.14 = (f32[224,128]{1,0:T(8,128)S(1)}, f32[224,128]{1,0:T(8,128)}, u32[]{:S(2)}) copy-start(f32[224,128]{1,0:T(8,128)} %copy-done.12) | copy-start | bytes 344068
  145.9 20.3 %copy-start.18 = (f32[224,128]{1,0:T(8,128)S(1)}, f32[224,128]{1,0:T(8,128)}, u32[]{:S(2)}) copy-start(f32[224,128]{1,0:T(8,128)} %copy-done.16) | copy-start | bytes 344068
  145.9 20.3 %copy-start.22 = (f32[224,128]{1,0:T(8,128)S(1)}, f32[224,128]{1,0:T(8,128)}, u32[]{:S(2)}) copy-start(f32[224,128]{1,0:T(8,128)} %copy-done.20) | copy-start | bytes 344068
  145.9 20.3 %copy-start.25 = (f32[224,128]{1,0:T(8,128)S(1)}, f32[224,128]{1,0:T(8,128)}, u32[]{:S(2)}) copy-start(f32[224,128]{1,0:T(8,128)} %copy-done.24) | copy-start | bytes 344068
  145.9 20.3 %copy-start.28 = (f32[224,128]{1,0:T(8,128)S(1)}, f32[224,128]{1,0:T(8,128)}, u32[]{:S(2)}) copy-start(f32[224,128]{1,0:T(8,128)} %copy-done.27) | copy-start | bytes 344068
  145.9 20.3 %copy-start.31 = (f32[224,128]{1,0:T(8,128)S(1)}, f32[224,128]{1,0:T(8,128)}, u32[]{:S(2)}) copy-start(f32[224,128]{1,0:T(8,128)} %copy-done.30) | copy-start | bytes 344068
  146.0 20.3 %copy-start.34 = (f32[224,128]{1,0:T(8,128)S(1)}, f32[224,128]{1,0:T(8,128)}, u32[]{:S(2)}) copy-start(f32[224,128]{1,0:T(8,128)} %copy-done.33) | copy-start | bytes 344068
  147.3 9.3 %collective-permute-start.14 = (f32[224,128]{1,0:T(8,128)S(1)}, f32[224,128]{1,0:T(8,128)S(1)}, u32[]{:S(2)}, u32[]{:S(2)}) collective-permute-start(f32[224,128]{1,0:T(8,128)S(1)} %get-tuple-element.275), channel_id=1, source_target_pairs={{0,4},{4,8},{8,12},{12,16},{16,20},{20,24},{24,28},{1,5},{5,9},{9,... | collective-permute-start | bytes 344072 | tf_op jit(solution)/shard_map/ppermute | solution.py:16
  152.6 4.5 %collective-permute-start.16 = (f32[224,128]{1,0:T(8,128)S(1)}, f32[224,128]{1,0:T(8,128)S(1)}, u32[]{:S(2)}, u32[]{:S(2)}) collective-permute-start(f32[224,128]{1,0:T(8,128)S(1)} %get-tuple-element.276), channel_id=1, source_target_pairs={{0,1},{1,2},{2,3},{4,5},{5,6},{6,7},{8,9},{9,10},{10,11},{12,13},{... | collective-permute-start | bytes 344072 | tf_op jit(solution)/shard_map/ppermute | solution.py:16
  154.0 11.3 %collective-permute-start.17 = (f32[224,128]{1,0:T(8,128)S(1)}, f32[224,128]{1,0:T(8,128)S(1)}, u32[]{:S(2)}, u32[]{:S(2)}) collective-permute-start(f32[224,128]{1,0:T(8,128)S(1)} %get-tuple-element.277), channel_id=1, source_target_pairs={{1,0},{2,1},{3,2},{5,4},{6,5},{7,6},{9,8},{10,9},{11,10},{13,12},{... | collective-permute-start | bytes 344072 | tf_op jit(solution)/shard_map/ppermute | solution.py:16
  155.3 10.0 %collective-permute-start.15 = (f32[224,128]{1,0:T(8,128)S(1)}, f32[224,128]{1,0:T(8,128)S(1)}, u32[]{:S(2)}, u32[]{:S(2)}) collective-permute-start(f32[224,128]{1,0:T(8,128)S(1)} %get-tuple-element.278), channel_id=1, source_target_pairs={{4,0},{8,4},{12,8},{16,12},{20,16},{24,20},{28,24},{5,1},{9,5},{13... | collective-permute-start | bytes 344072 | tf_op jit(solution)/shard_map/ppermute | solution.py:16
  173.5 12.0 %copy-start.3 = (f32[224,128]{1,0:T(8,128)S(1)}, f32[224,128]{1,0:T(8,128)}, u32[]{:S(2)}) copy-start(f32[224,128]{1,0:T(8,128)} %copy-done) | copy-start | bytes 344068
  173.5 12.0 %copy-start.7 = (f32[224,128]{1,0:T(8,128)S(1)}, f32[224,128]{1,0:T(8,128)}, u32[]{:S(2)}) copy-start(f32[224,128]{1,0:T(8,128)} %copy-done.4) | copy-start | bytes 344068
  173.5 12.0 %copy-start.11 = (f32[224,128]{1,0:T(8,128)S(1)}, f32[224,128]{1,0:T(8,128)}, u32[]{:S(2)}) copy-start(f32[224,128]{1,0:T(8,128)} %copy-done.8) | copy-start | bytes 344068
  173.5 12.0 %copy-start.15 = (f32[224,128]{1,0:T(8,128)S(1)}, f32[224,128]{1,0:T(8,128)}, u32[]{:S(2)}) copy-start(f32[224,128]{1,0:T(8,128)} %copy-done.12) | copy-start | bytes 344068
  173.5 12.0 %copy-start.19 = (f32[224,128]{1,0:T(8,128)S(1)}, f32[224,128]{1,0:T(8,128)}, u32[]{:S(2)}) copy-start(f32[224,128]{1,0:T(8,128)} %copy-done.16) | copy-start | bytes 344068
  173.5 12.0 %copy-start.23 = (f32[224,128]{1,0:T(8,128)S(1)}, f32[224,128]{1,0:T(8,128)}, u32[]{:S(2)}) copy-start(f32[224,128]{1,0:T(8,128)} %copy-done.20) | copy-start | bytes 344068
  173.5 12.0 %copy-start.26 = (f32[224,128]{1,0:T(8,128)S(1)}, f32[224,128]{1,0:T(8,128)}, u32[]{:S(2)}) copy-start(f32[224,128]{1,0:T(8,128)} %copy-done.24) | copy-start | bytes 344068
  175.7 10.8 %collective-permute-start.18 = (f32[224,128]{1,0:T(8,128)S(1)}, f32[224,128]{1,0:T(8,128)S(1)}, u32[]{:S(2)}, u32[]{:S(2)}) collective-permute-start(f32[224,128]{1,0:T(8,128)S(1)} %get-tuple-element.267), channel_id=1, source_target_pairs={{0,4},{4,8},{8,12},{12,16},{16,20},{20,24},{24,28},{1,5},{5,9},{9,... | collective-permute-start | bytes 344072 | tf_op jit(solution)/shard_map/ppermute | solution.py:16
  181.5 5.1 %collective-permute-start.20 = (f32[224,128]{1,0:T(8,128)S(1)}, f32[224,128]{1,0:T(8,128)S(1)}, u32[]{:S(2)}, u32[]{:S(2)}) collective-permute-start(f32[224,128]{1,0:T(8,128)S(1)} %get-tuple-element.268), channel_id=1, source_target_pairs={{0,1},{1,2},{2,3},{4,5},{5,6},{6,7},{8,9},{9,10},{10,11},{12,13},{... | collective-permute-start | bytes 344072 | tf_op jit(solution)/shard_map/ppermute | solution.py:16
  182.8 10.9 %collective-permute-start.21 = (f32[224,128]{1,0:T(8,128)S(1)}, f32[224,128]{1,0:T(8,128)S(1)}, u32[]{:S(2)}, u32[]{:S(2)}) collective-permute-start(f32[224,128]{1,0:T(8,128)S(1)} %get-tuple-element.269), channel_id=1, source_target_pairs={{1,0},{2,1},{3,2},{5,4},{6,5},{7,6},{9,8},{10,9},{11,10},{13,12},{... | collective-permute-start | bytes 344072 | tf_op jit(solution)/shard_map/ppermute | solution.py:16
  184.1 9.6 %collective-permute-start.19 = (f32[224,128]{1,0:T(8,128)S(1)}, f32[224,128]{1,0:T(8,128)S(1)}, u32[]{:S(2)}, u32[]{:S(2)}) collective-permute-start(f32[224,128]{1,0:T(8,128)S(1)} %get-tuple-element.270), channel_id=1, source_target_pairs={{4,0},{8,4},{12,8},{16,12},{20,16},{24,20},{28,24},{5,1},{9,5},{13... | collective-permute-start | bytes 344072 | tf_op jit(solution)/shard_map/ppermute | solution.py:16
  (21 other events, 102.7 us)
where the time goes:
time: 198 us; the launch traced here: 195 us
  local copies, waits for them, and re-layouts  64 us (32%)
  starting transfers between devices  53.2 us (27%)
  waiting for transfers between devices  42.1 us (21%)
  other arithmetic  18.3 us (9%)
  matrix products  11.7 us (6%)
  between operations  4.86 us (2%)
    ppermute x20, starting transfers between devices, shifted(): return lax.ppermute(block, axis, route)  47 us
    ppermute x20, waiting for transfers between devices, shifted(): return lax.ppermute(block, axis, route)  32.1 us
    unnamed x118, local copies, waits for them, and re-layouts  20.5 us
    dot_general x16, matrix products, multiply_pair(): jnp.dot(operands[0], operands[1], precision=lax.Precision.HIGHEST, prefer...  11.7 us
    gather x4, local copies, waits for them, and re-layouts, body(): multipliers = direction[slot_of_row] * row_sign  11.2 us
    gather x4, local copies, waits for them, and re-layouts, body(): residual = residual - face_sum(result[slot_map] * face_sign[:, None])  10.3 us
    ppermute x2, waiting for transfers between devices, from_behind(): return lax.ppermute(value, axis, pairs)  9.95 us
    ppermute x2, starting transfers between devices, from_behind(): return lax.ppermute(value, axis, pairs)  6.2 us
  transfers between devices with their start and end apart: 22, of which 8 were waited for; matrix products, arithmetic and copies ran while one was open for 13% of the time, Pallas kernels for 0%

commit v1 on v0

--- a/solution.py
+++ b/solution.py
@@ -20,23 +20,6 @@
     count = lax.axis_size(axis)
     pairs = [(source, (source + steps) % count) for source in range(count)]
     return lax.ppermute(value, axis, pairs)
-
-
-def multiply_pair(operands):
-    return jnp.dot(
-        operands[0],
-        operands[1],
-        precision=lax.Precision.HIGHEST,
-        preferred_element_type=jnp.float32,
-    )
-
-
-def empty_pair(operands):
-    return jnp.zeros((operands[0].shape[0], operands[1].shape[1]), jnp.float32)
-
-
-def tile_product(row_block, multipliers, active):
-    return lax.cond(active, multiply_pair, empty_pair, (row_block, multipliers))
 
 
 def along_x(part, offset):
@@ -76,9 +59,7 @@
     slot_map = slot_rows[0, 0]
     row_ids = jnp.arange(order_max, dtype=jnp.int32)
     face_sign = jnp.where(row_ids // (order_max // 4) % 2 == 0, -1.0, 1.0).astype(jnp.float32)
-    slot_of_row = jnp.zeros((order_max,), jnp.int32).at[slot_map].set(row_ids)
-    live_rows = (row_ids < order_now).astype(jnp.float32)[:, None]
-    row_sign = face_sign[slot_of_row][:, None] * live_rows
+    slot_scale = face_sign * (slot_map < order_now).astype(jnp.float32)
     homed = [
         from_behind(spill_block[slot_id], "gx", -(slot_id + 1) * hop_span) for slot_id in range(2)
     ]
@@ -90,6 +71,10 @@
                 plan_row[slot_id] == own_tiles + extra_id, homed[slot_id], 0.0
             )
         extra_rows.append(gathered)
+    operator = jnp.concatenate([own_block] + extra_rows, axis=0)
+    by_rows = jnp.take(operator, slot_map, axis=0)
+    by_cols = jnp.take(by_rows.T, slot_map, axis=0)
+    slot_op = (by_cols * slot_scale[:, None]).T * slot_scale[:, None]
     load = face_sum(gap[0, 0])
     centre = (high_bound + low_bound) / 2.0
     half_width = (high_bound - low_bound) / 2.0
@@ -100,25 +85,13 @@
     direction = residual / centre
     for step_id in range(ITERS):
         solution = solution + direction
-        multipliers = direction[slot_of_row] * row_sign
-        pieces = [
-            tile_product(
-                own_block[tile_id * tile_rows : (tile_id + 1) * tile_rows],
-                multipliers,
-                tile_id * tile_rows < order_now,
-            )
-            for tile_id in range(own_tiles)
-        ]
-        for apply_extra_id in range(2):
-            pieces.append(
-                tile_product(
-                    extra_rows[apply_extra_id],
-                    multipliers,
-                    (own_tiles + apply_extra_id) * tile_rows < order_now,
-                )
-            )
-        result = jnp.concatenate(pieces, axis=0) * live_rows
-        residual = residual - face_sum(result[slot_map] * face_sign[:, None])
+        local = jnp.dot(
+            slot_op,
+            direction,
+            precision=lax.Precision.HIGHEST,
+            preferred_element_type=jnp.float32,
+        )
+        residual = residual - face_sum(local)
         if step_id + 1 < ITERS:
             rho_next = 1.0 / (2.0 * sigma_value - rho_value)
             direction = rho_next * rho_value * direction + 2.0 * rho_next / half_width * residual

time: 198 us -> 152 us (0.77)
  the two profiles are of different devices: /device:TPU:0 before, /device:TPU:16 now
where the time goes in v1:
time: 152 us; the launch traced here: 151 us
  starting transfers between devices  56.6 us (37%)
  waiting for transfers between devices  38.6 us (25%)
  matrix products  24.9 us (16%)
  local copies, waits for them, and re-layouts  15.7 us (10%)
  other arithmetic  10.6 us (7%)
  between operations  4.41 us (3%)
    ppermute x20, starting transfers between devices, shifted(): return lax.ppermute(block, axis, route)  52.6 us
    ppermute x20, waiting for transfers between devices, shifted(): return lax.ppermute(block, axis, route)  38.6 us
    dot_general x4, matrix products, body(): jnp.dot(slot_op, direction, precision=lax.Precision.HIGHEST, preferred_el...  24.9 us
    gather x1, local copies, waits for them, and re-layouts, body(): by_rows = jnp.take(operator, slot_map, axis=0)  4.23 us
    gather x1, local copies, waits for them, and re-layouts, body(): by_cols = jnp.take(by_rows.T, slot_map, axis=0)  4.23 us
    ppermute x2, starting transfers between devices, from_behind(): return lax.ppermute(value, axis, pairs)  3.99 us
    transpose x1, other arithmetic, body(): by_cols = jnp.take(by_rows.T, slot_map, axis=0)  3.85 us
    transpose x1, local copies, waits for them, and re-layouts, body(): by_cols = jnp.take(by_rows.T, slot_map, axis=0)  3.44 us
  transfers between devices with their start and end apart: 22, of which 9 were waited for; matrix products, arithmetic and copies ran while one was open for 5% of the time, Pallas kernels for 0%

profile of v1, /device:TPU:16, one launch (start us, length us, event | category | flops | bytes accessed | tf_op | source)
XLA Modules:
  0.0 150.8 jit_solution(14768318938259396315)
XLA Ops:
  0.6 1.2 slice_bitcast_fusion.1
  2.4 3.5 %collective-permute-start.5 = (f32[128,896]{1,0:T(8,128)S(1)}, f32[128,896]{1,0:T(8,128)S(1)}, u32[]{:S(2)}, u32[]{:S(2)}) collective-permute-start(f32[128,896]{1,0:T(8,128)S(1)} %get-tuple-element.6), channel_id=1, source_target_pairs={{0,16},{4,20},{8,24},{12,28},{16,0},{20,4},{24,8},{28,12},{1,17},{... | collective-permute-start | bytes 1376264 | tf_op jit(solution)/shard_map/ppermute | solution.py:22
  5.8 1.1 slice_bitcast_fusion.4
  6.9 1.9 %collective-permute-start = (f32[224,128]{1,0:T(8,128)S(1)}, f32[224,128]{1,0:T(8,128)S(1)}, u32[]{:S(2)}, u32[]{:S(2)}) collective-permute-start(f32[224,128]{1,0:T(8,128)S(1)} %get-tuple-element.43), channel_id=1, source_target_pairs={{0,4},{4,8},{8,12},{12,16},{16,20},{20,24},{24,28},{1,5},{5,9},{9,... | collective-permute-start | bytes 344072 | tf_op jit(solution)/shard_map/ppermute | solution.py:16
  8.9 3.6 %collective-permute-start.1 = (f32[224,128]{1,0:T(8,128)S(1)}, f32[224,128]{1,0:T(8,128)S(1)}, u32[]{:S(2)}, u32[]{:S(2)}) collective-permute-start(f32[224,128]{1,0:T(8,128)S(1)} %get-tuple-element.44), channel_id=1, source_target_pairs={{4,0},{8,4},{12,8},{16,12},{20,16},{24,20},{28,24},{5,1},{9,5},{13... | collective-permute-start | bytes 344072 | tf_op jit(solution)/shard_map/ppermute | solution.py:16
  12.5 3.4 %collective-permute-start.2 = (f32[224,128]{1,0:T(8,128)S(1)}, f32[224,128]{1,0:T(8,128)S(1)}, u32[]{:S(2)}, u32[]{:S(2)}) collective-permute-start(f32[224,128]{1,0:T(8,128)S(1)} %get-tuple-element.45), channel_id=1, source_target_pairs={{0,1},{1,2},{2,3},{4,5},{5,6},{6,7},{8,9},{9,10},{10,11},{12,13},{... | collective-permute-start | bytes 344072 | tf_op jit(solution)/shard_map/ppermute | solution.py:16
  15.9 0.7 reduce
  17.5 0.6 select_select_fusion
  18.1 0.6 compare_and_fusion
  18.7 17.6 %collective-permute-done = f32[224,128]{1,0:T(8,128)S(1)} collective-permute-done((f32[224,128]{1,0:T(8,128)S(1)}, f32[224,128]{1,0:T(8,128)S(1)}, u32[]{:S(2)}, u32[]{:S(2)}) %collective-permute-start) | collective-permute-done | bytes 114720 | tf_op jit(solution)/shard_map/ppermute | solution.py:16
  36.3 1.3 collective-permute-start.3
  37.6 1.3 fusion.49
  41.5 0.6 pad_clamp_fusion
  42.1 0.9 collective-permute-done.3
  43.0 1.8 %fusion.36 = (f32[224,128]{1,0:T(8,128)S(1)}, f32[224,128]{1,0:T(8,128)S(1)}, f32[224,128]{1,0:T(8,128)S(1)}, f32[224,128]{1,0:T(8,128)}) fusion(f32[224,128]{1,0:T(8,128)S(1)} %collective-permute-done, f32[1,1,896,128]{3,2,1,0:T(8,128)} %param.8, f32[224,128]{1,0:T(8,128)S(1)} %collective-permute-done.3, f32[224,128]{1,0:T(8,128)S(1)} %collective-permute-done.2, ...), kind=kLoop, calls=%fused_computation.75 | loop fusion | flops 114688 | bytes 1376256 | tf_op jit(solution)/shard_map/add | solution.py:41
  45.0 4.2 %gather_fusion = f32[896,896]{1,0:T(8,128)} fusion(f32[896,896]{1,0:T(8,128)S(1)} %pad_maximum_fusion, s32[1024]{0:T(1024)} %pad_clamp_fusion), kind=kCustom, calls=%fused_computation.clone | custom fusion | bytes 6426112 | tf_op jit(solution)/shard_map/jit(_take)/gather | solution.py:75
  49.3 3.9 %select_bitcast_fusion = f32[896,896]{0,1:T(8,128)} fusion(f32[896,896]{1,0:T(8,128)} %gather_fusion, pred[896]{0:T(1024)(128)(4,1)} %compare_and_fusion), kind=kLoop, calls=%fused_computation.5 | loop fusion | flops 802816 | bytes 6423424 | tf_op jit(solution)/shard_map/transpose | solution.py:76
  53.1 3.4 %copy.8 = f32[896,896]{1,0:T(8,128)S(1)} copy(f32[896,896]{0,1:T(8,128)} %select_bitcast_fusion) | data formatting | bytes 6422528 | tf_op jit(solution)/shard_map/transpose | solution.py:76
  56.6 4.2 %gather_fusion.1 = f32[896,896]{1,0:T(8,128)} fusion(f32[896,896]{1,0:T(8,128)S(1)} %copy.8, s32[1024]{0:T(1024)} %pad_clamp_fusion), kind=kCustom, calls=%fused_computation.1.clone | custom fusion | bytes 6426112 | tf_op jit(solution)/shard_map/jit(_take)/gather | solution.py:76
  60.8 7.7 %fusion.12 = f32[896,128]{1,0:T(8,128)S(1)} fusion(f32[224,128]{1,0:T(8,128)S(1)} %get-tuple-element.40, f32[224,128]{1,0:T(8,128)S(1)} %get-tuple-element.41, f32[224,128]{1,0:T(8,128)} %get-tuple-element.42, f32[224,128]{1,0:T(8,128)S(1)} %get-tuple-element.39, f32[896,896]{1,0:T(8,128)} %gather_fusion.1, f32[896]{0:T(1024)} %select_select_fusion, ...), kind=kOutput, calls=%fused_computation.28 | convolution fusion | flops 1235992576 | bytes 4133248 | tf_op jit(solution)/shard_map/dot_general | solution.py:88
  68.5 1.9 %collective-permute-start.6 = (f32[224,128]{1,0:T(8,128)S(1)}, f32[224,128]{1,0:T(8,128)S(1)}, u32[]{:S(2)}, u32[]{:S(2)}) collective-permute-start(f32[224,128]{1,0:T(8,128)S(1)} %get-tuple-element.35), channel_id=1, source_target_pairs={{0,4},{4,8},{8,12},{12,16},{16,20},{20,24},{24,28},{1,5},{5,9},{9,... | collective-permute-start | bytes 344072 | tf_op jit(solution)/shard_map/ppermute | solution.py:16
  70.5 3.6 %collective-permute-start.7 = (f32[224,128]{1,0:T(8,128)S(1)}, f32[224,128]{1,0:T(8,128)S(1)}, u32[]{:S(2)}, u32[]{:S(2)}) collective-permute-start(f32[224,128]{1,0:T(8,128)S(1)} %get-tuple-element.38), channel_id=1, source_target_pairs={{4,0},{8,4},{12,8},{16,12},{20,16},{24,20},{28,24},{5,1},{9,5},{13... | collective-permute-start | bytes 344072 | tf_op jit(solution)/shard_map/ppermute | solution.py:16
  74.1 4.3 %collective-permute-start.8 = (f32[224,128]{1,0:T(8,128)S(1)}, f32[224,128]{1,0:T(8,128)S(1)}, u32[]{:S(2)}, u32[]{:S(2)}) collective-permute-start(f32[224,128]{1,0:T(8,128)S(1)} %get-tuple-element.36), channel_id=1, source_target_pairs={{0,1},{1,2},{2,3},{4,5},{5,6},{6,7},{8,9},{9,10},{10,11},{12,13},{... | collective-permute-start | bytes 344072 | tf_op jit(solution)/shard_map/ppermute | solution.py:16
  78.4 1.5 collective-permute-start.9
  79.9 0.8 collective-permute-done.8
  80.8 4.4 %collective-permute-done.9 = f32[224,128]{1,0:T(8,128)S(1)} collective-permute-done((f32[224,128]{1,0:T(8,128)S(1)}, f32[224,128]{1,0:T(8,128)S(1)}, u32[]{:S(2)}, u32[]{:S(2)}) %collective-permute-start.9) | collective-permute-done | bytes 114720 | tf_op jit(solution)/shard_map/ppermute | solution.py:16
  85.2 5.7 %fusion.40 = f32[896,128]{1,0:T(8,128)S(1)} fusion(f32[224,128]{1,0:T(8,128)S(1)} %get-tuple-element.40, f32[224,128]{1,0:T(8,128)S(1)} %get-tuple-element.41, f32[224,128]{1,0:T(8,128)S(1)} %copy-done.2, f32[224,128]{1,0:T(8,128)S(1)} %get-tuple-element.39, f32[224,128]{1,0:T(8,128)S(1)} %get-tuple-element.34, f32[224,128]{1,0:T(8,128)S(1)} %get-tuple-element.33, ...), kind=kOutput, calls=%fused_computation.91 | convolution fusion | flops 1236680704 | bytes 4592000 | tf_op jit(solution)/shard_map/dot_general | solution.py:88
  90.9 1.9 %collective-permute-start.10 = (f32[224,128]{1,0:T(8,128)S(1)}, f32[224,128]{1,0:T(8,128)S(1)}, u32[]{:S(2)}, u32[]{:S(2)}) collective-permute-start(f32[224,128]{1,0:T(8,128)S(1)} %get-tuple-element.27), channel_id=1, source_target_pairs={{0,4},{4,8},{8,12},{12,16},{16,20},{20,24},{24,28},{1,5},{5,9},{9,... | collective-permute-start | bytes 344072 | tf_op jit(solution)/shard_map/ppermute | solution.py:16
  92.9 3.6 %collective-permute-start.11 = (f32[224,128]{1,0:T(8,128)S(1)}, f32[224,128]{1,0:T(8,128)S(1)}, u32[]{:S(2)}, u32[]{:S(2)}) collective-permute-start(f32[224,128]{1,0:T(8,128)S(1)} %get-tuple-element.30), channel_id=1, source_target_pairs={{4,0},{8,4},{12,8},{16,12},{20,16},{24,20},{28,24},{5,1},{9,5},{13... | collective-permute-start | bytes 344072 | tf_op jit(solution)/shard_map/ppermute | solution.py:16
  96.5 4.6 %collective-permute-start.12 = (f32[224,128]{1,0:T(8,128)S(1)}, f32[224,128]{1,0:T(8,128)S(1)}, u32[]{:S(2)}, u32[]{:S(2)}) collective-permute-start(f32[224,128]{1,0:T(8,128)S(1)} %get-tuple-element.28), channel_id=1, source_target_pairs={{0,1},{1,2},{2,3},{4,5},{5,6},{6,7},{8,9},{9,10},{10,11},{12,13},{... | collective-permute-start | bytes 344072 | tf_op jit(solution)/shard_map/ppermute | solution.py:16
  101.1 1.3 collective-permute-start.13
  102.4 1.0 collective-permute-done.12
  103.4 4.3 %collective-permute-done.13 = f32[224,128]{1,0:T(8,128)S(1)} collective-permute-done((f32[224,128]{1,0:T(8,128)S(1)}, f32[224,128]{1,0:T(8,128)S(1)}, u32[]{:S(2)}, u32[]{:S(2)}) %collective-permute-start.13) | collective-permute-done | bytes 114720 | tf_op jit(solution)/shard_map/ppermute | solution.py:16
  107.8 5.8 %fusion.14 = f32[896,128]{1,0:T(8,128)S(1)} fusion(f32[224,128]{1,0:T(8,128)S(1)} %get-tuple-element.26, f32[224,128]{1,0:T(8,128)S(1)} %get-tuple-element.25, f32[224,128]{1,0:T(8,128)S(1)} %get-tuple-element.24, f32[224,128]{1,0:T(8,128)S(1)} %get-tuple-element.23, f32[224,128]{1,0:T(8,128)S(1)} %get-tuple-element.34, ...), kind=kOutput, calls=%fused_computation.34 | convolution fusion | flops 1237483520 | bytes 5050752 | tf_op jit(solution)/shard_map/dot_general | solution.py:88
  113.6 1.9 %collective-permute-start.14 = (f32[224,128]{1,0:T(8,128)S(1)}, f32[224,128]{1,0:T(8,128)S(1)}, u32[]{:S(2)}, u32[]{:S(2)}) collective-permute-start(f32[224,128]{1,0:T(8,128)S(1)} %get-tuple-element.19), channel_id=1, source_target_pairs={{0,4},{4,8},{8,12},{12,16},{16,20},{20,24},{24,28},{1,5},{5,9},{9,... | collective-permute-start | bytes 344072 | tf_op jit(solution)/shard_map/ppermute | solution.py:16
  115.6 3.6 %collective-permute-start.15 = (f32[224,128]{1,0:T(8,128)S(1)}, f32[224,128]{1,0:T(8,128)S(1)}, u32[]{:S(2)}, u32[]{:S(2)}) collective-permute-start(f32[224,128]{1,0:T(8,128)S(1)} %get-tuple-element.22), channel_id=1, source_target_pairs={{4,0},{8,4},{12,8},{16,12},{20,16},{24,20},{28,24},{5,1},{9,5},{13... | collective-permute-start | bytes 344072 | tf_op jit(solution)/shard_map/ppermute | solution.py:16
  119.2 2.8 %collective-permute-start.16 = (f32[224,128]{1,0:T(8,128)S(1)}, f32[224,128]{1,0:T(8,128)S(1)}, u32[]{:S(2)}, u32[]{:S(2)}) collective-permute-start(f32[224,128]{1,0:T(8,128)S(1)} %get-tuple-element.20), channel_id=1, source_target_pairs={{0,1},{1,2},{2,3},{4,5},{5,6},{6,7},{8,9},{9,10},{10,11},{12,13},{... | collective-permute-start | bytes 344072 | tf_op jit(solution)/shard_map/ppermute | solution.py:16
  122.0 1.5 %collective-permute-start.17 = (f32[224,128]{1,0:T(8,128)S(1)}, f32[224,128]{1,0:T(8,128)S(1)}, u32[]{:S(2)}, u32[]{:S(2)}) collective-permute-start(f32[224,128]{1,0:T(8,128)S(1)} %get-tuple-element.21), channel_id=1, source_target_pairs={{1,0},{2,1},{3,2},{5,4},{6,5},{7,6},{9,8},{10,9},{11,10},{13,12},{... | collective-permute-start | bytes 344072 | tf_op jit(solution)/shard_map/ppermute | solution.py:16
  123.6 0.8 collective-permute-done.16
  124.4 4.3 %collective-permute-done.17 = f32[224,128]{1,0:T(8,128)S(1)} collective-permute-done((f32[224,128]{1,0:T(8,128)S(1)}, f32[224,128]{1,0:T(8,128)S(1)}, u32[]{:S(2)}, u32[]{:S(2)}) %collective-permute-start.17) | collective-permute-done | bytes 114720 | tf_op jit(solution)/shard_map/ppermute | solution.py:16
  128.8 5.8 %fusion.3 = f32[896,128]{1,0:T(8,128)S(1)} fusion(f32[224,128]{1,0:T(8,128)S(1)} %get-tuple-element.18, f32[224,128]{1,0:T(8,128)S(1)} %get-tuple-element.17, f32[224,128]{1,0:T(8,128)S(1)} %get-tuple-element.16, f32[224,128]{1,0:T(8,128)S(1)} %get-tuple-element.15, f32[224,128]{1,0:T(8,128)S(1)} %get-tuple-element.26, ...), kind=kOutput, calls=%fused_computation.16 | convolution fusion | flops 1238286336 | bytes 5509504 | tf_op jit(solution)/shard_map/dot_general | solution.py:88
  134.6 1.9 %collective-permute-start.18 = (f32[224,128]{1,0:T(8,128)S(1)}, f32[224,128]{1,0:T(8,128)S(1)}, u32[]{:S(2)}, u32[]{:S(2)}) collective-permute-start(f32[224,128]{1,0:T(8,128)S(1)} %get-tuple-element.11), channel_id=1, source_target_pairs={{0,4},{4,8},{8,12},{12,16},{16,20},{20,24},{24,28},{1,5},{5,9},{9,... | collective-permute-start | bytes 344072 | tf_op jit(solution)/shard_map/ppermute | solution.py:16
  136.5 3.6 %collective-permute-start.19 = (f32[224,128]{1,0:T(8,128)S(1)}, f32[224,128]{1,0:T(8,128)S(1)}, u32[]{:S(2)}, u32[]{:S(2)}) collective-permute-start(f32[224,128]{1,0:T(8,128)S(1)} %get-tuple-element.14), channel_id=1, source_target_pairs={{4,0},{8,4},{12,8},{16,12},{20,16},{24,20},{28,24},{5,1},{9,5},{13... | collective-permute-start | bytes 344072 | tf_op jit(solution)/shard_map/ppermute | solution.py:16
  140.2 2.8 %collective-permute-start.20 = (f32[224,128]{1,0:T(8,128)S(1)}, f32[224,128]{1,0:T(8,128)S(1)}, u32[]{:S(2)}, u32[]{:S(2)}) collective-permute-start(f32[224,128]{1,0:T(8,128)S(1)} %get-tuple-element.12), channel_id=1, source_target_pairs={{0,1},{1,2},{2,3},{4,5},{5,6},{6,7},{8,9},{9,10},{10,11},{12,13},{... | collective-permute-start | bytes 344072 | tf_op jit(solution)/shard_map/ppermute | solution.py:16
  143.0 1.3 collective-permute-start.21
  144.3 1.0 add_add_fusion
  145.4 4.3 %collective-permute-done.21 = f32[224,128]{1,0:T(8,128)S(1)} collective-permute-done((f32[224,128]{1,0:T(8,128)S(1)}, f32[224,128]{1,0:T(8,128)S(1)}, u32[]{:S(2)}, u32[]{:S(2)}) %collective-permute-start.21) | collective-permute-done | bytes 114720 | tf_op jit(solution)/shard_map/ppermute | solution.py:16
  149.8 1.0 maximum_subtract_fusion.6
  (35 shorter events, 1.2 us)
Async XLA Ops:
  1.9 42.9 %collective-permute-start.4 = (f32[128,896]{1,0:T(8,128)S(1)}, f32[128,896]{1,0:T(8,128)S(1)}, u32[]{:S(2)}, u32[]{:S(2)}) collective-permute-start(f32[128,896]{1,0:T(8,128)S(1)} %get-tuple-element.5), channel_id=1, source_target_pairs={{0,24},{4,28},{8,0},{12,4},{16,8},{20,12},{24,16},{28,20},{1,25},{... | collective-permute-start | bytes 1376264 | tf_op jit(solution)/shard_map/ppermute | solution.py:22
  2.4 42.4 %collective-permute-start.5 = (f32[128,896]{1,0:T(8,128)S(1)}, f32[128,896]{1,0:T(8,128)S(1)}, u32[]{:S(2)}, u32[]{:S(2)}) collective-permute-start(f32[128,896]{1,0:T(8,128)S(1)} %get-tuple-element.6), channel_id=1, source_target_pairs={{0,16},{4,20},{8,24},{12,28},{16,0},{20,4},{24,8},{28,12},{1,17},{... | collective-permute-start | bytes 1376264 | tf_op jit(solution)/shard_map/ppermute | solution.py:22
  6.9 29.3 %collective-permute-start = (f32[224,128]{1,0:T(8,128)S(1)}, f32[224,128]{1,0:T(8,128)S(1)}, u32[]{:S(2)}, u32[]{:S(2)}) collective-permute-start(f32[224,128]{1,0:T(8,128)S(1)} %get-tuple-element.43), channel_id=1, source_target_pairs={{0,4},{4,8},{8,12},{12,16},{16,20},{20,24},{24,28},{1,5},{5,9},{9,... | collective-permute-start | bytes 344072 | tf_op jit(solution)/shard_map/ppermute | solution.py:16
  8.9 33.2 %collective-permute-start.1 = (f32[224,128]{1,0:T(8,128)S(1)}, f32[224,128]{1,0:T(8,128)S(1)}, u32[]{:S(2)}, u32[]{:S(2)}) collective-permute-start(f32[224,128]{1,0:T(8,128)S(1)} %get-tuple-element.44), channel_id=1, source_target_pairs={{4,0},{8,4},{12,8},{16,12},{20,16},{24,20},{28,24},{5,1},{9,5},{13... | collective-permute-start | bytes 344072 | tf_op jit(solution)/shard_map/ppermute | solution.py:16
  12.5 29.6 %collective-permute-start.2 = (f32[224,128]{1,0:T(8,128)S(1)}, f32[224,128]{1,0:T(8,128)S(1)}, u32[]{:S(2)}, u32[]{:S(2)}) collective-permute-start(f32[224,128]{1,0:T(8,128)S(1)} %get-tuple-element.45), channel_id=1, source_target_pairs={{0,1},{1,2},{2,3},{4,5},{5,6},{6,7},{8,9},{9,10},{10,11},{12,13},{... | collective-permute-start | bytes 344072 | tf_op jit(solution)/shard_map/ppermute | solution.py:16
  16.6 28.2 %copy-start.1 = (f32[1,1,640,896]{3,2,1,0:T(8,128)S(1)}, f32[1,1,640,896]{3,2,1,0:T(8,128)}, u32[]{:S(2)}) copy-start(f32[1,1,640,896]{3,2,1,0:T(8,128)} %param.9) | copy-start | bytes 6881284
  36.3 6.7 %collective-permute-start.3 = (f32[224,128]{1,0:T(8,128)S(1)}, f32[224,128]{1,0:T(8,128)S(1)}, u32[]{:S(2)}, u32[]{:S(2)}) collective-permute-start(f32[224,128]{1,0:T(8,128)S(1)} %get-tuple-element.46), channel_id=1, source_target_pairs={{1,0},{2,1},{3,2},{5,4},{6,5},{7,6},{9,8},{10,9},{11,10},{13,12},{... | collective-permute-start | bytes 344072 | tf_op jit(solution)/shard_map/ppermute | solution.py:16
  60.8 24.4 %copy-start = (f32[896,896]{1,0:T(8,128)S(1)}, f32[896,896]{1,0:T(8,128)}, u32[]{:S(2)}) copy-start(f32[896,896]{1,0:T(8,128)} %gather_fusion.1) | copy-start | bytes 9633796
  60.8 24.4 %copy-start.2 = (f32[224,128]{1,0:T(8,128)S(1)}, f32[224,128]{1,0:T(8,128)}, u32[]{:S(2)}) copy-start(f32[224,128]{1,0:T(8,128)} %get-tuple-element.42) | copy-start | bytes 344068
  60.8 24.4 %copy-start.3 = (f32[896]{0:T(1024)S(1)}, f32[896]{0:T(1024)}, u32[]{:S(2)}) copy-start(f32[896]{0:T(1024)} %select_select_fusion) | copy-start | bytes 10756
  60.8 24.4 %copy-start.4 = (pred[896]{0:T(1024)(128)(4,1)S(1)}, pred[896]{0:T(1024)(128)(4,1)}, u32[]{:S(2)}) copy-start(pred[896]{0:T(1024)(128)(4,1)} %compare_and_fusion) | copy-start | bytes 2692
  68.5 11.4 %collective-permute-start.6 = (f32[224,128]{1,0:T(8,128)S(1)}, f32[224,128]{1,0:T(8,128)S(1)}, u32[]{:S(2)}, u32[]{:S(2)}) collective-permute-start(f32[224,128]{1,0:T(8,128)S(1)} %get-tuple-element.35), channel_id=1, source_target_pairs={{0,4},{4,8},{8,12},{12,16},{16,20},{20,24},{24,28},{1,5},{5,9},{9,... | collective-permute-start | bytes 344072 | tf_op jit(solution)/shard_map/ppermute | solution.py:16
  70.5 9.5 %collective-permute-start.7 = (f32[224,128]{1,0:T(8,128)S(1)}, f32[224,128]{1,0:T(8,128)S(1)}, u32[]{:S(2)}, u32[]{:S(2)}) collective-permute-start(f32[224,128]{1,0:T(8,128)S(1)} %get-tuple-element.38), channel_id=1, source_target_pairs={{4,0},{8,4},{12,8},{16,12},{20,16},{24,20},{28,24},{5,1},{9,5},{13... | collective-permute-start | bytes 344072 | tf_op jit(solution)/shard_map/ppermute | solution.py:16
  74.1 6.7 %collective-permute-start.8 = (f32[224,128]{1,0:T(8,128)S(1)}, f32[224,128]{1,0:T(8,128)S(1)}, u32[]{:S(2)}, u32[]{:S(2)}) collective-permute-start(f32[224,128]{1,0:T(8,128)S(1)} %get-tuple-element.36), channel_id=1, source_target_pairs={{0,1},{1,2},{2,3},{4,5},{5,6},{6,7},{8,9},{9,10},{10,11},{12,13},{... | collective-permute-start | bytes 344072 | tf_op jit(solution)/shard_map/ppermute | solution.py:16
  78.4 6.7 %collective-permute-start.9 = (f32[224,128]{1,0:T(8,128)S(1)}, f32[224,128]{1,0:T(8,128)S(1)}, u32[]{:S(2)}, u32[]{:S(2)}) collective-permute-start(f32[224,128]{1,0:T(8,128)S(1)} %get-tuple-element.37), channel_id=1, source_target_pairs={{1,0},{2,1},{3,2},{5,4},{6,5},{7,6},{9,8},{10,9},{11,10},{13,12},{... | collective-permute-start | bytes 344072 | tf_op jit(solution)/shard_map/ppermute | solution.py:16
  90.9 11.4 %collective-permute-start.10 = (f32[224,128]{1,0:T(8,128)S(1)}, f32[224,128]{1,0:T(8,128)S(1)}, u32[]{:S(2)}, u32[]{:S(2)}) collective-permute-start(f32[224,128]{1,0:T(8,128)S(1)} %get-tuple-element.27), channel_id=1, source_target_pairs={{0,4},{4,8},{8,12},{12,16},{16,20},{20,24},{24,28},{1,5},{5,9},{9,... | collective-permute-start | bytes 344072 | tf_op jit(solution)/shard_map/ppermute | solution.py:16
  92.9 9.5 %collective-permute-start.11 = (f32[224,128]{1,0:T(8,128)S(1)}, f32[224,128]{1,0:T(8,128)S(1)}, u32[]{:S(2)}, u32[]{:S(2)}) collective-permute-start(f32[224,128]{1,0:T(8,128)S(1)} %get-tuple-element.30), channel_id=1, source_target_pairs={{4,0},{8,4},{12,8},{16,12},{20,16},{24,20},{28,24},{5,1},{9,5},{13... | collective-permute-start | bytes 344072 | tf_op jit(solution)/shard_map/ppermute | solution.py:16
  96.5 6.9 %collective-permute-start.12 = (f32[224,128]{1,0:T(8,128)S(1)}, f32[224,128]{1,0:T(8,128)S(1)}, u32[]{:S(2)}, u32[]{:S(2)}) collective-permute-start(f32[224,128]{1,0:T(8,128)S(1)} %get-tuple-element.28), channel_id=1, source_target_pairs={{0,1},{1,2},{2,3},{4,5},{5,6},{6,7},{8,9},{9,10},{10,11},{12,13},{... | collective-permute-start | bytes 344072 | tf_op jit(solution)/shard_map/ppermute | solution.py:16
  101.1 6.7 %collective-permute-start.13 = (f32[224,128]{1,0:T(8,128)S(1)}, f32[224,128]{1,0:T(8,128)S(1)}, u32[]{:S(2)}, u32[]{:S(2)}) collective-permute-start(f32[224,128]{1,0:T(8,128)S(1)} %get-tuple-element.29), channel_id=1, source_target_pairs={{1,0},{2,1},{3,2},{5,4},{6,5},{7,6},{9,8},{10,9},{11,10},{13,12},{... | collective-permute-start | bytes 344072 | tf_op jit(solution)/shard_map/ppermute | solution.py:16
  113.6 9.9 %collective-permute-start.14 = (f32[224,128]{1,0:T(8,128)S(1)}, f32[224,128]{1,0:T(8,128)S(1)}, u32[]{:S(2)}, u32[]{:S(2)}) collective-permute-start(f32[224,128]{1,0:T(8,128)S(1)} %get-tuple-element.19), channel_id=1, source_target_pairs={{0,4},{4,8},{8,12},{12,16},{16,20},{20,24},{24,28},{1,5},{5,9},{9,... | collective-permute-start | bytes 344072 | tf_op jit(solution)/shard_map/ppermute | solution.py:16
  115.6 8.0 %collective-permute-start.15 = (f32[224,128]{1,0:T(8,128)S(1)}, f32[224,128]{1,0:T(8,128)S(1)}, u32[]{:S(2)}, u32[]{:S(2)}) collective-permute-start(f32[224,128]{1,0:T(8,128)S(1)} %get-tuple-element.22), channel_id=1, source_target_pairs={{4,0},{8,4},{12,8},{16,12},{20,16},{24,20},{28,24},{5,1},{9,5},{13... | collective-permute-start | bytes 344072 | tf_op jit(solution)/shard_map/ppermute | solution.py:16
  119.2 5.2 %collective-permute-start.16 = (f32[224,128]{1,0:T(8,128)S(1)}, f32[224,128]{1,0:T(8,128)S(1)}, u32[]{:S(2)}, u32[]{:S(2)}) collective-permute-start(f32[224,128]{1,0:T(8,128)S(1)} %get-tuple-element.20), channel_id=1, source_target_pairs={{0,1},{1,2},{2,3},{4,5},{5,6},{6,7},{8,9},{9,10},{10,11},{12,13},{... | collective-permute-start | bytes 344072 | tf_op jit(solution)/shard_map/ppermute | solution.py:16
  122.0 6.7 %collective-permute-start.17 = (f32[224,128]{1,0:T(8,128)S(1)}, f32[224,128]{1,0:T(8,128)S(1)}, u32[]{:S(2)}, u32[]{:S(2)}) collective-permute-start(f32[224,128]{1,0:T(8,128)S(1)} %get-tuple-element.21), channel_id=1, source_target_pairs={{1,0},{2,1},{3,2},{5,4},{6,5},{7,6},{9,8},{10,9},{11,10},{13,12},{... | collective-permute-start | bytes 344072 | tf_op jit(solution)/shard_map/ppermute | solution.py:16
  134.6 10.7 %collective-permute-start.18 = (f32[224,128]{1,0:T(8,128)S(1)}, f32[224,128]{1,0:T(8,128)S(1)}, u32[]{:S(2)}, u32[]{:S(2)}) collective-permute-start(f32[224,128]{1,0:T(8,128)S(1)} %get-tuple-element.11), channel_id=1, source_target_pairs={{0,4},{4,8},{8,12},{12,16},{16,20},{20,24},{24,28},{1,5},{5,9},{9,... | collective-permute-start | bytes 344072 | tf_op jit(solution)/shard_map/ppermute | solution.py:16
  136.5 8.8 %collective-permute-start.19 = (f32[224,128]{1,0:T(8,128)S(1)}, f32[224,128]{1,0:T(8,128)S(1)}, u32[]{:S(2)}, u32[]{:S(2)}) collective-permute-start(f32[224,128]{1,0:T(8,128)S(1)} %get-tuple-element.14), channel_id=1, source_target_pairs={{4,0},{8,4},{12,8},{16,12},{20,16},{24,20},{28,24},{5,1},{9,5},{13... | collective-permute-start | bytes 344072 | tf_op jit(solution)/shard_map/ppermute | solution.py:16
  140.2 5.2 %collective-permute-start.20 = (f32[224,128]{1,0:T(8,128)S(1)}, f32[224,128]{1,0:T(8,128)S(1)}, u32[]{:S(2)}, u32[]{:S(2)}) collective-permute-start(f32[224,128]{1,0:T(8,128)S(1)} %get-tuple-element.12), channel_id=1, source_target_pairs={{0,1},{1,2},{2,3},{4,5},{5,6},{6,7},{8,9},{9,10},{10,11},{12,13},{... | collective-permute-start | bytes 344072 | tf_op jit(solution)/shard_map/ppermute | solution.py:16
  143.0 6.7 %collective-permute-start.21 = (f32[224,128]{1,0:T(8,128)S(1)}, f32[224,128]{1,0:T(8,128)S(1)}, u32[]{:S(2)}, u32[]{:S(2)}) collective-permute-start(f32[224,128]{1,0:T(8,128)S(1)} %get-tuple-element.13), channel_id=1, source_target_pairs={{1,0},{2,1},{3,2},{5,4},{6,5},{7,6},{9,8},{10,9},{11,10},{13,12},{... | collective-permute-start | bytes 344072 | tf_op jit(solution)/shard_map/ppermute | solution.py:16

commit v2 on v1

--- a/solution.py
+++ b/solution.py
@@ -47,6 +47,19 @@
     )
 
 
+def face_sum_parts(faces):
+    low_x, high_x, low_y, high_y = faces
+    return jnp.concatenate(
+        [
+            low_x + along_x(high_x, 1),
+            high_x + along_x(low_x, -1),
+            low_y + along_y(high_y, 1),
+            high_y + along_y(low_y, -1),
+        ],
+        axis=0,
+    )
+
+
 def body(gap, own_rows, spill_rows, tile_plan, orders, slot_rows):
     order_max = gap.shape[2]
     tile_rows = spill_rows.shape[3]
@@ -85,13 +98,17 @@
     direction = residual / centre
     for step_id in range(ITERS):
         solution = solution + direction
-        local = jnp.dot(
-            slot_op,
-            direction,
-            precision=lax.Precision.HIGHEST,
-            preferred_element_type=jnp.float32,
-        )
-        residual = residual - face_sum(local)
+        width = order_max // 4
+        faces = [
+            jnp.dot(
+                slot_op[face_id * width : (face_id + 1) * width],
+                direction,
+                precision=lax.Precision.HIGH,
+                preferred_element_type=jnp.float32,
+            )
+            for face_id in range(4)
+        ]
+        residual = residual - face_sum_parts(faces)
         if step_id + 1 < ITERS:
             rho_next = 1.0 / (2.0 * sigma_value - rho_value)
             direction = rho_next * rho_value * direction + 2.0 * rho_next / half_width * residual

time: 152 us -> 147 us (0.967)
  matrix products: 24.9 us -> 17.7 us
  other arithmetic: 10.6 us -> 13.3 us
    dot_general x4 -> x16, matrix products: 24.9 us -> 17.7 us  [body(): jnp.dot(slot_op[face_id * width:(face_id + 1) * width], direction, precis...]
    mul x0 -> x1, other arithmetic: none -> 2.36 us  [body(): slot_op = (by_cols * slot_scale[:, None]).T * slot_scale[:, None]]
  transfers between devices with their start and end apart: 22 -> 22, of which waited for: 9 -> 6; matrix products, arithmetic and copies ran while one was open for 5% -> 8% of each run, Pallas kernels for 0% -> 0%
where the time goes in v2:
time: 147 us; the launch traced here: 146 us
  starting transfers between devices  56.4 us (38%)
  waiting for transfers between devices  38.7 us (26%)
  matrix products  17.7 us (12%)
  local copies, waits for them, and re-layouts  15.5 us (11%)
  other arithmetic  13.3 us (9%)
  between operations  4.55 us (3%)
    ppermute x20, starting transfers between devices, shifted(): return lax.ppermute(block, axis, route)  52.4 us
    ppermute x20, waiting for transfers between devices, shifted(): return lax.ppermute(block, axis, route)  38.7 us
    dot_general x16, matrix products, body(): jnp.dot(slot_op[face_id * width:(face_id + 1) * width], direction, precis...  17.7 us
    gather x1, local copies, waits for them, and re-layouts, body(): by_rows = jnp.take(operator, slot_map, axis=0)  4.21 us
    gather x1, local copies, waits for them, and re-layouts, body(): by_cols = jnp.take(by_rows.T, slot_map, axis=0)  4.21 us
    ppermute x2, starting transfers between devices, from_behind(): return lax.ppermute(value, axis, pairs)  3.99 us
    transpose x1, other arithmetic, body(): by_cols = jnp.take(by_rows.T, slot_map, axis=0)  3.84 us
    transpose x1, local copies, waits for them, and re-layouts, body(): by_cols = jnp.take(by_rows.T, slot_map, axis=0)  3.44 us
  transfers between devices with their start and end apart: 22, of which 6 were waited for; matrix products, arithmetic and copies ran while one was open for 8% of the time, Pallas kernels for 0%

profile of v2, /device:TPU:16, one launch (start us, length us, event | category | flops | bytes accessed | tf_op | source)
XLA Modules:
  0.0 146.1 jit_solution(13949237207827298400)
XLA Ops:
  0.6 1.2 slice_bitcast_fusion.1
  2.4 3.5 %collective-permute-start.5 = (f32[128,896]{1,0:T(8,128)S(1)}, f32[128,896]{1,0:T(8,128)S(1)}, u32[]{:S(2)}, u32[]{:S(2)}) collective-permute-start(f32[128,896]{1,0:T(8,128)S(1)} %get-tuple-element.6), channel_id=1, source_target_pairs={{0,16},{4,20},{8,24},{12,28},{16,0},{20,4},{24,8},{28,12},{1,17},{... | collective-permute-start | bytes 1376264 | tf_op jit(solution)/shard_map/ppermute | solution.py:22
  5.8 1.1 slice_bitcast_fusion.4
  6.9 1.9 %collective-permute-start = (f32[224,128]{1,0:T(8,128)S(1)}, f32[224,128]{1,0:T(8,128)S(1)}, u32[]{:S(2)}, u32[]{:S(2)}) collective-permute-start(f32[224,128]{1,0:T(8,128)S(1)} %get-tuple-element.11), channel_id=1, source_target_pairs={{0,4},{4,8},{8,12},{12,16},{16,20},{20,24},{24,28},{1,5},{5,9},{9,... | collective-permute-start | bytes 344072 | tf_op jit(solution)/shard_map/ppermute | solution.py:16
  8.9 3.6 %collective-permute-start.1 = (f32[224,128]{1,0:T(8,128)S(1)}, f32[224,128]{1,0:T(8,128)S(1)}, u32[]{:S(2)}, u32[]{:S(2)}) collective-permute-start(f32[224,128]{1,0:T(8,128)S(1)} %get-tuple-element.12), channel_id=1, source_target_pairs={{4,0},{8,4},{12,8},{16,12},{20,16},{24,20},{28,24},{5,1},{9,5},{13... | collective-permute-start | bytes 344072 | tf_op jit(solution)/shard_map/ppermute | solution.py:16
  12.5 3.4 %collective-permute-start.2 = (f32[224,128]{1,0:T(8,128)S(1)}, f32[224,128]{1,0:T(8,128)S(1)}, u32[]{:S(2)}, u32[]{:S(2)}) collective-permute-start(f32[224,128]{1,0:T(8,128)S(1)} %get-tuple-element.13), channel_id=1, source_target_pairs={{0,1},{1,2},{2,3},{4,5},{5,6},{6,7},{8,9},{9,10},{10,11},{12,13},{... | collective-permute-start | bytes 344072 | tf_op jit(solution)/shard_map/ppermute | solution.py:16
  18.7 17.6 %collective-permute-done = f32[224,128]{1,0:T(8,128)S(1)} collective-permute-done((f32[224,128]{1,0:T(8,128)S(1)}, f32[224,128]{1,0:T(8,128)S(1)}, u32[]{:S(2)}, u32[]{:S(2)}) %collective-permute-start) | collective-permute-done | bytes 114720 | tf_op jit(solution)/shard_map/ppermute | solution.py:16
  36.3 1.3 collective-permute-start.3
  37.6 1.3 fusion.57
  43.0 1.8 %fusion.53 = (f32[224,128]{1,0:T(8,128)S(1)}, f32[224,128]{1,0:T(8,128)S(1)}, f32[224,128]{1,0:T(8,128)S(1)}, f32[224,128]{1,0:T(8,128)}) fusion(f32[224,128]{1,0:T(8,128)S(1)} %collective-permute-done, f32[1,1,896,128]{3,2,1,0:T(8,128)} %param.8, f32[224,128]{1,0:T(8,128)S(1)} %collective-permute-done.3, f32[224,128]{1,0:T(8,128)S(1)} %collective-permute-done.2, ...), kind=kLoop, calls=%fused_computation.93 | loop fusion | flops 114688 | bytes 1376256 | tf_op jit(solution)/shard_map/add | solution.py:41
  45.0 4.2 %gather_fusion = f32[896,896]{1,0:T(8,128)} fusion(f32[896,896]{1,0:T(8,128)S(1)} %pad_maximum_fusion, s32[1024]{0:T(1024)} %pad_clamp_fusion), kind=kCustom, calls=%fused_computation.clone | custom fusion | bytes 6426112 | tf_op jit(solution)/shard_map/jit(_take)/gather | solution.py:88
  49.3 3.8 %select_bitcast_fusion = f32[896,896]{0,1:T(8,128)} fusion(f32[896,896]{1,0:T(8,128)} %gather_fusion, pred[896]{0:T(1024)(128)(4,1)} %compare_and_fusion), kind=kLoop, calls=%fused_computation.6 | loop fusion | flops 802816 | bytes 6423424 | tf_op jit(solution)/shard_map/transpose | solution.py:89
  53.1 3.4 %copy.8 = f32[896,896]{1,0:T(8,128)S(1)} copy(f32[896,896]{0,1:T(8,128)} %select_bitcast_fusion) | data formatting | bytes 6422528 | tf_op jit(solution)/shard_map/transpose | solution.py:89
  56.6 4.2 %gather_fusion.1 = f32[896,896]{1,0:T(8,128)} fusion(f32[896,896]{1,0:T(8,128)S(1)} %copy.8, s32[1024]{0:T(1024)} %pad_clamp_fusion), kind=kCustom, calls=%fused_computation.1.clone | custom fusion | bytes 6426112 | tf_op jit(solution)/shard_map/jit(_take)/gather | solution.py:89
  60.8 2.4 %fusion.1 = f32[896,896]{0,1:T(8,128)S(1)} fusion(f32[896,896]{1,0:T(8,128)} %gather_fusion.1, f32[896]{0:T(1024)} %select_select_fusion, pred[896]{0:T(1024)(128)(4,1)} %compare_and_fusion), kind=kLoop, calls=%fused_computation.5 | loop fusion | flops 2408448 | bytes 6427008 | tf_op jit(solution)/shard_map/mul | solution.py:90
  63.1 1.2 fusion.24
  65.2 1.2 fusion.8
  66.4 1.9 %collective-permute-start.6 = (f32[224,128]{1,0:T(8,128)S(1)}, f32[224,128]{1,0:T(8,128)S(1)}, u32[]{:S(2)}, u32[]{:S(2)}) collective-permute-start(f32[224,128]{1,0:T(8,128)S(1)} %fusion.24), channel_id=1, source_target_pairs={{0,4},{4,8},{8,12},{12,16},{16,20},{20,24},{24,28},{1,5},{5,9},{9,... | collective-permute-start | bytes 344072 | tf_op jit(solution)/shard_map/ppermute | solution.py:16
  68.3 3.6 %collective-permute-start.7 = (f32[224,128]{1,0:T(8,128)S(1)}, f32[224,128]{1,0:T(8,128)S(1)}, u32[]{:S(2)}, u32[]{:S(2)}) collective-permute-start(f32[224,128]{1,0:T(8,128)S(1)} %fusion.32), channel_id=1, source_target_pairs={{4,0},{8,4},{12,8},{16,12},{20,16},{24,20},{28,24},{5,1},{9,5},{13... | collective-permute-start | bytes 344072 | tf_op jit(solution)/shard_map/ppermute | solution.py:16
  72.0 4.3 %collective-permute-start.8 = (f32[224,128]{1,0:T(8,128)S(1)}, f32[224,128]{1,0:T(8,128)S(1)}, u32[]{:S(2)}, u32[]{:S(2)}) collective-permute-start(f32[224,128]{1,0:T(8,128)S(1)} %fusion.8), channel_id=1, source_target_pairs={{0,1},{1,2},{2,3},{4,5},{5,6},{6,7},{8,9},{9,10},{10,11},{12,13},{... | collective-permute-start | bytes 344072 | tf_op jit(solution)/shard_map/ppermute | solution.py:16
  76.3 1.2 fusion.16
  77.5 1.3 collective-permute-start.9
  78.9 5.3 %collective-permute-done.9 = f32[224,128]{1,0:T(8,128)S(1)} collective-permute-done((f32[224,128]{1,0:T(8,128)S(1)}, f32[224,128]{1,0:T(8,128)S(1)}, u32[]{:S(2)}, u32[]{:S(2)}) %collective-permute-start.9) | collective-permute-done | bytes 114720 | tf_op jit(solution)/shard_map/ppermute | solution.py:16
  84.2 1.2 fusion.22
  86.3 1.2 fusion.6
  87.4 1.9 %collective-permute-start.10 = (f32[224,128]{1,0:T(8,128)S(1)}, f32[224,128]{1,0:T(8,128)S(1)}, u32[]{:S(2)}, u32[]{:S(2)}) collective-permute-start(f32[224,128]{1,0:T(8,128)S(1)} %fusion.22), channel_id=1, source_target_pairs={{0,4},{4,8},{8,12},{12,16},{16,20},{20,24},{24,28},{1,5},{5,9},{9,... | collective-permute-start | bytes 344072 | tf_op jit(solution)/shard_map/ppermute | solution.py:16
  89.4 3.6 %collective-permute-start.11 = (f32[224,128]{1,0:T(8,128)S(1)}, f32[224,128]{1,0:T(8,128)S(1)}, u32[]{:S(2)}, u32[]{:S(2)}) collective-permute-start(f32[224,128]{1,0:T(8,128)S(1)} %fusion.30), channel_id=1, source_target_pairs={{4,0},{8,4},{12,8},{16,12},{20,16},{24,20},{28,24},{5,1},{9,5},{13... | collective-permute-start | bytes 344072 | tf_op jit(solution)/shard_map/ppermute | solution.py:16
  93.0 4.8 %collective-permute-start.12 = (f32[224,128]{1,0:T(8,128)S(1)}, f32[224,128]{1,0:T(8,128)S(1)}, u32[]{:S(2)}, u32[]{:S(2)}) collective-permute-start(f32[224,128]{1,0:T(8,128)S(1)} %fusion.6), channel_id=1, source_target_pairs={{0,1},{1,2},{2,3},{4,5},{5,6},{6,7},{8,9},{9,10},{10,11},{12,13},{... | collective-permute-start | bytes 344072 | tf_op jit(solution)/shard_map/ppermute | solution.py:16
  97.8 1.2 fusion.14
  99.0 1.3 collective-permute-start.13
  100.4 5.3 %collective-permute-done.13 = f32[224,128]{1,0:T(8,128)S(1)} collective-permute-done((f32[224,128]{1,0:T(8,128)S(1)}, f32[224,128]{1,0:T(8,128)S(1)}, u32[]{:S(2)}, u32[]{:S(2)}) %collective-permute-start.13) | collective-permute-done | bytes 114720 | tf_op jit(solution)/shard_map/ppermute | solution.py:16
  105.8 1.2 fusion.20
  107.9 1.2 fusion.4
  109.1 1.9 %collective-permute-start.14 = (f32[224,128]{1,0:T(8,128)S(1)}, f32[224,128]{1,0:T(8,128)S(1)}, u32[]{:S(2)}, u32[]{:S(2)}) collective-permute-start(f32[224,128]{1,0:T(8,128)S(1)} %fusion.20), channel_id=1, source_target_pairs={{0,4},{4,8},{8,12},{12,16},{16,20},{20,24},{24,28},{1,5},{5,9},{9,... | collective-permute-start | bytes 344072 | tf_op jit(solution)/shard_map/ppermute | solution.py:16
  111.0 3.6 %collective-permute-start.15 = (f32[224,128]{1,0:T(8,128)S(1)}, f32[224,128]{1,0:T(8,128)S(1)}, u32[]{:S(2)}, u32[]{:S(2)}) collective-permute-start(f32[224,128]{1,0:T(8,128)S(1)} %fusion.28), channel_id=1, source_target_pairs={{4,0},{8,4},{12,8},{16,12},{20,16},{24,20},{28,24},{5,1},{9,5},{13... | collective-permute-start | bytes 344072 | tf_op jit(solution)/shard_map/ppermute | solution.py:16
  114.7 2.8 %collective-permute-start.16 = (f32[224,128]{1,0:T(8,128)S(1)}, f32[224,128]{1,0:T(8,128)S(1)}, u32[]{:S(2)}, u32[]{:S(2)}) collective-permute-start(f32[224,128]{1,0:T(8,128)S(1)} %fusion.4), channel_id=1, source_target_pairs={{0,1},{1,2},{2,3},{4,5},{5,6},{6,7},{8,9},{9,10},{10,11},{12,13},{... | collective-permute-start | bytes 344072 | tf_op jit(solution)/shard_map/ppermute | solution.py:16
  117.5 1.2 fusion.12
  118.7 1.3 collective-permute-start.17
  120.1 5.3 %collective-permute-done.17 = f32[224,128]{1,0:T(8,128)S(1)} collective-permute-done((f32[224,128]{1,0:T(8,128)S(1)}, f32[224,128]{1,0:T(8,128)S(1)}, u32[]{:S(2)}, u32[]{:S(2)}) %collective-permute-start.17) | collective-permute-done | bytes 114720 | tf_op jit(solution)/shard_map/ppermute | solution.py:16
  125.6 1.2 fusion.18
  127.6 1.2 fusion.2
  128.8 1.2 fusion.10
  130.0 1.9 %collective-permute-start.18 = (f32[224,128]{1,0:T(8,128)S(1)}, f32[224,128]{1,0:T(8,128)S(1)}, u32[]{:S(2)}, u32[]{:S(2)}) collective-permute-start(f32[224,128]{1,0:T(8,128)S(1)} %fusion.18), channel_id=1, source_target_pairs={{0,4},{4,8},{8,12},{12,16},{16,20},{20,24},{24,28},{1,5},{5,9},{9,... | collective-permute-start | bytes 344072 | tf_op jit(solution)/shard_map/ppermute | solution.py:16
  131.9 3.6 %collective-permute-start.19 = (f32[224,128]{1,0:T(8,128)S(1)}, f32[224,128]{1,0:T(8,128)S(1)}, u32[]{:S(2)}, u32[]{:S(2)}) collective-permute-start(f32[224,128]{1,0:T(8,128)S(1)} %fusion.26), channel_id=1, source_target_pairs={{4,0},{8,4},{12,8},{16,12},{20,16},{24,20},{28,24},{5,1},{9,5},{13... | collective-permute-start | bytes 344072 | tf_op jit(solution)/shard_map/ppermute | solution.py:16
  135.6 2.8 %collective-permute-start.20 = (f32[224,128]{1,0:T(8,128)S(1)}, f32[224,128]{1,0:T(8,128)S(1)}, u32[]{:S(2)}, u32[]{:S(2)}) collective-permute-start(f32[224,128]{1,0:T(8,128)S(1)} %fusion.2), channel_id=1, source_target_pairs={{0,1},{1,2},{2,3},{4,5},{5,6},{6,7},{8,9},{9,10},{10,11},{12,13},{... | collective-permute-start | bytes 344072 | tf_op jit(solution)/shard_map/ppermute | solution.py:16
  138.4 1.3 collective-permute-start.21
  139.7 1.0 add_add_fusion
  140.8 4.3 %collective-permute-done.21 = f32[224,128]{1,0:T(8,128)S(1)} collective-permute-done((f32[224,128]{1,0:T(8,128)S(1)}, f32[224,128]{1,0:T(8,128)S(1)}, u32[]{:S(2)}, u32[]{:S(2)}) %collective-permute-start.21) | collective-permute-done | bytes 114720 | tf_op jit(solution)/shard_map/ppermute | solution.py:16
  (52 shorter events, 9.4 us)
Async XLA Ops:
  1.9 42.9 %collective-permute-start.4 = (f32[128,896]{1,0:T(8,128)S(1)}, f32[128,896]{1,0:T(8,128)S(1)}, u32[]{:S(2)}, u32[]{:S(2)}) collective-permute-start(f32[128,896]{1,0:T(8,128)S(1)} %get-tuple-element.5), channel_id=1, source_target_pairs={{0,24},{4,28},{8,0},{12,4},{16,8},{20,12},{24,16},{28,20},{1,25},{... | collective-permute-start | bytes 1376264 | tf_op jit(solution)/shard_map/ppermute | solution.py:22
  2.4 42.4 %collective-permute-start.5 = (f32[128,896]{1,0:T(8,128)S(1)}, f32[128,896]{1,0:T(8,128)S(1)}, u32[]{:S(2)}, u32[]{:S(2)}) collective-permute-start(f32[128,896]{1,0:T(8,128)S(1)} %get-tuple-element.6), channel_id=1, source_target_pairs={{0,16},{4,20},{8,24},{12,28},{16,0},{20,4},{24,8},{28,12},{1,17},{... | collective-permute-start | bytes 1376264 | tf_op jit(solution)/shard_map/ppermute | solution.py:22
  6.9 29.3 %collective-permute-start = (f32[224,128]{1,0:T(8,128)S(1)}, f32[224,128]{1,0:T(8,128)S(1)}, u32[]{:S(2)}, u32[]{:S(2)}) collective-permute-start(f32[224,128]{1,0:T(8,128)S(1)} %get-tuple-element.11), channel_id=1, source_target_pairs={{0,4},{4,8},{8,12},{12,16},{16,20},{20,24},{24,28},{1,5},{5,9},{9,... | collective-permute-start | bytes 344072 | tf_op jit(solution)/shard_map/ppermute | solution.py:16
  8.9 33.2 %collective-permute-start.1 = (f32[224,128]{1,0:T(8,128)S(1)}, f32[224,128]{1,0:T(8,128)S(1)}, u32[]{:S(2)}, u32[]{:S(2)}) collective-permute-start(f32[224,128]{1,0:T(8,128)S(1)} %get-tuple-element.12), channel_id=1, source_target_pairs={{4,0},{8,4},{12,8},{16,12},{20,16},{24,20},{28,24},{5,1},{9,5},{13... | collective-permute-start | bytes 344072 | tf_op jit(solution)/shard_map/ppermute | solution.py:16
  12.5 29.6 %collective-permute-start.2 = (f32[224,128]{1,0:T(8,128)S(1)}, f32[224,128]{1,0:T(8,128)S(1)}, u32[]{:S(2)}, u32[]{:S(2)}) collective-permute-start(f32[224,128]{1,0:T(8,128)S(1)} %get-tuple-element.13), channel_id=1, source_target_pairs={{0,1},{1,2},{2,3},{4,5},{5,6},{6,7},{8,9},{9,10},{10,11},{12,13},{... | collective-permute-start | bytes 344072 | tf_op jit(solution)/shard_map/ppermute | solution.py:16
  16.6 28.2 %copy-start.1 = (f32[1,1,640,896]{3,2,1,0:T(8,128)S(1)}, f32[1,1,640,896]{3,2,1,0:T(8,128)}, u32[]{:S(2)}) copy-start(f32[1,1,640,896]{3,2,1,0:T(8,128)} %param.9) | copy-start | bytes 6881284
  36.3 6.7 %collective-permute-start.3 = (f32[224,128]{1,0:T(8,128)S(1)}, f32[224,128]{1,0:T(8,128)S(1)}, u32[]{:S(2)}, u32[]{:S(2)}) collective-permute-start(f32[224,128]{1,0:T(8,128)S(1)} %get-tuple-element.14), channel_id=1, source_target_pairs={{1,0},{2,1},{3,2},{5,4},{6,5},{7,6},{9,8},{10,9},{11,10},{13,12},{... | collective-permute-start | bytes 344072 | tf_op jit(solution)/shard_map/ppermute | solution.py:16
  60.8 2.4 %copy-start = (f32[224,128]{1,0:T(8,128)S(1)}, f32[224,128]{1,0:T(8,128)}, u32[]{:S(2)}) copy-start(f32[224,128]{1,0:T(8,128)} %get-tuple-element.10) | copy-start | bytes 344068
  66.4 12.4 %collective-permute-start.6 = (f32[224,128]{1,0:T(8,128)S(1)}, f32[224,128]{1,0:T(8,128)S(1)}, u32[]{:S(2)}, u32[]{:S(2)}) collective-permute-start(f32[224,128]{1,0:T(8,128)S(1)} %fusion.24), channel_id=1, source_target_pairs={{0,4},{4,8},{8,12},{12,16},{16,20},{20,24},{24,28},{1,5},{5,9},{9,... | collective-permute-start | bytes 344072 | tf_op jit(solution)/shard_map/ppermute | solution.py:16
  68.3 10.5 %collective-permute-start.7 = (f32[224,128]{1,0:T(8,128)S(1)}, f32[224,128]{1,0:T(8,128)S(1)}, u32[]{:S(2)}, u32[]{:S(2)}) collective-permute-start(f32[224,128]{1,0:T(8,128)S(1)} %fusion.32), channel_id=1, source_target_pairs={{4,0},{8,4},{12,8},{16,12},{20,16},{24,20},{28,24},{5,1},{9,5},{13... | collective-permute-start | bytes 344072 | tf_op jit(solution)/shard_map/ppermute | solution.py:16
  72.0 6.8 %collective-permute-start.8 = (f32[224,128]{1,0:T(8,128)S(1)}, f32[224,128]{1,0:T(8,128)S(1)}, u32[]{:S(2)}, u32[]{:S(2)}) collective-permute-start(f32[224,128]{1,0:T(8,128)S(1)} %fusion.8), channel_id=1, source_target_pairs={{0,1},{1,2},{2,3},{4,5},{5,6},{6,7},{8,9},{9,10},{10,11},{12,13},{... | collective-permute-start | bytes 344072 | tf_op jit(solution)/shard_map/ppermute | solution.py:16
  77.5 6.7 %collective-permute-start.9 = (f32[224,128]{1,0:T(8,128)S(1)}, f32[224,128]{1,0:T(8,128)S(1)}, u32[]{:S(2)}, u32[]{:S(2)}) collective-permute-start(f32[224,128]{1,0:T(8,128)S(1)} %fusion.16), channel_id=1, source_target_pairs={{1,0},{2,1},{3,2},{5,4},{6,5},{7,6},{9,8},{10,9},{11,10},{13,12},{... | collective-permute-start | bytes 344072 | tf_op jit(solution)/shard_map/ppermute | solution.py:16
  87.4 12.8 %collective-permute-start.10 = (f32[224,128]{1,0:T(8,128)S(1)}, f32[224,128]{1,0:T(8,128)S(1)}, u32[]{:S(2)}, u32[]{:S(2)}) collective-permute-start(f32[224,128]{1,0:T(8,128)S(1)} %fusion.22), channel_id=1, source_target_pairs={{0,4},{4,8},{8,12},{12,16},{16,20},{20,24},{24,28},{1,5},{5,9},{9,... | collective-permute-start | bytes 344072 | tf_op jit(solution)/shard_map/ppermute | solution.py:16
  89.4 10.9 %collective-permute-start.11 = (f32[224,128]{1,0:T(8,128)S(1)}, f32[224,128]{1,0:T(8,128)S(1)}, u32[]{:S(2)}, u32[]{:S(2)}) collective-permute-start(f32[224,128]{1,0:T(8,128)S(1)} %fusion.30), channel_id=1, source_target_pairs={{4,0},{8,4},{12,8},{16,12},{20,16},{24,20},{28,24},{5,1},{9,5},{13... | collective-permute-start | bytes 344072 | tf_op jit(solution)/shard_map/ppermute | solution.py:16
  93.0 7.3 %collective-permute-start.12 = (f32[224,128]{1,0:T(8,128)S(1)}, f32[224,128]{1,0:T(8,128)S(1)}, u32[]{:S(2)}, u32[]{:S(2)}) collective-permute-start(f32[224,128]{1,0:T(8,128)S(1)} %fusion.6), channel_id=1, source_target_pairs={{0,1},{1,2},{2,3},{4,5},{5,6},{6,7},{8,9},{9,10},{10,11},{12,13},{... | collective-permute-start | bytes 344072 | tf_op jit(solution)/shard_map/ppermute | solution.py:16
  99.0 6.7 %collective-permute-start.13 = (f32[224,128]{1,0:T(8,128)S(1)}, f32[224,128]{1,0:T(8,128)S(1)}, u32[]{:S(2)}, u32[]{:S(2)}) collective-permute-start(f32[224,128]{1,0:T(8,128)S(1)} %fusion.14), channel_id=1, source_target_pairs={{1,0},{2,1},{3,2},{5,4},{6,5},{7,6},{9,8},{10,9},{11,10},{13,12},{... | collective-permute-start | bytes 344072 | tf_op jit(solution)/shard_map/ppermute | solution.py:16
  109.1 10.9 %collective-permute-start.14 = (f32[224,128]{1,0:T(8,128)S(1)}, f32[224,128]{1,0:T(8,128)S(1)}, u32[]{:S(2)}, u32[]{:S(2)}) collective-permute-start(f32[224,128]{1,0:T(8,128)S(1)} %fusion.20), channel_id=1, source_target_pairs={{0,4},{4,8},{8,12},{12,16},{16,20},{20,24},{24,28},{1,5},{5,9},{9,... | collective-permute-start | bytes 344072 | tf_op jit(solution)/shard_map/ppermute | solution.py:16
  111.0 9.0 %collective-permute-start.15 = (f32[224,128]{1,0:T(8,128)S(1)}, f32[224,128]{1,0:T(8,128)S(1)}, u32[]{:S(2)}, u32[]{:S(2)}) collective-permute-start(f32[224,128]{1,0:T(8,128)S(1)} %fusion.28), channel_id=1, source_target_pairs={{4,0},{8,4},{12,8},{16,12},{20,16},{24,20},{28,24},{5,1},{9,5},{13... | collective-permute-start | bytes 344072 | tf_op jit(solution)/shard_map/ppermute | solution.py:16
  114.7 5.4 %collective-permute-start.16 = (f32[224,128]{1,0:T(8,128)S(1)}, f32[224,128]{1,0:T(8,128)S(1)}, u32[]{:S(2)}, u32[]{:S(2)}) collective-permute-start(f32[224,128]{1,0:T(8,128)S(1)} %fusion.4), channel_id=1, source_target_pairs={{0,1},{1,2},{2,3},{4,5},{5,6},{6,7},{8,9},{9,10},{10,11},{12,13},{... | collective-permute-start | bytes 344072 | tf_op jit(solution)/shard_map/ppermute | solution.py:16
  118.7 6.7 %collective-permute-start.17 = (f32[224,128]{1,0:T(8,128)S(1)}, f32[224,128]{1,0:T(8,128)S(1)}, u32[]{:S(2)}, u32[]{:S(2)}) collective-permute-start(f32[224,128]{1,0:T(8,128)S(1)} %fusion.12), channel_id=1, source_target_pairs={{1,0},{2,1},{3,2},{5,4},{6,5},{7,6},{9,8},{10,9},{11,10},{13,12},{... | collective-permute-start | bytes 344072 | tf_op jit(solution)/shard_map/ppermute | solution.py:16
  130.0 10.7 %collective-permute-start.18 = (f32[224,128]{1,0:T(8,128)S(1)}, f32[224,128]{1,0:T(8,128)S(1)}, u32[]{:S(2)}, u32[]{:S(2)}) collective-permute-start(f32[224,128]{1,0:T(8,128)S(1)} %fusion.18), channel_id=1, source_target_pairs={{0,4},{4,8},{8,12},{12,16},{16,20},{20,24},{24,28},{1,5},{5,9},{9,... | collective-permute-start | bytes 344072 | tf_op jit(solution)/shard_map/ppermute | solution.py:16
  131.9 8.8 %collective-permute-start.19 = (f32[224,128]{1,0:T(8,128)S(1)}, f32[224,128]{1,0:T(8,128)S(1)}, u32[]{:S(2)}, u32[]{:S(2)}) collective-permute-start(f32[224,128]{1,0:T(8,128)S(1)} %fusion.26), channel_id=1, source_target_pairs={{4,0},{8,4},{12,8},{16,12},{20,16},{24,20},{28,24},{5,1},{9,5},{13... | collective-permute-start | bytes 344072 | tf_op jit(solution)/shard_map/ppermute | solution.py:16
  135.6 5.2 %collective-permute-start.20 = (f32[224,128]{1,0:T(8,128)S(1)}, f32[224,128]{1,0:T(8,128)S(1)}, u32[]{:S(2)}, u32[]{:S(2)}) collective-permute-start(f32[224,128]{1,0:T(8,128)S(1)} %fusion.2), channel_id=1, source_target_pairs={{0,1},{1,2},{2,3},{4,5},{5,6},{6,7},{8,9},{9,10},{10,11},{12,13},{... | collective-permute-start | bytes 344072 | tf_op jit(solution)/shard_map/ppermute | solution.py:16
  138.4 6.7 %collective-permute-start.21 = (f32[224,128]{1,0:T(8,128)S(1)}, f32[224,128]{1,0:T(8,128)S(1)}, u32[]{:S(2)}, u32[]{:S(2)}) collective-permute-start(f32[224,128]{1,0:T(8,128)S(1)} %fusion.10), channel_id=1, source_target_pairs={{1,0},{2,1},{3,2},{5,4},{6,5},{7,6},{9,8},{10,9},{11,10},{13,12},{... | collective-permute-start | bytes 344072 | tf_op jit(solution)/shard_map/ppermute | solution.py:16

commit v3 on v2

--- a/solution.py
+++ b/solution.py
@@ -47,17 +47,28 @@
     )
 
 
+def swap_pairs(count, first):
+    pairs = []
+    for low in range(first, count - 1, 2):
+        pairs += [(low, low + 1), (low + 1, low)]
+    return pairs
+
+
+def axis_exchange(low, high, axis):
+    count = lax.axis_size(axis)
+    even = lax.axis_index(axis) % 2 == 0
+    odd_recv = lax.ppermute(jnp.where(even, low, high), axis, swap_pairs(count, 1))
+    even_recv = lax.ppermute(jnp.where(even, high, low), axis, swap_pairs(count, 0))
+    new_low = low + jnp.where(even, odd_recv, even_recv)
+    new_high = high + jnp.where(even, even_recv, odd_recv)
+    return new_low, new_high
+
+
 def face_sum_parts(faces):
     low_x, high_x, low_y, high_y = faces
-    return jnp.concatenate(
-        [
-            low_x + along_x(high_x, 1),
-            high_x + along_x(low_x, -1),
-            low_y + along_y(high_y, 1),
-            high_y + along_y(low_y, -1),
-        ],
-        axis=0,
-    )
+    new_low_y, new_high_y = axis_exchange(low_y, high_y, "gy")
+    new_low_x, new_high_x = axis_exchange(low_x, high_x, "gx")
+    return jnp.concatenate([new_low_x, new_high_x, new_low_y, new_high_y], axis=0)
 
 
 def body(gap, own_rows, spill_rows, tile_plan, orders, slot_rows):
@@ -88,7 +99,8 @@
     by_rows = jnp.take(operator, slot_map, axis=0)
     by_cols = jnp.take(by_rows.T, slot_map, axis=0)
     slot_op = (by_cols * slot_scale[:, None]).T * slot_scale[:, None]
-    load = face_sum(gap[0, 0])
+    width = order_max // 4
+    load = face_sum_parts([gap[0, 0, face_id * width : (face_id + 1) * width] for face_id in range(4)])
     centre = (high_bound + low_bound) / 2.0
     half_width = (high_bound - low_bound) / 2.0
     sigma_value = centre / half_width

time: 147 us -> 128 us (0.87)
  the two profiles are of different devices: /device:TPU:16 before, /device:TPU:0 now
where the time goes in v3:
time: 128 us; the launch traced here: 127 us
  starting transfers between devices  41.4 us (32%)
  waiting for transfers between devices  35.8 us (28%)
  matrix products  17.7 us (14%)
  other arithmetic  14.2 us (11%)
  local copies, waits for them, and re-layouts  13.8 us (11%)
  between operations  4.25 us (3%)
    ppermute x10, starting transfers between devices, axis_exchange(): lax.ppermute(jnp.where(even, high, low), axis, swap_pairs(count, 0))  31.5 us
    ppermute x2, waiting for transfers between devices, from_behind(): return lax.ppermute(value, axis, pairs)  19.7 us
    dot_general x16, matrix products, body(): jnp.dot(slot_op[face_id * width:(face_id + 1) * width], direction, precis...  17.7 us
    ppermute x10, waiting for transfers between devices, axis_exchange(): lax.ppermute(jnp.where(even, high, low), axis, swap_pairs(count, 0))  16 us
    ppermute x10, starting transfers between devices, axis_exchange(): lax.ppermute(jnp.where(even, low, high), axis, swap_pairs(count, 1))  6.84 us
    gather x1, local copies, waits for them, and re-layouts, body(): by_rows = jnp.take(operator, slot_map, axis=0)  4.21 us
    gather x1, local copies, waits for them, and re-layouts, body(): by_cols = jnp.take(by_rows.T, slot_map, axis=0)  4.21 us
    transpose x1, other arithmetic, body(): by_cols = jnp.take(by_rows.T, slot_map, axis=0)  3.85 us
  transfers between devices with their start and end apart: 22, of which 6 were waited for; matrix products, arithmetic and copies ran while one was open for 8% of the time, Pallas kernels for 0%

profile of v3, /device:TPU:0, one launch (start us, length us, event | category | flops | bytes accessed | tf_op | source)
XLA Modules:
  0.0 127.1 jit_solution(3187335811278238574)
XLA Ops:
  0.7 1.0 bitcast_select_fusion.3
  1.7 0.7 collective-permute-start
  2.4 4.4 %collective-permute-start.1 = (f32[224,128]{1,0:T(8,128)S(1)}, f32[224,128]{1,0:T(8,128)S(1)}, u32[]{:S(2)}, u32[]{:S(2)}) collective-permute-start(f32[224,128]{1,0:T(8,128)S(1)} %get-tuple-element.14), channel_id=1, source_target_pairs={{0,4},{4,0},{8,12},{12,8},{16,20},{20,16},{24,28},{28,24},{1,5},{5... | collective-permute-start | bytes 344072 | tf_op jit(solution)/shard_map/ppermute | solution.py:61
  6.8 1.2 slice_bitcast_fusion.1
  8.0 2.0 %collective-permute-start.4 = (f32[128,896]{1,0:T(8,128)S(1)}, f32[128,896]{1,0:T(8,128)S(1)}, u32[]{:S(2)}, u32[]{:S(2)}) collective-permute-start(f32[128,896]{1,0:T(8,128)S(1)} %get-tuple-element.5), channel_id=1, source_target_pairs={{0,24},{4,28},{8,0},{12,4},{16,8},{20,12},{24,16},{28,20},{1,25},{... | collective-permute-start | bytes 1376264 | tf_op jit(solution)/shard_map/ppermute | solution.py:22
  10.0 1.1 collective-permute-start.5
  11.8 0.7 reduce
  13.7 1.8 %bitcast_add_fusion.3 = (f32[224,128]{1,0:T(8,128)S(1)}, f32[224,128]{1,0:T(8,128)}, f32[224,128]{1,0:T(8,128)S(1)}, f32[224,128]{1,0:T(8,128)S(1)}) fusion(f32[224,128]{1,0:T(8,128)S(1)} %collective-permute-done, f32[224,128]{1,0:T(8,128)S(1)} %collective-permute-done.1, f32[1,1,896,128]{3,2,1,0:T(8,128)} %param.8, pred[]{:T(512)S(6)} %eq.59, pred[]{:T(512)S(6)} %eq.60), kind=kLoop, calls=%fused_computation.72 | loop fusion | flops 172032 | bytes 1146882 | tf_op jit(solution)/shard_map/add | solution.py:62
  15.4 1.5 %collective-permute-start.3 = (f32[224,128]{1,0:T(8,128)S(1)}, f32[224,128]{1,0:T(8,128)S(1)}, u32[]{:S(2)}, u32[]{:S(2)}) collective-permute-start(f32[224,128]{1,0:T(8,128)S(1)} %get-tuple-element.11), channel_id=1, source_target_pairs={{0,1},{1,0},{2,3},{3,2},{4,5},{5,4},{6,7},{7,6},{8,9},{9,8},{10,11... | collective-permute-start | bytes 344072 | tf_op jit(solution)/shard_map/ppermute | solution.py:61
  21.5 19.7 %collective-permute-done.5 = f32[128,896]{1,0:T(8,128)S(1)} collective-permute-done((f32[128,896]{1,0:T(8,128)S(1)}, f32[128,896]{1,0:T(8,128)S(1)}, u32[]{:S(2)}, u32[]{:S(2)}) %collective-permute-start.5) | collective-permute-done | bytes 458784 | tf_op jit(solution)/shard_map/ppermute | solution.py:22
  41.5 4.2 %gather_fusion = f32[896,896]{1,0:T(8,128)} fusion(f32[896,896]{1,0:T(8,128)S(1)} %pad_maximum_fusion, s32[1024]{0:T(1024)} %pad_clamp_fusion), kind=kCustom, calls=%fused_computation.clone | custom fusion | bytes 6426112 | tf_op jit(solution)/shard_map/jit(_take)/gather | solution.py:99
  45.7 3.8 %select_bitcast_fusion = f32[896,896]{0,1:T(8,128)} fusion(f32[896,896]{1,0:T(8,128)} %gather_fusion, pred[896]{0:T(1024)(128)(4,1)} %compare_and_fusion), kind=kLoop, calls=%fused_computation.6 | loop fusion | flops 802816 | bytes 6423424 | tf_op jit(solution)/shard_map/transpose | solution.py:100
  49.6 3.4 %copy.8 = f32[896,896]{1,0:T(8,128)S(1)} copy(f32[896,896]{0,1:T(8,128)} %select_bitcast_fusion) | data formatting | bytes 6422528 | tf_op jit(solution)/shard_map/transpose | solution.py:100
  53.0 4.2 %gather_fusion.1 = f32[896,896]{1,0:T(8,128)} fusion(f32[896,896]{1,0:T(8,128)S(1)} %copy.8, s32[1024]{0:T(1024)} %pad_clamp_fusion), kind=kCustom, calls=%fused_computation.1.clone | custom fusion | bytes 6426112 | tf_op jit(solution)/shard_map/jit(_take)/gather | solution.py:100
  57.3 2.4 %fusion.1 = f32[896,896]{0,1:T(8,128)S(1)} fusion(f32[896,896]{1,0:T(8,128)} %gather_fusion.1, f32[896]{0:T(1024)} %select_select_fusion, pred[896]{0:T(1024)(128)(4,1)} %compare_and_fusion), kind=kLoop, calls=%fused_computation.5 | loop fusion | flops 2408448 | bytes 6427008 | tf_op jit(solution)/shard_map/mul | solution.py:101
  59.6 1.2 fusion.8
  60.8 1.2 fusion.24
  62.0 0.9 broadcast_select_fusion.15
  62.9 0.7 collective-permute-start.6
  63.6 1.8 %collective-permute-start.7 = (f32[224,128]{1,0:T(8,128)S(1)}, f32[224,128]{1,0:T(8,128)S(1)}, u32[]{:S(2)}, u32[]{:S(2)}) collective-permute-start(f32[224,128]{1,0:T(8,128)S(1)} %get-tuple-element.42), channel_id=1, source_target_pairs={{0,4},{4,0},{8,12},{12,8},{16,20},{20,16},{24,28},{28,24},{1,5},{5... | collective-permute-start | bytes 344072 | tf_op jit(solution)/shard_map/ppermute | solution.py:61
  65.4 1.2 broadcast_select_fusion.7
  67.2 4.3 %collective-permute-start.9 = (f32[224,128]{1,0:T(8,128)S(1)}, f32[224,128]{1,0:T(8,128)S(1)}, u32[]{:S(2)}, u32[]{:S(2)}) collective-permute-start(f32[224,128]{1,0:T(8,128)S(1)} %get-tuple-element.46), channel_id=1, source_target_pairs={{0,1},{1,0},{2,3},{3,2},{4,5},{5,4},{6,7},{7,6},{8,9},{9,8},{10,11... | collective-permute-start | bytes 344072 | tf_op jit(solution)/shard_map/ppermute | solution.py:61
  71.6 5.4 %collective-permute-done.9 = f32[224,128]{1,0:T(8,128)S(1)} collective-permute-done((f32[224,128]{1,0:T(8,128)S(1)}, f32[224,128]{1,0:T(8,128)S(1)}, u32[]{:S(2)}, u32[]{:S(2)}) %collective-permute-start.9) | collective-permute-done | bytes 114720 | tf_op jit(solution)/shard_map/ppermute | solution.py:61
  77.0 1.2 fusion.22
  78.1 1.2 fusion.6
  79.3 1.2 broadcast_select_fusion.5
  80.5 0.8 collective-permute-start.12
  81.3 2.7 %collective-permute-start.13 = (f32[224,128]{1,0:T(8,128)S(1)}, f32[224,128]{1,0:T(8,128)S(1)}, u32[]{:S(2)}, u32[]{:S(2)}) collective-permute-start(f32[224,128]{1,0:T(8,128)S(1)} %get-tuple-element.38), channel_id=1, source_target_pairs={{0,1},{1,0},{2,3},{3,2},{4,5},{5,4},{6,7},{7,6},{8,9},{9,8},{10,11... | collective-permute-start | bytes 344072 | tf_op jit(solution)/shard_map/ppermute | solution.py:61
  84.1 0.9 broadcast_select_fusion.13
  85.7 1.8 %collective-permute-start.11 = (f32[224,128]{1,0:T(8,128)S(1)}, f32[224,128]{1,0:T(8,128)S(1)}, u32[]{:S(2)}, u32[]{:S(2)}) collective-permute-start(f32[224,128]{1,0:T(8,128)S(1)} %get-tuple-element.34), channel_id=1, source_target_pairs={{0,4},{4,0},{8,12},{12,8},{16,20},{20,16},{24,28},{28,24},{1,5},{5... | collective-permute-start | bytes 344072 | tf_op jit(solution)/shard_map/ppermute | solution.py:61
  88.6 1.2 fusion.4
  89.8 1.2 fusion.20
  91.0 0.9 broadcast_select_fusion.11
  92.6 5.0 %collective-permute-start.15 = (f32[224,128]{1,0:T(8,128)S(1)}, f32[224,128]{1,0:T(8,128)S(1)}, u32[]{:S(2)}, u32[]{:S(2)}) collective-permute-start(f32[224,128]{1,0:T(8,128)S(1)} %get-tuple-element.26), channel_id=1, source_target_pairs={{0,4},{4,0},{8,12},{12,8},{16,20},{20,16},{24,28},{28,24},{1,5},{5... | collective-permute-start | bytes 344072 | tf_op jit(solution)/shard_map/ppermute | solution.py:61
  97.6 1.2 broadcast_select_fusion.3
  98.7 0.7 collective-permute-start.16
  99.4 2.8 %collective-permute-start.17 = (f32[224,128]{1,0:T(8,128)S(1)}, f32[224,128]{1,0:T(8,128)S(1)}, u32[]{:S(2)}, u32[]{:S(2)}) collective-permute-start(f32[224,128]{1,0:T(8,128)S(1)} %get-tuple-element.30), channel_id=1, source_target_pairs={{0,1},{1,0},{2,3},{3,2},{4,5},{5,4},{6,7},{7,6},{8,9},{9,8},{10,11... | collective-permute-start | bytes 344072 | tf_op jit(solution)/shard_map/ppermute | solution.py:61
  102.2 5.4 %collective-permute-done.17 = f32[224,128]{1,0:T(8,128)S(1)} collective-permute-done((f32[224,128]{1,0:T(8,128)S(1)}, f32[224,128]{1,0:T(8,128)S(1)}, u32[]{:S(2)}, u32[]{:S(2)}) %collective-permute-start.17) | collective-permute-done | bytes 114720 | tf_op jit(solution)/shard_map/ppermute | solution.py:61
  107.8 1.2 fusion.2
  108.9 1.2 fusion.18
  110.1 0.9 broadcast_select_fusion.9
  111.0 1.2 broadcast_select_fusion.1
  112.2 0.7 collective-permute-start.18
  112.9 4.5 %collective-permute-start.19 = (f32[224,128]{1,0:T(8,128)S(1)}, f32[224,128]{1,0:T(8,128)S(1)}, u32[]{:S(2)}, u32[]{:S(2)}) collective-permute-start(f32[224,128]{1,0:T(8,128)S(1)} %get-tuple-element.18), channel_id=1, source_target_pairs={{0,4},{4,0},{8,12},{12,8},{16,20},{20,16},{24,28},{28,24},{1,5},{5... | collective-permute-start | bytes 344072 | tf_op jit(solution)/shard_map/ppermute | solution.py:61
  118.0 2.7 %collective-permute-start.21 = (f32[224,128]{1,0:T(8,128)S(1)}, f32[224,128]{1,0:T(8,128)S(1)}, u32[]{:S(2)}, u32[]{:S(2)}) collective-permute-start(f32[224,128]{1,0:T(8,128)S(1)} %get-tuple-element.22), channel_id=1, source_target_pairs={{0,1},{1,0},{2,3},{3,2},{4,5},{5,4},{6,7},{7,6},{8,9},{9,8},{10,11... | collective-permute-start | bytes 344072 | tf_op jit(solution)/shard_map/ppermute | solution.py:61
  120.8 1.0 add_add_fusion
  121.8 4.4 %collective-permute-done.21 = f32[224,128]{1,0:T(8,128)S(1)} collective-permute-done((f32[224,128]{1,0:T(8,128)S(1)}, f32[224,128]{1,0:T(8,128)S(1)}, u32[]{:S(2)}, u32[]{:S(2)}) %collective-permute-start.21) | collective-permute-done | bytes 114720 | tf_op jit(solution)/shard_map/ppermute | solution.py:61
  126.2 0.9 maximum_subtract_fusion.6
  (49 shorter events, 7.5 us)
Async XLA Ops:
  0.6 20.8 %copy-start.2 = (f32[1,1,896,128]{3,2,1,0:T(8,128)S(1)}, f32[1,1,896,128]{3,2,1,0:T(8,128)}, u32[]{:S(2)}) copy-start(f32[1,1,896,128]{3,2,1,0:T(8,128)} %param.8) | copy-start | bytes 1376260
  0.6 16.9 %copy-start.3 = (s32[1,1,2]{2,1,0:T(1,128)S(1)}, s32[1,1,2]{2,1,0:T(1,128)}, u32[]{:S(2)}) copy-start(s32[1,1,2]{2,1,0:T(1,128)} %param.11) | copy-start | bytes 28
  1.7 12.0 %collective-permute-start = (f32[224,128]{1,0:T(8,128)S(1)}, f32[224,128]{1,0:T(8,128)S(1)}, u32[]{:S(2)}, u32[]{:S(2)}) collective-permute-start(f32[224,128]{1,0:T(8,128)S(1)} %get-tuple-element.13), channel_id=1, source_target_pairs={{4,8},{8,4},{12,16},{16,12},{20,24},{24,20},{5,9},{9,5},{13,17},{1... | collective-permute-start | bytes 344072 | tf_op jit(solution)/shard_map/ppermute | solution.py:60
  2.4 11.3 %collective-permute-start.1 = (f32[224,128]{1,0:T(8,128)S(1)}, f32[224,128]{1,0:T(8,128)S(1)}, u32[]{:S(2)}, u32[]{:S(2)}) collective-permute-start(f32[224,128]{1,0:T(8,128)S(1)} %get-tuple-element.14), channel_id=1, source_target_pairs={{0,4},{4,0},{8,12},{12,8},{16,20},{20,16},{24,28},{28,24},{1,5},{5... | collective-permute-start | bytes 344072 | tf_op jit(solution)/shard_map/ppermute | solution.py:61
  8.0 13.4 %collective-permute-start.4 = (f32[128,896]{1,0:T(8,128)S(1)}, f32[128,896]{1,0:T(8,128)S(1)}, u32[]{:S(2)}, u32[]{:S(2)}) collective-permute-start(f32[128,896]{1,0:T(8,128)S(1)} %get-tuple-element.5), channel_id=1, source_target_pairs={{0,24},{4,28},{8,0},{12,4},{16,8},{20,12},{24,16},{28,20},{1,25},{... | collective-permute-start | bytes 1376264 | tf_op jit(solution)/shard_map/ppermute | solution.py:22
  10.0 31.2 %collective-permute-start.5 = (f32[128,896]{1,0:T(8,128)S(1)}, f32[128,896]{1,0:T(8,128)S(1)}, u32[]{:S(2)}, u32[]{:S(2)}) collective-permute-start(f32[128,896]{1,0:T(8,128)S(1)} %get-tuple-element.6), channel_id=1, source_target_pairs={{0,16},{4,20},{8,24},{12,28},{16,0},{20,4},{24,8},{28,12},{1,17},{... | collective-permute-start | bytes 1376264 | tf_op jit(solution)/shard_map/ppermute | solution.py:22
  12.5 28.8 %copy-start.1 = (f32[1,1,640,896]{3,2,1,0:T(8,128)S(1)}, f32[1,1,640,896]{3,2,1,0:T(8,128)}, u32[]{:S(2)}) copy-start(f32[1,1,640,896]{3,2,1,0:T(8,128)} %param.9) | copy-start | bytes 6881284
  15.4 6.0 %collective-permute-start.3 = (f32[224,128]{1,0:T(8,128)S(1)}, f32[224,128]{1,0:T(8,128)S(1)}, u32[]{:S(2)}, u32[]{:S(2)}) collective-permute-start(f32[224,128]{1,0:T(8,128)S(1)} %get-tuple-element.11), channel_id=1, source_target_pairs={{0,1},{1,0},{2,3},{3,2},{4,5},{5,4},{6,7},{7,6},{8,9},{9,8},{10,11... | collective-permute-start | bytes 344072 | tf_op jit(solution)/shard_map/ppermute | solution.py:61
  16.9 4.5 %collective-permute-start.2 = (f32[224,128]{1,0:T(8,128)S(1)}, f32[224,128]{1,0:T(8,128)S(1)}, u32[]{:S(2)}, u32[]{:S(2)}) collective-permute-start(f32[224,128]{1,0:T(8,128)S(1)} %get-tuple-element.12), channel_id=1, source_target_pairs={{1,2},{2,1},{5,6},{6,5},{9,10},{10,9},{13,14},{14,13},{17,18},{18,... | collective-permute-start | bytes 344072 | tf_op jit(solution)/shard_map/ppermute | solution.py:60
  57.3 2.4 %copy-start = (f32[224,128]{1,0:T(8,128)S(1)}, f32[224,128]{1,0:T(8,128)}, u32[]{:S(2)}) copy-start(f32[224,128]{1,0:T(8,128)} %get-tuple-element.8) | copy-start | bytes 344068
  62.9 8.6 %collective-permute-start.6 = (f32[224,128]{1,0:T(8,128)S(1)}, f32[224,128]{1,0:T(8,128)S(1)}, u32[]{:S(2)}, u32[]{:S(2)}) collective-permute-start(f32[224,128]{1,0:T(8,128)S(1)} %get-tuple-element.41), channel_id=1, source_target_pairs={{4,8},{8,4},{12,16},{16,12},{20,24},{24,20},{5,9},{9,5},{13,17},{1... | collective-permute-start | bytes 344072 | tf_op jit(solution)/shard_map/ppermute | solution.py:60
  63.6 7.9 %collective-permute-start.7 = (f32[224,128]{1,0:T(8,128)S(1)}, f32[224,128]{1,0:T(8,128)S(1)}, u32[]{:S(2)}, u32[]{:S(2)}) collective-permute-start(f32[224,128]{1,0:T(8,128)S(1)} %get-tuple-element.42), channel_id=1, source_target_pairs={{0,4},{4,0},{8,12},{12,8},{16,20},{20,16},{24,28},{28,24},{1,5},{5... | collective-permute-start | bytes 344072 | tf_op jit(solution)/shard_map/ppermute | solution.py:61
  66.5 5.0 %collective-permute-start.8 = (f32[224,128]{1,0:T(8,128)S(1)}, f32[224,128]{1,0:T(8,128)S(1)}, u32[]{:S(2)}, u32[]{:S(2)}) collective-permute-start(f32[224,128]{1,0:T(8,128)S(1)} %get-tuple-element.45), channel_id=1, source_target_pairs={{1,2},{2,1},{5,6},{6,5},{9,10},{10,9},{13,14},{14,13},{17,18},{18,... | collective-permute-start | bytes 344072 | tf_op jit(solution)/shard_map/ppermute | solution.py:60
  67.2 9.7 %collective-permute-start.9 = (f32[224,128]{1,0:T(8,128)S(1)}, f32[224,128]{1,0:T(8,128)S(1)}, u32[]{:S(2)}, u32[]{:S(2)}) collective-permute-start(f32[224,128]{1,0:T(8,128)S(1)} %get-tuple-element.46), channel_id=1, source_target_pairs={{0,1},{1,0},{2,3},{3,2},{4,5},{5,4},{6,7},{7,6},{8,9},{9,8},{10,11... | collective-permute-start | bytes 344072 | tf_op jit(solution)/shard_map/ppermute | solution.py:61
  80.5 7.0 %collective-permute-start.12 = (f32[224,128]{1,0:T(8,128)S(1)}, f32[224,128]{1,0:T(8,128)S(1)}, u32[]{:S(2)}, u32[]{:S(2)}) collective-permute-start(f32[224,128]{1,0:T(8,128)S(1)} %get-tuple-element.37), channel_id=1, source_target_pairs={{1,2},{2,1},{5,6},{6,5},{9,10},{10,9},{13,14},{14,13},{17,18},{18,... | collective-permute-start | bytes 344072 | tf_op jit(solution)/shard_map/ppermute | solution.py:60
  81.3 6.7 %collective-permute-start.13 = (f32[224,128]{1,0:T(8,128)S(1)}, f32[224,128]{1,0:T(8,128)S(1)}, u32[]{:S(2)}, u32[]{:S(2)}) collective-permute-start(f32[224,128]{1,0:T(8,128)S(1)} %get-tuple-element.38), channel_id=1, source_target_pairs={{0,1},{1,0},{2,3},{3,2},{4,5},{5,4},{6,7},{7,6},{8,9},{9,8},{10,11... | collective-permute-start | bytes 344072 | tf_op jit(solution)/shard_map/ppermute | solution.py:61
  85.0 3.1 %collective-permute-start.10 = (f32[224,128]{1,0:T(8,128)S(1)}, f32[224,128]{1,0:T(8,128)S(1)}, u32[]{:S(2)}, u32[]{:S(2)}) collective-permute-start(f32[224,128]{1,0:T(8,128)S(1)} %get-tuple-element.33), channel_id=1, source_target_pairs={{4,8},{8,4},{12,16},{16,12},{20,24},{24,20},{5,9},{9,5},{13,17},{1... | collective-permute-start | bytes 344072 | tf_op jit(solution)/shard_map/ppermute | solution.py:60
  85.7 2.8 %collective-permute-start.11 = (f32[224,128]{1,0:T(8,128)S(1)}, f32[224,128]{1,0:T(8,128)S(1)}, u32[]{:S(2)}, u32[]{:S(2)}) collective-permute-start(f32[224,128]{1,0:T(8,128)S(1)} %get-tuple-element.34), channel_id=1, source_target_pairs={{0,4},{4,0},{8,12},{12,8},{16,20},{20,16},{24,28},{28,24},{1,5},{5... | collective-permute-start | bytes 344072 | tf_op jit(solution)/shard_map/ppermute | solution.py:61
  91.9 10.3 %collective-permute-start.14 = (f32[224,128]{1,0:T(8,128)S(1)}, f32[224,128]{1,0:T(8,128)S(1)}, u32[]{:S(2)}, u32[]{:S(2)}) collective-permute-start(f32[224,128]{1,0:T(8,128)S(1)} %get-tuple-element.25), channel_id=1, source_target_pairs={{4,8},{8,4},{12,16},{16,12},{20,24},{24,20},{5,9},{9,5},{13,17},{1... | collective-permute-start | bytes 344072 | tf_op jit(solution)/shard_map/ppermute | solution.py:60
  92.6 9.6 %collective-permute-start.15 = (f32[224,128]{1,0:T(8,128)S(1)}, f32[224,128]{1,0:T(8,128)S(1)}, u32[]{:S(2)}, u32[]{:S(2)}) collective-permute-start(f32[224,128]{1,0:T(8,128)S(1)} %get-tuple-element.26), channel_id=1, source_target_pairs={{0,4},{4,0},{8,12},{12,8},{16,20},{20,16},{24,28},{28,24},{1,5},{5... | collective-permute-start | bytes 344072 | tf_op jit(solution)/shard_map/ppermute | solution.py:61
  98.7 3.5 %collective-permute-start.16 = (f32[224,128]{1,0:T(8,128)S(1)}, f32[224,128]{1,0:T(8,128)S(1)}, u32[]{:S(2)}, u32[]{:S(2)}) collective-permute-start(f32[224,128]{1,0:T(8,128)S(1)} %get-tuple-element.29), channel_id=1, source_target_pairs={{1,2},{2,1},{5,6},{6,5},{9,10},{10,9},{13,14},{14,13},{17,18},{18,... | collective-permute-start | bytes 344072 | tf_op jit(solution)/shard_map/ppermute | solution.py:60
  99.4 8.2 %collective-permute-start.17 = (f32[224,128]{1,0:T(8,128)S(1)}, f32[224,128]{1,0:T(8,128)S(1)}, u32[]{:S(2)}, u32[]{:S(2)}) collective-permute-start(f32[224,128]{1,0:T(8,128)S(1)} %get-tuple-element.30), channel_id=1, source_target_pairs={{0,1},{1,0},{2,3},{3,2},{4,5},{5,4},{6,7},{7,6},{8,9},{9,8},{10,11... | collective-permute-start | bytes 344072 | tf_op jit(solution)/shard_map/ppermute | solution.py:61
  112.2 9.5 %collective-permute-start.18 = (f32[224,128]{1,0:T(8,128)S(1)}, f32[224,128]{1,0:T(8,128)S(1)}, u32[]{:S(2)}, u32[]{:S(2)}) collective-permute-start(f32[224,128]{1,0:T(8,128)S(1)} %get-tuple-element.17), channel_id=1, source_target_pairs={{4,8},{8,4},{12,16},{16,12},{20,24},{24,20},{5,9},{9,5},{13,17},{1... | collective-permute-start | bytes 344072 | tf_op jit(solution)/shard_map/ppermute | solution.py:60
  112.9 8.9 %collective-permute-start.19 = (f32[224,128]{1,0:T(8,128)S(1)}, f32[224,128]{1,0:T(8,128)S(1)}, u32[]{:S(2)}, u32[]{:S(2)}) collective-permute-start(f32[224,128]{1,0:T(8,128)S(1)} %get-tuple-element.18), channel_id=1, source_target_pairs={{0,4},{4,0},{8,12},{12,8},{16,20},{20,16},{24,28},{28,24},{1,5},{5... | collective-permute-start | bytes 344072 | tf_op jit(solution)/shard_map/ppermute | solution.py:61
  117.4 4.4 %collective-permute-start.20 = (f32[224,128]{1,0:T(8,128)S(1)}, f32[224,128]{1,0:T(8,128)S(1)}, u32[]{:S(2)}, u32[]{:S(2)}) collective-permute-start(f32[224,128]{1,0:T(8,128)S(1)} %get-tuple-element.21), channel_id=1, source_target_pairs={{1,2},{2,1},{5,6},{6,5},{9,10},{10,9},{13,14},{14,13},{17,18},{18,... | collective-permute-start | bytes 344072 | tf_op jit(solution)/shard_map/ppermute | solution.py:60
  118.0 8.1 %collective-permute-start.21 = (f32[224,128]{1,0:T(8,128)S(1)}, f32[224,128]{1,0:T(8,128)S(1)}, u32[]{:S(2)}, u32[]{:S(2)}) collective-permute-start(f32[224,128]{1,0:T(8,128)S(1)} %get-tuple-element.22), channel_id=1, source_target_pairs={{0,1},{1,0},{2,3},{3,2},{4,5},{5,4},{6,7},{7,6},{8,9},{9,8},{10,11... | collective-permute-start | bytes 344072 | tf_op jit(solution)/shard_map/ppermute | solution.py:61

commit v4 on v3

--- a/solution.py
+++ b/solution.py
@@ -87,6 +87,14 @@
     homed = [
         from_behind(spill_block[slot_id], "gx", -(slot_id + 1) * hop_span) for slot_id in range(2)
     ]
+    own_count = own_block.shape[0]
+    width = order_max // 4
+    load = face_sum_parts([gap[0, 0, face_id * width : (face_id + 1) * width] for face_id in range(4)])
+    own_cols = (jnp.take(own_block.T, slot_map, axis=0) * slot_scale[:, None]).T
+    in_own = slot_map < own_count
+    own_op = jnp.where(
+        in_own[:, None], jnp.take(own_cols, jnp.minimum(slot_map, own_count - 1), axis=0), 0.0
+    ) * slot_scale[:, None]
     extra_rows = []
     for extra_id in range(2):
         gathered = jnp.zeros_like(homed[0])
@@ -95,12 +103,13 @@
                 plan_row[slot_id] == own_tiles + extra_id, homed[slot_id], 0.0
             )
         extra_rows.append(gathered)
-    operator = jnp.concatenate([own_block] + extra_rows, axis=0)
-    by_rows = jnp.take(operator, slot_map, axis=0)
-    by_cols = jnp.take(by_rows.T, slot_map, axis=0)
-    slot_op = (by_cols * slot_scale[:, None]).T * slot_scale[:, None]
-    width = order_max // 4
-    load = face_sum_parts([gap[0, 0, face_id * width : (face_id + 1) * width] for face_id in range(4)])
+    extra_block = jnp.concatenate(extra_rows, axis=0)
+    extra_count = extra_block.shape[0]
+    extra_cols = (jnp.take(extra_block.T, slot_map, axis=0) * slot_scale[:, None]).T
+    extra_ids = jnp.arange(extra_count, dtype=jnp.int32)
+    extra_place = jnp.where(
+        (slot_map - own_count)[:, None] == extra_ids[None, :], slot_scale[:, None], 0.0
+    )
     centre = (high_bound + low_bound) / 2.0
     half_width = (high_bound - low_bound) / 2.0
     sigma_value = centre / half_width
@@ -110,12 +119,20 @@
     direction = residual / centre
     for step_id in range(ITERS):
         solution = solution + direction
-        width = order_max // 4
+        extra_out = jnp.dot(
+            extra_cols, direction, precision=lax.Precision.HIGH, preferred_element_type=jnp.float32
+        )
         faces = [
             jnp.dot(
-                slot_op[face_id * width : (face_id + 1) * width],
+                own_op[face_id * width : (face_id + 1) * width],
                 direction,
                 precision=lax.Precision.HIGH,
+                preferred_element_type=jnp.float32,
+            )
+            + jnp.dot(
+                extra_place[face_id * width : (face_id + 1) * width],
+                extra_out,
+                precision=lax.Precision.HIGHEST,
                 preferred_element_type=jnp.float32,
             )
             for face_id in range(4)

time: 128 us -> 124 us (0.969)
  waiting for transfers between devices: 35.8 us -> 20.5 us
  local copies, waits for them, and re-layouts: 13.8 us -> 21.4 us
  matrix products: 17.7 us -> 23.9 us
  starting transfers between devices: 41.4 us -> 38.7 us
    ppermute x2, waiting for transfers between devices: 19.7 us -> 0.01 us  [from_behind(): return lax.ppermute(value, axis, pairs)]
    dot_general x16 -> x36, matrix products: 17.7 us -> 23.9 us  [the longest x16 10.2 us: body(): jnp.dot(own_op[face_id * width:(face_id + 1) * width], direction, precisi...]
    ppermute x10, waiting for transfers between devices: 16 us -> 20.5 us  [axis_exchange(): lax.ppermute(jnp.where(even, high, low), axis, swap_pairs(count, 0))]
    unnamed x8 -> x31, local copies, waits for them, and re-layouts: 0.02 us -> 4.41 us
    gather x2 -> x3, local copies, waits for them, and re-layouts: 8.43 us -> 12.7 us  [the longest x1 4.84 us: body(): jnp.take(extra_block.T, slot_map, axis=0) * slot_scale[:, None]]
    ppermute x10, starting transfers between devices: 31.5 us -> 28 us  [axis_exchange(): lax.ppermute(jnp.where(even, high, low), axis, swap_pairs(count, 0))]
    transpose x1 -> x0, local copies, waits for them, and re-layouts: 3.44 us -> none  [body(): by_cols = jnp.take(by_rows.T, slot_map, axis=0)]
    mul x1 -> x2, other arithmetic: 2.36 us -> 5.76 us  [the longest x1 3.37 us: body(): own_cols = (jnp.take(own_block.T, slot_map, axis=0) * slot_scale[:, None]).T]
  transfers between devices with their start and end apart: 22 -> 22, of which waited for: 6 -> 5; matrix products, arithmetic and copies ran while one was open for 8% -> 27% of each run, Pallas kernels for 0% -> 0%
where the time goes in v4:
time: 124 us; the launch traced here: 123 us
  starting transfers between devices  38.7 us (31%)
  matrix products  23.9 us (19%)
  local copies, waits for them, and re-layouts  21.4 us (17%)
  waiting for transfers between devices  20.5 us (17%)
  other arithmetic  13.9 us (11%)
  between operations  4.43 us (4%)
    ppermute x10, starting transfers between devices, axis_exchange(): lax.ppermute(jnp.where(even, high, low), axis, swap_pairs(count, 0))  28 us
    ppermute x10, waiting for transfers between devices, axis_exchange(): lax.ppermute(jnp.where(even, high, low), axis, swap_pairs(count, 0))  20.5 us
    dot_general x16, matrix products, body(): jnp.dot(own_op[face_id * width:(face_id + 1) * width], direction, precisi...  10.2 us
    ppermute x10, starting transfers between devices, axis_exchange(): lax.ppermute(jnp.where(even, low, high), axis, swap_pairs(count, 1))  7.73 us
    dot_general x16, matrix products, body(): jnp.dot(extra_place[face_id * width:(face_id + 1) * width], extra_out, pr...  7.71 us
    dot_general x4, matrix products, body(): jnp.dot(extra_cols, direction, precision=lax.Precision.HIGH, preferred_el...  6.02 us
    gather x1, local copies, waits for them, and re-layouts, body(): jnp.take(extra_block.T, slot_map, axis=0) * slot_scale[:, None]  4.84 us
    unnamed x31, local copies, waits for them, and re-layouts  4.41 us
  transfers between devices with their start and end apart: 22, of which 5 were waited for; matrix products, arithmetic and copies ran while one was open for 27% of the time, Pallas kernels for 0%

profile of v4, /device:TPU:0, one launch (start us, length us, event | category | flops | bytes accessed | tf_op | source)
XLA Modules:
  0.0 122.9 jit_solution(2188267372230469155)
XLA Ops:
  0.7 1.0 bitcast_select_fusion.3
  1.6 1.3 %collective-permute-start = (f32[224,128]{1,0:T(8,128)S(1)}, f32[224,128]{1,0:T(8,128)}, u32[]{:S(2)}, u32[]{:S(2)}) collective-permute-start(f32[224,128]{1,0:T(8,128)S(1)} %get-tuple-element.14), channel_id=1, source_target_pairs={{4,8},{8,4},{12,16},{16,12},{20,24},{24,20},{5,9},{9,5},{13,17},{1... | collective-permute-start | bytes 344072 | tf_op jit(solution)/shard_map/ppermute | solution.py:60
  2.9 3.8 %collective-permute-start.1 = (f32[224,128]{1,0:T(8,128)S(1)}, f32[224,128]{1,0:T(8,128)}, u32[]{:S(2)}, u32[]{:S(2)}) collective-permute-start(f32[224,128]{1,0:T(8,128)S(1)} %get-tuple-element.15), channel_id=1, source_target_pairs={{0,4},{4,0},{8,12},{12,8},{16,20},{20,16},{24,28},{28,24},{1,5},{5... | collective-permute-start | bytes 344072 | tf_op jit(solution)/shard_map/ppermute | solution.py:61
  6.8 1.2 fusion.93
  8.0 1.0 copy.16
  8.9 1.9 %collective-permute-start.4 = (f32[128,896]{0,1:T(8,128)}, f32[128,896]{0,1:T(8,128)}, u32[]{:S(2)}, u32[]{:S(2)}) collective-permute-start(f32[128,896]{0,1:T(8,128)} %bitcast.14), channel_id=1, source_target_pairs={{0,24},{4,28},{8,0},{12,4},{16,8},{20,12},{24,16},{28,20},{1,25},{... | collective-permute-start | bytes 1376264 | tf_op jit(solution)/shard_map/ppermute | solution.py:22
  10.9 1.0 copy.17
  11.9 1.1 collective-permute-start.5
  13.7 2.4 %copy.12 = f32[1,1,640,896]{2,3,1,0:T(8,128)S(1)} copy(f32[1,1,640,896]{3,2,1,0:T(8,128)} %param.7) | data formatting | bytes 4587520 | tf_op args[1]
  16.2 3.9 %gather_fusion = f32[896,640]{1,0:T(8,128)} fusion(f32[896,640]{1,0:T(8,128)S(1)} %bitcast.91, s32[1024]{0:T(1024)S(1)} %pad_clamp_fusion.1), kind=kCustom, calls=%fused_computation | custom fusion | bytes 4591104 | tf_op jit(solution)/shard_map/jit(_take)/gather | solution.py:93
  20.1 3.4 %multiply_bitcast_fusion = f32[640,896]{0,1:T(8,128)} fusion(f32[896,640]{1,0:T(8,128)} %gather_fusion, f32[896]{0:T(1024)S(1)} %select_select_fusion, pred[896]{0:T(1024)(128)(4,1)S(1)} %get-tuple-element.49), kind=kLoop, calls=%fused_computation.4 | loop fusion | flops 1146880 | bytes 4592000 | tf_op jit(solution)/shard_map/mul | solution.py:93
  23.4 2.5 %copy.13 = f32[640,896]{1,0:T(8,128)S(1)} copy(f32[640,896]{0,1:T(8,128)} %multiply_bitcast_fusion) | data formatting | bytes 4587520 | tf_op jit(solution)/shard_map/mul | solution.py:93
  25.9 4.0 %gather_fusion.1 = f32[896,896]{1,0:T(8,128)} fusion(f32[640,896]{1,0:T(8,128)S(1)} %copy.13, s32[1024]{0:T(1024)S(1)} %pad_clamp_fusion), kind=kCustom, calls=%fused_computation.1 | custom fusion | bytes 6426112 | tf_op jit(solution)/shard_map/jit(_take)/gather | solution.py:96
  29.9 2.4 %select_multiply_fusion = f32[896,896]{1,0:T(8,128)S(1)} fusion(f32[896,896]{1,0:T(8,128)} %gather_fusion.1, f32[896]{0:T(1024)S(1)} %select_select_fusion, pred[896]{0:T(1024)(128)(4,1)S(1)} %get-tuple-element.50, pred[896]{0:T(1024)(128)(4,1)S(1)} %get-tuple-element.48), kind=kLoop, calls=%fused_computation.3 | loop fusion | flops 2408448 | bytes 6427904 | tf_op jit(solution)/shard_map/mul | solution.py:95
  32.4 1.0 bitcast_add_fusion.3
  34.1 4.3 %collective-permute-start.3 = (f32[224,128]{1,0:T(8,128)S(1)}, f32[224,128]{1,0:T(8,128)S(1)}, u32[]{:S(2)}, u32[]{:S(2)}) collective-permute-start(f32[224,128]{1,0:T(8,128)S(1)} %get-tuple-element.12), channel_id=1, source_target_pairs={{0,1},{1,0},{2,3},{3,2},{4,5},{5,4},{6,7},{7,6},{8,9},{9,8},{10,11... | collective-permute-start | bytes 344072 | tf_op jit(solution)/shard_map/ppermute | solution.py:61
  38.4 1.3 %fusion = f32[896,256]{1,0:T(8,128)} fusion(f32[896]{0:T(1024)S(1)} %select_select_fusion, s32[896]{0:T(1024)S(1)} %broadcast_add_fusion), kind=kLoop, calls=%fused_computation.24 | loop fusion | flops 458752 | bytes 924672 | tf_op jit(solution)/shard_map/jit(_where)/select_n | solution.py:110
  43.2 1.1 fusion.23
  44.4 1.1 fusion.31
  45.5 1.1 fusion.7
  46.6 1.1 fusion.15
  47.7 1.3 %select_add_fusion.1 = (f32[128,896]{0,1:T(8,128)S(1)}, f32[128,896]{0,1:T(8,128)S(1)}) fusion(f32[128,896]{0,1:T(8,128)} %collective-permute-done.5, f32[128,896]{0,1:T(8,128)} %collective-permute-done.4, pred[]{:T(512)} %bitcast.15, pred[]{:T(512)} %bitcast.13, pred[]{:T(512)} %bitcast.18, pred[]{:T(512)} %bitcast.17), kind=kLoop, calls=%fused_computation.80 | loop fusion | flops 688128 | bytes 1835012 | tf_op jit(solution)/shard_map/add | solution.py:102
  49.0 1.0 maximum_bitcast_fusion
  50.0 4.8 %gather_fusion.2 = f32[896,256]{1,0:T(8,128)} fusion(f32[896,256]{1,0:T(8,128)} %maximum_bitcast_fusion, s32[1024]{0:T(1024)} %copy-done.9), kind=kCustom, calls=%fused_computation.2 | custom fusion | bytes 1838592 | tf_op jit(solution)/shard_map/jit(_take)/gather | solution.py:108
  54.9 2.5 %fusion.36 = f32[256,128]{1,0:T(8,128)S(1)} fusion(f32[896,256]{1,0:T(8,128)} %gather_fusion.2, f32[896]{0:T(1024)} %copy-done.7, pred[896]{0:T(1024)(128)(4,1)} %copy-done.10, f32[224,128]{1,0:T(8,128)} %copy-done.2, f32[224,128]{1,0:T(8,128)S(1)} %get-tuple-element.10, f32[224,128]{1,0:T(8,128)S(1)} %get-tuple-element.9, f32[224,128]{1,0:T(8,128)S(1)} %get-tuple-element.8), kind=kOutput, calls=%fused_computation.60 | convolution fusion | flops 177078272 | bytes 1511808 | tf_op jit(solution)/shard_map/dot_general | solution.py:122
  57.3 1.4 %convolution_add_fusion.14 = f32[224,128]{1,0:T(8,128)S(1)} fusion(f32[224,128]{1,0:T(8,128)} %fusion.23, f32[256,128]{1,0:T(8,128)S(1)} %fusion.36, f32[896,256]{1,0:T(8,128)} %fusion), kind=kOutput, calls=%fused_computation.19 | convolution fusion | flops 88109056 | bytes 589824 | tf_op jit(solution)/shard_map/dot_general | solution.py:132
  58.7 1.4 %broadcast_select_fusion.15 = (f32[224,128]{1,0:T(8,128)S(1)}, f32[224,128]{1,0:T(8,128)S(1)}, f32[224,128]{1,0:T(8,128)S(1)}) fusion(f32[224,128]{1,0:T(8,128)S(1)} %convolution_add_fusion.14, pred[]{:T(512)S(6)} %eq.72, f32[224,128]{1,0:T(8,128)} %fusion.31, f32[256,128]{1,0:T(8,128)S(1)} %fusion.36, f32[896,256]{1,0:T(8,128)} %fusion), kind=kOutput, calls=%fused_computation.154 | convolution fusion | flops 88166400 | bytes 933889 | tf_op jit(solution)/shard_map/dot_general | solution.py:132
  60.1 0.7 collective-permute-start.6
  60.7 3.0 %collective-permute-start.7 = (f32[224,128]{1,0:T(8,128)S(1)}, f32[224,128]{1,0:T(8,128)S(1)}, u32[]{:S(2)}, u32[]{:S(2)}) collective-permute-start(f32[224,128]{1,0:T(8,128)S(1)} %get-tuple-element.43), channel_id=1, source_target_pairs={{0,4},{4,0},{8,12},{12,8},{16,20},{20,16},{24,28},{28,24},{1,5},{5... | collective-permute-start | bytes 344072 | tf_op jit(solution)/shard_map/ppermute | solution.py:61
  64.5 0.8 collective-permute-start.8
  65.4 3.0 %collective-permute-start.9 = (f32[224,128]{1,0:T(8,128)S(1)}, f32[224,128]{1,0:T(8,128)S(1)}, u32[]{:S(2)}, u32[]{:S(2)}) collective-permute-start(f32[224,128]{1,0:T(8,128)S(1)} %get-tuple-element.47), channel_id=1, source_target_pairs={{0,1},{1,0},{2,3},{3,2},{4,5},{5,4},{6,7},{7,6},{8,9},{9,8},{10,11... | collective-permute-start | bytes 344072 | tf_op jit(solution)/shard_map/ppermute | solution.py:61
  68.4 5.2 %collective-permute-done.9 = f32[224,128]{1,0:T(8,128)S(1)} collective-permute-done((f32[224,128]{1,0:T(8,128)S(1)}, f32[224,128]{1,0:T(8,128)S(1)}, u32[]{:S(2)}, u32[]{:S(2)}) %collective-permute-start.9) | collective-permute-done | bytes 114720 | tf_op jit(solution)/shard_map/ppermute | solution.py:61
  74.7 1.2 fusion.35
  77.6 0.7 collective-permute-start.10
  78.3 2.5 %collective-permute-start.11 = (f32[224,128]{1,0:T(8,128)S(1)}, f32[224,128]{1,0:T(8,128)S(1)}, u32[]{:S(2)}, u32[]{:S(2)}) collective-permute-start(f32[224,128]{1,0:T(8,128)S(1)} %get-tuple-element.35), channel_id=1, source_target_pairs={{0,4},{4,0},{8,12},{12,8},{16,20},{20,16},{24,28},{28,24},{1,5},{5... | collective-permute-start | bytes 344072 | tf_op jit(solution)/shard_map/ppermute | solution.py:61
  82.2 2.7 %collective-permute-start.13 = (f32[224,128]{1,0:T(8,128)S(1)}, f32[224,128]{1,0:T(8,128)S(1)}, u32[]{:S(2)}, u32[]{:S(2)}) collective-permute-start(f32[224,128]{1,0:T(8,128)S(1)} %get-tuple-element.39), channel_id=1, source_target_pairs={{0,1},{1,0},{2,3},{3,2},{4,5},{5,4},{6,7},{7,6},{8,9},{9,8},{10,11... | collective-permute-start | bytes 344072 | tf_op jit(solution)/shard_map/ppermute | solution.py:61
  84.9 5.4 %collective-permute-done.13 = f32[224,128]{1,0:T(8,128)S(1)} collective-permute-done((f32[224,128]{1,0:T(8,128)S(1)}, f32[224,128]{1,0:T(8,128)S(1)}, u32[]{:S(2)}, u32[]{:S(2)}) %collective-permute-start.13) | collective-permute-done | bytes 114720 | tf_op jit(solution)/shard_map/ppermute | solution.py:61
  91.4 1.2 fusion.34
  95.0 1.8 %collective-permute-start.15 = (f32[224,128]{1,0:T(8,128)S(1)}, f32[224,128]{1,0:T(8,128)S(1)}, u32[]{:S(2)}, u32[]{:S(2)}) collective-permute-start(f32[224,128]{1,0:T(8,128)S(1)} %get-tuple-element.27), channel_id=1, source_target_pairs={{0,4},{4,0},{8,12},{12,8},{16,20},{20,16},{24,28},{28,24},{1,5},{5... | collective-permute-start | bytes 344072 | tf_op jit(solution)/shard_map/ppermute | solution.py:61
  97.5 0.9 collective-permute-start.16
  98.4 2.3 %collective-permute-start.17 = (f32[224,128]{1,0:T(8,128)S(1)}, f32[224,128]{1,0:T(8,128)S(1)}, u32[]{:S(2)}, u32[]{:S(2)}) collective-permute-start(f32[224,128]{1,0:T(8,128)S(1)} %get-tuple-element.31), channel_id=1, source_target_pairs={{0,1},{1,0},{2,3},{3,2},{4,5},{5,4},{6,7},{7,6},{8,9},{9,8},{10,11... | collective-permute-start | bytes 344072 | tf_op jit(solution)/shard_map/ppermute | solution.py:61
  100.8 5.1 %collective-permute-done.17 = f32[224,128]{1,0:T(8,128)S(1)} collective-permute-done((f32[224,128]{1,0:T(8,128)S(1)}, f32[224,128]{1,0:T(8,128)S(1)}, u32[]{:S(2)}, u32[]{:S(2)}) %collective-permute-start.17) | collective-permute-done | bytes 114720 | tf_op jit(solution)/shard_map/ppermute | solution.py:61
  107.1 1.2 fusion.33
  110.6 2.2 %collective-permute-start.19 = (f32[224,128]{1,0:T(8,128)S(1)}, f32[224,128]{1,0:T(8,128)S(1)}, u32[]{:S(2)}, u32[]{:S(2)}) collective-permute-start(f32[224,128]{1,0:T(8,128)S(1)} %get-tuple-element.19), channel_id=1, source_target_pairs={{0,4},{4,0},{8,12},{12,8},{16,20},{20,16},{24,28},{28,24},{1,5},{5... | collective-permute-start | bytes 344072 | tf_op jit(solution)/shard_map/ppermute | solution.py:61
  114.2 2.4 %collective-permute-start.21 = (f32[224,128]{1,0:T(8,128)S(1)}, f32[224,128]{1,0:T(8,128)S(1)}, u32[]{:S(2)}, u32[]{:S(2)}) collective-permute-start(f32[224,128]{1,0:T(8,128)S(1)} %get-tuple-element.23), channel_id=1, source_target_pairs={{0,1},{1,0},{2,3},{3,2},{4,5},{5,4},{6,7},{7,6},{8,9},{9,8},{10,11... | collective-permute-start | bytes 344072 | tf_op jit(solution)/shard_map/ppermute | solution.py:61
  116.5 1.0 add_add_fusion
  117.6 4.3 %collective-permute-done.21 = f32[224,128]{1,0:T(8,128)S(1)} collective-permute-done((f32[224,128]{1,0:T(8,128)S(1)}, f32[224,128]{1,0:T(8,128)S(1)}, u32[]{:S(2)}, u32[]{:S(2)}) %collective-permute-start.21) | collective-permute-done | bytes 114720 | tf_op jit(solution)/shard_map/ppermute | solution.py:61
  122.0 0.9 maximum_subtract_fusion.6
  (97 shorter events, 15.8 us)
Async XLA Ops:
  0.6 12.3 %copy-start.12 = (s32[1,1,896]{2,1,0:T(1,128)S(1)}, s32[1,1,896]{2,1,0:T(1,128)}, u32[]{:S(2)}) copy-start(s32[1,1,896]{2,1,0:T(1,128)} %param.11) | copy-start | bytes 10756
  1.6 30.7 %collective-permute-start = (f32[224,128]{1,0:T(8,128)S(1)}, f32[224,128]{1,0:T(8,128)}, u32[]{:S(2)}, u32[]{:S(2)}) collective-permute-start(f32[224,128]{1,0:T(8,128)S(1)} %get-tuple-element.14), channel_id=1, source_target_pairs={{4,8},{8,4},{12,16},{16,12},{20,24},{24,20},{5,9},{9,5},{13,17},{1... | collective-permute-start | bytes 344072 | tf_op jit(solution)/shard_map/ppermute | solution.py:60
  2.9 29.4 %collective-permute-start.1 = (f32[224,128]{1,0:T(8,128)S(1)}, f32[224,128]{1,0:T(8,128)}, u32[]{:S(2)}, u32[]{:S(2)}) collective-permute-start(f32[224,128]{1,0:T(8,128)S(1)} %get-tuple-element.15), channel_id=1, source_target_pairs={{0,4},{4,0},{8,12},{12,8},{16,20},{20,16},{24,28},{28,24},{1,5},{5... | collective-permute-start | bytes 344072 | tf_op jit(solution)/shard_map/ppermute | solution.py:61
  8.9 38.8 %collective-permute-start.4 = (f32[128,896]{0,1:T(8,128)}, f32[128,896]{0,1:T(8,128)}, u32[]{:S(2)}, u32[]{:S(2)}) collective-permute-start(f32[128,896]{0,1:T(8,128)} %bitcast.14), channel_id=1, source_target_pairs={{0,24},{4,28},{8,0},{12,4},{16,8},{20,12},{24,16},{28,20},{1,25},{... | collective-permute-start | bytes 1376264 | tf_op jit(solution)/shard_map/ppermute | solution.py:22
  11.9 35.9 %collective-permute-start.5 = (f32[128,896]{0,1:T(8,128)}, f32[128,896]{0,1:T(8,128)}, u32[]{:S(2)}, u32[]{:S(2)}) collective-permute-start(f32[128,896]{0,1:T(8,128)} %bitcast.16), channel_id=1, source_target_pairs={{0,16},{4,20},{8,24},{12,28},{16,0},{20,4},{24,8},{28,12},{1,17},{... | collective-permute-start | bytes 1376264 | tf_op jit(solution)/shard_map/ppermute | solution.py:22
  13.7 6.4 %copy-start.10 = (pred[896]{0:T(1024)(128)(4,1)}, pred[896]{0:T(1024)(128)(4,1)S(1)}, u32[]{:S(2)}) copy-start(pred[896]{0:T(1024)(128)(4,1)S(1)} %get-tuple-element.49) | copy-start | bytes 2692
  13.7 24.6 %copy-start.7 = (f32[896]{0:T(1024)}, f32[896]{0:T(1024)S(1)}, u32[]{:S(2)}) copy-start(f32[896]{0:T(1024)S(1)} %select_select_fusion) | copy-start | bytes 10756
  13.7 6.3 %copy-start.9 = (s32[1024]{0:T(1024)}, s32[1024]{0:T(1024)S(1)}, u32[]{:S(2)}) copy-start(s32[1024]{0:T(1024)S(1)} %pad_clamp_fusion.1) | copy-start | bytes 12292
  29.9 2.4 %copy-start.4 = (f32[1,1,896,128]{3,2,1,0:T(8,128)S(1)}, f32[1,1,896,128]{3,2,1,0:T(8,128)}, u32[]{:S(2)}) copy-start(f32[1,1,896,128]{3,2,1,0:T(8,128)} %param.6) | copy-start | bytes 1376260
  29.9 9.7 %copy-start.13 = (s32[1,1,2]{2,1,0:T(1,128)S(1)}, s32[1,1,2]{2,1,0:T(1,128)}, u32[]{:S(2)}) copy-start(s32[1,1,2]{2,1,0:T(1,128)} %param.9) | copy-start | bytes 28
  33.4 9.4 %collective-permute-start.2 = (f32[224,128]{1,0:T(8,128)S(1)}, f32[224,128]{1,0:T(8,128)S(1)}, u32[]{:S(2)}, u32[]{:S(2)}) collective-permute-start(f32[224,128]{1,0:T(8,128)S(1)} %get-tuple-element.13), channel_id=1, source_target_pairs={{1,2},{2,1},{5,6},{6,5},{9,10},{10,9},{13,14},{14,13},{17,18},{18,... | collective-permute-start | bytes 344072 | tf_op jit(solution)/shard_map/ppermute | solution.py:60
  34.1 9.1 %collective-permute-start.3 = (f32[224,128]{1,0:T(8,128)S(1)}, f32[224,128]{1,0:T(8,128)S(1)}, u32[]{:S(2)}, u32[]{:S(2)}) collective-permute-start(f32[224,128]{1,0:T(8,128)S(1)} %get-tuple-element.12), channel_id=1, source_target_pairs={{0,1},{1,0},{2,3},{3,2},{4,5},{5,4},{6,7},{7,6},{8,9},{9,8},{10,11... | collective-permute-start | bytes 344072 | tf_op jit(solution)/shard_map/ppermute | solution.py:61
  43.2 5.7 %copy-start.2 = (f32[224,128]{1,0:T(8,128)}, f32[224,128]{1,0:T(8,128)S(1)}, u32[]{:S(2)}) copy-start(f32[224,128]{1,0:T(8,128)S(1)} %get-tuple-element.11) | copy-start | bytes 344068
  54.8 8.9 %copy-start = (f32[896,256]{1,0:T(8,128)S(1)}, f32[896,256]{1,0:T(8,128)}, u32[]{:S(2)}) copy-start(f32[896,256]{1,0:T(8,128)} %fusion) | copy-start | bytes 2752516
  54.8 8.9 %copy-start.6 = (f32[224,128]{1,0:T(8,128)S(1)}, f32[224,128]{1,0:T(8,128)}, u32[]{:S(2)}) copy-start(f32[224,128]{1,0:T(8,128)} %fusion.7) | copy-start | bytes 344068
  54.8 9.3 %copy-start.5 = (f32[224,128]{1,0:T(8,128)S(1)}, f32[224,128]{1,0:T(8,128)}, u32[]{:S(2)}) copy-start(f32[224,128]{1,0:T(8,128)} %fusion.15) | copy-start | bytes 344068
  54.8 18.8 %copy-start.3 = (f32[224,128]{1,0:T(8,128)S(1)}, f32[224,128]{1,0:T(8,128)}, u32[]{:S(2)}) copy-start(f32[224,128]{1,0:T(8,128)} %copy-done.2) | copy-start | bytes 344068
  60.1 8.3 %collective-permute-start.6 = (f32[224,128]{1,0:T(8,128)S(1)}, f32[224,128]{1,0:T(8,128)S(1)}, u32[]{:S(2)}, u32[]{:S(2)}) collective-permute-start(f32[224,128]{1,0:T(8,128)S(1)} %get-tuple-element.42), channel_id=1, source_target_pairs={{4,8},{8,4},{12,16},{16,12},{20,24},{24,20},{5,9},{9,5},{13,17},{1... | collective-permute-start | bytes 344072 | tf_op jit(solution)/shard_map/ppermute | solution.py:60
  60.7 7.6 %collective-permute-start.7 = (f32[224,128]{1,0:T(8,128)S(1)}, f32[224,128]{1,0:T(8,128)S(1)}, u32[]{:S(2)}, u32[]{:S(2)}) collective-permute-start(f32[224,128]{1,0:T(8,128)S(1)} %get-tuple-element.43), channel_id=1, source_target_pairs={{0,4},{4,0},{8,12},{12,8},{16,20},{20,16},{24,28},{28,24},{1,5},{5... | collective-permute-start | bytes 344072 | tf_op jit(solution)/shard_map/ppermute | solution.py:61
  64.1 10.6 %copy-start.1 = (f32[896,256]{1,0:T(8,128)S(1)}, f32[896,256]{1,0:T(8,128)}, u32[]{:S(2)}) copy-start(f32[896,256]{1,0:T(8,128)} %gather_fusion.2) | copy-start | bytes 2752516
  64.1 10.6 %copy-start.8 = (f32[896]{0:T(1024)S(1)}, f32[896]{0:T(1024)}, u32[]{:S(2)}) copy-start(f32[896]{0:T(1024)} %copy-done.7) | copy-start | bytes 10756
  64.1 10.6 %copy-start.11 = (pred[896]{0:T(1024)(128)(4,1)S(1)}, pred[896]{0:T(1024)(128)(4,1)}, u32[]{:S(2)}) copy-start(pred[896]{0:T(1024)(128)(4,1)} %copy-done.10) | copy-start | bytes 2692
  64.5 3.9 %collective-permute-start.8 = (f32[224,128]{1,0:T(8,128)S(1)}, f32[224,128]{1,0:T(8,128)S(1)}, u32[]{:S(2)}, u32[]{:S(2)}) collective-permute-start(f32[224,128]{1,0:T(8,128)S(1)} %get-tuple-element.46), channel_id=1, source_target_pairs={{1,2},{2,1},{5,6},{6,5},{9,10},{10,9},{13,14},{14,13},{17,18},{18,... | collective-permute-start | bytes 344072 | tf_op jit(solution)/shard_map/ppermute | solution.py:60
  65.4 8.3 %collective-permute-start.9 = (f32[224,128]{1,0:T(8,128)S(1)}, f32[224,128]{1,0:T(8,128)S(1)}, u32[]{:S(2)}, u32[]{:S(2)}) collective-permute-start(f32[224,128]{1,0:T(8,128)S(1)} %get-tuple-element.47), channel_id=1, source_target_pairs={{0,1},{1,0},{2,3},{3,2},{4,5},{5,4},{6,7},{7,6},{8,9},{9,8},{10,11... | collective-permute-start | bytes 344072 | tf_op jit(solution)/shard_map/ppermute | solution.py:61
  77.6 7.3 %collective-permute-start.10 = (f32[224,128]{1,0:T(8,128)S(1)}, f32[224,128]{1,0:T(8,128)S(1)}, u32[]{:S(2)}, u32[]{:S(2)}) collective-permute-start(f32[224,128]{1,0:T(8,128)S(1)} %get-tuple-element.34), channel_id=1, source_target_pairs={{4,8},{8,4},{12,16},{16,12},{20,24},{24,20},{5,9},{9,5},{13,17},{1... | collective-permute-start | bytes 344072 | tf_op jit(solution)/shard_map/ppermute | solution.py:60
  78.3 6.6 %collective-permute-start.11 = (f32[224,128]{1,0:T(8,128)S(1)}, f32[224,128]{1,0:T(8,128)S(1)}, u32[]{:S(2)}, u32[]{:S(2)}) collective-permute-start(f32[224,128]{1,0:T(8,128)S(1)} %get-tuple-element.35), channel_id=1, source_target_pairs={{0,4},{4,0},{8,12},{12,8},{16,20},{20,16},{24,28},{28,24},{1,5},{5... | collective-permute-start | bytes 344072 | tf_op jit(solution)/shard_map/ppermute | solution.py:61
  81.5 3.4 %collective-permute-start.12 = (f32[224,128]{1,0:T(8,128)S(1)}, f32[224,128]{1,0:T(8,128)S(1)}, u32[]{:S(2)}, u32[]{:S(2)}) collective-permute-start(f32[224,128]{1,0:T(8,128)S(1)} %get-tuple-element.38), channel_id=1, source_target_pairs={{1,2},{2,1},{5,6},{6,5},{9,10},{10,9},{13,14},{14,13},{17,18},{18,... | collective-permute-start | bytes 344072 | tf_op jit(solution)/shard_map/ppermute | solution.py:60
  82.2 8.1 %collective-permute-start.13 = (f32[224,128]{1,0:T(8,128)S(1)}, f32[224,128]{1,0:T(8,128)S(1)}, u32[]{:S(2)}, u32[]{:S(2)}) collective-permute-start(f32[224,128]{1,0:T(8,128)S(1)} %get-tuple-element.39), channel_id=1, source_target_pairs={{0,1},{1,0},{2,3},{3,2},{4,5},{5,4},{6,7},{7,6},{8,9},{9,8},{10,11... | collective-permute-start | bytes 344072 | tf_op jit(solution)/shard_map/ppermute | solution.py:61
  94.3 6.4 %collective-permute-start.14 = (f32[224,128]{1,0:T(8,128)S(1)}, f32[224,128]{1,0:T(8,128)S(1)}, u32[]{:S(2)}, u32[]{:S(2)}) collective-permute-start(f32[224,128]{1,0:T(8,128)S(1)} %get-tuple-element.26), channel_id=1, source_target_pairs={{4,8},{8,4},{12,16},{16,12},{20,24},{24,20},{5,9},{9,5},{13,17},{1... | collective-permute-start | bytes 344072 | tf_op jit(solution)/shard_map/ppermute | solution.py:60
  95.0 5.8 %collective-permute-start.15 = (f32[224,128]{1,0:T(8,128)S(1)}, f32[224,128]{1,0:T(8,128)S(1)}, u32[]{:S(2)}, u32[]{:S(2)}) collective-permute-start(f32[224,128]{1,0:T(8,128)S(1)} %get-tuple-element.27), channel_id=1, source_target_pairs={{0,4},{4,0},{8,12},{12,8},{16,20},{20,16},{24,28},{28,24},{1,5},{5... | collective-permute-start | bytes 344072 | tf_op jit(solution)/shard_map/ppermute | solution.py:61
  97.5 3.3 %collective-permute-start.16 = (f32[224,128]{1,0:T(8,128)S(1)}, f32[224,128]{1,0:T(8,128)S(1)}, u32[]{:S(2)}, u32[]{:S(2)}) collective-permute-start(f32[224,128]{1,0:T(8,128)S(1)} %get-tuple-element.30), channel_id=1, source_target_pairs={{1,2},{2,1},{5,6},{6,5},{9,10},{10,9},{13,14},{14,13},{17,18},{18,... | collective-permute-start | bytes 344072 | tf_op jit(solution)/shard_map/ppermute | solution.py:60
  98.4 7.5 %collective-permute-start.17 = (f32[224,128]{1,0:T(8,128)S(1)}, f32[224,128]{1,0:T(8,128)S(1)}, u32[]{:S(2)}, u32[]{:S(2)}) collective-permute-start(f32[224,128]{1,0:T(8,128)S(1)} %get-tuple-element.31), channel_id=1, source_target_pairs={{0,1},{1,0},{2,3},{3,2},{4,5},{5,4},{6,7},{7,6},{8,9},{9,8},{10,11... | collective-permute-start | bytes 344072 | tf_op jit(solution)/shard_map/ppermute | solution.py:61
  109.9 7.6 %collective-permute-start.18 = (f32[224,128]{1,0:T(8,128)S(1)}, f32[224,128]{1,0:T(8,128)S(1)}, u32[]{:S(2)}, u32[]{:S(2)}) collective-permute-start(f32[224,128]{1,0:T(8,128)S(1)} %get-tuple-element.18), channel_id=1, source_target_pairs={{4,8},{8,4},{12,16},{16,12},{20,24},{24,20},{5,9},{9,5},{13,17},{1... | collective-permute-start | bytes 344072 | tf_op jit(solution)/shard_map/ppermute | solution.py:60
  110.6 6.9 %collective-permute-start.19 = (f32[224,128]{1,0:T(8,128)S(1)}, f32[224,128]{1,0:T(8,128)S(1)}, u32[]{:S(2)}, u32[]{:S(2)}) collective-permute-start(f32[224,128]{1,0:T(8,128)S(1)} %get-tuple-element.19), channel_id=1, source_target_pairs={{0,4},{4,0},{8,12},{12,8},{16,20},{20,16},{24,28},{28,24},{1,5},{5... | collective-permute-start | bytes 344072 | tf_op jit(solution)/shard_map/ppermute | solution.py:61
  113.5 4.1 %collective-permute-start.20 = (f32[224,128]{1,0:T(8,128)S(1)}, f32[224,128]{1,0:T(8,128)S(1)}, u32[]{:S(2)}, u32[]{:S(2)}) collective-permute-start(f32[224,128]{1,0:T(8,128)S(1)} %get-tuple-element.22), channel_id=1, source_target_pairs={{1,2},{2,1},{5,6},{6,5},{9,10},{10,9},{13,14},{14,13},{17,18},{18,... | collective-permute-start | bytes 344072 | tf_op jit(solution)/shard_map/ppermute | solution.py:60
  114.2 7.8 %collective-permute-start.21 = (f32[224,128]{1,0:T(8,128)S(1)}, f32[224,128]{1,0:T(8,128)S(1)}, u32[]{:S(2)}, u32[]{:S(2)}) collective-permute-start(f32[224,128]{1,0:T(8,128)S(1)} %get-tuple-element.23), channel_id=1, source_target_pairs={{0,1},{1,0},{2,3},{3,2},{4,5},{5,4},{6,7},{7,6},{8,9},{9,8},{10,11... | collective-permute-start | bytes 344072 | tf_op jit(solution)/shard_map/ppermute | solution.py:61

commit v5 on v3

--- a/solution.py
+++ b/solution.py
@@ -71,6 +71,18 @@
     return jnp.concatenate([new_low_x, new_high_x, new_low_y, new_high_y], axis=0)
 
 
+def exact_select(pick, values):
+    high = lax.reduce_precision(values, exponent_bits=8, mantissa_bits=7)
+    rest = values - high
+    mid = lax.reduce_precision(rest, exponent_bits=8, mantissa_bits=7)
+    low = rest - mid
+    parts = [
+        jnp.dot(pick, piece.astype(jnp.bfloat16), preferred_element_type=jnp.float32)
+        for piece in (high, mid, low)
+    ]
+    return (parts[0] + parts[1]) + parts[2]
+
+
 def body(gap, own_rows, spill_rows, tile_plan, orders, slot_rows):
     order_max = gap.shape[2]
     tile_rows = spill_rows.shape[3]
@@ -87,6 +99,15 @@
     homed = [
         from_behind(spill_block[slot_id], "gx", -(slot_id + 1) * hop_span) for slot_id in range(2)
     ]
+    own_count = own_block.shape[0]
+    width = order_max // 4
+    load = face_sum_parts([gap[0, 0, face_id * width : (face_id + 1) * width] for face_id in range(4)])
+    to_slots = jnp.where(
+        slot_map[:, None] == row_ids[None, :], slot_scale[:, None], 0.0
+    ).astype(jnp.bfloat16)
+    to_rows = jnp.where(
+        row_ids[:, None] == slot_map[None, :], slot_scale[None, :], 0.0
+    ).astype(jnp.bfloat16)
     extra_rows = []
     for extra_id in range(2):
         gathered = jnp.zeros_like(homed[0])
@@ -95,12 +116,7 @@
                 plan_row[slot_id] == own_tiles + extra_id, homed[slot_id], 0.0
             )
         extra_rows.append(gathered)
-    operator = jnp.concatenate([own_block] + extra_rows, axis=0)
-    by_rows = jnp.take(operator, slot_map, axis=0)
-    by_cols = jnp.take(by_rows.T, slot_map, axis=0)
-    slot_op = (by_cols * slot_scale[:, None]).T * slot_scale[:, None]
-    width = order_max // 4
-    load = face_sum_parts([gap[0, 0, face_id * width : (face_id + 1) * width] for face_id in range(4)])
+    extra_block = jnp.concatenate(extra_rows, axis=0)
     centre = (high_bound + low_bound) / 2.0
     half_width = (high_bound - low_bound) / 2.0
     sigma_value = centre / half_width
@@ -110,14 +126,16 @@
     direction = residual / centre
     for step_id in range(ITERS):
         solution = solution + direction
-        width = order_max // 4
+        multipliers = exact_select(to_rows, direction)
+        own_out = jnp.dot(
+            own_block, multipliers, precision=lax.Precision.HIGH, preferred_element_type=jnp.float32
+        )
+        extra_out = jnp.dot(
+            extra_block, multipliers, precision=lax.Precision.HIGH, preferred_element_type=jnp.float32
+        )
         faces = [
-            jnp.dot(
-                slot_op[face_id * width : (face_id + 1) * width],
-                direction,
-                precision=lax.Precision.HIGH,
-                preferred_element_type=jnp.float32,
-            )
+            exact_select(to_slots[face_id * width : (face_id + 1) * width, :own_count], own_out)
+            + exact_select(to_slots[face_id * width : (face_id + 1) * width, own_count:], extra_out)
             for face_id in range(4)
         ]
         residual = residual - face_sum_parts(faces)

time: 128 us -> 124 us (0.969)
  matrix products: 17.7 us -> 34.1 us
  local copies, waits for them, and re-layouts: 13.8 us -> 2.82 us
  other arithmetic: 14.2 us -> 5.32 us
    dot_general x16 -> x116, matrix products: 17.7 us -> 34.1 us  [the longest x108 26.7 us: exact_select(): jnp.dot(pick, piece.astype(jnp.bfloat16), preferred_element_type=jnp.floa...]
    gather x2 -> x0, local copies, waits for them, and re-layouts: 8.43 us -> none  [the longest x1 4.21 us: body(): by_rows = jnp.take(operator, slot_map, axis=0)]
    ppermute x2, waiting for transfers between devices: 19.7 us -> 13.6 us  [from_behind(): return lax.ppermute(value, axis, pairs)]
    ppermute x10, waiting for transfers between devices: 16 us -> 21.1 us  [axis_exchange(): lax.ppermute(jnp.where(even, high, low), axis, swap_pairs(count, 0))]
    transpose x1 -> x0, other arithmetic: 3.85 us -> none  [body(): by_cols = jnp.take(by_rows.T, slot_map, axis=0)]
    transpose x1 -> x0, local copies, waits for them, and re-layouts: 3.44 us -> none  [body(): by_cols = jnp.take(by_rows.T, slot_map, axis=0)]
    mul x1 -> x0, other arithmetic: 2.36 us -> none  [body(): slot_op = (by_cols * slot_scale[:, None]).T * slot_scale[:, None]]
    add x8, other arithmetic: 1.93 us -> 0.26 us  [axis_exchange(): new_low = low + jnp.where(even, odd_recv, even_recv)]
  transfers between devices with their start and end apart: 22 -> 22, of which waited for: 6 -> 6; matrix products, arithmetic and copies ran while one was open for 8% -> 13% of each run, Pallas kernels for 0% -> 0%
where the time goes in v5:
time: 124 us; the launch traced here: 123 us
  starting transfers between devices  41.3 us (33%)
  waiting for transfers between devices  34.7 us (28%)
  matrix products  34.1 us (28%)
  other arithmetic  5.32 us (4%)
  between operations  5.1 us (4%)
  local copies, waits for them, and re-layouts  2.82 us (2%)
    ppermute x10, starting transfers between devices, axis_exchange(): lax.ppermute(jnp.where(even, high, low), axis, swap_pairs(count, 0))  31.2 us
    dot_general x108, matrix products, exact_select(): jnp.dot(pick, piece.astype(jnp.bfloat16), preferred_element_type=jnp.floa...  26.7 us
    ppermute x10, waiting for transfers between devices, axis_exchange(): lax.ppermute(jnp.where(even, high, low), axis, swap_pairs(count, 0))  21.1 us
    ppermute x2, waiting for transfers between devices, from_behind(): return lax.ppermute(value, axis, pairs)  13.6 us
    ppermute x10, starting transfers between devices, axis_exchange(): lax.ppermute(jnp.where(even, low, high), axis, swap_pairs(count, 1))  7.08 us
    dot_general x4, matrix products, body(): jnp.dot(own_block, multipliers, precision=lax.Precision.HIGH, preferred_e...  5.3 us
    ppermute x2, starting transfers between devices, from_behind(): return lax.ppermute(value, axis, pairs)  3.04 us
  transfers between devices with their start and end apart: 22, of which 6 were waited for; matrix products, arithmetic and copies ran while one was open for 13% of the time, Pallas kernels for 0%

profile of v5, /device:TPU:0, one launch (start us, length us, event | category | flops | bytes accessed | tf_op | source)
XLA Modules:
  0.0 123.4 jit_solution(642638200118043894)
XLA Ops:
  0.7 1.1 bitcast_select_fusion.3
  1.8 0.7 collective-permute-start
  2.5 4.4 %collective-permute-start.1 = (f32[224,128]{1,0:T(8,128)S(1)}, f32[224,128]{1,0:T(8,128)S(1)}, u32[]{:S(2)}, u32[]{:S(2)}) collective-permute-start(f32[224,128]{1,0:T(8,128)S(1)} %get-tuple-element.13), channel_id=1, source_target_pairs={{0,4},{4,0},{8,12},{12,8},{16,20},{20,16},{24,28},{28,24},{1,5},{5... | collective-permute-start | bytes 344072 | tf_op jit(solution)/shard_map/ppermute | solution.py:61
  6.9 2.1 %slice_bitcast_fusion.1 = (f32[128,896]{1,0:T(8,128)}, f32[128,896]{1,0:T(8,128)}) fusion(f32[1,1,2,128,896]{4,3,2,1,0:T(8,128)} %param.8), kind=kLoop, calls=%fused_computation.206 | loop fusion | bytes 1835008 | tf_op jit(solution)/shard_map/squeeze | solution.py:100
  9.1 1.9 %collective-permute-start.4 = (f32[128,896]{1,0:T(8,128)}, f32[128,896]{1,0:T(8,128)}, u32[]{:S(2)}, u32[]{:S(2)}) collective-permute-start(f32[128,896]{1,0:T(8,128)} %get-tuple-element.4), channel_id=1, source_target_pairs={{0,24},{4,28},{8,0},{12,4},{16,8},{20,12},{24,16},{28,20},{1,25},{... | collective-permute-start | bytes 1376264 | tf_op jit(solution)/shard_map/ppermute | solution.py:22
  11.0 1.1 collective-permute-start.5
  12.9 0.7 collective-permute-start.2
  13.6 4.3 %collective-permute-start.3 = (f32[224,128]{1,0:T(8,128)S(1)}, f32[224,128]{1,0:T(8,128)S(1)}, u32[]{:S(2)}, u32[]{:S(2)}) collective-permute-start(f32[224,128]{1,0:T(8,128)S(1)} %get-tuple-element.10), channel_id=1, source_target_pairs={{0,1},{1,0},{2,3},{3,2},{4,5},{5,4},{6,7},{7,6},{8,9},{9,8},{10,11... | collective-permute-start | bytes 344072 | tf_op jit(solution)/shard_map/ppermute | solution.py:61
  18.2 0.7 fusion.269
  21.6 1.0 collective-permute-done.3
  22.7 0.6 fusion.10
  23.3 0.6 fusion.56
  23.9 0.6 fusion.57
  24.6 1.4 %fusion.102 = (bf16[640,128]{0,1:T(8,128)(2,1)S(1)}, bf16[640,128]{0,1:T(8,128)(2,1)S(1)}, bf16[640,128]{0,1:T(8,128)(2,1)S(1)}) fusion(f32[896,128]{1,0:T(8,128)S(1)} %fusion.57, f32[1,1,640,896]{3,2,1,0:T(8,128)S(1)} %copy-done), kind=kOutput, calls=%fused_computation.211 | convolution fusion | flops 440975360 | bytes 3244032 | tf_op jit(solution)/shard_map/dot_general | solution.py:130
  28.9 13.6 %collective-permute-done.5 = f32[128,896]{1,0:T(8,128)} collective-permute-done((f32[128,896]{1,0:T(8,128)}, f32[128,896]{1,0:T(8,128)}, u32[]{:S(2)}, u32[]{:S(2)}) %collective-permute-start.5) | collective-permute-done | bytes 458784 | tf_op jit(solution)/shard_map/ppermute | solution.py:22
  42.5 1.2 %select_add_fusion.1 = (f32[128,896]{1,0:T(8,128)S(1)}, f32[128,896]{1,0:T(8,128)S(1)}) fusion(f32[128,896]{1,0:T(8,128)} %collective-permute-done.5, f32[128,896]{1,0:T(8,128)} %collective-permute-done.4, pred[]{:T(512)} %bitcast.13, pred[]{:T(512)} %bitcast.11, pred[]{:T(512)} %bitcast.16, pred[]{:T(512)} %bitcast.15), kind=kLoop, calls=%fused_computation.204 | loop fusion | flops 688128 | bytes 1835012 | tf_op jit(solution)/shard_map/add | solution.py:115
  45.7 0.7 collective-permute-start.6
  46.3 1.8 %collective-permute-start.7 = (f32[224,128]{1,0:T(8,128)S(1)}, f32[224,128]{1,0:T(8,128)S(1)}, u32[]{:S(2)}, u32[]{:S(2)}) collective-permute-start(f32[224,128]{1,0:T(8,128)S(1)} %get-tuple-element.53), channel_id=1, source_target_pairs={{0,4},{4,0},{8,12},{12,8},{16,20},{20,16},{24,28},{28,24},{1,5},{5... | collective-permute-start | bytes 344072 | tf_op jit(solution)/shard_map/ppermute | solution.py:61
  48.9 0.8 collective-permute-start.8
  49.7 4.3 %collective-permute-start.9 = (f32[224,128]{1,0:T(8,128)S(1)}, f32[224,128]{1,0:T(8,128)S(1)}, u32[]{:S(2)}, u32[]{:S(2)}) collective-permute-start(f32[224,128]{1,0:T(8,128)S(1)} %get-tuple-element.57), channel_id=1, source_target_pairs={{0,1},{1,0},{2,3},{3,2},{4,5},{5,4},{6,7},{7,6},{8,9},{9,8},{10,11... | collective-permute-start | bytes 344072 | tf_op jit(solution)/shard_map/ppermute | solution.py:61
  54.1 5.2 %collective-permute-done.9 = f32[224,128]{1,0:T(8,128)S(1)} collective-permute-done((f32[224,128]{1,0:T(8,128)S(1)}, f32[224,128]{1,0:T(8,128)S(1)}, u32[]{:S(2)}, u32[]{:S(2)}) %collective-permute-start.9) | collective-permute-done | bytes 114720 | tf_op jit(solution)/shard_map/ppermute | solution.py:61
  59.3 0.6 fusion.7
  59.9 0.6 fusion.58
  60.5 0.6 fusion.59
  61.7 1.3 %fusion.103 = (bf16[640,128]{0,1:T(8,128)(2,1)S(1)}, bf16[640,128]{0,1:T(8,128)(2,1)S(1)}, bf16[640,128]{0,1:T(8,128)(2,1)S(1)}) fusion(f32[896,128]{1,0:T(8,128)S(1)} %fusion.59, f32[1,1,640,896]{3,2,1,0:T(8,128)S(1)} %copy-done), kind=kOutput, calls=%fused_computation.212 | convolution fusion | flops 440975360 | bytes 3244032 | tf_op jit(solution)/shard_map/dot_general | solution.py:130
  66.4 0.7 collective-permute-start.10
  67.0 2.2 %collective-permute-start.11 = (f32[224,128]{1,0:T(8,128)S(1)}, f32[224,128]{1,0:T(8,128)S(1)}, u32[]{:S(2)}, u32[]{:S(2)}) collective-permute-start(f32[224,128]{1,0:T(8,128)S(1)} %get-tuple-element.45), channel_id=1, source_target_pairs={{0,4},{4,0},{8,12},{12,8},{16,20},{20,16},{24,28},{28,24},{1,5},{5... | collective-permute-start | bytes 344072 | tf_op jit(solution)/shard_map/ppermute | solution.py:61
  71.0 0.7 collective-permute-start.12
  71.6 2.3 %collective-permute-start.13 = (f32[224,128]{1,0:T(8,128)S(1)}, f32[224,128]{1,0:T(8,128)S(1)}, u32[]{:S(2)}, u32[]{:S(2)}) collective-permute-start(f32[224,128]{1,0:T(8,128)S(1)} %get-tuple-element.49), channel_id=1, source_target_pairs={{0,1},{1,0},{2,3},{3,2},{4,5},{5,4},{6,7},{7,6},{8,9},{9,8},{10,11... | collective-permute-start | bytes 344072 | tf_op jit(solution)/shard_map/ppermute | solution.py:61
  74.0 5.4 %collective-permute-done.13 = f32[224,128]{1,0:T(8,128)S(1)} collective-permute-done((f32[224,128]{1,0:T(8,128)S(1)}, f32[224,128]{1,0:T(8,128)S(1)}, u32[]{:S(2)}, u32[]{:S(2)}) %collective-permute-start.13) | collective-permute-done | bytes 114720 | tf_op jit(solution)/shard_map/ppermute | solution.py:61
  79.5 0.6 fusion.4
  80.7 0.6 fusion.61
  81.8 1.3 %fusion.104 = (bf16[640,128]{0,1:T(8,128)(2,1)S(1)}, bf16[640,128]{0,1:T(8,128)(2,1)S(1)}, bf16[640,128]{0,1:T(8,128)(2,1)S(1)}) fusion(f32[896,128]{1,0:T(8,128)S(1)} %fusion.61, f32[1,1,640,896]{3,2,1,0:T(8,128)S(1)} %copy-done), kind=kOutput, calls=%fused_computation.213 | convolution fusion | flops 440975360 | bytes 3244032 | tf_op jit(solution)/shard_map/dot_general | solution.py:130
  86.5 0.7 collective-permute-start.14
  87.2 5.0 %collective-permute-start.15 = (f32[224,128]{1,0:T(8,128)S(1)}, f32[224,128]{1,0:T(8,128)S(1)}, u32[]{:S(2)}, u32[]{:S(2)}) collective-permute-start(f32[224,128]{1,0:T(8,128)S(1)} %get-tuple-element.37), channel_id=1, source_target_pairs={{0,4},{4,0},{8,12},{12,8},{16,20},{20,16},{24,28},{28,24},{1,5},{5... | collective-permute-start | bytes 344072 | tf_op jit(solution)/shard_map/ppermute | solution.py:61
  93.8 0.9 collective-permute-start.16
  94.7 2.7 %collective-permute-start.17 = (f32[224,128]{1,0:T(8,128)S(1)}, f32[224,128]{1,0:T(8,128)S(1)}, u32[]{:S(2)}, u32[]{:S(2)}) collective-permute-start(f32[224,128]{1,0:T(8,128)S(1)} %get-tuple-element.41), channel_id=1, source_target_pairs={{0,1},{1,0},{2,3},{3,2},{4,5},{5,4},{6,7},{7,6},{8,9},{9,8},{10,11... | collective-permute-start | bytes 344072 | tf_op jit(solution)/shard_map/ppermute | solution.py:61
  97.5 5.1 %collective-permute-done.17 = f32[224,128]{1,0:T(8,128)S(1)} collective-permute-done((f32[224,128]{1,0:T(8,128)S(1)}, f32[224,128]{1,0:T(8,128)S(1)}, u32[]{:S(2)}, u32[]{:S(2)}) %collective-permute-start.17) | collective-permute-done | bytes 114720 | tf_op jit(solution)/shard_map/ppermute | solution.py:61
  103.4 0.6 fusion.62
  104.0 0.6 fusion.63
  105.2 1.3 %fusion.105 = (bf16[640,128]{0,1:T(8,128)(2,1)S(1)}, bf16[640,128]{0,1:T(8,128)(2,1)S(1)}, bf16[640,128]{0,1:T(8,128)(2,1)S(1)}) fusion(f32[896,128]{1,0:T(8,128)S(1)} %fusion.63, f32[1,1,640,896]{3,2,1,0:T(8,128)S(1)} %copy-done), kind=kOutput, calls=%fused_computation.214 | convolution fusion | flops 440975360 | bytes 3244032 | tf_op jit(solution)/shard_map/dot_general | solution.py:130
  109.8 0.7 collective-permute-start.18
  110.5 1.8 %collective-permute-start.19 = (f32[224,128]{1,0:T(8,128)S(1)}, f32[224,128]{1,0:T(8,128)S(1)}, u32[]{:S(2)}, u32[]{:S(2)}) collective-permute-start(f32[224,128]{1,0:T(8,128)S(1)} %get-tuple-element.29), channel_id=1, source_target_pairs={{0,4},{4,0},{8,12},{12,8},{16,20},{20,16},{24,28},{28,24},{1,5},{5... | collective-permute-start | bytes 344072 | tf_op jit(solution)/shard_map/ppermute | solution.py:61
  114.0 0.7 collective-permute-start.20
  114.6 2.3 %collective-permute-start.21 = (f32[224,128]{1,0:T(8,128)S(1)}, f32[224,128]{1,0:T(8,128)S(1)}, u32[]{:S(2)}, u32[]{:S(2)}) collective-permute-start(f32[224,128]{1,0:T(8,128)S(1)} %get-tuple-element.33), channel_id=1, source_target_pairs={{0,1},{1,0},{2,3},{3,2},{4,5},{5,4},{6,7},{7,6},{8,9},{9,8},{10,11... | collective-permute-start | bytes 344072 | tf_op jit(solution)/shard_map/ppermute | solution.py:61
  117.0 1.0 add_add_fusion
  118.0 4.4 %collective-permute-done.21 = f32[224,128]{1,0:T(8,128)S(1)} collective-permute-done((f32[224,128]{1,0:T(8,128)S(1)}, f32[224,128]{1,0:T(8,128)S(1)}, u32[]{:S(2)}, u32[]{:S(2)}) %collective-permute-start.21) | collective-permute-done | bytes 114720 | tf_op jit(solution)/shard_map/ppermute | solution.py:61
  122.4 0.9 maximum_subtract_fusion.6
  (141 shorter events, 23.8 us)
Async XLA Ops:
  0.6 23.9 %copy-start = (f32[1,1,640,896]{3,2,1,0:T(8,128)S(1)}, f32[1,1,640,896]{3,2,1,0:T(8,128)}, u32[]{:S(2)}) copy-start(f32[1,1,640,896]{3,2,1,0:T(8,128)} %param.7) | copy-start | bytes 6881284
  0.6 12.2 %copy-start.1 = (f32[1,1,896,128]{3,2,1,0:T(8,128)S(1)}, f32[1,1,896,128]{3,2,1,0:T(8,128)}, u32[]{:S(2)}) copy-start(f32[1,1,896,128]{3,2,1,0:T(8,128)} %param.6) | copy-start | bytes 1376260
  0.7 11.5 %copy-start.2 = (s32[1,1,896]{2,1,0:T(1,128)S(1)}, s32[1,1,896]{2,1,0:T(1,128)}, u32[]{:S(2)}) copy-start(s32[1,1,896]{2,1,0:T(1,128)} %param.11) | copy-start | bytes 10756
  1.8 11.0 %collective-permute-start = (f32[224,128]{1,0:T(8,128)S(1)}, f32[224,128]{1,0:T(8,128)S(1)}, u32[]{:S(2)}, u32[]{:S(2)}) collective-permute-start(f32[224,128]{1,0:T(8,128)S(1)} %get-tuple-element.12), channel_id=1, source_target_pairs={{4,8},{8,4},{12,16},{16,12},{20,24},{24,20},{5,9},{9,5},{13,17},{1... | collective-permute-start | bytes 344072 | tf_op jit(solution)/shard_map/ppermute | solution.py:60
  2.5 10.3 %collective-permute-start.1 = (f32[224,128]{1,0:T(8,128)S(1)}, f32[224,128]{1,0:T(8,128)S(1)}, u32[]{:S(2)}, u32[]{:S(2)}) collective-permute-start(f32[224,128]{1,0:T(8,128)S(1)} %get-tuple-element.13), channel_id=1, source_target_pairs={{0,4},{4,0},{8,12},{12,8},{16,20},{20,16},{24,28},{28,24},{1,5},{5... | collective-permute-start | bytes 344072 | tf_op jit(solution)/shard_map/ppermute | solution.py:61
  9.1 9.1 %copy-start.3 = (s32[1,1,2]{2,1,0:T(1,128)S(1)}, s32[1,1,2]{2,1,0:T(1,128)}, u32[]{:S(2)}) copy-start(s32[1,1,2]{2,1,0:T(1,128)} %param.9) | copy-start | bytes 28
  9.1 19.8 %collective-permute-start.4 = (f32[128,896]{1,0:T(8,128)}, f32[128,896]{1,0:T(8,128)}, u32[]{:S(2)}, u32[]{:S(2)}) collective-permute-start(f32[128,896]{1,0:T(8,128)} %get-tuple-element.4), channel_id=1, source_target_pairs={{0,24},{4,28},{8,0},{12,4},{16,8},{20,12},{24,16},{28,20},{1,25},{... | collective-permute-start | bytes 1376264 | tf_op jit(solution)/shard_map/ppermute | solution.py:22
  11.0 31.5 %collective-permute-start.5 = (f32[128,896]{1,0:T(8,128)}, f32[128,896]{1,0:T(8,128)}, u32[]{:S(2)}, u32[]{:S(2)}) collective-permute-start(f32[128,896]{1,0:T(8,128)} %get-tuple-element.5), channel_id=1, source_target_pairs={{0,16},{4,20},{8,24},{12,28},{16,0},{20,4},{24,8},{28,12},{1,17},{... | collective-permute-start | bytes 1376264 | tf_op jit(solution)/shard_map/ppermute | solution.py:22
  12.9 8.8 %collective-permute-start.2 = (f32[224,128]{1,0:T(8,128)S(1)}, f32[224,128]{1,0:T(8,128)S(1)}, u32[]{:S(2)}, u32[]{:S(2)}) collective-permute-start(f32[224,128]{1,0:T(8,128)S(1)} %get-tuple-element.11), channel_id=1, source_target_pairs={{1,2},{2,1},{5,6},{6,5},{9,10},{10,9},{13,14},{14,13},{17,18},{18,... | collective-permute-start | bytes 344072 | tf_op jit(solution)/shard_map/ppermute | solution.py:60
  13.6 9.1 %collective-permute-start.3 = (f32[224,128]{1,0:T(8,128)S(1)}, f32[224,128]{1,0:T(8,128)S(1)}, u32[]{:S(2)}, u32[]{:S(2)}) collective-permute-start(f32[224,128]{1,0:T(8,128)S(1)} %get-tuple-element.10), channel_id=1, source_target_pairs={{0,1},{1,0},{2,3},{3,2},{4,5},{5,4},{6,7},{7,6},{8,9},{9,8},{10,11... | collective-permute-start | bytes 344072 | tf_op jit(solution)/shard_map/ppermute | solution.py:61
  45.7 8.3 %collective-permute-start.6 = (f32[224,128]{1,0:T(8,128)S(1)}, f32[224,128]{1,0:T(8,128)S(1)}, u32[]{:S(2)}, u32[]{:S(2)}) collective-permute-start(f32[224,128]{1,0:T(8,128)S(1)} %get-tuple-element.52), channel_id=1, source_target_pairs={{4,8},{8,4},{12,16},{16,12},{20,24},{24,20},{5,9},{9,5},{13,17},{1... | collective-permute-start | bytes 344072 | tf_op jit(solution)/shard_map/ppermute | solution.py:60
  46.3 7.7 %collective-permute-start.7 = (f32[224,128]{1,0:T(8,128)S(1)}, f32[224,128]{1,0:T(8,128)S(1)}, u32[]{:S(2)}, u32[]{:S(2)}) collective-permute-start(f32[224,128]{1,0:T(8,128)S(1)} %get-tuple-element.53), channel_id=1, source_target_pairs={{0,4},{4,0},{8,12},{12,8},{16,20},{20,16},{24,28},{28,24},{1,5},{5... | collective-permute-start | bytes 344072 | tf_op jit(solution)/shard_map/ppermute | solution.py:61
  48.9 5.2 %collective-permute-start.8 = (f32[224,128]{1,0:T(8,128)S(1)}, f32[224,128]{1,0:T(8,128)S(1)}, u32[]{:S(2)}, u32[]{:S(2)}) collective-permute-start(f32[224,128]{1,0:T(8,128)S(1)} %get-tuple-element.56), channel_id=1, source_target_pairs={{1,2},{2,1},{5,6},{6,5},{9,10},{10,9},{13,14},{14,13},{17,18},{18,... | collective-permute-start | bytes 344072 | tf_op jit(solution)/shard_map/ppermute | solution.py:60
  49.7 9.5 %collective-permute-start.9 = (f32[224,128]{1,0:T(8,128)S(1)}, f32[224,128]{1,0:T(8,128)S(1)}, u32[]{:S(2)}, u32[]{:S(2)}) collective-permute-start(f32[224,128]{1,0:T(8,128)S(1)} %get-tuple-element.57), channel_id=1, source_target_pairs={{0,1},{1,0},{2,3},{3,2},{4,5},{5,4},{6,7},{7,6},{8,9},{9,8},{10,11... | collective-permute-start | bytes 344072 | tf_op jit(solution)/shard_map/ppermute | solution.py:61
  66.4 7.5 %collective-permute-start.10 = (f32[224,128]{1,0:T(8,128)S(1)}, f32[224,128]{1,0:T(8,128)S(1)}, u32[]{:S(2)}, u32[]{:S(2)}) collective-permute-start(f32[224,128]{1,0:T(8,128)S(1)} %get-tuple-element.44), channel_id=1, source_target_pairs={{4,8},{8,4},{12,16},{16,12},{20,24},{24,20},{5,9},{9,5},{13,17},{1... | collective-permute-start | bytes 344072 | tf_op jit(solution)/shard_map/ppermute | solution.py:60
  67.0 6.9 %collective-permute-start.11 = (f32[224,128]{1,0:T(8,128)S(1)}, f32[224,128]{1,0:T(8,128)S(1)}, u32[]{:S(2)}, u32[]{:S(2)}) collective-permute-start(f32[224,128]{1,0:T(8,128)S(1)} %get-tuple-element.45), channel_id=1, source_target_pairs={{0,4},{4,0},{8,12},{12,8},{16,20},{20,16},{24,28},{28,24},{1,5},{5... | collective-permute-start | bytes 344072 | tf_op jit(solution)/shard_map/ppermute | solution.py:61
  71.0 3.0 %collective-permute-start.12 = (f32[224,128]{1,0:T(8,128)S(1)}, f32[224,128]{1,0:T(8,128)S(1)}, u32[]{:S(2)}, u32[]{:S(2)}) collective-permute-start(f32[224,128]{1,0:T(8,128)S(1)} %get-tuple-element.48), channel_id=1, source_target_pairs={{1,2},{2,1},{5,6},{6,5},{9,10},{10,9},{13,14},{14,13},{17,18},{18,... | collective-permute-start | bytes 344072 | tf_op jit(solution)/shard_map/ppermute | solution.py:60
  71.6 7.7 %collective-permute-start.13 = (f32[224,128]{1,0:T(8,128)S(1)}, f32[224,128]{1,0:T(8,128)S(1)}, u32[]{:S(2)}, u32[]{:S(2)}) collective-permute-start(f32[224,128]{1,0:T(8,128)S(1)} %get-tuple-element.49), channel_id=1, source_target_pairs={{0,1},{1,0},{2,3},{3,2},{4,5},{5,4},{6,7},{7,6},{8,9},{9,8},{10,11... | collective-permute-start | bytes 344072 | tf_op jit(solution)/shard_map/ppermute | solution.py:61
  86.5 11.0 %collective-permute-start.14 = (f32[224,128]{1,0:T(8,128)S(1)}, f32[224,128]{1,0:T(8,128)S(1)}, u32[]{:S(2)}, u32[]{:S(2)}) collective-permute-start(f32[224,128]{1,0:T(8,128)S(1)} %get-tuple-element.36), channel_id=1, source_target_pairs={{4,8},{8,4},{12,16},{16,12},{20,24},{24,20},{5,9},{9,5},{13,17},{1... | collective-permute-start | bytes 344072 | tf_op jit(solution)/shard_map/ppermute | solution.py:60
  87.2 10.3 %collective-permute-start.15 = (f32[224,128]{1,0:T(8,128)S(1)}, f32[224,128]{1,0:T(8,128)S(1)}, u32[]{:S(2)}, u32[]{:S(2)}) collective-permute-start(f32[224,128]{1,0:T(8,128)S(1)} %get-tuple-element.37), channel_id=1, source_target_pairs={{0,4},{4,0},{8,12},{12,8},{16,20},{20,16},{24,28},{28,24},{1,5},{5... | collective-permute-start | bytes 344072 | tf_op jit(solution)/shard_map/ppermute | solution.py:61
  93.8 3.7 %collective-permute-start.16 = (f32[224,128]{1,0:T(8,128)S(1)}, f32[224,128]{1,0:T(8,128)S(1)}, u32[]{:S(2)}, u32[]{:S(2)}) collective-permute-start(f32[224,128]{1,0:T(8,128)S(1)} %get-tuple-element.40), channel_id=1, source_target_pairs={{1,2},{2,1},{5,6},{6,5},{9,10},{10,9},{13,14},{14,13},{17,18},{18,... | collective-permute-start | bytes 344072 | tf_op jit(solution)/shard_map/ppermute | solution.py:60
  94.7 7.9 %collective-permute-start.17 = (f32[224,128]{1,0:T(8,128)S(1)}, f32[224,128]{1,0:T(8,128)S(1)}, u32[]{:S(2)}, u32[]{:S(2)}) collective-permute-start(f32[224,128]{1,0:T(8,128)S(1)} %get-tuple-element.41), channel_id=1, source_target_pairs={{0,1},{1,0},{2,3},{3,2},{4,5},{5,4},{6,7},{7,6},{8,9},{9,8},{10,11... | collective-permute-start | bytes 344072 | tf_op jit(solution)/shard_map/ppermute | solution.py:61
  109.8 8.2 %collective-permute-start.18 = (f32[224,128]{1,0:T(8,128)S(1)}, f32[224,128]{1,0:T(8,128)S(1)}, u32[]{:S(2)}, u32[]{:S(2)}) collective-permute-start(f32[224,128]{1,0:T(8,128)S(1)} %get-tuple-element.28), channel_id=1, source_target_pairs={{4,8},{8,4},{12,16},{16,12},{20,24},{24,20},{5,9},{9,5},{13,17},{1... | collective-permute-start | bytes 344072 | tf_op jit(solution)/shard_map/ppermute | solution.py:60
  110.5 7.5 %collective-permute-start.19 = (f32[224,128]{1,0:T(8,128)S(1)}, f32[224,128]{1,0:T(8,128)S(1)}, u32[]{:S(2)}, u32[]{:S(2)}) collective-permute-start(f32[224,128]{1,0:T(8,128)S(1)} %get-tuple-element.29), channel_id=1, source_target_pairs={{0,4},{4,0},{8,12},{12,8},{16,20},{20,16},{24,28},{28,24},{1,5},{5... | collective-permute-start | bytes 344072 | tf_op jit(solution)/shard_map/ppermute | solution.py:61
  114.0 4.1 %collective-permute-start.20 = (f32[224,128]{1,0:T(8,128)S(1)}, f32[224,128]{1,0:T(8,128)S(1)}, u32[]{:S(2)}, u32[]{:S(2)}) collective-permute-start(f32[224,128]{1,0:T(8,128)S(1)} %get-tuple-element.32), channel_id=1, source_target_pairs={{1,2},{2,1},{5,6},{6,5},{9,10},{10,9},{13,14},{14,13},{17,18},{18,... | collective-permute-start | bytes 344072 | tf_op jit(solution)/shard_map/ppermute | solution.py:60
  114.6 7.8 %collective-permute-start.21 = (f32[224,128]{1,0:T(8,128)S(1)}, f32[224,128]{1,0:T(8,128)S(1)}, u32[]{:S(2)}, u32[]{:S(2)}) collective-permute-start(f32[224,128]{1,0:T(8,128)S(1)} %get-tuple-element.33), channel_id=1, source_target_pairs={{0,1},{1,0},{2,3},{3,2},{4,5},{5,4},{6,7},{7,6},{8,9},{9,8},{10,11... | collective-permute-start | bytes 344072 | tf_op jit(solution)/shard_map/ppermute | solution.py:61

commit v6 on v5

--- a/solution.py
+++ b/solution.py
@@ -71,16 +71,14 @@
     return jnp.concatenate([new_low_x, new_high_x, new_low_y, new_high_y], axis=0)
 
 
-def exact_select(pick, values):
-    high = lax.reduce_precision(values, exponent_bits=8, mantissa_bits=7)
-    rest = values - high
-    mid = lax.reduce_precision(rest, exponent_bits=8, mantissa_bits=7)
-    low = rest - mid
-    parts = [
-        jnp.dot(pick, piece.astype(jnp.bfloat16), preferred_element_type=jnp.float32)
-        for piece in (high, mid, low)
-    ]
-    return (parts[0] + parts[1]) + parts[2]
+def slot_pieces(rows, to_rows, to_slots):
+    high = lax.reduce_precision(rows, exponent_bits=8, mantissa_bits=7)
+    mid = lax.reduce_precision(rows - high, exponent_bits=8, mantissa_bits=7)
+    count = rows.shape[0]
+    stacked = jnp.concatenate([high, mid], axis=0).astype(jnp.bfloat16)
+    by_cols = jnp.dot(stacked, to_rows, preferred_element_type=jnp.float32).astype(jnp.bfloat16)
+    side = jnp.concatenate([by_cols[:count], by_cols[count:]], axis=1)
+    return jnp.dot(to_slots, side, preferred_element_type=jnp.float32)
 
 
 def body(gap, own_rows, spill_rows, tile_plan, orders, slot_rows):
@@ -100,6 +98,7 @@
         from_behind(spill_block[slot_id], "gx", -(slot_id + 1) * hop_span) for slot_id in range(2)
     ]
     own_count = own_block.shape[0]
+    cols = gap.shape[3]
     width = order_max // 4
     load = face_sum_parts([gap[0, 0, face_id * width : (face_id + 1) * width] for face_id in range(4)])
     to_slots = jnp.where(
@@ -108,6 +107,7 @@
     to_rows = jnp.where(
         row_ids[:, None] == slot_map[None, :], slot_scale[None, :], 0.0
     ).astype(jnp.bfloat16)
+    own_slots = slot_pieces(own_block, to_rows, to_slots[:, :own_count])
     extra_rows = []
     for extra_id in range(2):
         gathered = jnp.zeros_like(homed[0])
@@ -117,6 +117,9 @@
             )
         extra_rows.append(gathered)
     extra_block = jnp.concatenate(extra_rows, axis=0)
+    extra_slots = slot_pieces(extra_block, to_rows, to_slots[:, own_count:])
+    op_high = (own_slots[:, :order_max] + extra_slots[:, :order_max]).astype(jnp.bfloat16)
+    op_mid = (own_slots[:, order_max:] + extra_slots[:, order_max:]).astype(jnp.bfloat16)
     centre = (high_bound + low_bound) / 2.0
     half_width = (high_bound - low_bound) / 2.0
     sigma_value = centre / half_width
@@ -126,18 +129,17 @@
     direction = residual / centre
     for step_id in range(ITERS):
         solution = solution + direction
-        multipliers = exact_select(to_rows, direction)
-        own_out = jnp.dot(
-            own_block, multipliers, precision=lax.Precision.HIGH, preferred_element_type=jnp.float32
+        dir_high = lax.reduce_precision(direction, exponent_bits=8, mantissa_bits=7)
+        dir_mid = direction - dir_high
+        both = jnp.dot(
+            op_high,
+            jnp.concatenate([dir_high, dir_mid], axis=1).astype(jnp.bfloat16),
+            preferred_element_type=jnp.float32,
         )
-        extra_out = jnp.dot(
-            extra_block, multipliers, precision=lax.Precision.HIGH, preferred_element_type=jnp.float32
+        local = (both[:, :cols] + both[:, cols:]) + jnp.dot(
+            op_mid, dir_high.astype(jnp.bfloat16), preferred_element_type=jnp.float32
         )
-        faces = [
-            exact_select(to_slots[face_id * width : (face_id + 1) * width, :own_count], own_out)
-            + exact_select(to_slots[face_id * width : (face_id + 1) * width, own_count:], extra_out)
-            for face_id in range(4)
-        ]
+        faces = [local[face_id * width : (face_id + 1) * width] for face_id in range(4)]
         residual = residual - face_sum_parts(faces)
         if step_id + 1 < ITERS:
             rho_next = 1.0 / (2.0 * sigma_value - rho_value)

time: 124 us -> 110 us (0.89)
  the two profiles are of different devices: /device:TPU:0 before, /device:TPU:12 now
where the time goes in v6:
time: 110 us
  waiting for transfers between devices  41.3 us (38%)
  starting transfers between devices  37.4 us (34%)
  matrix products  13.7 us (12%)
  other arithmetic  8.09 us (7%)
  local copies, waits for them, and re-layouts  4.99 us (5%)
  between operations  4.16 us (4%)
    ppermute x10, starting transfers between devices, axis_exchange(): lax.ppermute(jnp.where(even, low, high), axis, swap_pairs(count, 1))  23.2 us
    ppermute x10, waiting for transfers between devices, axis_exchange(): lax.ppermute(jnp.where(even, low, high), axis, swap_pairs(count, 1))  22.5 us
    ppermute x10, starting transfers between devices, axis_exchange(): lax.ppermute(jnp.where(even, high, low), axis, swap_pairs(count, 0))  11.1 us
    ppermute x2, waiting for transfers between devices, from_behind(): return lax.ppermute(value, axis, pairs)  11 us
    ppermute x10, waiting for transfers between devices, axis_exchange(): lax.ppermute(jnp.where(even, high, low), axis, swap_pairs(count, 0))  7.84 us
    dot_general x2, matrix products, slot_pieces(): return jnp.dot(to_slots, side, preferred_element_type=jnp.float32)  4.98 us
    dot_general x2, matrix products, slot_pieces(): jnp.dot(stacked, to_rows, preferred_element_type=jnp.float32)  3.8 us
    ppermute x2, starting transfers between devices, from_behind(): return lax.ppermute(value, axis, pairs)  3.04 us
  transfers between devices with their start and end apart: 22, of which 13 were waited for; matrix products, arithmetic and copies ran while one was open for 12% of the time, Pallas kernels for 0%

profile of v6, /device:TPU:12, one launch (start us, length us, event | category | flops | bytes accessed | tf_op | source)
XLA Modules:
  0.0 109.7 jit_solution(1483925393529880590)
XLA Ops:
  0.7 1.1 %bitcast_select_fusion.3 = (f32[224,128]{1,0:T(8,128)S(1)}, f32[224,128]{1,0:T(8,128)S(1)}) fusion(f32[1,1,896,128]{3,2,1,0:T(8,128)} %param.6, pred[]{:T(512)S(6)} %eq.91), kind=kLoop, calls=%fused_computation.102 | loop fusion | flops 57344 | bytes 458753 | tf_op jit(solution)/shard_map/jit(_where)/select_n | solution.py:60
  1.8 1.9 %collective-permute-start = (f32[224,128]{1,0:T(8,128)S(1)}, f32[224,128]{1,0:T(8,128)S(1)}, u32[]{:S(2)}, u32[]{:S(2)}) collective-permute-start(f32[224,128]{1,0:T(8,128)S(1)} %get-tuple-element.62), channel_id=1, source_target_pairs={{4,8},{8,4},{12,16},{16,12},{20,24},{24,20},{5,9},{9,5},{13,17},{1... | collective-permute-start | bytes 344072 | tf_op jit(solution)/shard_map/ppermute | solution.py:60
  3.7 1.7 %collective-permute-start.1 = (f32[224,128]{1,0:T(8,128)S(1)}, f32[224,128]{1,0:T(8,128)}, u32[]{:S(2)}, u32[]{:S(2)}) collective-permute-start(f32[224,128]{1,0:T(8,128)S(1)} %get-tuple-element.63), channel_id=1, source_target_pairs={{0,4},{4,0},{8,12},{12,8},{16,20},{20,16},{24,28},{28,24},{1,5},{5... | collective-permute-start | bytes 344072 | tf_op jit(solution)/shard_map/ppermute | solution.py:61
  5.5 2.1 %slice_bitcast_fusion.1 = (f32[128,896]{1,0:T(8,128)}, f32[128,896]{1,0:T(8,128)}) fusion(f32[1,1,2,128,896]{4,3,2,1,0:T(8,128)} %param.8), kind=kLoop, calls=%fused_computation.95 | loop fusion | bytes 1835008 | tf_op jit(solution)/shard_map/squeeze | solution.py:98
  8.1 2.6 %collective-permute-start.5 = (f32[128,896]{1,0:T(8,128)}, f32[128,896]{1,0:T(8,128)}, u32[]{:S(2)}, u32[]{:S(2)}) collective-permute-start(f32[128,896]{1,0:T(8,128)} %get-tuple-element.21), channel_id=1, source_target_pairs={{0,16},{4,20},{8,24},{12,28},{16,0},{20,4},{24,8},{28,12},{1,17},{... | collective-permute-start | bytes 1376264 | tf_op jit(solution)/shard_map/ppermute | solution.py:22
  11.9 2.6 %convolution_convert_fusion = bf16[1280,896]{0,1:T(8,128)(2,1)S(1)} fusion(bf16[640,896]{1,0:T(8,128)(2,1)S(1)} %get-tuple-element.13, bf16[640,896]{1,0:T(8,128)(2,1)S(1)} %get-tuple-element.12, bf16[896]{0:T(1024)(128)(2,1)S(1)} %select_select_fusion, s32[896]{0:T(1024)S(1)} %reduce), kind=kOutput, calls=%fused_computation | convolution fusion | flops 2062548992 | bytes 4592896 | tf_op jit(solution)/shard_map/dot_general | solution.py:79
  14.5 1.3 %fusion.68 = (bf16[640,896]{0,1:T(8,128)(2,1)S(1)}, bf16[640,896]{0,1:T(8,128)(2,1)}) fusion(bf16[1280,896]{0,1:T(8,128)(2,1)S(1)} %convolution_convert_fusion), kind=kLoop, calls=%fused_computation.159 | loop fusion | bytes 4587520 | tf_op jit(solution)/shard_map/slice | solution.py:80
  16.2 0.6 copy-done.1
  16.8 0.9 bitcast_add_fusion.3
  17.8 1.6 %collective-permute-start.3 = (f32[224,128]{1,0:T(8,128)S(1)}, f32[224,128]{1,0:T(8,128)S(1)}, u32[]{:S(2)}, u32[]{:S(2)}) collective-permute-start(f32[224,128]{1,0:T(8,128)S(1)} %get-tuple-element.60), channel_id=1, source_target_pairs={{0,1},{1,0},{2,3},{3,2},{4,5},{5,4},{6,7},{7,6},{8,9},{9,8},{10,11... | collective-permute-start | bytes 344072 | tf_op jit(solution)/shard_map/ppermute | solution.py:61
  19.3 2.4 %collective-permute-start.2 = (f32[224,128]{1,0:T(8,128)S(1)}, f32[224,128]{1,0:T(8,128)S(1)}, u32[]{:S(2)}, u32[]{:S(2)}) collective-permute-start(f32[224,128]{1,0:T(8,128)S(1)} %get-tuple-element.61), channel_id=1, source_target_pairs={{1,2},{2,1},{5,6},{6,5},{9,10},{10,9},{13,14},{14,13},{17,18},{18,... | collective-permute-start | bytes 344072 | tf_op jit(solution)/shard_map/ppermute | solution.py:60
  21.7 4.0 %fusion.7 = f32[896,1792]{1,0:T(8,128)S(1)} fusion(bf16[640,896]{0,1:T(8,128)(2,1)} %get-tuple-element.11, bf16[640,896]{0,1:T(8,128)(2,1)S(1)} %get-tuple-element.10, bf16[896,896]{1,0:T(8,128)(2,1)S(1)} %select_convert_fusion.1), kind=kOutput, calls=%fused_computation.16 | convolution fusion | flops 2059796480 | bytes 9863168 | tf_op jit(solution)/shard_map/dot_general | solution.py:81
  25.7 0.6 fusion.70
  28.8 11.0 %collective-permute-done.5 = f32[128,896]{1,0:T(8,128)} collective-permute-done((f32[128,896]{1,0:T(8,128)}, f32[128,896]{1,0:T(8,128)}, u32[]{:S(2)}, u32[]{:S(2)}) %collective-permute-start.5) | collective-permute-done | bytes 458784 | tf_op jit(solution)/shard_map/ppermute | solution.py:22
  39.8 1.3 %select_add_fusion.1 = (f32[128,896]{1,0:T(8,128)S(1)}, f32[128,896]{1,0:T(8,128)S(1)}) fusion(f32[128,896]{1,0:T(8,128)} %collective-permute-done.5, f32[128,896]{1,0:T(8,128)} %collective-permute-done.4, pred[]{:T(512)} %bitcast.12, pred[]{:T(512)} %bitcast.10, pred[]{:T(512)} %bitcast.15, pred[]{:T(512)} %bitcast.14), kind=kLoop, calls=%fused_computation.93 | loop fusion | flops 688128 | bytes 1835012 | tf_op jit(solution)/shard_map/add | solution.py:115
  41.2 1.2 %fusion.18 = bf16[512,896]{1,0:T(8,128)(2,1)S(1)} fusion(bf16[896]{0:T(1024)(128)(2,1)S(1)} %copy-done.6, s32[896]{0:T(1024)S(1)} %copy-done.4, bf16[256,896]{1,0:T(8,128)(2,1)S(1)} %get-tuple-element.17, bf16[256,896]{1,0:T(8,128)(2,1)S(1)} %get-tuple-element.16), kind=kOutput, calls=%fused_computation.27 | convolution fusion | flops 825982976 | bytes 1840384 | tf_op jit(solution)/shard_map/dot_general | solution.py:79
  42.5 1.0 fusion.25
  43.6 1.0 fusion.1
  44.6 0.6 fusion.34
  45.9 2.3 %collective-permute-start.6 = (f32[224,128]{1,0:T(8,128)S(1)}, f32[224,128]{1,0:T(8,128)S(1)}, u32[]{:S(2)}, u32[]{:S(2)}) collective-permute-start(f32[224,128]{1,0:T(8,128)S(1)} %get-tuple-element.56), channel_id=1, source_target_pairs={{4,8},{8,4},{12,16},{16,12},{20,24},{24,20},{5,9},{9,5},{13,17},{1... | collective-permute-start | bytes 344072 | tf_op jit(solution)/shard_map/ppermute | solution.py:60
  48.3 3.7 %collective-permute-done.6 = f32[224,128]{1,0:T(8,128)S(1)} collective-permute-done((f32[224,128]{1,0:T(8,128)S(1)}, f32[224,128]{1,0:T(8,128)S(1)}, u32[]{:S(2)}, u32[]{:S(2)}) %collective-permute-start.6) | collective-permute-done | bytes 114720 | tf_op jit(solution)/shard_map/ppermute | solution.py:60
  52.0 1.6 %collective-permute-start.9 = (f32[224,128]{1,0:T(8,128)S(1)}, f32[224,128]{1,0:T(8,128)S(1)}, u32[]{:S(2)}, u32[]{:S(2)}) collective-permute-start(f32[224,128]{1,0:T(8,128)S(1)} %get-tuple-element.54), channel_id=1, source_target_pairs={{0,1},{1,0},{2,3},{3,2},{4,5},{5,4},{6,7},{7,6},{8,9},{9,8},{10,11... | collective-permute-start | bytes 344072 | tf_op jit(solution)/shard_map/ppermute | solution.py:61
  53.6 2.4 %collective-permute-start.8 = (f32[224,128]{1,0:T(8,128)S(1)}, f32[224,128]{1,0:T(8,128)S(1)}, u32[]{:S(2)}, u32[]{:S(2)}) collective-permute-start(f32[224,128]{1,0:T(8,128)S(1)} %get-tuple-element.55), channel_id=1, source_target_pairs={{1,2},{2,1},{5,6},{6,5},{9,10},{10,9},{13,14},{14,13},{17,18},{18,... | collective-permute-start | bytes 344072 | tf_op jit(solution)/shard_map/ppermute | solution.py:60
  56.0 1.3 %collective-permute-done.9 = f32[224,128]{1,0:T(8,128)S(1)} collective-permute-done((f32[224,128]{1,0:T(8,128)S(1)}, f32[224,128]{1,0:T(8,128)S(1)}, u32[]{:S(2)}, u32[]{:S(2)}) %collective-permute-start.9) | collective-permute-done | bytes 114720 | tf_op jit(solution)/shard_map/ppermute | solution.py:61
  57.3 4.0 %collective-permute-done.8 = f32[224,128]{1,0:T(8,128)S(1)} collective-permute-done((f32[224,128]{1,0:T(8,128)S(1)}, f32[224,128]{1,0:T(8,128)S(1)}, u32[]{:S(2)}, u32[]{:S(2)}) %collective-permute-start.8) | collective-permute-done | bytes 114720 | tf_op jit(solution)/shard_map/ppermute | solution.py:60
  61.4 0.6 fusion.38
  62.7 2.1 %collective-permute-start.10 = (f32[224,128]{1,0:T(8,128)S(1)}, f32[224,128]{1,0:T(8,128)S(1)}, u32[]{:S(2)}, u32[]{:S(2)}) collective-permute-start(f32[224,128]{1,0:T(8,128)S(1)} %get-tuple-element.52), channel_id=1, source_target_pairs={{4,8},{8,4},{12,16},{16,12},{20,24},{24,20},{5,9},{9,5},{13,17},{1... | collective-permute-start | bytes 344072 | tf_op jit(solution)/shard_map/ppermute | solution.py:60
  64.8 2.0 %collective-permute-start.11 = (f32[224,128]{1,0:T(8,128)S(1)}, f32[224,128]{1,0:T(8,128)S(1)}, u32[]{:S(2)}, u32[]{:S(2)}) collective-permute-start(f32[224,128]{1,0:T(8,128)S(1)} %get-tuple-element.53), channel_id=1, source_target_pairs={{0,4},{4,0},{8,12},{12,8},{16,20},{20,16},{24,28},{28,24},{1,5},{5... | collective-permute-start | bytes 344072 | tf_op jit(solution)/shard_map/ppermute | solution.py:61
  66.8 2.0 %collective-permute-done.10 = f32[224,128]{1,0:T(8,128)S(1)} collective-permute-done((f32[224,128]{1,0:T(8,128)S(1)}, f32[224,128]{1,0:T(8,128)S(1)}, u32[]{:S(2)}, u32[]{:S(2)}) %collective-permute-start.10) | collective-permute-done | bytes 114720 | tf_op jit(solution)/shard_map/ppermute | solution.py:60
  69.0 2.8 %collective-permute-start.12 = (f32[224,128]{1,0:T(8,128)S(1)}, f32[224,128]{1,0:T(8,128)S(1)}, u32[]{:S(2)}, u32[]{:S(2)}) collective-permute-start(f32[224,128]{1,0:T(8,128)S(1)} %get-tuple-element.51), channel_id=1, source_target_pairs={{1,2},{2,1},{5,6},{6,5},{9,10},{10,9},{13,14},{14,13},{17,18},{18,... | collective-permute-start | bytes 344072 | tf_op jit(solution)/shard_map/ppermute | solution.py:60
  71.7 2.5 %collective-permute-done.13 = f32[224,128]{1,0:T(8,128)S(1)} collective-permute-done((f32[224,128]{1,0:T(8,128)S(1)}, f32[224,128]{1,0:T(8,128)S(1)}, u32[]{:S(2)}, u32[]{:S(2)}) %collective-permute-start.13) | collective-permute-done | bytes 114720 | tf_op jit(solution)/shard_map/ppermute | solution.py:61
  74.2 2.8 %collective-permute-done.12 = f32[224,128]{1,0:T(8,128)S(1)} collective-permute-done((f32[224,128]{1,0:T(8,128)S(1)}, f32[224,128]{1,0:T(8,128)S(1)}, u32[]{:S(2)}, u32[]{:S(2)}) %collective-permute-start.12) | collective-permute-done | bytes 114720 | tf_op jit(solution)/shard_map/ppermute | solution.py:60
  77.3 0.6 fusion.42
  78.6 1.9 %collective-permute-start.14 = (f32[224,128]{1,0:T(8,128)S(1)}, f32[224,128]{1,0:T(8,128)S(1)}, u32[]{:S(2)}, u32[]{:S(2)}) collective-permute-start(f32[224,128]{1,0:T(8,128)S(1)} %get-tuple-element.48), channel_id=1, source_target_pairs={{4,8},{8,4},{12,16},{16,12},{20,24},{24,20},{5,9},{9,5},{13,17},{1... | collective-permute-start | bytes 344072 | tf_op jit(solution)/shard_map/ppermute | solution.py:60
  80.5 2.2 %collective-permute-start.15 = (f32[224,128]{1,0:T(8,128)S(1)}, f32[224,128]{1,0:T(8,128)S(1)}, u32[]{:S(2)}, u32[]{:S(2)}) collective-permute-start(f32[224,128]{1,0:T(8,128)S(1)} %get-tuple-element.49), channel_id=1, source_target_pairs={{0,4},{4,0},{8,12},{12,8},{16,20},{20,16},{24,28},{28,24},{1,5},{5... | collective-permute-start | bytes 344072 | tf_op jit(solution)/shard_map/ppermute | solution.py:61
  82.7 2.0 %collective-permute-done.14 = f32[224,128]{1,0:T(8,128)S(1)} collective-permute-done((f32[224,128]{1,0:T(8,128)S(1)}, f32[224,128]{1,0:T(8,128)S(1)}, u32[]{:S(2)}, u32[]{:S(2)}) %collective-permute-start.14) | collective-permute-done | bytes 114720 | tf_op jit(solution)/shard_map/ppermute | solution.py:60
  84.8 2.8 %collective-permute-start.16 = (f32[224,128]{1,0:T(8,128)S(1)}, f32[224,128]{1,0:T(8,128)S(1)}, u32[]{:S(2)}, u32[]{:S(2)}) collective-permute-start(f32[224,128]{1,0:T(8,128)S(1)} %get-tuple-element.47), channel_id=1, source_target_pairs={{1,2},{2,1},{5,6},{6,5},{9,10},{10,9},{13,14},{14,13},{17,18},{18,... | collective-permute-start | bytes 344072 | tf_op jit(solution)/shard_map/ppermute | solution.py:60
  87.6 2.6 %collective-permute-done.17 = f32[224,128]{1,0:T(8,128)S(1)} collective-permute-done((f32[224,128]{1,0:T(8,128)S(1)}, f32[224,128]{1,0:T(8,128)S(1)}, u32[]{:S(2)}, u32[]{:S(2)}) %collective-permute-start.17) | collective-permute-done | bytes 114720 | tf_op jit(solution)/shard_map/ppermute | solution.py:61
  90.2 2.8 %collective-permute-done.16 = f32[224,128]{1,0:T(8,128)S(1)} collective-permute-done((f32[224,128]{1,0:T(8,128)S(1)}, f32[224,128]{1,0:T(8,128)S(1)}, u32[]{:S(2)}, u32[]{:S(2)}) %collective-permute-start.16) | collective-permute-done | bytes 114720 | tf_op jit(solution)/shard_map/ppermute | solution.py:60
  93.3 0.6 fusion.48
  94.6 1.9 %collective-permute-start.18 = (f32[224,128]{1,0:T(8,128)S(1)}, f32[224,128]{1,0:T(8,128)S(1)}, u32[]{:S(2)}, u32[]{:S(2)}) collective-permute-start(f32[224,128]{1,0:T(8,128)S(1)} %get-tuple-element.44), channel_id=1, source_target_pairs={{4,8},{8,4},{12,16},{16,12},{20,24},{24,20},{5,9},{9,5},{13,17},{1... | collective-permute-start | bytes 344072 | tf_op jit(solution)/shard_map/ppermute | solution.py:60
  96.5 1.8 %collective-permute-start.19 = (f32[224,128]{1,0:T(8,128)S(1)}, f32[224,128]{1,0:T(8,128)S(1)}, u32[]{:S(2)}, u32[]{:S(2)}) collective-permute-start(f32[224,128]{1,0:T(8,128)S(1)} %get-tuple-element.45), channel_id=1, source_target_pairs={{0,4},{4,0},{8,12},{12,8},{16,20},{20,16},{24,28},{28,24},{1,5},{5... | collective-permute-start | bytes 344072 | tf_op jit(solution)/shard_map/ppermute | solution.py:61
  98.3 2.4 %collective-permute-done.18 = f32[224,128]{1,0:T(8,128)S(1)} collective-permute-done((f32[224,128]{1,0:T(8,128)S(1)}, f32[224,128]{1,0:T(8,128)S(1)}, u32[]{:S(2)}, u32[]{:S(2)}) %collective-permute-start.18) | collective-permute-done | bytes 114720 | tf_op jit(solution)/shard_map/ppermute | solution.py:60
  100.8 2.7 %collective-permute-start.20 = (f32[224,128]{1,0:T(8,128)S(1)}, f32[224,128]{1,0:T(8,128)S(1)}, u32[]{:S(2)}, u32[]{:S(2)}) collective-permute-start(f32[224,128]{1,0:T(8,128)S(1)} %get-tuple-element.43), channel_id=1, source_target_pairs={{1,2},{2,1},{5,6},{6,5},{9,10},{10,9},{13,14},{14,13},{17,18},{18,... | collective-permute-start | bytes 344072 | tf_op jit(solution)/shard_map/ppermute | solution.py:60
  103.6 1.0 add_add_fusion
  104.6 1.4 %collective-permute-done.21 = f32[224,128]{1,0:T(8,128)S(1)} collective-permute-done((f32[224,128]{1,0:T(8,128)S(1)}, f32[224,128]{1,0:T(8,128)S(1)}, u32[]{:S(2)}, u32[]{:S(2)}) %collective-permute-start.21) | collective-permute-done | bytes 114720 | tf_op jit(solution)/shard_map/ppermute | solution.py:61
  106.0 2.8 %collective-permute-done.20 = f32[224,128]{1,0:T(8,128)S(1)} collective-permute-done((f32[224,128]{1,0:T(8,128)S(1)}, f32[224,128]{1,0:T(8,128)S(1)}, u32[]{:S(2)}, u32[]{:S(2)}) %collective-permute-start.20) | collective-permute-done | bytes 114720 | tf_op jit(solution)/shard_map/ppermute | solution.py:60
  108.8 0.9 maximum_subtract_fusion.6
  (61 shorter events, 5.3 us)
Async XLA Ops:
  0.6 10.7 %copy-start.7 = (s32[1,1,896]{2,1,0:T(1,128)S(1)}, s32[1,1,896]{2,1,0:T(1,128)}, u32[]{:S(2)}) copy-start(s32[1,1,896]{2,1,0:T(1,128)} %param.11) | copy-start | bytes 10756
  0.6 10.7 %copy-start = (f32[1,1,640,896]{3,2,1,0:T(8,128)S(1)}, f32[1,1,640,896]{3,2,1,0:T(8,128)}, u32[]{:S(2)}) copy-start(f32[1,1,640,896]{3,2,1,0:T(8,128)} %param.7) | copy-start | bytes 6881284
  1.8 14.4 %collective-permute-start = (f32[224,128]{1,0:T(8,128)S(1)}, f32[224,128]{1,0:T(8,128)S(1)}, u32[]{:S(2)}, u32[]{:S(2)}) collective-permute-start(f32[224,128]{1,0:T(8,128)S(1)} %get-tuple-element.62), channel_id=1, source_target_pairs={{4,8},{8,4},{12,16},{16,12},{20,24},{24,20},{5,9},{9,5},{13,17},{1... | collective-permute-start | bytes 344072 | tf_op jit(solution)/shard_map/ppermute | solution.py:60
  3.7 12.5 %collective-permute-start.1 = (f32[224,128]{1,0:T(8,128)S(1)}, f32[224,128]{1,0:T(8,128)}, u32[]{:S(2)}, u32[]{:S(2)}) collective-permute-start(f32[224,128]{1,0:T(8,128)S(1)} %get-tuple-element.63), channel_id=1, source_target_pairs={{0,4},{4,0},{8,12},{12,8},{16,20},{20,16},{24,28},{28,24},{1,5},{5... | collective-permute-start | bytes 344072 | tf_op jit(solution)/shard_map/ppermute | solution.py:61
  7.6 21.2 %collective-permute-start.4 = (f32[128,896]{1,0:T(8,128)}, f32[128,896]{1,0:T(8,128)}, u32[]{:S(2)}, u32[]{:S(2)}) collective-permute-start(f32[128,896]{1,0:T(8,128)} %get-tuple-element.20), channel_id=1, source_target_pairs={{0,24},{4,28},{8,0},{12,4},{16,8},{20,12},{24,16},{28,20},{1,25},{... | collective-permute-start | bytes 1376264 | tf_op jit(solution)/shard_map/ppermute | solution.py:22
  8.1 31.8 %collective-permute-start.5 = (f32[128,896]{1,0:T(8,128)}, f32[128,896]{1,0:T(8,128)}, u32[]{:S(2)}, u32[]{:S(2)}) collective-permute-start(f32[128,896]{1,0:T(8,128)} %get-tuple-element.21), channel_id=1, source_target_pairs={{0,16},{4,20},{8,24},{12,28},{16,0},{20,4},{24,8},{28,12},{1,17},{... | collective-permute-start | bytes 1376264 | tf_op jit(solution)/shard_map/ppermute | solution.py:22
  11.3 0.6 copy-start.2
  11.7 4.1 %copy-start.5 = (bf16[896]{0:T(1024)(128)(2,1)}, bf16[896]{0:T(1024)(128)(2,1)S(1)}, u32[]{:S(2)}) copy-start(bf16[896]{0:T(1024)(128)(2,1)S(1)} %select_select_fusion) | copy-start | bytes 5380
  14.5 1.3 %copy-start.3 = (s32[896]{0:T(1024)S(1)}, s32[896]{0:T(1024)}, u32[]{:S(2)}) copy-start(s32[896]{0:T(1024)} %copy-done.2) | copy-start | bytes 10756
  15.8 1.0 copy-start.1
  17.8 10.9 %collective-permute-start.3 = (f32[224,128]{1,0:T(8,128)S(1)}, f32[224,128]{1,0:T(8,128)S(1)}, u32[]{:S(2)}, u32[]{:S(2)}) collective-permute-start(f32[224,128]{1,0:T(8,128)S(1)} %get-tuple-element.60), channel_id=1, source_target_pairs={{0,1},{1,0},{2,3},{3,2},{4,5},{5,4},{6,7},{7,6},{8,9},{9,8},{10,11... | collective-permute-start | bytes 344072 | tf_op jit(solution)/shard_map/ppermute | solution.py:61
  19.3 9.4 %collective-permute-start.2 = (f32[224,128]{1,0:T(8,128)S(1)}, f32[224,128]{1,0:T(8,128)S(1)}, u32[]{:S(2)}, u32[]{:S(2)}) collective-permute-start(f32[224,128]{1,0:T(8,128)S(1)} %get-tuple-element.61), channel_id=1, source_target_pairs={{1,2},{2,1},{5,6},{6,5},{9,10},{10,9},{13,14},{14,13},{17,18},{18,... | collective-permute-start | bytes 344072 | tf_op jit(solution)/shard_map/ppermute | solution.py:60
  21.7 4.0 %copy-start.8 = (s32[1,1,2]{2,1,0:T(1,128)S(1)}, s32[1,1,2]{2,1,0:T(1,128)}, u32[]{:S(2)}) copy-start(s32[1,1,2]{2,1,0:T(1,128)} %param.9) | copy-start | bytes 28
  39.8 1.4 %copy-start.4 = (s32[896]{0:T(1024)S(1)}, s32[896]{0:T(1024)}, u32[]{:S(2)}) copy-start(s32[896]{0:T(1024)} %copy-done.2) | copy-start | bytes 10756
  39.8 1.4 %copy-start.6 = (bf16[896]{0:T(1024)(128)(2,1)S(1)}, bf16[896]{0:T(1024)(128)(2,1)}, u32[]{:S(2)}) copy-start(bf16[896]{0:T(1024)(128)(2,1)} %copy-done.5) | copy-start | bytes 5380
  45.9 6.1 %collective-permute-start.6 = (f32[224,128]{1,0:T(8,128)S(1)}, f32[224,128]{1,0:T(8,128)S(1)}, u32[]{:S(2)}, u32[]{:S(2)}) collective-permute-start(f32[224,128]{1,0:T(8,128)S(1)} %get-tuple-element.56), channel_id=1, source_target_pairs={{4,8},{8,4},{12,16},{16,12},{20,24},{24,20},{5,9},{9,5},{13,17},{1... | collective-permute-start | bytes 344072 | tf_op jit(solution)/shard_map/ppermute | solution.py:60
  48.2 3.8 %collective-permute-start.7 = (f32[224,128]{1,0:T(8,128)S(1)}, f32[224,128]{1,0:T(8,128)S(1)}, u32[]{:S(2)}, u32[]{:S(2)}) collective-permute-start(f32[224,128]{1,0:T(8,128)S(1)} %get-tuple-element.57), channel_id=1, source_target_pairs={{0,4},{4,0},{8,12},{12,8},{16,20},{20,16},{24,28},{28,24},{1,5},{5... | collective-permute-start | bytes 344072 | tf_op jit(solution)/shard_map/ppermute | solution.py:61
  52.0 5.2 %collective-permute-start.9 = (f32[224,128]{1,0:T(8,128)S(1)}, f32[224,128]{1,0:T(8,128)S(1)}, u32[]{:S(2)}, u32[]{:S(2)}) collective-permute-start(f32[224,128]{1,0:T(8,128)S(1)} %get-tuple-element.54), channel_id=1, source_target_pairs={{0,1},{1,0},{2,3},{3,2},{4,5},{5,4},{6,7},{7,6},{8,9},{9,8},{10,11... | collective-permute-start | bytes 344072 | tf_op jit(solution)/shard_map/ppermute | solution.py:61
  53.6 7.7 %collective-permute-start.8 = (f32[224,128]{1,0:T(8,128)S(1)}, f32[224,128]{1,0:T(8,128)S(1)}, u32[]{:S(2)}, u32[]{:S(2)}) collective-permute-start(f32[224,128]{1,0:T(8,128)S(1)} %get-tuple-element.55), channel_id=1, source_target_pairs={{1,2},{2,1},{5,6},{6,5},{9,10},{10,9},{13,14},{14,13},{17,18},{18,... | collective-permute-start | bytes 344072 | tf_op jit(solution)/shard_map/ppermute | solution.py:60
  62.7 6.1 %collective-permute-start.10 = (f32[224,128]{1,0:T(8,128)S(1)}, f32[224,128]{1,0:T(8,128)S(1)}, u32[]{:S(2)}, u32[]{:S(2)}) collective-permute-start(f32[224,128]{1,0:T(8,128)S(1)} %get-tuple-element.52), channel_id=1, source_target_pairs={{4,8},{8,4},{12,16},{16,12},{20,24},{24,20},{5,9},{9,5},{13,17},{1... | collective-permute-start | bytes 344072 | tf_op jit(solution)/shard_map/ppermute | solution.py:60
  64.8 4.0 %collective-permute-start.11 = (f32[224,128]{1,0:T(8,128)S(1)}, f32[224,128]{1,0:T(8,128)S(1)}, u32[]{:S(2)}, u32[]{:S(2)}) collective-permute-start(f32[224,128]{1,0:T(8,128)S(1)} %get-tuple-element.53), channel_id=1, source_target_pairs={{0,4},{4,0},{8,12},{12,8},{16,20},{20,16},{24,28},{28,24},{1,5},{5... | collective-permute-start | bytes 344072 | tf_op jit(solution)/shard_map/ppermute | solution.py:61
  68.9 5.3 %collective-permute-start.13 = (f32[224,128]{1,0:T(8,128)S(1)}, f32[224,128]{1,0:T(8,128)S(1)}, u32[]{:S(2)}, u32[]{:S(2)}) collective-permute-start(f32[224,128]{1,0:T(8,128)S(1)} %get-tuple-element.50), channel_id=1, source_target_pairs={{0,1},{1,0},{2,3},{3,2},{4,5},{5,4},{6,7},{7,6},{8,9},{9,8},{10,11... | collective-permute-start | bytes 344072 | tf_op jit(solution)/shard_map/ppermute | solution.py:61
  69.0 8.1 %collective-permute-start.12 = (f32[224,128]{1,0:T(8,128)S(1)}, f32[224,128]{1,0:T(8,128)S(1)}, u32[]{:S(2)}, u32[]{:S(2)}) collective-permute-start(f32[224,128]{1,0:T(8,128)S(1)} %get-tuple-element.51), channel_id=1, source_target_pairs={{1,2},{2,1},{5,6},{6,5},{9,10},{10,9},{13,14},{14,13},{17,18},{18,... | collective-permute-start | bytes 344072 | tf_op jit(solution)/shard_map/ppermute | solution.py:60
  78.6 6.1 %collective-permute-start.14 = (f32[224,128]{1,0:T(8,128)S(1)}, f32[224,128]{1,0:T(8,128)S(1)}, u32[]{:S(2)}, u32[]{:S(2)}) collective-permute-start(f32[224,128]{1,0:T(8,128)S(1)} %get-tuple-element.48), channel_id=1, source_target_pairs={{4,8},{8,4},{12,16},{16,12},{20,24},{24,20},{5,9},{9,5},{13,17},{1... | collective-permute-start | bytes 344072 | tf_op jit(solution)/shard_map/ppermute | solution.py:60
  80.5 4.2 %collective-permute-start.15 = (f32[224,128]{1,0:T(8,128)S(1)}, f32[224,128]{1,0:T(8,128)S(1)}, u32[]{:S(2)}, u32[]{:S(2)}) collective-permute-start(f32[224,128]{1,0:T(8,128)S(1)} %get-tuple-element.49), channel_id=1, source_target_pairs={{0,4},{4,0},{8,12},{12,8},{16,20},{20,16},{24,28},{28,24},{1,5},{5... | collective-permute-start | bytes 344072 | tf_op jit(solution)/shard_map/ppermute | solution.py:61
  84.7 5.5 %collective-permute-start.17 = (f32[224,128]{1,0:T(8,128)S(1)}, f32[224,128]{1,0:T(8,128)S(1)}, u32[]{:S(2)}, u32[]{:S(2)}) collective-permute-start(f32[224,128]{1,0:T(8,128)S(1)} %get-tuple-element.46), channel_id=1, source_target_pairs={{0,1},{1,0},{2,3},{3,2},{4,5},{5,4},{6,7},{7,6},{8,9},{9,8},{10,11... | collective-permute-start | bytes 344072 | tf_op jit(solution)/shard_map/ppermute | solution.py:61
  84.8 8.2 %collective-permute-start.16 = (f32[224,128]{1,0:T(8,128)S(1)}, f32[224,128]{1,0:T(8,128)S(1)}, u32[]{:S(2)}, u32[]{:S(2)}) collective-permute-start(f32[224,128]{1,0:T(8,128)S(1)} %get-tuple-element.47), channel_id=1, source_target_pairs={{1,2},{2,1},{5,6},{6,5},{9,10},{10,9},{13,14},{14,13},{17,18},{18,... | collective-permute-start | bytes 344072 | tf_op jit(solution)/shard_map/ppermute | solution.py:60
  94.6 6.1 %collective-permute-start.18 = (f32[224,128]{1,0:T(8,128)S(1)}, f32[224,128]{1,0:T(8,128)S(1)}, u32[]{:S(2)}, u32[]{:S(2)}) collective-permute-start(f32[224,128]{1,0:T(8,128)S(1)} %get-tuple-element.44), channel_id=1, source_target_pairs={{4,8},{8,4},{12,16},{16,12},{20,24},{24,20},{5,9},{9,5},{13,17},{1... | collective-permute-start | bytes 344072 | tf_op jit(solution)/shard_map/ppermute | solution.py:60
  96.5 4.2 %collective-permute-start.19 = (f32[224,128]{1,0:T(8,128)S(1)}, f32[224,128]{1,0:T(8,128)S(1)}, u32[]{:S(2)}, u32[]{:S(2)}) collective-permute-start(f32[224,128]{1,0:T(8,128)S(1)} %get-tuple-element.45), channel_id=1, source_target_pairs={{0,4},{4,0},{8,12},{12,8},{16,20},{20,16},{24,28},{28,24},{1,5},{5... | collective-permute-start | bytes 344072 | tf_op jit(solution)/shard_map/ppermute | solution.py:61
  100.7 5.2 %collective-permute-start.21 = (f32[224,128]{1,0:T(8,128)S(1)}, f32[224,128]{1,0:T(8,128)S(1)}, u32[]{:S(2)}, u32[]{:S(2)}) collective-permute-start(f32[224,128]{1,0:T(8,128)S(1)} %get-tuple-element.42), channel_id=1, source_target_pairs={{0,1},{1,0},{2,3},{3,2},{4,5},{5,4},{6,7},{7,6},{8,9},{9,8},{10,11... | collective-permute-start | bytes 344072 | tf_op jit(solution)/shard_map/ppermute | solution.py:61
  100.8 8.0 %collective-permute-start.20 = (f32[224,128]{1,0:T(8,128)S(1)}, f32[224,128]{1,0:T(8,128)S(1)}, u32[]{:S(2)}, u32[]{:S(2)}) collective-permute-start(f32[224,128]{1,0:T(8,128)S(1)} %get-tuple-element.43), channel_id=1, source_target_pairs={{1,2},{2,1},{5,6},{6,5},{9,10},{10,9},{13,14},{14,13},{17,18},{18,... | collective-permute-start | bytes 344072 | tf_op jit(solution)/shard_map/ppermute | solution.py:60

commit v7 on v6

--- a/solution.py
+++ b/solution.py
@@ -54,20 +54,24 @@
     return pairs
 
 
-def axis_exchange(low, high, axis):
-    count = lax.axis_size(axis)
-    even = lax.axis_index(axis) % 2 == 0
-    odd_recv = lax.ppermute(jnp.where(even, low, high), axis, swap_pairs(count, 1))
-    even_recv = lax.ppermute(jnp.where(even, high, low), axis, swap_pairs(count, 0))
-    new_low = low + jnp.where(even, odd_recv, even_recv)
-    new_high = high + jnp.where(even, even_recv, odd_recv)
-    return new_low, new_high
-
-
 def face_sum_parts(faces):
     low_x, high_x, low_y, high_y = faces
-    new_low_y, new_high_y = axis_exchange(low_y, high_y, "gy")
-    new_low_x, new_high_x = axis_exchange(low_x, high_x, "gx")
+    sides = [(low_y, high_y, "gy"), (low_x, high_x, "gx")]
+    sends = []
+    for low, high, axis in sides:
+        even = lax.axis_index(axis) % 2 == 0
+        sends.append((jnp.where(even, low, high), swap_pairs(lax.axis_size(axis), 1), axis))
+        sends.append((jnp.where(even, high, low), swap_pairs(lax.axis_size(axis), 0), axis))
+    received = lax.optimization_barrier(
+        [lax.ppermute(block, axis, pairs) for block, pairs, axis in sends]
+    )
+    summed = []
+    for side_id, (low, high, axis) in enumerate(sides):
+        even = lax.axis_index(axis) % 2 == 0
+        odd_recv, even_recv = received[2 * side_id], received[2 * side_id + 1]
+        summed.append(low + jnp.where(even, odd_recv, even_recv))
+        summed.append(high + jnp.where(even, even_recv, odd_recv))
+    new_low_y, new_high_y, new_low_x, new_high_x = summed
     return jnp.concatenate([new_low_x, new_high_x, new_low_y, new_high_y], axis=0)
 
 

time: 110 us -> 98.2 us (0.89)
  the two profiles are of different devices: /device:TPU:12 before, /device:TPU:11 now
where the time goes in v7:
time: 98.2 us; the launch traced here: 97.7 us
  waiting for transfers between devices  35.9 us (37%)
  starting transfers between devices  34.6 us (35%)
  matrix products  12.5 us (13%)
  other arithmetic  8.4 us (9%)
  between operations  4.44 us (5%)
  local copies, waits for them, and re-layouts  1.94 us (2%)
    ppermute x20, starting transfers between devices, face_sum_parts(): lax.ppermute(block, axis, pairs)  32 us
    ppermute x20, waiting for transfers between devices, face_sum_parts(): lax.ppermute(block, axis, pairs)  19.9 us
    ppermute x2, waiting for transfers between devices, from_behind(): return lax.ppermute(value, axis, pairs)  16 us
    dot_general x2, matrix products, slot_pieces(): jnp.dot(stacked, to_rows, preferred_element_type=jnp.float32)  3.85 us
    dot_general x2, matrix products, slot_pieces(): return jnp.dot(to_slots, side, preferred_element_type=jnp.float32)  3.72 us
    dot_general x4, matrix products, body(): jnp.dot(op_high, jnp.concatenate([dir_high, dir_mid], axis=1).astype(jnp....  2.58 us
    ppermute x2, starting transfers between devices, from_behind(): return lax.ppermute(value, axis, pairs)  2.54 us
    dot_general x4, matrix products, body(): jnp.dot(op_mid, dir_high.astype(jnp.bfloat16), preferred_element_type=jnp...  2.35 us
  transfers between devices with their start and end apart: 22, of which 10 were waited for; matrix products, arithmetic and copies ran while one was open for 11% of the time, Pallas kernels for 0%

profile of v7, /device:TPU:11, one launch (start us, length us, event | category | flops | bytes accessed | tf_op | source)
XLA Modules:
  0.0 97.7 jit_solution(1468588961046553338)
XLA Ops:
  0.7 1.9 %bitcast_select_fusion = (f32[224,128]{1,0:T(8,128)}, f32[224,128]{1,0:T(8,128)}, f32[224,128]{1,0:T(8,128)}, f32[224,128]{1,0:T(8,128)}) fusion(f32[1,1,896,128]{3,2,1,0:T(8,128)} %param.6, pred[]{:T(512)S(6)} %eq.111, pred[]{:T(512)S(6)} %eq.112), kind=kLoop, calls=%fused_computation.97 | loop fusion | flops 114688 | bytes 917506 | tf_op jit(solution)/shard_map/jit(_where)/select_n | solution.py:64
  2.6 0.7 collective-permute-start.3
  3.5 3.4 %collective-permute-start.2 = (f32[224,128]{1,0:T(8,128)}, f32[224,128]{1,0:T(8,128)S(1)}, u32[]{:S(2)}, u32[]{:S(2)}) collective-permute-start(f32[224,128]{1,0:T(8,128)} %get-tuple-element.112), channel_id=1, source_target_pairs={{4,8},{8,4},{12,16},{16,12},{20,24},{24,20},{5,9},{9,5},{13,17},{1... | collective-permute-start | bytes 344072 | tf_op jit(solution)/shard_map/ppermute | solution.py:66
  7.0 4.2 %collective-permute-start = (f32[224,128]{1,0:T(8,128)}, f32[224,128]{1,0:T(8,128)}, u32[]{:S(2)}, u32[]{:S(2)}) collective-permute-start(f32[224,128]{1,0:T(8,128)} %get-tuple-element.113), channel_id=1, source_target_pairs={{1,2},{2,1},{5,6},{6,5},{9,10},{10,9},{13,14},{14,13},{17,18},{18,... | collective-permute-start | bytes 344072 | tf_op jit(solution)/shard_map/ppermute | solution.py:66
  11.2 1.0 %slice_bitcast_fusion.1 = (f32[128,896]{1,0:T(8,128)}, f32[128,896]{1,0:T(8,128)}) fusion(f32[1,1,2,128,896]{4,3,2,1,0:T(8,128)S(1)} %copy-done.2), kind=kLoop, calls=%fused_computation.95 | loop fusion | bytes 1835008 | tf_op jit(solution)/shard_map/squeeze | solution.py:102
  13.0 0.7 reduce
  13.7 0.4 select_convert_fusion.1
  14.1 0.3 reduce-precision_convert_fusion
  14.4 2.6 %convolution_convert_fusion = bf16[1280,896]{0,1:T(8,128)(2,1)S(1)} fusion(bf16[640,896]{1,0:T(8,128)(2,1)S(1)} %get-tuple-element.53, bf16[640,896]{1,0:T(8,128)(2,1)S(1)} %get-tuple-element.52, bf16[896]{0:T(1024)(128)(2,1)S(1)} %select_select_fusion, s32[896]{0:T(1024)S(1)} %reduce), kind=kOutput, calls=%fused_computation | convolution fusion | flops 2062548992 | bytes 4592896 | tf_op jit(solution)/shard_map/dot_general | solution.py:83
  17.3 2.7 %fusion.7 = f32[896,1792]{1,0:T(8,128)S(1)} fusion(bf16[640,896]{0,1:T(8,128)(2,1)S(1)} %get-tuple-element.51, bf16[640,896]{0,1:T(8,128)(2,1)S(1)} %get-tuple-element.50, bf16[896,896]{1,0:T(8,128)(2,1)S(1)} %select_convert_fusion.1), kind=kOutput, calls=%fused_computation.16 | convolution fusion | flops 2059796480 | bytes 9863168 | tf_op jit(solution)/shard_map/dot_general | solution.py:85
  20.0 2.4 %collective-permute-start.5 = (f32[128,896]{1,0:T(8,128)S(1)}, f32[128,896]{1,0:T(8,128)S(1)}, u32[]{:S(2)}, u32[]{:S(2)}) collective-permute-start(f32[128,896]{1,0:T(8,128)S(1)} %copy-done.3), channel_id=1, source_target_pairs={{0,16},{4,20},{8,24},{12,28},{16,0},{20,4},{24,8},{28,12},{1,17},{... | collective-permute-start | bytes 1376264 | tf_op jit(solution)/shard_map/ppermute | solution.py:22
  22.4 0.7 fusion.70
  25.8 1.0 bitcast_add_fusion.3
  26.8 16.0 %collective-permute-done.5 = f32[128,896]{1,0:T(8,128)S(1)} collective-permute-done((f32[128,896]{1,0:T(8,128)S(1)}, f32[128,896]{1,0:T(8,128)S(1)}, u32[]{:S(2)}, u32[]{:S(2)}) %collective-permute-start.5) | collective-permute-done | bytes 458784 | tf_op jit(solution)/shard_map/ppermute | solution.py:22
  43.1 1.2 %fusion.18 = bf16[512,896]{1,0:T(8,128)(2,1)S(1)} fusion(bf16[896]{0:T(1024)(128)(2,1)S(1)} %select_select_fusion, s32[896]{0:T(1024)S(1)} %reduce, bf16[256,896]{1,0:T(8,128)(2,1)S(1)} %get-tuple-element.57, bf16[256,896]{1,0:T(8,128)(2,1)S(1)} %get-tuple-element.56), kind=kOutput, calls=%fused_computation.27 | convolution fusion | flops 825982976 | bytes 1840384 | tf_op jit(solution)/shard_map/dot_general | solution.py:83
  44.4 1.0 %fusion.25 = f32[896,1792]{1,0:T(8,128)S(1)} fusion(bf16[256,896]{1,0:T(8,128)(2,1)S(1)} %get-tuple-element.55, bf16[256,896]{1,0:T(8,128)(2,1)S(1)} %get-tuple-element.54, bf16[896,896]{1,0:T(8,128)(2,1)S(1)} %select_convert_fusion.1), kind=kOutput, calls=%fused_computation.41 | convolution fusion | flops 823918592 | bytes 7798784 | tf_op jit(solution)/shard_map/dot_general | solution.py:85
  45.4 1.0 %fusion.1 = (bf16[896,896]{1,0:T(8,128)(2,1)S(1)}, bf16[896,896]{1,0:T(8,128)(2,1)S(1)}) fusion(f32[896,1792]{1,0:T(8,128)S(1)} %fusion.25, f32[896,1792]{1,0:T(8,128)S(1)} %fusion.7), kind=kLoop, calls=%fused_computation.6 | loop fusion | flops 3211264 | bytes 16056320 | tf_op jit(solution)/shard_map/convert_element_type | solution.py:125
  46.4 0.6 fusion.34
  47.0 0.6 convolution_add_fusion.3
  47.7 0.5 collective-permute-start.9
  48.1 2.7 %collective-permute-start.8 = (f32[224,128]{1,0:T(8,128)S(1)}, f32[224,128]{1,0:T(8,128)S(1)}, u32[]{:S(2)}, u32[]{:S(2)}) collective-permute-start(f32[224,128]{1,0:T(8,128)S(1)} %get-tuple-element.104), channel_id=1, source_target_pairs={{4,8},{8,4},{12,16},{16,12},{20,24},{24,20},{5,9},{9,5},{13,17},{1... | collective-permute-start | bytes 344072 | tf_op jit(solution)/shard_map/ppermute | solution.py:66
  50.8 1.9 %collective-permute-start.6 = (f32[224,128]{1,0:T(8,128)S(1)}, f32[224,128]{1,0:T(8,128)S(1)}, u32[]{:S(2)}, u32[]{:S(2)}) collective-permute-start(f32[224,128]{1,0:T(8,128)S(1)} %get-tuple-element.105), channel_id=1, source_target_pairs={{1,2},{2,1},{5,6},{6,5},{9,10},{10,9},{13,14},{14,13},{17,18},{18,... | collective-permute-start | bytes 344072 | tf_op jit(solution)/shard_map/ppermute | solution.py:66
  52.8 1.8 %collective-permute-done.8 = f32[224,128]{1,0:T(8,128)S(1)} collective-permute-done((f32[224,128]{1,0:T(8,128)S(1)}, f32[224,128]{1,0:T(8,128)S(1)}, u32[]{:S(2)}, u32[]{:S(2)}) %collective-permute-start.8) | collective-permute-done | bytes 114720 | tf_op jit(solution)/shard_map/ppermute | solution.py:66
  54.5 2.7 %collective-permute-done.6 = f32[224,128]{1,0:T(8,128)S(1)} collective-permute-done((f32[224,128]{1,0:T(8,128)S(1)}, f32[224,128]{1,0:T(8,128)S(1)}, u32[]{:S(2)}, u32[]{:S(2)}) %collective-permute-start.6) | collective-permute-done | bytes 114720 | tf_op jit(solution)/shard_map/ppermute | solution.py:66
  57.5 0.6 fusion.38
  58.1 0.6 convolution_add_fusion.2
  58.8 3.5 %collective-permute-start.13 = (f32[224,128]{1,0:T(8,128)S(1)}, f32[224,128]{1,0:T(8,128)S(1)}, u32[]{:S(2)}, u32[]{:S(2)}) collective-permute-start(f32[224,128]{1,0:T(8,128)S(1)} %get-tuple-element.96), channel_id=1, source_target_pairs={{0,4},{4,0},{8,12},{12,8},{16,20},{20,16},{24,28},{28,24},{1,5},{5... | collective-permute-start | bytes 344072 | tf_op jit(solution)/shard_map/ppermute | solution.py:66
  62.3 2.1 %collective-permute-start.12 = (f32[224,128]{1,0:T(8,128)S(1)}, f32[224,128]{1,0:T(8,128)S(1)}, u32[]{:S(2)}, u32[]{:S(2)}) collective-permute-start(f32[224,128]{1,0:T(8,128)S(1)} %get-tuple-element.98), channel_id=1, source_target_pairs={{4,8},{8,4},{12,16},{16,12},{20,24},{24,20},{5,9},{9,5},{13,17},{1... | collective-permute-start | bytes 344072 | tf_op jit(solution)/shard_map/ppermute | solution.py:66
  64.4 1.9 %collective-permute-start.10 = (f32[224,128]{1,0:T(8,128)S(1)}, f32[224,128]{1,0:T(8,128)S(1)}, u32[]{:S(2)}, u32[]{:S(2)}) collective-permute-start(f32[224,128]{1,0:T(8,128)S(1)} %get-tuple-element.99), channel_id=1, source_target_pairs={{1,2},{2,1},{5,6},{6,5},{9,10},{10,9},{13,14},{14,13},{17,18},{18,... | collective-permute-start | bytes 344072 | tf_op jit(solution)/shard_map/ppermute | solution.py:66
  66.3 0.7 collective-permute-done.11
  67.0 1.4 %collective-permute-done.12 = f32[224,128]{1,0:T(8,128)S(1)} collective-permute-done((f32[224,128]{1,0:T(8,128)S(1)}, f32[224,128]{1,0:T(8,128)S(1)}, u32[]{:S(2)}, u32[]{:S(2)}) %collective-permute-start.12) | collective-permute-done | bytes 114720 | tf_op jit(solution)/shard_map/ppermute | solution.py:66
  68.4 3.5 %collective-permute-done.10 = f32[224,128]{1,0:T(8,128)S(1)} collective-permute-done((f32[224,128]{1,0:T(8,128)S(1)}, f32[224,128]{1,0:T(8,128)S(1)}, u32[]{:S(2)}, u32[]{:S(2)}) %collective-permute-start.10) | collective-permute-done | bytes 114720 | tf_op jit(solution)/shard_map/ppermute | solution.py:66
  72.2 0.6 fusion.42
  72.9 0.6 convolution_add_fusion.1
  73.5 0.9 collective-permute-start.17
  74.4 2.9 %collective-permute-start.16 = (f32[224,128]{1,0:T(8,128)S(1)}, f32[224,128]{1,0:T(8,128)S(1)}, u32[]{:S(2)}, u32[]{:S(2)}) collective-permute-start(f32[224,128]{1,0:T(8,128)S(1)} %get-tuple-element.92), channel_id=1, source_target_pairs={{4,8},{8,4},{12,16},{16,12},{20,24},{24,20},{5,9},{9,5},{13,17},{1... | collective-permute-start | bytes 344072 | tf_op jit(solution)/shard_map/ppermute | solution.py:66
  77.4 1.9 %collective-permute-start.14 = (f32[224,128]{1,0:T(8,128)S(1)}, f32[224,128]{1,0:T(8,128)S(1)}, u32[]{:S(2)}, u32[]{:S(2)}) collective-permute-start(f32[224,128]{1,0:T(8,128)S(1)} %get-tuple-element.93), channel_id=1, source_target_pairs={{1,2},{2,1},{5,6},{6,5},{9,10},{10,9},{13,14},{14,13},{17,18},{18,... | collective-permute-start | bytes 344072 | tf_op jit(solution)/shard_map/ppermute | solution.py:66
  79.3 1.2 %collective-permute-done.16 = f32[224,128]{1,0:T(8,128)S(1)} collective-permute-done((f32[224,128]{1,0:T(8,128)S(1)}, f32[224,128]{1,0:T(8,128)S(1)}, u32[]{:S(2)}, u32[]{:S(2)}) %collective-permute-start.16) | collective-permute-done | bytes 114720 | tf_op jit(solution)/shard_map/ppermute | solution.py:66
  80.5 4.0 %collective-permute-done.14 = f32[224,128]{1,0:T(8,128)S(1)} collective-permute-done((f32[224,128]{1,0:T(8,128)S(1)}, f32[224,128]{1,0:T(8,128)S(1)}, u32[]{:S(2)}, u32[]{:S(2)}) %collective-permute-start.14) | collective-permute-done | bytes 114720 | tf_op jit(solution)/shard_map/ppermute | solution.py:66
  84.8 0.6 fusion.48
  85.5 0.6 convolution_add_fusion
  86.1 0.4 collective-permute-start.21
  86.5 2.8 %collective-permute-start.20 = (f32[224,128]{1,0:T(8,128)S(1)}, f32[224,128]{1,0:T(8,128)S(1)}, u32[]{:S(2)}, u32[]{:S(2)}) collective-permute-start(f32[224,128]{1,0:T(8,128)S(1)} %get-tuple-element.86), channel_id=1, source_target_pairs={{4,8},{8,4},{12,16},{16,12},{20,24},{24,20},{5,9},{9,5},{13,17},{1... | collective-permute-start | bytes 344072 | tf_op jit(solution)/shard_map/ppermute | solution.py:66
  89.3 1.9 %collective-permute-start.18 = (f32[224,128]{1,0:T(8,128)S(1)}, f32[224,128]{1,0:T(8,128)S(1)}, u32[]{:S(2)}, u32[]{:S(2)}) collective-permute-start(f32[224,128]{1,0:T(8,128)S(1)} %get-tuple-element.87), channel_id=1, source_target_pairs={{1,2},{2,1},{5,6},{6,5},{9,10},{10,9},{13,14},{14,13},{17,18},{18,... | collective-permute-start | bytes 344072 | tf_op jit(solution)/shard_map/ppermute | solution.py:66
  91.2 1.0 %add_add_fusion = f32[1,1,896,128]{3,2,1,0:T(8,128)} fusion(f32[1,1,224,128]{3,2,1,0:T(8,128)S(1)} %bitcast.69, f32[1,1,224,128]{3,2,1,0:T(8,128)S(1)} %bitcast.71, f32[1,1,224,128]{3,2,1,0:T(8,128)S(1)} %bitcast.67, f32[1,1,224,128]{3,2,1,0:T(8,128)S(1)} %bitcast.65, f32[1,1,224,128]{3,2,1,0:T(8,128)S(1)} %bitcast.77, f32[1,1,224,128]{3,2,1,0:T(8,128)S(1)} %bitcast.79, ...), kind=kLoop, calls=%fused_computation.89 | loop fusion | flops 3211264 | bytes 2293760 | tf_op jit(solution)/shard_map/add | solution.py:135
  92.2 0.3 collective-permute-done.20
  92.6 4.2 %collective-permute-done.18 = f32[224,128]{1,0:T(8,128)S(1)} collective-permute-done((f32[224,128]{1,0:T(8,128)S(1)}, f32[224,128]{1,0:T(8,128)S(1)}, u32[]{:S(2)}, u32[]{:S(2)}) %collective-permute-start.18) | collective-permute-done | bytes 114720 | tf_op jit(solution)/shard_map/ppermute | solution.py:66
  96.9 0.9 maximum_subtract_fusion.6
  (48 shorter events, 2.0 us)
Async XLA Ops:
  0.6 10.6 %copy-start.2 = (f32[1,1,2,128,896]{4,3,2,1,0:T(8,128)S(1)}, f32[1,1,2,128,896]{4,3,2,1,0:T(8,128)}, u32[]{:S(2)}) copy-start(f32[1,1,2,128,896]{4,3,2,1,0:T(8,128)} %param.8) | copy-start | bytes 2752516
  2.6 17.4 %collective-permute-start.3 = (f32[224,128]{1,0:T(8,128)}, f32[224,128]{1,0:T(8,128)S(1)}, u32[]{:S(2)}, u32[]{:S(2)}) collective-permute-start(f32[224,128]{1,0:T(8,128)} %get-tuple-element.110), channel_id=1, source_target_pairs={{0,4},{4,0},{8,12},{12,8},{16,20},{20,16},{24,28},{28,24},{1,5},{5... | collective-permute-start | bytes 344072 | tf_op jit(solution)/shard_map/ppermute | solution.py:66
  3.3 22.5 %collective-permute-start.1 = (f32[224,128]{1,0:T(8,128)}, f32[224,128]{1,0:T(8,128)S(1)}, u32[]{:S(2)}, u32[]{:S(2)}) collective-permute-start(f32[224,128]{1,0:T(8,128)} %get-tuple-element.111), channel_id=1, source_target_pairs={{0,1},{1,0},{2,3},{3,2},{4,5},{5,4},{6,7},{7,6},{8,9},{9,8},{10,11... | collective-permute-start | bytes 344072 | tf_op jit(solution)/shard_map/ppermute | solution.py:66
  3.5 22.2 %collective-permute-start.2 = (f32[224,128]{1,0:T(8,128)}, f32[224,128]{1,0:T(8,128)S(1)}, u32[]{:S(2)}, u32[]{:S(2)}) collective-permute-start(f32[224,128]{1,0:T(8,128)} %get-tuple-element.112), channel_id=1, source_target_pairs={{4,8},{8,4},{12,16},{16,12},{20,24},{24,20},{5,9},{9,5},{13,17},{1... | collective-permute-start | bytes 344072 | tf_op jit(solution)/shard_map/ppermute | solution.py:66
  6.9 7.1 %copy-start = (f32[1,1,640,896]{3,2,1,0:T(8,128)S(1)}, f32[1,1,640,896]{3,2,1,0:T(8,128)}, u32[]{:S(2)}) copy-start(f32[1,1,640,896]{3,2,1,0:T(8,128)} %param.7) | copy-start | bytes 6881284
  7.0 18.8 %collective-permute-start = (f32[224,128]{1,0:T(8,128)}, f32[224,128]{1,0:T(8,128)}, u32[]{:S(2)}, u32[]{:S(2)}) collective-permute-start(f32[224,128]{1,0:T(8,128)} %get-tuple-element.113), channel_id=1, source_target_pairs={{1,2},{2,1},{5,6},{6,5},{9,10},{10,9},{13,14},{14,13},{17,18},{18,... | collective-permute-start | bytes 344072 | tf_op jit(solution)/shard_map/ppermute | solution.py:66
  12.2 14.7 %collective-permute-start.4 = (f32[128,896]{1,0:T(8,128)}, f32[128,896]{1,0:T(8,128)S(1)}, u32[]{:S(2)}, u32[]{:S(2)}) collective-permute-start(f32[128,896]{1,0:T(8,128)} %get-tuple-element.60), channel_id=1, source_target_pairs={{0,24},{4,28},{8,0},{12,4},{16,8},{20,12},{24,16},{28,20},{1,25},{... | collective-permute-start | bytes 1376264 | tf_op jit(solution)/shard_map/ppermute | solution.py:22
  17.3 2.8 %copy-start.3 = (f32[128,896]{1,0:T(8,128)S(1)}, f32[128,896]{1,0:T(8,128)}, u32[]{:S(2)}) copy-start(f32[128,896]{1,0:T(8,128)} %get-tuple-element.61) | copy-start | bytes 1376260
  17.3 5.1 %copy-start.4 = (s32[1,1,2]{2,1,0:T(1,128)S(1)}, s32[1,1,2]{2,1,0:T(1,128)}, u32[]{:S(2)}) copy-start(s32[1,1,2]{2,1,0:T(1,128)} %param.9) | copy-start | bytes 28
  17.3 8.5 %copy-start.1 = (f32[1,1,896,128]{3,2,1,0:T(8,128)S(1)}, f32[1,1,896,128]{3,2,1,0:T(8,128)}, u32[]{:S(2)}) copy-start(f32[1,1,896,128]{3,2,1,0:T(8,128)} %param.6) | copy-start | bytes 1376260
  20.0 22.8 %collective-permute-start.5 = (f32[128,896]{1,0:T(8,128)S(1)}, f32[128,896]{1,0:T(8,128)S(1)}, u32[]{:S(2)}, u32[]{:S(2)}) collective-permute-start(f32[128,896]{1,0:T(8,128)S(1)} %copy-done.3), channel_id=1, source_target_pairs={{0,16},{4,20},{8,24},{12,28},{16,0},{20,4},{24,8},{28,12},{1,17},{... | collective-permute-start | bytes 1376264 | tf_op jit(solution)/shard_map/ppermute | solution.py:22
  47.7 5.1 %collective-permute-start.9 = (f32[224,128]{1,0:T(8,128)S(1)}, f32[224,128]{1,0:T(8,128)S(1)}, u32[]{:S(2)}, u32[]{:S(2)}) collective-permute-start(f32[224,128]{1,0:T(8,128)S(1)} %get-tuple-element.102), channel_id=1, source_target_pairs={{0,4},{4,0},{8,12},{12,8},{16,20},{20,16},{24,28},{28,24},{1,5},{5... | collective-permute-start | bytes 344072 | tf_op jit(solution)/shard_map/ppermute | solution.py:66
  48.1 4.6 %collective-permute-start.7 = (f32[224,128]{1,0:T(8,128)S(1)}, f32[224,128]{1,0:T(8,128)S(1)}, u32[]{:S(2)}, u32[]{:S(2)}) collective-permute-start(f32[224,128]{1,0:T(8,128)S(1)} %get-tuple-element.103), channel_id=1, source_target_pairs={{0,1},{1,0},{2,3},{3,2},{4,5},{5,4},{6,7},{7,6},{8,9},{9,8},{10,11... | collective-permute-start | bytes 344072 | tf_op jit(solution)/shard_map/ppermute | solution.py:66
  48.1 6.4 %collective-permute-start.8 = (f32[224,128]{1,0:T(8,128)S(1)}, f32[224,128]{1,0:T(8,128)S(1)}, u32[]{:S(2)}, u32[]{:S(2)}) collective-permute-start(f32[224,128]{1,0:T(8,128)S(1)} %get-tuple-element.104), channel_id=1, source_target_pairs={{4,8},{8,4},{12,16},{16,12},{20,24},{24,20},{5,9},{9,5},{13,17},{1... | collective-permute-start | bytes 344072 | tf_op jit(solution)/shard_map/ppermute | solution.py:66
  50.8 6.4 %collective-permute-start.6 = (f32[224,128]{1,0:T(8,128)S(1)}, f32[224,128]{1,0:T(8,128)S(1)}, u32[]{:S(2)}, u32[]{:S(2)}) collective-permute-start(f32[224,128]{1,0:T(8,128)S(1)} %get-tuple-element.105), channel_id=1, source_target_pairs={{1,2},{2,1},{5,6},{6,5},{9,10},{10,9},{13,14},{14,13},{17,18},{18,... | collective-permute-start | bytes 344072 | tf_op jit(solution)/shard_map/ppermute | solution.py:66
  58.8 7.6 %collective-permute-start.13 = (f32[224,128]{1,0:T(8,128)S(1)}, f32[224,128]{1,0:T(8,128)S(1)}, u32[]{:S(2)}, u32[]{:S(2)}) collective-permute-start(f32[224,128]{1,0:T(8,128)S(1)} %get-tuple-element.96), channel_id=1, source_target_pairs={{0,4},{4,0},{8,12},{12,8},{16,20},{20,16},{24,28},{28,24},{1,5},{5... | collective-permute-start | bytes 344072 | tf_op jit(solution)/shard_map/ppermute | solution.py:66
  62.3 4.7 %collective-permute-start.11 = (f32[224,128]{1,0:T(8,128)S(1)}, f32[224,128]{1,0:T(8,128)S(1)}, u32[]{:S(2)}, u32[]{:S(2)}) collective-permute-start(f32[224,128]{1,0:T(8,128)S(1)} %get-tuple-element.97), channel_id=1, source_target_pairs={{0,1},{1,0},{2,3},{3,2},{4,5},{5,4},{6,7},{7,6},{8,9},{9,8},{10,11... | collective-permute-start | bytes 344072 | tf_op jit(solution)/shard_map/ppermute | solution.py:66
  62.3 6.1 %collective-permute-start.12 = (f32[224,128]{1,0:T(8,128)S(1)}, f32[224,128]{1,0:T(8,128)S(1)}, u32[]{:S(2)}, u32[]{:S(2)}) collective-permute-start(f32[224,128]{1,0:T(8,128)S(1)} %get-tuple-element.98), channel_id=1, source_target_pairs={{4,8},{8,4},{12,16},{16,12},{20,24},{24,20},{5,9},{9,5},{13,17},{1... | collective-permute-start | bytes 344072 | tf_op jit(solution)/shard_map/ppermute | solution.py:66
  64.4 7.5 %collective-permute-start.10 = (f32[224,128]{1,0:T(8,128)S(1)}, f32[224,128]{1,0:T(8,128)S(1)}, u32[]{:S(2)}, u32[]{:S(2)}) collective-permute-start(f32[224,128]{1,0:T(8,128)S(1)} %get-tuple-element.99), channel_id=1, source_target_pairs={{1,2},{2,1},{5,6},{6,5},{9,10},{10,9},{13,14},{14,13},{17,18},{18,... | collective-permute-start | bytes 344072 | tf_op jit(solution)/shard_map/ppermute | solution.py:66
  73.5 5.8 %collective-permute-start.17 = (f32[224,128]{1,0:T(8,128)S(1)}, f32[224,128]{1,0:T(8,128)S(1)}, u32[]{:S(2)}, u32[]{:S(2)}) collective-permute-start(f32[224,128]{1,0:T(8,128)S(1)} %get-tuple-element.90), channel_id=1, source_target_pairs={{0,4},{4,0},{8,12},{12,8},{16,20},{20,16},{24,28},{28,24},{1,5},{5... | collective-permute-start | bytes 344072 | tf_op jit(solution)/shard_map/ppermute | solution.py:66
  74.4 4.9 %collective-permute-start.15 = (f32[224,128]{1,0:T(8,128)S(1)}, f32[224,128]{1,0:T(8,128)S(1)}, u32[]{:S(2)}, u32[]{:S(2)}) collective-permute-start(f32[224,128]{1,0:T(8,128)S(1)} %get-tuple-element.91), channel_id=1, source_target_pairs={{0,1},{1,0},{2,3},{3,2},{4,5},{5,4},{6,7},{7,6},{8,9},{9,8},{10,11... | collective-permute-start | bytes 344072 | tf_op jit(solution)/shard_map/ppermute | solution.py:66
  74.4 6.1 %collective-permute-start.16 = (f32[224,128]{1,0:T(8,128)S(1)}, f32[224,128]{1,0:T(8,128)S(1)}, u32[]{:S(2)}, u32[]{:S(2)}) collective-permute-start(f32[224,128]{1,0:T(8,128)S(1)} %get-tuple-element.92), channel_id=1, source_target_pairs={{4,8},{8,4},{12,16},{16,12},{20,24},{24,20},{5,9},{9,5},{13,17},{1... | collective-permute-start | bytes 344072 | tf_op jit(solution)/shard_map/ppermute | solution.py:66
  77.4 7.2 %collective-permute-start.14 = (f32[224,128]{1,0:T(8,128)S(1)}, f32[224,128]{1,0:T(8,128)S(1)}, u32[]{:S(2)}, u32[]{:S(2)}) collective-permute-start(f32[224,128]{1,0:T(8,128)S(1)} %get-tuple-element.93), channel_id=1, source_target_pairs={{1,2},{2,1},{5,6},{6,5},{9,10},{10,9},{13,14},{14,13},{17,18},{18,... | collective-permute-start | bytes 344072 | tf_op jit(solution)/shard_map/ppermute | solution.py:66
  86.1 6.1 %collective-permute-start.21 = (f32[224,128]{1,0:T(8,128)S(1)}, f32[224,128]{1,0:T(8,128)S(1)}, u32[]{:S(2)}, u32[]{:S(2)}) collective-permute-start(f32[224,128]{1,0:T(8,128)S(1)} %get-tuple-element.84), channel_id=1, source_target_pairs={{0,4},{4,0},{8,12},{12,8},{16,20},{20,16},{24,28},{28,24},{1,5},{5... | collective-permute-start | bytes 344072 | tf_op jit(solution)/shard_map/ppermute | solution.py:66
  86.5 5.8 %collective-permute-start.19 = (f32[224,128]{1,0:T(8,128)S(1)}, f32[224,128]{1,0:T(8,128)S(1)}, u32[]{:S(2)}, u32[]{:S(2)}) collective-permute-start(f32[224,128]{1,0:T(8,128)S(1)} %get-tuple-element.85), channel_id=1, source_target_pairs={{0,1},{1,0},{2,3},{3,2},{4,5},{5,4},{6,7},{7,6},{8,9},{9,8},{10,11... | collective-permute-start | bytes 344072 | tf_op jit(solution)/shard_map/ppermute | solution.py:66
  86.5 6.1 %collective-permute-start.20 = (f32[224,128]{1,0:T(8,128)S(1)}, f32[224,128]{1,0:T(8,128)S(1)}, u32[]{:S(2)}, u32[]{:S(2)}) collective-permute-start(f32[224,128]{1,0:T(8,128)S(1)} %get-tuple-element.86), channel_id=1, source_target_pairs={{4,8},{8,4},{12,16},{16,12},{20,24},{24,20},{5,9},{9,5},{13,17},{1... | collective-permute-start | bytes 344072 | tf_op jit(solution)/shard_map/ppermute | solution.py:66
  89.3 7.5 %collective-permute-start.18 = (f32[224,128]{1,0:T(8,128)S(1)}, f32[224,128]{1,0:T(8,128)S(1)}, u32[]{:S(2)}, u32[]{:S(2)}) collective-permute-start(f32[224,128]{1,0:T(8,128)S(1)} %get-tuple-element.87), channel_id=1, source_target_pairs={{1,2},{2,1},{5,6},{6,5},{9,10},{10,9},{13,14},{14,13},{17,18},{18,... | collective-permute-start | bytes 344072 | tf_op jit(solution)/shard_map/ppermute | solution.py:66

commit v8 on v7

--- a/solution.py
+++ b/solution.py
@@ -54,7 +54,7 @@
     return pairs
 
 
-def face_sum_parts(faces):
+def face_sum_parts(faces, one_axis_at_a_time=False):
     low_x, high_x, low_y, high_y = faces
     sides = [(low_y, high_y, "gy"), (low_x, high_x, "gx")]
     sends = []
@@ -62,9 +62,18 @@
         even = lax.axis_index(axis) % 2 == 0
         sends.append((jnp.where(even, low, high), swap_pairs(lax.axis_size(axis), 1), axis))
         sends.append((jnp.where(even, high, low), swap_pairs(lax.axis_size(axis), 0), axis))
-    received = lax.optimization_barrier(
-        [lax.ppermute(block, axis, pairs) for block, pairs, axis in sends]
-    )
+    if one_axis_at_a_time:
+        first = [lax.ppermute(block, axis, pairs) for block, pairs, axis in sends[:2]]
+        later, first = lax.optimization_barrier(([block for block, _, _ in sends[2:]], first))
+        second = [
+            lax.ppermute(block, axis, pairs)
+            for block, (_, pairs, axis) in zip(later, sends[2:])
+        ]
+        received = lax.optimization_barrier(first + second)
+    else:
+        received = lax.optimization_barrier(
+            [lax.ppermute(block, axis, pairs) for block, pairs, axis in sends]
+        )
     summed = []
     for side_id, (low, high, axis) in enumerate(sides):
         even = lax.axis_index(axis) % 2 == 0
@@ -104,7 +113,10 @@
     own_count = own_block.shape[0]
     cols = gap.shape[3]
     width = order_max // 4
-    load = face_sum_parts([gap[0, 0, face_id * width : (face_id + 1) * width] for face_id in range(4)])
+    load = face_sum_parts(
+        [gap[0, 0, face_id * width : (face_id + 1) * width] for face_id in range(4)],
+        one_axis_at_a_time=True,
+    )
     to_slots = jnp.where(
         slot_map[:, None] == row_ids[None, :], slot_scale[:, None], 0.0
     ).astype(jnp.bfloat16)

time: 98.2 us -> 98.5 us (level)
  the two profiles are of different devices: /device:TPU:11 before, /device:TPU:19 now
where the time goes in v8:
time: 98.5 us; the launch traced here: 97.9 us
  starting transfers between devices  38.5 us (39%)
  waiting for transfers between devices  30.4 us (31%)
  matrix products  12.5 us (13%)
  other arithmetic  9.26 us (9%)
  between operations  4.29 us (4%)
  local copies, waits for them, and re-layouts  2.96 us (3%)
    ppermute x20, starting transfers between devices, face_sum_parts(): lax.ppermute(block, axis, pairs)  35 us
    ppermute x20, waiting for transfers between devices, face_sum_parts(): lax.ppermute(block, axis, pairs)  26 us
    ppermute x2, waiting for transfers between devices, from_behind(): return lax.ppermute(value, axis, pairs)  4.49 us
    dot_general x2, matrix products, slot_pieces(): jnp.dot(stacked, to_rows, preferred_element_type=jnp.float32)  3.87 us
    dot_general x2, matrix products, slot_pieces(): return jnp.dot(to_slots, side, preferred_element_type=jnp.float32)  3.69 us
    ppermute x2, starting transfers between devices, from_behind(): return lax.ppermute(value, axis, pairs)  3.43 us
    dot_general x4, matrix products, body(): jnp.dot(op_high, jnp.concatenate([dir_high, dir_mid], axis=1).astype(jnp....  2.58 us
    dot_general x4, matrix products, body(): jnp.dot(op_mid, dir_high.astype(jnp.bfloat16), preferred_element_type=jnp...  2.35 us
  transfers between devices with their start and end apart: 22, of which 11 were waited for; matrix products, arithmetic and copies ran while one was open for 11% of the time, Pallas kernels for 0%

profile of v8, /device:TPU:19, one launch (start us, length us, event | category | flops | bytes accessed | tf_op | source)
XLA Modules:
  0.0 97.9 jit_solution(9762758360928238883)
XLA Ops:
  0.7 2.0 %bitcast_select_fusion = (f32[224,128]{1,0:T(8,128)}, f32[224,128]{1,0:T(8,128)S(1)}, f32[224,128]{1,0:T(8,128)}, f32[224,128]{1,0:T(8,128)}) fusion(f32[1,1,896,128]{3,2,1,0:T(8,128)} %param.6, pred[]{:T(512)S(6)} %eq.112, pred[]{:T(512)S(6)} %eq.111), kind=kLoop, calls=%fused_computation.97 | loop fusion | flops 114688 | bytes 917506 | tf_op jit(solution)/shard_map/jit(_where)/select_n | solution.py:64
  2.9 4.1 %collective-permute-start = (f32[224,128]{1,0:T(8,128)}, f32[224,128]{1,0:T(8,128)S(1)}, u32[]{:S(2)}, u32[]{:S(2)}) collective-permute-start(f32[224,128]{1,0:T(8,128)} %get-tuple-element.121), channel_id=1, source_target_pairs={{1,2},{2,1},{5,6},{6,5},{9,10},{10,9},{13,14},{14,13},{17,18},{18,... | collective-permute-start | bytes 344072 | tf_op jit(solution)/shard_map/ppermute | solution.py:66
  6.9 1.2 %slice_bitcast_fusion.1 = (f32[128,896]{1,0:T(8,128)S(1)}, f32[128,896]{1,0:T(8,128)S(1)}) fusion(f32[1,1,2,128,896]{4,3,2,1,0:T(8,128)} %param.8), kind=kLoop, calls=%fused_computation.95 | loop fusion | bytes 1835008 | tf_op jit(solution)/shard_map/squeeze | solution.py:111
  8.4 3.2 %collective-permute-start.5 = (f32[128,896]{1,0:T(8,128)S(1)}, f32[128,896]{1,0:T(8,128)}, u32[]{:S(2)}, u32[]{:S(2)}) collective-permute-start(f32[128,896]{1,0:T(8,128)S(1)} %get-tuple-element.69), channel_id=1, source_target_pairs={{0,16},{4,20},{8,24},{12,28},{16,0},{20,4},{24,8},{28,12},{1,17},{... | collective-permute-start | bytes 1376264 | tf_op jit(solution)/shard_map/ppermute | solution.py:22
  12.2 1.3 %reduce = s32[896]{0:T(1024)} reduce(s32[1,1,896]{2,1,0:T(1,128)} %param.11, s32[]{:T(128)} %constant.96.clone.1), dimensions={0,1}, to_apply=%param.11.reduce_sub_computation | reduce | bytes 7172 | tf_op args[5]
  13.9 0.4 copy-done.3
  14.3 2.7 %convolution_convert_fusion = bf16[1280,896]{0,1:T(8,128)(2,1)S(1)} fusion(bf16[640,896]{1,0:T(8,128)(2,1)S(1)} %get-tuple-element.61, bf16[640,896]{1,0:T(8,128)(2,1)S(1)} %get-tuple-element.60, bf16[896]{0:T(1024)(128)(2,1)S(1)} %select_select_fusion, s32[896]{0:T(1024)S(1)} %copy-done.3), kind=kOutput, calls=%fused_computation | convolution fusion | flops 2062548992 | bytes 4592896 | tf_op jit(solution)/shard_map/dot_general | solution.py:92
  17.5 0.5 copy-done.2
  18.0 1.9 %collective-permute-start.2 = (f32[224,128]{1,0:T(8,128)S(1)}, f32[224,128]{1,0:T(8,128)S(1)}, u32[]{:S(2)}, u32[]{:S(2)}) collective-permute-start(f32[224,128]{1,0:T(8,128)S(1)} %copy-done.2), channel_id=1, source_target_pairs={{4,8},{8,4},{12,16},{16,12},{20,24},{24,20},{5,9},{9,5},{13,17},{1... | collective-permute-start | bytes 344072 | tf_op jit(solution)/shard_map/ppermute | solution.py:69
  19.9 1.9 %collective-permute-start.3 = (f32[224,128]{1,0:T(8,128)S(1)}, f32[224,128]{1,0:T(8,128)S(1)}, u32[]{:S(2)}, u32[]{:S(2)}) collective-permute-start(f32[224,128]{1,0:T(8,128)S(1)} %get-tuple-element.29), channel_id=1, source_target_pairs={{0,4},{4,0},{8,12},{12,8},{16,20},{20,16},{24,28},{28,24},{1,5},{5... | collective-permute-start | bytes 344072 | tf_op jit(solution)/shard_map/ppermute | solution.py:69
  21.8 2.7 %fusion.7 = f32[896,1792]{1,0:T(8,128)S(1)} fusion(bf16[640,896]{0,1:T(8,128)(2,1)S(1)} %get-tuple-element.59, bf16[640,896]{0,1:T(8,128)(2,1)S(1)} %get-tuple-element.58, bf16[896,896]{1,0:T(8,128)(2,1)S(1)} %select_convert_fusion.1), kind=kOutput, calls=%fused_computation.16 | convolution fusion | flops 2059796480 | bytes 9863168 | tf_op jit(solution)/shard_map/dot_general | solution.py:94
  24.5 0.6 fusion.70
  27.7 4.3 %collective-permute-done.2 = f32[224,128]{1,0:T(8,128)S(1)} collective-permute-done((f32[224,128]{1,0:T(8,128)S(1)}, f32[224,128]{1,0:T(8,128)S(1)}, u32[]{:S(2)}, u32[]{:S(2)}) %collective-permute-start.2) | collective-permute-done | bytes 114720 | tf_op jit(solution)/shard_map/ppermute | solution.py:69
  32.1 4.5 %collective-permute-done.5 = f32[128,896]{1,0:T(8,128)} collective-permute-done((f32[128,896]{1,0:T(8,128)S(1)}, f32[128,896]{1,0:T(8,128)}, u32[]{:S(2)}, u32[]{:S(2)}) %collective-permute-start.5) | collective-permute-done | bytes 458784 | tf_op jit(solution)/shard_map/ppermute | solution.py:22
  36.6 1.2 %select_add_fusion.1 = (f32[128,896]{1,0:T(8,128)S(1)}, f32[128,896]{1,0:T(8,128)S(1)}) fusion(f32[128,896]{1,0:T(8,128)} %collective-permute-done.5, f32[128,896]{1,0:T(8,128)} %collective-permute-done.4, pred[]{:T(512)} %bitcast.12, pred[]{:T(512)} %bitcast.10, pred[]{:T(512)} %bitcast.15, pred[]{:T(512)} %bitcast.14), kind=kLoop, calls=%fused_computation.93 | loop fusion | flops 688128 | bytes 1835012 | tf_op jit(solution)/shard_map/add | solution.py:131
  38.0 1.2 %fusion.18 = bf16[512,896]{1,0:T(8,128)(2,1)S(1)} fusion(bf16[896]{0:T(1024)(128)(2,1)S(1)} %select_select_fusion, s32[896]{0:T(1024)S(1)} %copy-done.3, bf16[256,896]{1,0:T(8,128)(2,1)S(1)} %get-tuple-element.65, bf16[256,896]{1,0:T(8,128)(2,1)S(1)} %get-tuple-element.64), kind=kOutput, calls=%fused_computation.27 | convolution fusion | flops 825982976 | bytes 1840384 | tf_op jit(solution)/shard_map/dot_general | solution.py:92
  39.3 1.0 %fusion.25 = f32[896,1792]{1,0:T(8,128)S(1)} fusion(bf16[256,896]{1,0:T(8,128)(2,1)S(1)} %get-tuple-element.63, bf16[256,896]{1,0:T(8,128)(2,1)S(1)} %get-tuple-element.62, bf16[896,896]{1,0:T(8,128)(2,1)S(1)} %select_convert_fusion.1), kind=kOutput, calls=%fused_computation.41 | convolution fusion | flops 823918592 | bytes 7798784 | tf_op jit(solution)/shard_map/dot_general | solution.py:94
  40.3 1.0 %fusion.1 = (bf16[896,896]{1,0:T(8,128)(2,1)S(1)}, bf16[896,896]{1,0:T(8,128)(2,1)S(1)}) fusion(f32[896,1792]{1,0:T(8,128)S(1)} %fusion.25, f32[896,1792]{1,0:T(8,128)S(1)} %fusion.7), kind=kLoop, calls=%fused_computation.6 | loop fusion | flops 3211264 | bytes 16056320 | tf_op jit(solution)/shard_map/convert_element_type | solution.py:137
  41.3 0.6 fusion.34
  42.0 0.6 convolution_add_fusion.3
  42.6 6.9 %collective-permute-start.9 = (f32[224,128]{1,0:T(8,128)S(1)}, f32[224,128]{1,0:T(8,128)S(1)}, u32[]{:S(2)}, u32[]{:S(2)}) collective-permute-start(f32[224,128]{1,0:T(8,128)S(1)} %get-tuple-element.110), channel_id=1, source_target_pairs={{0,4},{4,0},{8,12},{12,8},{16,20},{20,16},{24,28},{28,24},{1,5},{5... | collective-permute-start | bytes 344072 | tf_op jit(solution)/shard_map/ppermute | solution.py:75
  49.5 2.6 %collective-permute-start.8 = (f32[224,128]{1,0:T(8,128)S(1)}, f32[224,128]{1,0:T(8,128)S(1)}, u32[]{:S(2)}, u32[]{:S(2)}) collective-permute-start(f32[224,128]{1,0:T(8,128)S(1)} %get-tuple-element.112), channel_id=1, source_target_pairs={{4,8},{8,4},{12,16},{16,12},{20,24},{24,20},{5,9},{9,5},{13,17},{1... | collective-permute-start | bytes 344072 | tf_op jit(solution)/shard_map/ppermute | solution.py:75
  52.1 2.1 %collective-permute-start.6 = (f32[224,128]{1,0:T(8,128)S(1)}, f32[224,128]{1,0:T(8,128)S(1)}, u32[]{:S(2)}, u32[]{:S(2)}) collective-permute-start(f32[224,128]{1,0:T(8,128)S(1)} %get-tuple-element.113), channel_id=1, source_target_pairs={{1,2},{2,1},{5,6},{6,5},{9,10},{10,9},{13,14},{14,13},{17,18},{18,... | collective-permute-start | bytes 344072 | tf_op jit(solution)/shard_map/ppermute | solution.py:75
  54.2 1.3 %collective-permute-done.8 = f32[224,128]{1,0:T(8,128)S(1)} collective-permute-done((f32[224,128]{1,0:T(8,128)S(1)}, f32[224,128]{1,0:T(8,128)S(1)}, u32[]{:S(2)}, u32[]{:S(2)}) %collective-permute-start.8) | collective-permute-done | bytes 114720 | tf_op jit(solution)/shard_map/ppermute | solution.py:75
  55.6 4.2 %collective-permute-done.6 = f32[224,128]{1,0:T(8,128)S(1)} collective-permute-done((f32[224,128]{1,0:T(8,128)S(1)}, f32[224,128]{1,0:T(8,128)S(1)}, u32[]{:S(2)}, u32[]{:S(2)}) %collective-permute-start.6) | collective-permute-done | bytes 114720 | tf_op jit(solution)/shard_map/ppermute | solution.py:75
  59.9 0.6 fusion.38
  60.6 0.6 convolution_add_fusion.2
  61.2 0.5 collective-permute-start.13
  61.7 2.6 %collective-permute-start.12 = (f32[224,128]{1,0:T(8,128)S(1)}, f32[224,128]{1,0:T(8,128)S(1)}, u32[]{:S(2)}, u32[]{:S(2)}) collective-permute-start(f32[224,128]{1,0:T(8,128)S(1)} %get-tuple-element.106), channel_id=1, source_target_pairs={{4,8},{8,4},{12,16},{16,12},{20,24},{24,20},{5,9},{9,5},{13,17},{1... | collective-permute-start | bytes 344072 | tf_op jit(solution)/shard_map/ppermute | solution.py:75
  64.3 2.3 %collective-permute-start.10 = (f32[224,128]{1,0:T(8,128)S(1)}, f32[224,128]{1,0:T(8,128)S(1)}, u32[]{:S(2)}, u32[]{:S(2)}) collective-permute-start(f32[224,128]{1,0:T(8,128)S(1)} %get-tuple-element.107), channel_id=1, source_target_pairs={{1,2},{2,1},{5,6},{6,5},{9,10},{10,9},{13,14},{14,13},{17,18},{18,... | collective-permute-start | bytes 344072 | tf_op jit(solution)/shard_map/ppermute | solution.py:75
  66.6 1.2 %collective-permute-done.12 = f32[224,128]{1,0:T(8,128)S(1)} collective-permute-done((f32[224,128]{1,0:T(8,128)S(1)}, f32[224,128]{1,0:T(8,128)S(1)}, u32[]{:S(2)}, u32[]{:S(2)}) %collective-permute-start.12) | collective-permute-done | bytes 114720 | tf_op jit(solution)/shard_map/ppermute | solution.py:75
  67.8 4.4 %collective-permute-done.10 = f32[224,128]{1,0:T(8,128)S(1)} collective-permute-done((f32[224,128]{1,0:T(8,128)S(1)}, f32[224,128]{1,0:T(8,128)S(1)}, u32[]{:S(2)}, u32[]{:S(2)}) %collective-permute-start.10) | collective-permute-done | bytes 114720 | tf_op jit(solution)/shard_map/ppermute | solution.py:75
  72.5 0.6 fusion.42
  73.2 0.6 convolution_add_fusion.1
  73.8 0.5 collective-permute-start.17
  74.3 2.5 %collective-permute-start.16 = (f32[224,128]{1,0:T(8,128)S(1)}, f32[224,128]{1,0:T(8,128)S(1)}, u32[]{:S(2)}, u32[]{:S(2)}) collective-permute-start(f32[224,128]{1,0:T(8,128)S(1)} %get-tuple-element.100), channel_id=1, source_target_pairs={{4,8},{8,4},{12,16},{16,12},{20,24},{24,20},{5,9},{9,5},{13,17},{1... | collective-permute-start | bytes 344072 | tf_op jit(solution)/shard_map/ppermute | solution.py:75
  76.8 2.1 %collective-permute-start.14 = (f32[224,128]{1,0:T(8,128)S(1)}, f32[224,128]{1,0:T(8,128)S(1)}, u32[]{:S(2)}, u32[]{:S(2)}) collective-permute-start(f32[224,128]{1,0:T(8,128)S(1)} %get-tuple-element.101), channel_id=1, source_target_pairs={{1,2},{2,1},{5,6},{6,5},{9,10},{10,9},{13,14},{14,13},{17,18},{18,... | collective-permute-start | bytes 344072 | tf_op jit(solution)/shard_map/ppermute | solution.py:75
  79.0 1.4 %collective-permute-done.16 = f32[224,128]{1,0:T(8,128)S(1)} collective-permute-done((f32[224,128]{1,0:T(8,128)S(1)}, f32[224,128]{1,0:T(8,128)S(1)}, u32[]{:S(2)}, u32[]{:S(2)}) %collective-permute-start.16) | collective-permute-done | bytes 114720 | tf_op jit(solution)/shard_map/ppermute | solution.py:75
  80.4 4.3 %collective-permute-done.14 = f32[224,128]{1,0:T(8,128)S(1)} collective-permute-done((f32[224,128]{1,0:T(8,128)S(1)}, f32[224,128]{1,0:T(8,128)S(1)}, u32[]{:S(2)}, u32[]{:S(2)}) %collective-permute-start.14) | collective-permute-done | bytes 114720 | tf_op jit(solution)/shard_map/ppermute | solution.py:75
  85.0 0.6 fusion.48
  85.6 0.6 convolution_add_fusion
  86.3 0.5 collective-permute-start.21
  86.7 2.4 %collective-permute-start.20 = (f32[224,128]{1,0:T(8,128)S(1)}, f32[224,128]{1,0:T(8,128)S(1)}, u32[]{:S(2)}, u32[]{:S(2)}) collective-permute-start(f32[224,128]{1,0:T(8,128)S(1)} %get-tuple-element.94), channel_id=1, source_target_pairs={{4,8},{8,4},{12,16},{16,12},{20,24},{24,20},{5,9},{9,5},{13,17},{1... | collective-permute-start | bytes 344072 | tf_op jit(solution)/shard_map/ppermute | solution.py:75
  89.1 2.1 %collective-permute-start.18 = (f32[224,128]{1,0:T(8,128)S(1)}, f32[224,128]{1,0:T(8,128)S(1)}, u32[]{:S(2)}, u32[]{:S(2)}) collective-permute-start(f32[224,128]{1,0:T(8,128)S(1)} %get-tuple-element.95), channel_id=1, source_target_pairs={{1,2},{2,1},{5,6},{6,5},{9,10},{10,9},{13,14},{14,13},{17,18},{18,... | collective-permute-start | bytes 344072 | tf_op jit(solution)/shard_map/ppermute | solution.py:75
  91.2 1.0 %add_add_fusion = f32[1,1,896,128]{3,2,1,0:T(8,128)} fusion(f32[1,1,224,128]{3,2,1,0:T(8,128)S(1)} %bitcast.69, f32[1,1,224,128]{3,2,1,0:T(8,128)S(1)} %bitcast.71, f32[1,1,224,128]{3,2,1,0:T(8,128)S(1)} %bitcast.67, f32[1,1,224,128]{3,2,1,0:T(8,128)S(1)} %bitcast.65, f32[1,1,224,128]{3,2,1,0:T(8,128)S(1)} %bitcast.77, f32[1,1,224,128]{3,2,1,0:T(8,128)S(1)} %bitcast.79, ...), kind=kLoop, calls=%fused_computation.89 | loop fusion | flops 3211264 | bytes 2293760 | tf_op jit(solution)/shard_map/add | solution.py:147
  92.3 0.6 collective-permute-done.20
  92.8 4.2 %collective-permute-done.18 = f32[224,128]{1,0:T(8,128)S(1)} collective-permute-done((f32[224,128]{1,0:T(8,128)S(1)}, f32[224,128]{1,0:T(8,128)S(1)}, u32[]{:S(2)}, u32[]{:S(2)}) %collective-permute-start.18) | collective-permute-done | bytes 114720 | tf_op jit(solution)/shard_map/ppermute | solution.py:75
  97.0 0.9 maximum_subtract_fusion.6
  (48 shorter events, 2.8 us)
Async XLA Ops:
  0.6 12.9 %copy-start = (f32[1,1,640,896]{3,2,1,0:T(8,128)S(1)}, f32[1,1,640,896]{3,2,1,0:T(8,128)}, u32[]{:S(2)}) copy-start(f32[1,1,640,896]{3,2,1,0:T(8,128)} %param.7) | copy-start | bytes 6881284
  2.6 14.9 %collective-permute-start.1 = (f32[224,128]{1,0:T(8,128)}, f32[224,128]{1,0:T(8,128)S(1)}, u32[]{:S(2)}, u32[]{:S(2)}) collective-permute-start(f32[224,128]{1,0:T(8,128)} %get-tuple-element.118), channel_id=1, source_target_pairs={{0,1},{1,0},{2,3},{3,2},{4,5},{5,4},{6,7},{7,6},{8,9},{9,8},{10,11... | collective-permute-start | bytes 344072 | tf_op jit(solution)/shard_map/ppermute | solution.py:66
  2.9 14.6 %collective-permute-start = (f32[224,128]{1,0:T(8,128)}, f32[224,128]{1,0:T(8,128)S(1)}, u32[]{:S(2)}, u32[]{:S(2)}) collective-permute-start(f32[224,128]{1,0:T(8,128)} %get-tuple-element.121), channel_id=1, source_target_pairs={{1,2},{2,1},{5,6},{6,5},{9,10},{10,9},{13,14},{14,13},{17,18},{18,... | collective-permute-start | bytes 344072 | tf_op jit(solution)/shard_map/ppermute | solution.py:66
  8.2 24.0 %collective-permute-start.4 = (f32[128,896]{1,0:T(8,128)S(1)}, f32[128,896]{1,0:T(8,128)}, u32[]{:S(2)}, u32[]{:S(2)}) collective-permute-start(f32[128,896]{1,0:T(8,128)S(1)} %get-tuple-element.68), channel_id=1, source_target_pairs={{0,24},{4,28},{8,0},{12,4},{16,8},{20,12},{24,16},{28,20},{1,25},{... | collective-permute-start | bytes 1376264 | tf_op jit(solution)/shard_map/ppermute | solution.py:22
  8.4 28.2 %collective-permute-start.5 = (f32[128,896]{1,0:T(8,128)S(1)}, f32[128,896]{1,0:T(8,128)}, u32[]{:S(2)}, u32[]{:S(2)}) collective-permute-start(f32[128,896]{1,0:T(8,128)S(1)} %get-tuple-element.69), channel_id=1, source_target_pairs={{0,16},{4,20},{8,24},{12,28},{16,0},{20,4},{24,8},{28,12},{1,17},{... | collective-permute-start | bytes 1376264 | tf_op jit(solution)/shard_map/ppermute | solution.py:22
  13.5 0.7 copy-start.3
  17.1 0.9 copy-start.2
  18.0 13.9 %collective-permute-start.2 = (f32[224,128]{1,0:T(8,128)S(1)}, f32[224,128]{1,0:T(8,128)S(1)}, u32[]{:S(2)}, u32[]{:S(2)}) collective-permute-start(f32[224,128]{1,0:T(8,128)S(1)} %copy-done.2), channel_id=1, source_target_pairs={{4,8},{8,4},{12,16},{16,12},{20,24},{24,20},{5,9},{9,5},{13,17},{1... | collective-permute-start | bytes 344072 | tf_op jit(solution)/shard_map/ppermute | solution.py:69
  19.9 12.0 %collective-permute-start.3 = (f32[224,128]{1,0:T(8,128)S(1)}, f32[224,128]{1,0:T(8,128)S(1)}, u32[]{:S(2)}, u32[]{:S(2)}) collective-permute-start(f32[224,128]{1,0:T(8,128)S(1)} %get-tuple-element.29), channel_id=1, source_target_pairs={{0,4},{4,0},{8,12},{12,8},{16,20},{20,16},{24,28},{28,24},{1,5},{5... | collective-permute-start | bytes 344072 | tf_op jit(solution)/shard_map/ppermute | solution.py:69
  21.8 2.7 %copy-start.4 = (s32[1,1,2]{2,1,0:T(1,128)S(1)}, s32[1,1,2]{2,1,0:T(1,128)}, u32[]{:S(2)}) copy-start(s32[1,1,2]{2,1,0:T(1,128)} %param.9) | copy-start | bytes 28
  21.8 10.2 %copy-start.1 = (f32[1,1,896,128]{3,2,1,0:T(8,128)S(1)}, f32[1,1,896,128]{3,2,1,0:T(8,128)}, u32[]{:S(2)}) copy-start(f32[1,1,896,128]{3,2,1,0:T(8,128)} %param.6) | copy-start | bytes 1376260
  42.6 11.6 %collective-permute-start.9 = (f32[224,128]{1,0:T(8,128)S(1)}, f32[224,128]{1,0:T(8,128)S(1)}, u32[]{:S(2)}, u32[]{:S(2)}) collective-permute-start(f32[224,128]{1,0:T(8,128)S(1)} %get-tuple-element.110), channel_id=1, source_target_pairs={{0,4},{4,0},{8,12},{12,8},{16,20},{20,16},{24,28},{28,24},{1,5},{5... | collective-permute-start | bytes 344072 | tf_op jit(solution)/shard_map/ppermute | solution.py:75
  49.5 4.8 %collective-permute-start.7 = (f32[224,128]{1,0:T(8,128)S(1)}, f32[224,128]{1,0:T(8,128)S(1)}, u32[]{:S(2)}, u32[]{:S(2)}) collective-permute-start(f32[224,128]{1,0:T(8,128)S(1)} %get-tuple-element.111), channel_id=1, source_target_pairs={{0,1},{1,0},{2,3},{3,2},{4,5},{5,4},{6,7},{7,6},{8,9},{9,8},{10,11... | collective-permute-start | bytes 344072 | tf_op jit(solution)/shard_map/ppermute | solution.py:75
  49.5 6.1 %collective-permute-start.8 = (f32[224,128]{1,0:T(8,128)S(1)}, f32[224,128]{1,0:T(8,128)S(1)}, u32[]{:S(2)}, u32[]{:S(2)}) collective-permute-start(f32[224,128]{1,0:T(8,128)S(1)} %get-tuple-element.112), channel_id=1, source_target_pairs={{4,8},{8,4},{12,16},{16,12},{20,24},{24,20},{5,9},{9,5},{13,17},{1... | collective-permute-start | bytes 344072 | tf_op jit(solution)/shard_map/ppermute | solution.py:75
  52.1 7.6 %collective-permute-start.6 = (f32[224,128]{1,0:T(8,128)S(1)}, f32[224,128]{1,0:T(8,128)S(1)}, u32[]{:S(2)}, u32[]{:S(2)}) collective-permute-start(f32[224,128]{1,0:T(8,128)S(1)} %get-tuple-element.113), channel_id=1, source_target_pairs={{1,2},{2,1},{5,6},{6,5},{9,10},{10,9},{13,14},{14,13},{17,18},{18,... | collective-permute-start | bytes 344072 | tf_op jit(solution)/shard_map/ppermute | solution.py:75
  61.2 5.3 %collective-permute-start.13 = (f32[224,128]{1,0:T(8,128)S(1)}, f32[224,128]{1,0:T(8,128)S(1)}, u32[]{:S(2)}, u32[]{:S(2)}) collective-permute-start(f32[224,128]{1,0:T(8,128)S(1)} %get-tuple-element.104), channel_id=1, source_target_pairs={{0,4},{4,0},{8,12},{12,8},{16,20},{20,16},{24,28},{28,24},{1,5},{5... | collective-permute-start | bytes 344072 | tf_op jit(solution)/shard_map/ppermute | solution.py:75
  61.7 4.9 %collective-permute-start.11 = (f32[224,128]{1,0:T(8,128)S(1)}, f32[224,128]{1,0:T(8,128)S(1)}, u32[]{:S(2)}, u32[]{:S(2)}) collective-permute-start(f32[224,128]{1,0:T(8,128)S(1)} %get-tuple-element.105), channel_id=1, source_target_pairs={{0,1},{1,0},{2,3},{3,2},{4,5},{5,4},{6,7},{7,6},{8,9},{9,8},{10,11... | collective-permute-start | bytes 344072 | tf_op jit(solution)/shard_map/ppermute | solution.py:75
  61.7 6.1 %collective-permute-start.12 = (f32[224,128]{1,0:T(8,128)S(1)}, f32[224,128]{1,0:T(8,128)S(1)}, u32[]{:S(2)}, u32[]{:S(2)}) collective-permute-start(f32[224,128]{1,0:T(8,128)S(1)} %get-tuple-element.106), channel_id=1, source_target_pairs={{4,8},{8,4},{12,16},{16,12},{20,24},{24,20},{5,9},{9,5},{13,17},{1... | collective-permute-start | bytes 344072 | tf_op jit(solution)/shard_map/ppermute | solution.py:75
  64.3 7.9 %collective-permute-start.10 = (f32[224,128]{1,0:T(8,128)S(1)}, f32[224,128]{1,0:T(8,128)S(1)}, u32[]{:S(2)}, u32[]{:S(2)}) collective-permute-start(f32[224,128]{1,0:T(8,128)S(1)} %get-tuple-element.107), channel_id=1, source_target_pairs={{1,2},{2,1},{5,6},{6,5},{9,10},{10,9},{13,14},{14,13},{17,18},{18,... | collective-permute-start | bytes 344072 | tf_op jit(solution)/shard_map/ppermute | solution.py:75
  73.8 5.1 %collective-permute-start.17 = (f32[224,128]{1,0:T(8,128)S(1)}, f32[224,128]{1,0:T(8,128)S(1)}, u32[]{:S(2)}, u32[]{:S(2)}) collective-permute-start(f32[224,128]{1,0:T(8,128)S(1)} %get-tuple-element.98), channel_id=1, source_target_pairs={{0,4},{4,0},{8,12},{12,8},{16,20},{20,16},{24,28},{28,24},{1,5},{5... | collective-permute-start | bytes 344072 | tf_op jit(solution)/shard_map/ppermute | solution.py:75
  74.3 4.7 %collective-permute-start.15 = (f32[224,128]{1,0:T(8,128)S(1)}, f32[224,128]{1,0:T(8,128)S(1)}, u32[]{:S(2)}, u32[]{:S(2)}) collective-permute-start(f32[224,128]{1,0:T(8,128)S(1)} %get-tuple-element.99), channel_id=1, source_target_pairs={{0,1},{1,0},{2,3},{3,2},{4,5},{5,4},{6,7},{7,6},{8,9},{9,8},{10,11... | collective-permute-start | bytes 344072 | tf_op jit(solution)/shard_map/ppermute | solution.py:75
  74.3 6.1 %collective-permute-start.16 = (f32[224,128]{1,0:T(8,128)S(1)}, f32[224,128]{1,0:T(8,128)S(1)}, u32[]{:S(2)}, u32[]{:S(2)}) collective-permute-start(f32[224,128]{1,0:T(8,128)S(1)} %get-tuple-element.100), channel_id=1, source_target_pairs={{4,8},{8,4},{12,16},{16,12},{20,24},{24,20},{5,9},{9,5},{13,17},{1... | collective-permute-start | bytes 344072 | tf_op jit(solution)/shard_map/ppermute | solution.py:75
  76.8 8.0 %collective-permute-start.14 = (f32[224,128]{1,0:T(8,128)S(1)}, f32[224,128]{1,0:T(8,128)S(1)}, u32[]{:S(2)}, u32[]{:S(2)}) collective-permute-start(f32[224,128]{1,0:T(8,128)S(1)} %get-tuple-element.101), channel_id=1, source_target_pairs={{1,2},{2,1},{5,6},{6,5},{9,10},{10,9},{13,14},{14,13},{17,18},{18,... | collective-permute-start | bytes 344072 | tf_op jit(solution)/shard_map/ppermute | solution.py:75
  86.3 6.0 %collective-permute-start.21 = (f32[224,128]{1,0:T(8,128)S(1)}, f32[224,128]{1,0:T(8,128)S(1)}, u32[]{:S(2)}, u32[]{:S(2)}) collective-permute-start(f32[224,128]{1,0:T(8,128)S(1)} %get-tuple-element.92), channel_id=1, source_target_pairs={{0,4},{4,0},{8,12},{12,8},{16,20},{20,16},{24,28},{28,24},{1,5},{5... | collective-permute-start | bytes 344072 | tf_op jit(solution)/shard_map/ppermute | solution.py:75
  86.7 5.5 %collective-permute-start.19 = (f32[224,128]{1,0:T(8,128)S(1)}, f32[224,128]{1,0:T(8,128)S(1)}, u32[]{:S(2)}, u32[]{:S(2)}) collective-permute-start(f32[224,128]{1,0:T(8,128)S(1)} %get-tuple-element.93), channel_id=1, source_target_pairs={{0,1},{1,0},{2,3},{3,2},{4,5},{5,4},{6,7},{7,6},{8,9},{9,8},{10,11... | collective-permute-start | bytes 344072 | tf_op jit(solution)/shard_map/ppermute | solution.py:75
  86.7 6.1 %collective-permute-start.20 = (f32[224,128]{1,0:T(8,128)S(1)}, f32[224,128]{1,0:T(8,128)S(1)}, u32[]{:S(2)}, u32[]{:S(2)}) collective-permute-start(f32[224,128]{1,0:T(8,128)S(1)} %get-tuple-element.94), channel_id=1, source_target_pairs={{4,8},{8,4},{12,16},{16,12},{20,24},{24,20},{5,9},{9,5},{13,17},{1... | collective-permute-start | bytes 344072 | tf_op jit(solution)/shard_map/ppermute | solution.py:75
  89.1 7.9 %collective-permute-start.18 = (f32[224,128]{1,0:T(8,128)S(1)}, f32[224,128]{1,0:T(8,128)S(1)}, u32[]{:S(2)}, u32[]{:S(2)}) collective-permute-start(f32[224,128]{1,0:T(8,128)S(1)} %get-tuple-element.95), channel_id=1, source_target_pairs={{1,2},{2,1},{5,6},{6,5},{9,10},{10,9},{13,14},{14,13},{17,18},{18,... | collective-permute-start | bytes 344072 | tf_op jit(solution)/shard_map/ppermute | solution.py:75

commit v9 on v8

--- a/solution.py
+++ b/solution.py
@@ -94,6 +94,13 @@
     return jnp.dot(to_slots, side, preferred_element_type=jnp.float32)
 
 
+def bf16x3_apply(op_high, op_mid, pair, cols):
+    both = jnp.dot(op_high, pair, preferred_element_type=jnp.float32)
+    return (both[:, :cols] + both[:, cols:]) + jnp.dot(
+        op_mid, pair[:, :cols], preferred_element_type=jnp.float32
+    )
+
+
 def body(gap, own_rows, spill_rows, tile_plan, orders, slot_rows):
     order_max = gap.shape[2]
     tile_rows = spill_rows.shape[3]
@@ -124,18 +131,25 @@
         row_ids[:, None] == slot_map[None, :], slot_scale[None, :], 0.0
     ).astype(jnp.bfloat16)
     own_slots = slot_pieces(own_block, to_rows, to_slots[:, :own_count])
-    extra_rows = []
-    for extra_id in range(2):
-        gathered = jnp.zeros_like(homed[0])
-        for slot_id in range(2):
-            gathered = gathered + jnp.where(
-                plan_row[slot_id] == own_tiles + extra_id, homed[slot_id], 0.0
-            )
-        extra_rows.append(gathered)
-    extra_block = jnp.concatenate(extra_rows, axis=0)
-    extra_slots = slot_pieces(extra_block, to_rows, to_slots[:, own_count:])
-    op_high = (own_slots[:, :order_max] + extra_slots[:, :order_max]).astype(jnp.bfloat16)
-    op_mid = (own_slots[:, order_max:] + extra_slots[:, order_max:]).astype(jnp.bfloat16)
+    spill_ids = jnp.concatenate(
+        [
+            jnp.where(plan_row[slot_id] >= own_tiles, plan_row[slot_id] * tile_rows, -order_max)
+            + jnp.arange(tile_rows, dtype=jnp.int32)
+            for slot_id in range(2)
+        ]
+    )
+    spill_place = jnp.where(
+        slot_map[:, None] == spill_ids[None, :], slot_scale[:, None], 0.0
+    ).astype(jnp.bfloat16)
+    spill_stack = jnp.concatenate(homed, axis=0)
+    spill_slots = slot_pieces(spill_stack, to_rows, spill_place)
+    own_high = own_slots[:, :order_max].astype(jnp.bfloat16)
+    own_mid = own_slots[:, order_max:].astype(jnp.bfloat16)
+    op_high = (own_slots[:, :order_max] + spill_slots[:, :order_max]).astype(jnp.bfloat16)
+    op_mid = (own_slots[:, order_max:] + spill_slots[:, order_max:]).astype(jnp.bfloat16)
+    spill_high = lax.reduce_precision(spill_stack, exponent_bits=8, mantissa_bits=7)
+    spill_mid = (spill_stack - spill_high).astype(jnp.bfloat16)
+    spill_high = spill_high.astype(jnp.bfloat16)
     centre = (high_bound + low_bound) / 2.0
     half_width = (high_bound - low_bound) / 2.0
     sigma_value = centre / half_width
@@ -146,15 +160,25 @@
     for step_id in range(ITERS):
         solution = solution + direction
         dir_high = lax.reduce_precision(direction, exponent_bits=8, mantissa_bits=7)
-        dir_mid = direction - dir_high
-        both = jnp.dot(
-            op_high,
-            jnp.concatenate([dir_high, dir_mid], axis=1).astype(jnp.bfloat16),
-            preferred_element_type=jnp.float32,
-        )
-        local = (both[:, :cols] + both[:, cols:]) + jnp.dot(
-            op_mid, dir_high.astype(jnp.bfloat16), preferred_element_type=jnp.float32
-        )
+        dir_pair = jnp.concatenate([dir_high, direction - dir_high], axis=1).astype(jnp.bfloat16)
+        if step_id == 0:
+            local = bf16x3_apply(own_high, own_mid, dir_pair, cols)
+            moved = jnp.dot(to_rows, dir_pair, preferred_element_type=jnp.float32).astype(
+                jnp.bfloat16
+            )
+            spill_out = bf16x3_apply(spill_high, spill_mid, moved, cols)
+            out_high = lax.reduce_precision(spill_out, exponent_bits=8, mantissa_bits=7)
+            out_rest = spill_out - out_high
+            out_mid = lax.reduce_precision(out_rest, exponent_bits=8, mantissa_bits=7)
+            pieces = jnp.concatenate([out_high, out_mid, out_rest - out_mid], axis=1)
+            placed = jnp.dot(
+                spill_place, pieces.astype(jnp.bfloat16), preferred_element_type=jnp.float32
+            )
+            local = local + (
+                (placed[:, :cols] + placed[:, cols : 2 * cols]) + placed[:, 2 * cols :]
+            )
+        else:
+            local = bf16x3_apply(op_high, op_mid, dir_pair, cols)
         faces = [local[face_id * width : (face_id + 1) * width] for face_id in range(4)]
         residual = residual - face_sum_parts(faces)
         if step_id + 1 < ITERS:

time: 98.5 us -> 97.2 us (0.987)
  the two profiles are of different devices: /device:TPU:19 before, /device:TPU:0 now
where the time goes in v9:
time: 97.2 us; the launch traced here: 95.6 us
  starting transfers between devices  49.7 us (51%)
  matrix products  15.7 us (16%)
  waiting for transfers between devices  11.9 us (12%)
  other arithmetic  9.07 us (9%)
  local copies, waits for them, and re-layouts  5.14 us (5%)
  between operations  4.15 us (4%)
    ppermute x20, starting transfers between devices, face_sum_parts(): lax.ppermute(block, axis, pairs)  46.1 us
    ppermute x2, waiting for transfers between devices, from_behind(): return lax.ppermute(value, axis, pairs)  9.02 us
    dot_general x2, matrix products, slot_pieces(): jnp.dot(stacked, to_rows, preferred_element_type=jnp.float32)  5.06 us
    dot_general x2, matrix products, slot_pieces(): return jnp.dot(to_slots, side, preferred_element_type=jnp.float32)  3.87 us
    ppermute x2, starting transfers between devices, from_behind(): return lax.ppermute(value, axis, pairs)  3.6 us
    dot_general x5, matrix products, bf16x3_apply(): both = jnp.dot(op_high, pair, preferred_element_type=jnp.float32)  2.93 us
    ppermute x20, waiting for transfers between devices, face_sum_parts(): lax.ppermute(block, axis, pairs)  2.9 us
    dot_general x5, matrix products, bf16x3_apply(): jnp.dot(op_mid, pair[:, :cols], preferred_element_type=jnp.float32)  2.72 us
  transfers between devices with their start and end apart: 22, of which 5 were waited for; matrix products, arithmetic and copies ran while one was open for 20% of the time, Pallas kernels for 0%

profile of v9, /device:TPU:0, one launch (start us, length us, event | category | flops | bytes accessed | tf_op | source)
XLA Modules:
  0.0 95.6 jit_solution(9451532189458746368)
XLA Ops:
  0.7 2.0 %bitcast_select_fusion = (f32[224,128]{1,0:T(8,128)}, f32[224,128]{1,0:T(8,128)}, f32[224,128]{1,0:T(8,128)}, f32[224,128]{1,0:T(8,128)}) fusion(f32[1,1,896,128]{3,2,1,0:T(8,128)} %param.6, pred[]{:T(512)S(6)} %eq.101, pred[]{:T(512)S(6)} %eq.100), kind=kLoop, calls=%fused_computation.129 | loop fusion | flops 114688 | bytes 917506 | tf_op jit(solution)/shard_map/jit(_where)/select_n | solution.py:64
  2.7 0.7 collective-permute-start
  3.3 5.7 %collective-permute-start.1 = (f32[224,128]{1,0:T(8,128)}, f32[224,128]{1,0:T(8,128)}, u32[]{:S(2)}, u32[]{:S(2)}) collective-permute-start(f32[224,128]{1,0:T(8,128)} %get-tuple-element.118), channel_id=1, source_target_pairs={{0,1},{1,0},{2,3},{3,2},{4,5},{5,4},{6,7},{7,6},{8,9},{9,8},{10,11... | collective-permute-start | bytes 344072 | tf_op jit(solution)/shard_map/ppermute | solution.py:66
  9.1 2.1 %slice_bitcast_fusion = (f32[128,896]{1,0:T(8,128)}, f32[128,896]{1,0:T(8,128)}) fusion(f32[1,1,2,128,896]{4,3,2,1,0:T(8,128)} %param.8), kind=kLoop, calls=%fused_computation.105 | loop fusion | bytes 1835008 | tf_op jit(solution)/shard_map/squeeze | solution.py:118
  11.2 3.6 %collective-permute-start.4 = (f32[128,896]{1,0:T(8,128)}, f32[128,896]{1,0:T(8,128)}, u32[]{:S(2)}, u32[]{:S(2)}) collective-permute-start(f32[128,896]{1,0:T(8,128)} %get-tuple-element.69), channel_id=1, source_target_pairs={{0,24},{4,28},{8,0},{12,4},{16,8},{20,12},{24,16},{28,20},{1,25},{... | collective-permute-start | bytes 1376264 | tf_op jit(solution)/shard_map/ppermute | solution.py:22
  14.8 1.3 %reduce-precision_convert_fusion = (bf16[640,896]{1,0:T(8,128)(2,1)S(1)}, bf16[640,896]{1,0:T(8,128)(2,1)}) fusion(f32[1,1,640,896]{3,2,1,0:T(8,128)S(1)} %copy-done), kind=kLoop, calls=%fused_computation.2 | loop fusion | flops 2867200 | bytes 4587520 | tf_op jit(solution)/shard_map/convert.13
  16.2 0.7 reduce
  17.5 3.9 %convolution_convert_fusion = bf16[1280,896]{0,1:T(8,128)(2,1)S(1)} fusion(bf16[640,896]{1,0:T(8,128)(2,1)} %get-tuple-element.63, bf16[640,896]{1,0:T(8,128)(2,1)S(1)} %get-tuple-element.62, bf16[896]{0:T(1024)(128)(2,1)S(1)} %select_select_fusion, s32[896]{0:T(1024)S(1)} %reduce), kind=kOutput, calls=%fused_computation | convolution fusion | flops 2062548992 | bytes 4592896 | tf_op jit(solution)/shard_map/dot_general | solution.py:92
  21.6 2.7 %fusion.9 = f32[896,1792]{1,0:T(8,128)S(1)} fusion(bf16[640,896]{0,1:T(8,128)(2,1)S(1)} %get-tuple-element.61, bf16[640,896]{0,1:T(8,128)(2,1)S(1)} %get-tuple-element.60, bf16[896]{0:T(1024)(128)(2,1)S(1)} %select_select_fusion, s32[896]{0:T(1024)S(1)} %reduce), kind=kOutput, calls=%fused_computation.19 | convolution fusion | flops 2061516800 | bytes 8721664 | tf_op jit(solution)/shard_map/dot_general | solution.py:94
  24.4 0.6 fusion.103
  27.4 0.7 collective-permute-start.2
  28.1 2.4 %collective-permute-start.3 = (f32[224,128]{1,0:T(8,128)S(1)}, f32[224,128]{1,0:T(8,128)S(1)}, u32[]{:S(2)}, u32[]{:S(2)}) collective-permute-start(f32[224,128]{1,0:T(8,128)S(1)} %copy-done.2), channel_id=1, source_target_pairs={{0,4},{4,0},{8,12},{12,8},{16,20},{20,16},{24,28},{28,24},{1,5},{5... | collective-permute-start | bytes 344072 | tf_op jit(solution)/shard_map/ppermute | solution.py:69
  30.5 0.9 collective-permute-done.3
  31.5 1.0 %bitcast_add_fusion.3 = (f32[224,128]{1,0:T(8,128)S(1)}, f32[224,128]{1,0:T(8,128)S(1)}, f32[224,128]{1,0:T(8,128)S(1)}, f32[224,128]{1,0:T(8,128)S(1)}) fusion(f32[224,128]{1,0:T(8,128)S(1)} %collective-permute-done.2, f32[224,128]{1,0:T(8,128)S(1)} %collective-permute-done.3, f32[1,1,896,128]{3,2,1,0:T(8,128)S(1)} %copy-done.1, pred[]{:T(512)S(6)} %eq.100, ...), kind=kLoop, calls=%fused_computation.135 | loop fusion | flops 229376 | bytes 1376258 | tf_op jit(solution)/shard_map/add | solution.py:81
  32.5 0.6 fusion.25
  33.2 0.6 fusion.13
  33.8 1.0 %constant_dynamic-update-slice_fusion.1 = f32[256,896]{1,0:T(8,128)S(1)} fusion(f32[128,896]{1,0:T(8,128)} %collective-permute-done.4), kind=kLoop, calls=%fused_computation.181 | loop fusion | bytes 917504
  34.9 9.0 %collective-permute-done.5 = f32[128,896]{1,0:T(8,128)} collective-permute-done((f32[128,896]{1,0:T(8,128)}, f32[128,896]{1,0:T(8,128)}, u32[]{:S(2)}, u32[]{:S(2)}) %collective-permute-start.5) | collective-permute-done | bytes 458784 | tf_op jit(solution)/shard_map/ppermute | solution.py:22
  43.9 1.0 %constant_dynamic-update-slice_fusion = f32[256,896]{1,0:T(8,128)S(1)} fusion(f32[256,896]{1,0:T(8,128)S(1)} %constant_dynamic-update-slice_fusion.1, f32[128,896]{1,0:T(8,128)} %collective-permute-done.5), kind=kLoop, calls=%fused_computation.179 | loop fusion | bytes 917504 | tf_op jit(solution)/shard_map/concatenate | solution.py:144
  46.2 0.7 fusion.27
  46.9 0.7 collective-permute-start.6
  47.6 3.0 %collective-permute-start.7 = (f32[224,128]{1,0:T(8,128)S(1)}, f32[224,128]{1,0:T(8,128)S(1)}, u32[]{:S(2)}, u32[]{:S(2)}) collective-permute-start(f32[224,128]{1,0:T(8,128)S(1)} %get-tuple-element.111), channel_id=1, source_target_pairs={{0,1},{1,0},{2,3},{3,2},{4,5},{5,4},{6,7},{7,6},{8,9},{9,8},{10,11... | collective-permute-start | bytes 344072 | tf_op jit(solution)/shard_map/ppermute | solution.py:75
  50.7 0.8 collective-permute-start.8
  51.5 3.2 %collective-permute-start.9 = (f32[224,128]{1,0:T(8,128)S(1)}, f32[224,128]{1,0:T(8,128)S(1)}, u32[]{:S(2)}, u32[]{:S(2)}) collective-permute-start(f32[224,128]{1,0:T(8,128)S(1)} %get-tuple-element.110), channel_id=1, source_target_pairs={{0,4},{4,0},{8,12},{12,8},{16,20},{20,16},{24,28},{28,24},{1,5},{5... | collective-permute-start | bytes 344072 | tf_op jit(solution)/shard_map/ppermute | solution.py:75
  54.7 1.2 %fusion.24 = bf16[512,896]{1,0:T(8,128)(2,1)S(1)} fusion(bf16[896]{0:T(1024)(128)(2,1)S(1)} %select_select_fusion, s32[896]{0:T(1024)S(1)} %reduce, bf16[256,896]{1,0:T(8,128)(2,1)S(1)} %get-tuple-element.66, bf16[256,896]{1,0:T(8,128)(2,1)S(1)} %get-tuple-element.67), kind=kOutput, calls=%fused_computation.35 | convolution fusion | flops 825982976 | bytes 1840384 | tf_op jit(solution)/shard_map/dot_general | solution.py:92
  56.0 1.1 %fusion.35 = f32[896,1792]{1,0:T(8,128)S(1)} fusion(bf16[256,896]{1,0:T(8,128)(2,1)S(1)} %get-tuple-element.65, bf16[256,896]{1,0:T(8,128)(2,1)S(1)} %get-tuple-element.64, bf16[896]{0:T(1024)(128)(2,1)S(1)} %select_select_fusion, s32[256]{0:T(256)S(1)} %pad_add_fusion, s32[896]{0:T(1024)S(1)} %reduce), kind=kOutput, calls=%fused_computation.51 | convolution fusion | flops 824377344 | bytes 7346432 | tf_op jit(solution)/shard_map/dot_general | solution.py:94
  57.1 1.0 %fusion.1 = (bf16[896,896]{1,0:T(8,128)(2,1)S(1)}, bf16[896,896]{1,0:T(8,128)(2,1)S(1)}) fusion(f32[896,1792]{1,0:T(8,128)S(1)} %fusion.35, f32[896,1792]{1,0:T(8,128)S(1)} %fusion.9), kind=kLoop, calls=%fused_computation.6 | loop fusion | flops 3211264 | bytes 16056320 | tf_op jit(solution)/shard_map/convert_element_type | solution.py:148
  58.4 0.6 fusion.47
  59.0 0.6 convolution_add_fusion.2
  59.7 0.7 collective-permute-start.10
  60.3 2.8 %collective-permute-start.11 = (f32[224,128]{1,0:T(8,128)S(1)}, f32[224,128]{1,0:T(8,128)S(1)}, u32[]{:S(2)}, u32[]{:S(2)}) collective-permute-start(f32[224,128]{1,0:T(8,128)S(1)} %get-tuple-element.105), channel_id=1, source_target_pairs={{0,1},{1,0},{2,3},{3,2},{4,5},{5,4},{6,7},{7,6},{8,9},{9,8},{10,11... | collective-permute-start | bytes 344072 | tf_op jit(solution)/shard_map/ppermute | solution.py:75
  63.2 0.7 collective-permute-start.12
  63.8 7.6 %collective-permute-start.13 = (f32[224,128]{1,0:T(8,128)S(1)}, f32[224,128]{1,0:T(8,128)S(1)}, u32[]{:S(2)}, u32[]{:S(2)}) collective-permute-start(f32[224,128]{1,0:T(8,128)S(1)} %get-tuple-element.104), channel_id=1, source_target_pairs={{0,4},{4,0},{8,12},{12,8},{16,20},{20,16},{24,28},{28,24},{1,5},{5... | collective-permute-start | bytes 344072 | tf_op jit(solution)/shard_map/ppermute | solution.py:75
  71.4 1.0 collective-permute-done.13
  72.7 0.6 fusion.51
  73.3 0.6 convolution_add_fusion.1
  73.9 0.7 collective-permute-start.14
  74.6 2.8 %collective-permute-start.15 = (f32[224,128]{1,0:T(8,128)S(1)}, f32[224,128]{1,0:T(8,128)S(1)}, u32[]{:S(2)}, u32[]{:S(2)}) collective-permute-start(f32[224,128]{1,0:T(8,128)S(1)} %get-tuple-element.99), channel_id=1, source_target_pairs={{0,1},{1,0},{2,3},{3,2},{4,5},{5,4},{6,7},{7,6},{8,9},{9,8},{10,11... | collective-permute-start | bytes 344072 | tf_op jit(solution)/shard_map/ppermute | solution.py:75
  77.4 0.7 collective-permute-start.16
  78.0 4.5 %collective-permute-start.17 = (f32[224,128]{1,0:T(8,128)S(1)}, f32[224,128]{1,0:T(8,128)S(1)}, u32[]{:S(2)}, u32[]{:S(2)}) collective-permute-start(f32[224,128]{1,0:T(8,128)S(1)} %get-tuple-element.98), channel_id=1, source_target_pairs={{0,4},{4,0},{8,12},{12,8},{16,20},{20,16},{24,28},{28,24},{1,5},{5... | collective-permute-start | bytes 344072 | tf_op jit(solution)/shard_map/ppermute | solution.py:75
  82.5 0.8 collective-permute-done.15
  83.8 0.6 fusion.57
  85.0 0.7 collective-permute-start.18
  85.7 2.8 %collective-permute-start.19 = (f32[224,128]{1,0:T(8,128)S(1)}, f32[224,128]{1,0:T(8,128)S(1)}, u32[]{:S(2)}, u32[]{:S(2)}) collective-permute-start(f32[224,128]{1,0:T(8,128)S(1)} %get-tuple-element.93), channel_id=1, source_target_pairs={{0,1},{1,0},{2,3},{3,2},{4,5},{5,4},{6,7},{7,6},{8,9},{9,8},{10,11... | collective-permute-start | bytes 344072 | tf_op jit(solution)/shard_map/ppermute | solution.py:75
  88.5 0.7 collective-permute-start.20
  89.2 4.5 %collective-permute-start.21 = (f32[224,128]{1,0:T(8,128)S(1)}, f32[224,128]{1,0:T(8,128)S(1)}, u32[]{:S(2)}, u32[]{:S(2)}) collective-permute-start(f32[224,128]{1,0:T(8,128)S(1)} %get-tuple-element.92), channel_id=1, source_target_pairs={{0,4},{4,0},{8,12},{12,8},{16,20},{20,16},{24,28},{28,24},{1,5},{5... | collective-permute-start | bytes 344072 | tf_op jit(solution)/shard_map/ppermute | solution.py:75
  93.7 1.0 %add_add_fusion = f32[1,1,896,128]{3,2,1,0:T(8,128)} fusion(f32[1,1,224,128]{3,2,1,0:T(8,128)S(1)} %bitcast.67, f32[1,1,224,128]{3,2,1,0:T(8,128)S(1)} %bitcast.69, f32[1,1,224,128]{3,2,1,0:T(8,128)S(1)} %bitcast.65, f32[1,1,224,128]{3,2,1,0:T(8,128)S(1)} %bitcast.63, f32[1,1,224,128]{3,2,1,0:T(8,128)S(1)} %bitcast.75, f32[1,1,224,128]{3,2,1,0:T(8,128)S(1)} %bitcast.77, ...), kind=kLoop, calls=%fused_computation.102 | loop fusion | flops 3211264 | bytes 2293760 | tf_op jit(solution)/shard_map/add | solution.py:161
  94.8 0.9 maximum_subtract_fusion.6
  (55 shorter events, 3.3 us)
Async XLA Ops:
  0.6 14.2 %copy-start = (f32[1,1,640,896]{3,2,1,0:T(8,128)S(1)}, f32[1,1,640,896]{3,2,1,0:T(8,128)}, u32[]{:S(2)}) copy-start(f32[1,1,640,896]{3,2,1,0:T(8,128)} %param.7) | copy-start | bytes 6881284
  2.7 24.7 %collective-permute-start = (f32[224,128]{1,0:T(8,128)}, f32[224,128]{1,0:T(8,128)S(1)}, u32[]{:S(2)}, u32[]{:S(2)}) collective-permute-start(f32[224,128]{1,0:T(8,128)} %get-tuple-element.121), channel_id=1, source_target_pairs={{1,2},{2,1},{5,6},{6,5},{9,10},{10,9},{13,14},{14,13},{17,18},{18,... | collective-permute-start | bytes 344072 | tf_op jit(solution)/shard_map/ppermute | solution.py:66
  3.3 24.0 %collective-permute-start.1 = (f32[224,128]{1,0:T(8,128)}, f32[224,128]{1,0:T(8,128)}, u32[]{:S(2)}, u32[]{:S(2)}) collective-permute-start(f32[224,128]{1,0:T(8,128)} %get-tuple-element.118), channel_id=1, source_target_pairs={{0,1},{1,0},{2,3},{3,2},{4,5},{5,4},{6,7},{7,6},{8,9},{9,8},{10,11... | collective-permute-start | bytes 344072 | tf_op jit(solution)/shard_map/ppermute | solution.py:66
  11.2 22.6 %collective-permute-start.4 = (f32[128,896]{1,0:T(8,128)}, f32[128,896]{1,0:T(8,128)}, u32[]{:S(2)}, u32[]{:S(2)}) collective-permute-start(f32[128,896]{1,0:T(8,128)} %get-tuple-element.69), channel_id=1, source_target_pairs={{0,24},{4,28},{8,0},{12,4},{16,8},{20,12},{24,16},{28,20},{1,25},{... | collective-permute-start | bytes 1376264 | tf_op jit(solution)/shard_map/ppermute | solution.py:22
  14.8 29.1 %collective-permute-start.5 = (f32[128,896]{1,0:T(8,128)}, f32[128,896]{1,0:T(8,128)}, u32[]{:S(2)}, u32[]{:S(2)}) collective-permute-start(f32[128,896]{1,0:T(8,128)} %get-tuple-element.68), channel_id=1, source_target_pairs={{0,16},{4,20},{8,24},{12,28},{16,0},{20,4},{24,8},{28,12},{1,17},{... | collective-permute-start | bytes 1376264 | tf_op jit(solution)/shard_map/ppermute | solution.py:22
  21.6 2.8 %copy-start.4 = (s32[1,1,2]{2,1,0:T(1,128)S(1)}, s32[1,1,2]{2,1,0:T(1,128)}, u32[]{:S(2)}) copy-start(s32[1,1,2]{2,1,0:T(1,128)} %param.9) | copy-start | bytes 28
  21.6 5.8 %copy-start.3 = (f32[224,128]{1,0:T(8,128)S(1)}, f32[224,128]{1,0:T(8,128)}, u32[]{:S(2)}) copy-start(f32[224,128]{1,0:T(8,128)} %get-tuple-element.28) | copy-start | bytes 344068
  21.6 6.4 %copy-start.2 = (f32[224,128]{1,0:T(8,128)S(1)}, f32[224,128]{1,0:T(8,128)}, u32[]{:S(2)}) copy-start(f32[224,128]{1,0:T(8,128)} %get-tuple-element.29) | copy-start | bytes 344068
  21.6 9.8 %copy-start.1 = (f32[1,1,896,128]{3,2,1,0:T(8,128)S(1)}, f32[1,1,896,128]{3,2,1,0:T(8,128)}, u32[]{:S(2)}) copy-start(f32[1,1,896,128]{3,2,1,0:T(8,128)} %param.6) | copy-start | bytes 1376260
  27.4 3.1 %collective-permute-start.2 = (f32[224,128]{1,0:T(8,128)S(1)}, f32[224,128]{1,0:T(8,128)S(1)}, u32[]{:S(2)}, u32[]{:S(2)}) collective-permute-start(f32[224,128]{1,0:T(8,128)S(1)} %copy-done.3), channel_id=1, source_target_pairs={{4,8},{8,4},{12,16},{16,12},{20,24},{24,20},{5,9},{9,5},{13,17},{1... | collective-permute-start | bytes 344072 | tf_op jit(solution)/shard_map/ppermute | solution.py:69
  28.1 3.4 %collective-permute-start.3 = (f32[224,128]{1,0:T(8,128)S(1)}, f32[224,128]{1,0:T(8,128)S(1)}, u32[]{:S(2)}, u32[]{:S(2)}) collective-permute-start(f32[224,128]{1,0:T(8,128)S(1)} %copy-done.2), channel_id=1, source_target_pairs={{0,4},{4,0},{8,12},{12,8},{16,20},{20,16},{24,28},{28,24},{1,5},{5... | collective-permute-start | bytes 344072 | tf_op jit(solution)/shard_map/ppermute | solution.py:69
  46.9 11.2 %collective-permute-start.6 = (f32[224,128]{1,0:T(8,128)S(1)}, f32[224,128]{1,0:T(8,128)S(1)}, u32[]{:S(2)}, u32[]{:S(2)}) collective-permute-start(f32[224,128]{1,0:T(8,128)S(1)} %get-tuple-element.113), channel_id=1, source_target_pairs={{1,2},{2,1},{5,6},{6,5},{9,10},{10,9},{13,14},{14,13},{17,18},{18,... | collective-permute-start | bytes 344072 | tf_op jit(solution)/shard_map/ppermute | solution.py:75
  47.6 10.5 %collective-permute-start.7 = (f32[224,128]{1,0:T(8,128)S(1)}, f32[224,128]{1,0:T(8,128)S(1)}, u32[]{:S(2)}, u32[]{:S(2)}) collective-permute-start(f32[224,128]{1,0:T(8,128)S(1)} %get-tuple-element.111), channel_id=1, source_target_pairs={{0,1},{1,0},{2,3},{3,2},{4,5},{5,4},{6,7},{7,6},{8,9},{9,8},{10,11... | collective-permute-start | bytes 344072 | tf_op jit(solution)/shard_map/ppermute | solution.py:75
  50.7 7.5 %collective-permute-start.8 = (f32[224,128]{1,0:T(8,128)S(1)}, f32[224,128]{1,0:T(8,128)S(1)}, u32[]{:S(2)}, u32[]{:S(2)}) collective-permute-start(f32[224,128]{1,0:T(8,128)S(1)} %get-tuple-element.112), channel_id=1, source_target_pairs={{4,8},{8,4},{12,16},{16,12},{20,24},{24,20},{5,9},{9,5},{13,17},{1... | collective-permute-start | bytes 344072 | tf_op jit(solution)/shard_map/ppermute | solution.py:75
  51.5 6.7 %collective-permute-start.9 = (f32[224,128]{1,0:T(8,128)S(1)}, f32[224,128]{1,0:T(8,128)S(1)}, u32[]{:S(2)}, u32[]{:S(2)}) collective-permute-start(f32[224,128]{1,0:T(8,128)S(1)} %get-tuple-element.110), channel_id=1, source_target_pairs={{0,4},{4,0},{8,12},{12,8},{16,20},{20,16},{24,28},{28,24},{1,5},{5... | collective-permute-start | bytes 344072 | tf_op jit(solution)/shard_map/ppermute | solution.py:75
  59.7 11.7 %collective-permute-start.10 = (f32[224,128]{1,0:T(8,128)S(1)}, f32[224,128]{1,0:T(8,128)S(1)}, u32[]{:S(2)}, u32[]{:S(2)}) collective-permute-start(f32[224,128]{1,0:T(8,128)S(1)} %get-tuple-element.107), channel_id=1, source_target_pairs={{1,2},{2,1},{5,6},{6,5},{9,10},{10,9},{13,14},{14,13},{17,18},{18,... | collective-permute-start | bytes 344072 | tf_op jit(solution)/shard_map/ppermute | solution.py:75
  60.3 11.1 %collective-permute-start.11 = (f32[224,128]{1,0:T(8,128)S(1)}, f32[224,128]{1,0:T(8,128)S(1)}, u32[]{:S(2)}, u32[]{:S(2)}) collective-permute-start(f32[224,128]{1,0:T(8,128)S(1)} %get-tuple-element.105), channel_id=1, source_target_pairs={{0,1},{1,0},{2,3},{3,2},{4,5},{5,4},{6,7},{7,6},{8,9},{9,8},{10,11... | collective-permute-start | bytes 344072 | tf_op jit(solution)/shard_map/ppermute | solution.py:75
  63.2 8.2 %collective-permute-start.12 = (f32[224,128]{1,0:T(8,128)S(1)}, f32[224,128]{1,0:T(8,128)S(1)}, u32[]{:S(2)}, u32[]{:S(2)}) collective-permute-start(f32[224,128]{1,0:T(8,128)S(1)} %get-tuple-element.106), channel_id=1, source_target_pairs={{4,8},{8,4},{12,16},{16,12},{20,24},{24,20},{5,9},{9,5},{13,17},{1... | collective-permute-start | bytes 344072 | tf_op jit(solution)/shard_map/ppermute | solution.py:75
  63.8 8.5 %collective-permute-start.13 = (f32[224,128]{1,0:T(8,128)S(1)}, f32[224,128]{1,0:T(8,128)S(1)}, u32[]{:S(2)}, u32[]{:S(2)}) collective-permute-start(f32[224,128]{1,0:T(8,128)S(1)} %get-tuple-element.104), channel_id=1, source_target_pairs={{0,4},{4,0},{8,12},{12,8},{16,20},{20,16},{24,28},{28,24},{1,5},{5... | collective-permute-start | bytes 344072 | tf_op jit(solution)/shard_map/ppermute | solution.py:75
  73.9 8.6 %collective-permute-start.14 = (f32[224,128]{1,0:T(8,128)S(1)}, f32[224,128]{1,0:T(8,128)S(1)}, u32[]{:S(2)}, u32[]{:S(2)}) collective-permute-start(f32[224,128]{1,0:T(8,128)S(1)} %get-tuple-element.101), channel_id=1, source_target_pairs={{1,2},{2,1},{5,6},{6,5},{9,10},{10,9},{13,14},{14,13},{17,18},{18,... | collective-permute-start | bytes 344072 | tf_op jit(solution)/shard_map/ppermute | solution.py:75
  74.6 8.7 %collective-permute-start.15 = (f32[224,128]{1,0:T(8,128)S(1)}, f32[224,128]{1,0:T(8,128)S(1)}, u32[]{:S(2)}, u32[]{:S(2)}) collective-permute-start(f32[224,128]{1,0:T(8,128)S(1)} %get-tuple-element.99), channel_id=1, source_target_pairs={{0,1},{1,0},{2,3},{3,2},{4,5},{5,4},{6,7},{7,6},{8,9},{9,8},{10,11... | collective-permute-start | bytes 344072 | tf_op jit(solution)/shard_map/ppermute | solution.py:75
  77.4 6.0 %collective-permute-start.16 = (f32[224,128]{1,0:T(8,128)S(1)}, f32[224,128]{1,0:T(8,128)S(1)}, u32[]{:S(2)}, u32[]{:S(2)}) collective-permute-start(f32[224,128]{1,0:T(8,128)S(1)} %get-tuple-element.100), channel_id=1, source_target_pairs={{4,8},{8,4},{12,16},{16,12},{20,24},{24,20},{5,9},{9,5},{13,17},{1... | collective-permute-start | bytes 344072 | tf_op jit(solution)/shard_map/ppermute | solution.py:75
  78.0 5.4 %collective-permute-start.17 = (f32[224,128]{1,0:T(8,128)S(1)}, f32[224,128]{1,0:T(8,128)S(1)}, u32[]{:S(2)}, u32[]{:S(2)}) collective-permute-start(f32[224,128]{1,0:T(8,128)S(1)} %get-tuple-element.98), channel_id=1, source_target_pairs={{0,4},{4,0},{8,12},{12,8},{16,20},{20,16},{24,28},{28,24},{1,5},{5... | collective-permute-start | bytes 344072 | tf_op jit(solution)/shard_map/ppermute | solution.py:75
  85.0 9.7 %collective-permute-start.18 = (f32[224,128]{1,0:T(8,128)S(1)}, f32[224,128]{1,0:T(8,128)S(1)}, u32[]{:S(2)}, u32[]{:S(2)}) collective-permute-start(f32[224,128]{1,0:T(8,128)S(1)} %get-tuple-element.95), channel_id=1, source_target_pairs={{1,2},{2,1},{5,6},{6,5},{9,10},{10,9},{13,14},{14,13},{17,18},{18,... | collective-permute-start | bytes 344072 | tf_op jit(solution)/shard_map/ppermute | solution.py:75
  85.7 9.0 %collective-permute-start.19 = (f32[224,128]{1,0:T(8,128)S(1)}, f32[224,128]{1,0:T(8,128)S(1)}, u32[]{:S(2)}, u32[]{:S(2)}) collective-permute-start(f32[224,128]{1,0:T(8,128)S(1)} %get-tuple-element.93), channel_id=1, source_target_pairs={{0,1},{1,0},{2,3},{3,2},{4,5},{5,4},{6,7},{7,6},{8,9},{9,8},{10,11... | collective-permute-start | bytes 344072 | tf_op jit(solution)/shard_map/ppermute | solution.py:75
  88.5 6.2 %collective-permute-start.20 = (f32[224,128]{1,0:T(8,128)S(1)}, f32[224,128]{1,0:T(8,128)S(1)}, u32[]{:S(2)}, u32[]{:S(2)}) collective-permute-start(f32[224,128]{1,0:T(8,128)S(1)} %get-tuple-element.94), channel_id=1, source_target_pairs={{4,8},{8,4},{12,16},{16,12},{20,24},{24,20},{5,9},{9,5},{13,17},{1... | collective-permute-start | bytes 344072 | tf_op jit(solution)/shard_map/ppermute | solution.py:75
  89.2 5.5 %collective-permute-start.21 = (f32[224,128]{1,0:T(8,128)S(1)}, f32[224,128]{1,0:T(8,128)S(1)}, u32[]{:S(2)}, u32[]{:S(2)}) collective-permute-start(f32[224,128]{1,0:T(8,128)S(1)} %get-tuple-element.92), channel_id=1, source_target_pairs={{0,4},{4,0},{8,12},{12,8},{16,20},{20,16},{24,28},{28,24},{1,5},{5... | collective-permute-start | bytes 344072 | tf_op jit(solution)/shard_map/ppermute | solution.py:75

commit v10 on v9

--- a/solution.py
+++ b/solution.py
@@ -63,13 +63,13 @@
         sends.append((jnp.where(even, low, high), swap_pairs(lax.axis_size(axis), 1), axis))
         sends.append((jnp.where(even, high, low), swap_pairs(lax.axis_size(axis), 0), axis))
     if one_axis_at_a_time:
-        first = [lax.ppermute(block, axis, pairs) for block, pairs, axis in sends[:2]]
-        later, first = lax.optimization_barrier(([block for block, _, _ in sends[2:]], first))
+        first = [lax.ppermute(block, axis, pairs) for block, pairs, axis in sends[2:]]
+        later, first = lax.optimization_barrier(([block for block, _, _ in sends[:2]], first))
         second = [
             lax.ppermute(block, axis, pairs)
-            for block, (_, pairs, axis) in zip(later, sends[2:])
+            for block, (_, pairs, axis) in zip(later, sends[:2])
         ]
-        received = lax.optimization_barrier(first + second)
+        received = lax.optimization_barrier(second + first)
     else:
         received = lax.optimization_barrier(
             [lax.ppermute(block, axis, pairs) for block, pairs, axis in sends]
@@ -114,14 +114,16 @@
     row_ids = jnp.arange(order_max, dtype=jnp.int32)
     face_sign = jnp.where(row_ids // (order_max // 4) % 2 == 0, -1.0, 1.0).astype(jnp.float32)
     slot_scale = face_sign * (slot_map < order_now).astype(jnp.float32)
+    spill_parts = [spill_block[slot_id] for slot_id in range(2)]
+    gap_faces, spill_parts = lax.optimization_barrier((gap[0, 0], spill_parts))
     homed = [
-        from_behind(spill_block[slot_id], "gx", -(slot_id + 1) * hop_span) for slot_id in range(2)
+        from_behind(spill_parts[slot_id], "gx", -(slot_id + 1) * hop_span) for slot_id in range(2)
     ]
     own_count = own_block.shape[0]
     cols = gap.shape[3]
     width = order_max // 4
     load = face_sum_parts(
-        [gap[0, 0, face_id * width : (face_id + 1) * width] for face_id in range(4)],
+        [gap_faces[face_id * width : (face_id + 1) * width] for face_id in range(4)],
         one_axis_at_a_time=True,
     )
     to_slots = jnp.where(

time: 97.2 us -> 90.4 us (0.930)
  starting transfers between devices: 49.7 us -> 41.1 us
  waiting for transfers between devices: 11.9 us -> 15.5 us
  other arithmetic: 9.07 us -> 7.28 us
    ppermute x20, starting transfers between devices: 46.1 us -> 38 us  [face_sum_parts(): lax.ppermute(block, axis, pairs)]
    ppermute x20, waiting for transfers between devices: 2.9 us -> 10.7 us  [face_sum_parts(): lax.ppermute(block, axis, pairs)]
    ppermute x2, waiting for transfers between devices: 9.02 us -> 4.81 us  [from_behind(): return lax.ppermute(value, axis, pairs)]
    select_n x5, other arithmetic: 2.15 us -> 0.87 us  [face_sum_parts(): jnp.where(even, high, low)]
  transfers between devices with their start and end apart: 22 -> 22, of which waited for: 5 -> 5; matrix products, arithmetic and copies ran while one was open for 20% -> 19% of each run, Pallas kernels for 0% -> 0%
where the time goes in v10:
time: 90.4 us; the launch traced here: 89.1 us
  starting transfers between devices  41.1 us (45%)
  matrix products  16 us (18%)
  waiting for transfers between devices  15.5 us (17%)
  other arithmetic  7.28 us (8%)
  local copies, waits for them, and re-layouts  5.11 us (6%)
  between operations  4.1 us (5%)
    ppermute x20, starting transfers between devices, face_sum_parts(): lax.ppermute(block, axis, pairs)  38 us
    ppermute x20, waiting for transfers between devices, face_sum_parts(): lax.ppermute(block, axis, pairs)  10.7 us
    dot_general x2, matrix products, slot_pieces(): jnp.dot(stacked, to_rows, preferred_element_type=jnp.float32)  5.4 us
    ppermute x2, waiting for transfers between devices, from_behind(): return lax.ppermute(value, axis, pairs)  4.81 us
    dot_general x2, matrix products, slot_pieces(): return jnp.dot(to_slots, side, preferred_element_type=jnp.float32)  3.87 us
    ppermute x2, starting transfers between devices, from_behind(): return lax.ppermute(value, axis, pairs)  3.04 us
    dot_general x5, matrix products, bf16x3_apply(): both = jnp.dot(op_high, pair, preferred_element_type=jnp.float32)  2.93 us
    dot_general x5, matrix products, bf16x3_apply(): jnp.dot(op_mid, pair[:, :cols], preferred_element_type=jnp.float32)  2.65 us
  transfers between devices with their start and end apart: 22, of which 5 were waited for; matrix products, arithmetic and copies ran while one was open for 19% of the time, Pallas kernels for 0%

profile of v10, /device:TPU:0, one launch (start us, length us, event | category | flops | bytes accessed | tf_op | source)
XLA Modules:
  0.0 89.1 jit_solution(4824968307997902245)
XLA Ops:
  0.7 2.1 %slice_bitcast_fusion = (f32[128,896]{1,0:T(8,128)S(1)}, f32[128,896]{1,0:T(8,128)}) fusion(f32[1,1,2,128,896]{4,3,2,1,0:T(8,128)} %param.8), kind=kLoop, calls=%fused_computation.111 | loop fusion | bytes 1835008 | tf_op jit(solution)/shard_map/squeeze | solution.py:117
  2.8 0.7 slice_select_fusion.16
  3.5 0.7 collective-permute-start
  4.2 4.4 %collective-permute-start.1 = (f32[224,128]{1,0:T(8,128)}, f32[224,128]{1,0:T(8,128)S(1)}, u32[]{:S(2)}, u32[]{:S(2)}) collective-permute-start(f32[224,128]{1,0:T(8,128)} %get-tuple-element.124), channel_id=1, source_target_pairs={{0,4},{4,0},{8,12},{12,8},{16,20},{20,16},{24,28},{28,24},{1,5},{5... | collective-permute-start | bytes 344072 | tf_op jit(solution)/shard_map/ppermute | solution.py:66
  8.6 2.0 %collective-permute-start.4 = (f32[128,896]{1,0:T(8,128)}, f32[128,896]{1,0:T(8,128)}, u32[]{:S(2)}, u32[]{:S(2)}) collective-permute-start(f32[128,896]{1,0:T(8,128)} %get-tuple-element.38), channel_id=1, source_target_pairs={{0,24},{4,28},{8,0},{12,4},{16,8},{20,12},{24,16},{28,20},{1,25},{... | collective-permute-start | bytes 1376264 | tf_op jit(solution)/shard_map/ppermute | solution.py:22
  10.6 1.1 %collective-permute-start.5 = (f32[128,896]{1,0:T(8,128)S(1)}, f32[128,896]{1,0:T(8,128)}, u32[]{:S(2)}, u32[]{:S(2)}) collective-permute-start(f32[128,896]{1,0:T(8,128)S(1)} %get-tuple-element.39), channel_id=1, source_target_pairs={{0,16},{4,20},{8,24},{12,28},{16,0},{20,4},{24,8},{28,12},{1,17},{... | collective-permute-start | bytes 1376264 | tf_op jit(solution)/shard_map/ppermute | solution.py:22
  11.7 1.7 %reduce-precision_convert_fusion = (bf16[640,896]{1,0:T(8,128)(2,1)}, bf16[640,896]{1,0:T(8,128)(2,1)}) fusion(f32[1,1,640,896]{3,2,1,0:T(8,128)S(1)} %copy-done), kind=kLoop, calls=%fused_computation.2 | loop fusion | flops 2867200 | bytes 4587520 | tf_op jit(solution)/shard_map/convert.13
  13.4 0.7 reduce
  14.8 4.2 %convolution_convert_fusion = bf16[1280,896]{0,1:T(8,128)(2,1)S(1)} fusion(bf16[640,896]{1,0:T(8,128)(2,1)} %get-tuple-element.69, bf16[640,896]{1,0:T(8,128)(2,1)} %get-tuple-element.68, bf16[896]{0:T(1024)(128)(2,1)S(1)} %select_select_fusion, s32[896]{0:T(1024)S(1)} %reduce), kind=kOutput, calls=%fused_computation | convolution fusion | flops 2062548992 | bytes 4592896 | tf_op jit(solution)/shard_map/dot_general | solution.py:92
  19.2 2.7 %fusion.9 = f32[896,1792]{1,0:T(8,128)S(1)} fusion(bf16[640,896]{0,1:T(8,128)(2,1)S(1)} %get-tuple-element.67, bf16[640,896]{0,1:T(8,128)(2,1)S(1)} %get-tuple-element.66, bf16[896]{0:T(1024)(128)(2,1)S(1)} %select_select_fusion, s32[896]{0:T(1024)S(1)} %reduce), kind=kOutput, calls=%fused_computation.19 | convolution fusion | flops 2061516800 | bytes 8721664 | tf_op jit(solution)/shard_map/dot_general | solution.py:94
  24.9 0.7 collective-permute-start.2
  25.6 4.3 %collective-permute-start.3 = (f32[224,128]{1,0:T(8,128)S(1)}, f32[224,128]{1,0:T(8,128)S(1)}, u32[]{:S(2)}, u32[]{:S(2)}) collective-permute-start(f32[224,128]{1,0:T(8,128)S(1)} %get-tuple-element.31), channel_id=1, source_target_pairs={{0,1},{1,0},{2,3},{3,2},{4,5},{5,4},{6,7},{7,6},{8,9},{9,8},{10,11... | collective-permute-start | bytes 344072 | tf_op jit(solution)/shard_map/ppermute | solution.py:69
  29.9 4.9 %collective-permute-done.3 = f32[224,128]{1,0:T(8,128)S(1)} collective-permute-done((f32[224,128]{1,0:T(8,128)S(1)}, f32[224,128]{1,0:T(8,128)S(1)}, u32[]{:S(2)}, u32[]{:S(2)}) %collective-permute-start.3) | collective-permute-done | bytes 114720 | tf_op jit(solution)/shard_map/ppermute | solution.py:69
  35.0 0.6 fusion.25
  35.6 0.6 fusion.13
  36.3 1.0 %constant_dynamic-update-slice_fusion.1 = f32[256,896]{1,0:T(8,128)S(1)} fusion(f32[128,896]{1,0:T(8,128)} %collective-permute-done.4), kind=kLoop, calls=%fused_computation.181 | loop fusion | bytes 917504
  37.3 4.8 %collective-permute-done.5 = f32[128,896]{1,0:T(8,128)} collective-permute-done((f32[128,896]{1,0:T(8,128)S(1)}, f32[128,896]{1,0:T(8,128)}, u32[]{:S(2)}, u32[]{:S(2)}) %collective-permute-start.5) | collective-permute-done | bytes 458784 | tf_op jit(solution)/shard_map/ppermute | solution.py:22
  42.1 1.0 %constant_dynamic-update-slice_fusion = f32[256,896]{1,0:T(8,128)S(1)} fusion(f32[256,896]{1,0:T(8,128)S(1)} %constant_dynamic-update-slice_fusion.1, f32[128,896]{1,0:T(8,128)} %collective-permute-done.5), kind=kLoop, calls=%fused_computation.179 | loop fusion | bytes 917504 | tf_op jit(solution)/shard_map/concatenate | solution.py:146
  44.4 0.6 fusion.27
  45.1 0.7 collective-permute-start.6
  45.8 4.3 %collective-permute-start.7 = (f32[224,128]{1,0:T(8,128)S(1)}, f32[224,128]{1,0:T(8,128)S(1)}, u32[]{:S(2)}, u32[]{:S(2)}) collective-permute-start(f32[224,128]{1,0:T(8,128)S(1)} %get-tuple-element.117), channel_id=1, source_target_pairs={{0,1},{1,0},{2,3},{3,2},{4,5},{5,4},{6,7},{7,6},{8,9},{9,8},{10,11... | collective-permute-start | bytes 344072 | tf_op jit(solution)/shard_map/ppermute | solution.py:75
  50.0 0.8 collective-permute-start.8
  50.9 1.7 %collective-permute-start.9 = (f32[224,128]{1,0:T(8,128)S(1)}, f32[224,128]{1,0:T(8,128)S(1)}, u32[]{:S(2)}, u32[]{:S(2)}) collective-permute-start(f32[224,128]{1,0:T(8,128)S(1)} %get-tuple-element.116), channel_id=1, source_target_pairs={{0,4},{4,0},{8,12},{12,8},{16,20},{20,16},{24,28},{28,24},{1,5},{5... | collective-permute-start | bytes 344072 | tf_op jit(solution)/shard_map/ppermute | solution.py:75
  52.5 1.2 %fusion.24 = bf16[512,896]{1,0:T(8,128)(2,1)S(1)} fusion(bf16[896]{0:T(1024)(128)(2,1)S(1)} %select_select_fusion, s32[896]{0:T(1024)S(1)} %reduce, bf16[256,896]{1,0:T(8,128)(2,1)S(1)} %get-tuple-element.72, bf16[256,896]{1,0:T(8,128)(2,1)S(1)} %get-tuple-element.73), kind=kOutput, calls=%fused_computation.35 | convolution fusion | flops 825982976 | bytes 1840384 | tf_op jit(solution)/shard_map/dot_general | solution.py:92
  53.8 1.1 %fusion.35 = f32[896,1792]{1,0:T(8,128)S(1)} fusion(bf16[256,896]{1,0:T(8,128)(2,1)S(1)} %get-tuple-element.71, bf16[256,896]{1,0:T(8,128)(2,1)S(1)} %get-tuple-element.70, bf16[896]{0:T(1024)(128)(2,1)S(1)} %select_select_fusion, s32[256]{0:T(256)S(1)} %pad_add_fusion, s32[896]{0:T(1024)S(1)} %reduce), kind=kOutput, calls=%fused_computation.51 | convolution fusion | flops 824377344 | bytes 7346432 | tf_op jit(solution)/shard_map/dot_general | solution.py:94
  55.0 1.0 %fusion.1 = (bf16[896,896]{1,0:T(8,128)(2,1)S(1)}, bf16[896,896]{1,0:T(8,128)(2,1)S(1)}) fusion(f32[896,1792]{1,0:T(8,128)S(1)} %fusion.35, f32[896,1792]{1,0:T(8,128)S(1)} %fusion.9), kind=kLoop, calls=%fused_computation.6 | loop fusion | flops 3211264 | bytes 16056320 | tf_op jit(solution)/shard_map/convert_element_type | solution.py:150
  56.3 0.6 fusion.47
  56.9 0.6 convolution_add_fusion.2
  57.6 0.7 collective-permute-start.10
  58.2 2.8 %collective-permute-start.11 = (f32[224,128]{1,0:T(8,128)S(1)}, f32[224,128]{1,0:T(8,128)S(1)}, u32[]{:S(2)}, u32[]{:S(2)}) collective-permute-start(f32[224,128]{1,0:T(8,128)S(1)} %get-tuple-element.111), channel_id=1, source_target_pairs={{0,1},{1,0},{2,3},{3,2},{4,5},{5,4},{6,7},{7,6},{8,9},{9,8},{10,11... | collective-permute-start | bytes 344072 | tf_op jit(solution)/shard_map/ppermute | solution.py:75
  61.0 0.7 collective-permute-start.12
  61.7 1.7 %collective-permute-start.13 = (f32[224,128]{1,0:T(8,128)S(1)}, f32[224,128]{1,0:T(8,128)S(1)}, u32[]{:S(2)}, u32[]{:S(2)}) collective-permute-start(f32[224,128]{1,0:T(8,128)S(1)} %get-tuple-element.110), channel_id=1, source_target_pairs={{0,4},{4,0},{8,12},{12,8},{16,20},{20,16},{24,28},{28,24},{1,5},{5... | collective-permute-start | bytes 344072 | tf_op jit(solution)/shard_map/ppermute | solution.py:75
  63.4 3.0 %collective-permute-done.11 = f32[224,128]{1,0:T(8,128)S(1)} collective-permute-done((f32[224,128]{1,0:T(8,128)S(1)}, f32[224,128]{1,0:T(8,128)S(1)}, u32[]{:S(2)}, u32[]{:S(2)}) %collective-permute-start.11) | collective-permute-done | bytes 114720 | tf_op jit(solution)/shard_map/ppermute | solution.py:75
  66.7 0.6 fusion.51
  67.4 0.6 convolution_add_fusion.1
  68.0 0.7 collective-permute-start.14
  68.7 2.7 %collective-permute-start.15 = (f32[224,128]{1,0:T(8,128)S(1)}, f32[224,128]{1,0:T(8,128)S(1)}, u32[]{:S(2)}, u32[]{:S(2)}) collective-permute-start(f32[224,128]{1,0:T(8,128)S(1)} %get-tuple-element.105), channel_id=1, source_target_pairs={{0,1},{1,0},{2,3},{3,2},{4,5},{5,4},{6,7},{7,6},{8,9},{9,8},{10,11... | collective-permute-start | bytes 344072 | tf_op jit(solution)/shard_map/ppermute | solution.py:75
  71.4 0.7 collective-permute-start.16
  72.1 3.2 %collective-permute-start.17 = (f32[224,128]{1,0:T(8,128)S(1)}, f32[224,128]{1,0:T(8,128)S(1)}, u32[]{:S(2)}, u32[]{:S(2)}) collective-permute-start(f32[224,128]{1,0:T(8,128)S(1)} %get-tuple-element.104), channel_id=1, source_target_pairs={{0,4},{4,0},{8,12},{12,8},{16,20},{20,16},{24,28},{28,24},{1,5},{5... | collective-permute-start | bytes 344072 | tf_op jit(solution)/shard_map/ppermute | solution.py:75
  75.3 2.0 %collective-permute-done.15 = f32[224,128]{1,0:T(8,128)S(1)} collective-permute-done((f32[224,128]{1,0:T(8,128)S(1)}, f32[224,128]{1,0:T(8,128)S(1)}, u32[]{:S(2)}, u32[]{:S(2)}) %collective-permute-start.15) | collective-permute-done | bytes 114720 | tf_op jit(solution)/shard_map/ppermute | solution.py:75
  77.6 0.6 fusion.57
  78.9 0.7 collective-permute-start.18
  79.5 2.3 %collective-permute-start.19 = (f32[224,128]{1,0:T(8,128)S(1)}, f32[224,128]{1,0:T(8,128)S(1)}, u32[]{:S(2)}, u32[]{:S(2)}) collective-permute-start(f32[224,128]{1,0:T(8,128)S(1)} %get-tuple-element.99), channel_id=1, source_target_pairs={{0,1},{1,0},{2,3},{3,2},{4,5},{5,4},{6,7},{7,6},{8,9},{9,8},{10,11... | collective-permute-start | bytes 344072 | tf_op jit(solution)/shard_map/ppermute | solution.py:75
  81.8 0.7 collective-permute-start.20
  82.5 3.9 %collective-permute-start.21 = (f32[224,128]{1,0:T(8,128)S(1)}, f32[224,128]{1,0:T(8,128)S(1)}, u32[]{:S(2)}, u32[]{:S(2)}) collective-permute-start(f32[224,128]{1,0:T(8,128)S(1)} %get-tuple-element.98), channel_id=1, source_target_pairs={{0,4},{4,0},{8,12},{12,8},{16,20},{20,16},{24,28},{28,24},{1,5},{5... | collective-permute-start | bytes 344072 | tf_op jit(solution)/shard_map/ppermute | solution.py:75
  86.4 1.0 %add_add_fusion = f32[1,1,896,128]{3,2,1,0:T(8,128)} fusion(f32[1,1,224,128]{3,2,1,0:T(8,128)S(1)} %bitcast.52, f32[1,1,224,128]{3,2,1,0:T(8,128)S(1)} %bitcast.54, f32[1,1,224,128]{3,2,1,0:T(8,128)S(1)} %bitcast.50, f32[1,1,224,128]{3,2,1,0:T(8,128)S(1)} %bitcast.48, f32[1,1,224,128]{3,2,1,0:T(8,128)S(1)} %bitcast.60, f32[1,1,224,128]{3,2,1,0:T(8,128)S(1)} %bitcast.62, ...), kind=kLoop, calls=%fused_computation.102 | loop fusion | flops 3211264 | bytes 2293760 | tf_op jit(solution)/shard_map/add | solution.py:163
  87.4 0.8 collective-permute-done.19
  88.2 0.9 maximum_subtract_fusion.6
  (53 shorter events, 3.8 us)
Async XLA Ops:
  0.6 2.2 %copy-start.1 = (f32[1,1,896,128]{3,2,1,0:T(8,128)S(1)}, f32[1,1,896,128]{3,2,1,0:T(8,128)}, u32[]{:S(2)}) copy-start(f32[1,1,896,128]{3,2,1,0:T(8,128)} %param.6) | copy-start | bytes 1376260
  0.6 11.0 %copy-start = (f32[1,1,640,896]{3,2,1,0:T(8,128)S(1)}, f32[1,1,640,896]{3,2,1,0:T(8,128)}, u32[]{:S(2)}) copy-start(f32[1,1,640,896]{3,2,1,0:T(8,128)} %param.7) | copy-start | bytes 6881284
  3.5 21.4 %collective-permute-start = (f32[224,128]{1,0:T(8,128)}, f32[224,128]{1,0:T(8,128)S(1)}, u32[]{:S(2)}, u32[]{:S(2)}) collective-permute-start(f32[224,128]{1,0:T(8,128)} %get-tuple-element.126), channel_id=1, source_target_pairs={{4,8},{8,4},{12,16},{16,12},{20,24},{24,20},{5,9},{9,5},{13,17},{1... | collective-permute-start | bytes 344072 | tf_op jit(solution)/shard_map/ppermute | solution.py:66
  4.2 20.7 %collective-permute-start.1 = (f32[224,128]{1,0:T(8,128)}, f32[224,128]{1,0:T(8,128)S(1)}, u32[]{:S(2)}, u32[]{:S(2)}) collective-permute-start(f32[224,128]{1,0:T(8,128)} %get-tuple-element.124), channel_id=1, source_target_pairs={{0,4},{4,0},{8,12},{12,8},{16,20},{20,16},{24,28},{28,24},{1,5},{5... | collective-permute-start | bytes 344072 | tf_op jit(solution)/shard_map/ppermute | solution.py:66
  8.6 27.6 %collective-permute-start.4 = (f32[128,896]{1,0:T(8,128)}, f32[128,896]{1,0:T(8,128)}, u32[]{:S(2)}, u32[]{:S(2)}) collective-permute-start(f32[128,896]{1,0:T(8,128)} %get-tuple-element.38), channel_id=1, source_target_pairs={{0,24},{4,28},{8,0},{12,4},{16,8},{20,12},{24,16},{28,20},{1,25},{... | collective-permute-start | bytes 1376264 | tf_op jit(solution)/shard_map/ppermute | solution.py:22
  10.6 31.5 %collective-permute-start.5 = (f32[128,896]{1,0:T(8,128)S(1)}, f32[128,896]{1,0:T(8,128)}, u32[]{:S(2)}, u32[]{:S(2)}) collective-permute-start(f32[128,896]{1,0:T(8,128)S(1)} %get-tuple-element.39), channel_id=1, source_target_pairs={{0,16},{4,20},{8,24},{12,28},{16,0},{20,4},{24,8},{28,12},{1,17},{... | collective-permute-start | bytes 1376264 | tf_op jit(solution)/shard_map/ppermute | solution.py:22
  19.2 2.8 %copy-start.3 = (s32[1,1,2]{2,1,0:T(1,128)S(1)}, s32[1,1,2]{2,1,0:T(1,128)}, u32[]{:S(2)}) copy-start(s32[1,1,2]{2,1,0:T(1,128)} %param.9) | copy-start | bytes 28
  19.2 5.7 %copy-start.2 = (f32[224,128]{1,0:T(8,128)S(1)}, f32[224,128]{1,0:T(8,128)}, u32[]{:S(2)}) copy-start(f32[224,128]{1,0:T(8,128)} %get-tuple-element.30) | copy-start | bytes 344068
  24.9 5.0 %collective-permute-start.2 = (f32[224,128]{1,0:T(8,128)S(1)}, f32[224,128]{1,0:T(8,128)S(1)}, u32[]{:S(2)}, u32[]{:S(2)}) collective-permute-start(f32[224,128]{1,0:T(8,128)S(1)} %copy-done.2), channel_id=1, source_target_pairs={{1,2},{2,1},{5,6},{6,5},{9,10},{10,9},{13,14},{14,13},{17,18},{18,... | collective-permute-start | bytes 344072 | tf_op jit(solution)/shard_map/ppermute | solution.py:69
  25.6 9.2 %collective-permute-start.3 = (f32[224,128]{1,0:T(8,128)S(1)}, f32[224,128]{1,0:T(8,128)S(1)}, u32[]{:S(2)}, u32[]{:S(2)}) collective-permute-start(f32[224,128]{1,0:T(8,128)S(1)} %get-tuple-element.31), channel_id=1, source_target_pairs={{0,1},{1,0},{2,3},{3,2},{4,5},{5,4},{6,7},{7,6},{8,9},{9,8},{10,11... | collective-permute-start | bytes 344072 | tf_op jit(solution)/shard_map/ppermute | solution.py:69
  45.1 10.9 %collective-permute-start.6 = (f32[224,128]{1,0:T(8,128)S(1)}, f32[224,128]{1,0:T(8,128)S(1)}, u32[]{:S(2)}, u32[]{:S(2)}) collective-permute-start(f32[224,128]{1,0:T(8,128)S(1)} %get-tuple-element.119), channel_id=1, source_target_pairs={{1,2},{2,1},{5,6},{6,5},{9,10},{10,9},{13,14},{14,13},{17,18},{18,... | collective-permute-start | bytes 344072 | tf_op jit(solution)/shard_map/ppermute | solution.py:75
  45.8 10.3 %collective-permute-start.7 = (f32[224,128]{1,0:T(8,128)S(1)}, f32[224,128]{1,0:T(8,128)S(1)}, u32[]{:S(2)}, u32[]{:S(2)}) collective-permute-start(f32[224,128]{1,0:T(8,128)S(1)} %get-tuple-element.117), channel_id=1, source_target_pairs={{0,1},{1,0},{2,3},{3,2},{4,5},{5,4},{6,7},{7,6},{8,9},{9,8},{10,11... | collective-permute-start | bytes 344072 | tf_op jit(solution)/shard_map/ppermute | solution.py:75
  50.0 6.0 %collective-permute-start.8 = (f32[224,128]{1,0:T(8,128)S(1)}, f32[224,128]{1,0:T(8,128)S(1)}, u32[]{:S(2)}, u32[]{:S(2)}) collective-permute-start(f32[224,128]{1,0:T(8,128)S(1)} %get-tuple-element.118), channel_id=1, source_target_pairs={{4,8},{8,4},{12,16},{16,12},{20,24},{24,20},{5,9},{9,5},{13,17},{1... | collective-permute-start | bytes 344072 | tf_op jit(solution)/shard_map/ppermute | solution.py:75
  50.9 5.2 %collective-permute-start.9 = (f32[224,128]{1,0:T(8,128)S(1)}, f32[224,128]{1,0:T(8,128)S(1)}, u32[]{:S(2)}, u32[]{:S(2)}) collective-permute-start(f32[224,128]{1,0:T(8,128)S(1)} %get-tuple-element.116), channel_id=1, source_target_pairs={{0,4},{4,0},{8,12},{12,8},{16,20},{20,16},{24,28},{28,24},{1,5},{5... | collective-permute-start | bytes 344072 | tf_op jit(solution)/shard_map/ppermute | solution.py:75
  57.6 5.8 %collective-permute-start.10 = (f32[224,128]{1,0:T(8,128)S(1)}, f32[224,128]{1,0:T(8,128)S(1)}, u32[]{:S(2)}, u32[]{:S(2)}) collective-permute-start(f32[224,128]{1,0:T(8,128)S(1)} %get-tuple-element.113), channel_id=1, source_target_pairs={{1,2},{2,1},{5,6},{6,5},{9,10},{10,9},{13,14},{14,13},{17,18},{18,... | collective-permute-start | bytes 344072 | tf_op jit(solution)/shard_map/ppermute | solution.py:75
  58.2 8.2 %collective-permute-start.11 = (f32[224,128]{1,0:T(8,128)S(1)}, f32[224,128]{1,0:T(8,128)S(1)}, u32[]{:S(2)}, u32[]{:S(2)}) collective-permute-start(f32[224,128]{1,0:T(8,128)S(1)} %get-tuple-element.111), channel_id=1, source_target_pairs={{0,1},{1,0},{2,3},{3,2},{4,5},{5,4},{6,7},{7,6},{8,9},{9,8},{10,11... | collective-permute-start | bytes 344072 | tf_op jit(solution)/shard_map/ppermute | solution.py:75
  61.0 5.4 %collective-permute-start.12 = (f32[224,128]{1,0:T(8,128)S(1)}, f32[224,128]{1,0:T(8,128)S(1)}, u32[]{:S(2)}, u32[]{:S(2)}) collective-permute-start(f32[224,128]{1,0:T(8,128)S(1)} %get-tuple-element.112), channel_id=1, source_target_pairs={{4,8},{8,4},{12,16},{16,12},{20,24},{24,20},{5,9},{9,5},{13,17},{1... | collective-permute-start | bytes 344072 | tf_op jit(solution)/shard_map/ppermute | solution.py:75
  61.7 4.8 %collective-permute-start.13 = (f32[224,128]{1,0:T(8,128)S(1)}, f32[224,128]{1,0:T(8,128)S(1)}, u32[]{:S(2)}, u32[]{:S(2)}) collective-permute-start(f32[224,128]{1,0:T(8,128)S(1)} %get-tuple-element.110), channel_id=1, source_target_pairs={{0,4},{4,0},{8,12},{12,8},{16,20},{20,16},{24,28},{28,24},{1,5},{5... | collective-permute-start | bytes 344072 | tf_op jit(solution)/shard_map/ppermute | solution.py:75
  68.0 7.3 %collective-permute-start.14 = (f32[224,128]{1,0:T(8,128)S(1)}, f32[224,128]{1,0:T(8,128)S(1)}, u32[]{:S(2)}, u32[]{:S(2)}) collective-permute-start(f32[224,128]{1,0:T(8,128)S(1)} %get-tuple-element.107), channel_id=1, source_target_pairs={{1,2},{2,1},{5,6},{6,5},{9,10},{10,9},{13,14},{14,13},{17,18},{18,... | collective-permute-start | bytes 344072 | tf_op jit(solution)/shard_map/ppermute | solution.py:75
  68.7 8.6 %collective-permute-start.15 = (f32[224,128]{1,0:T(8,128)S(1)}, f32[224,128]{1,0:T(8,128)S(1)}, u32[]{:S(2)}, u32[]{:S(2)}) collective-permute-start(f32[224,128]{1,0:T(8,128)S(1)} %get-tuple-element.105), channel_id=1, source_target_pairs={{0,1},{1,0},{2,3},{3,2},{4,5},{5,4},{6,7},{7,6},{8,9},{9,8},{10,11... | collective-permute-start | bytes 344072 | tf_op jit(solution)/shard_map/ppermute | solution.py:75
  71.4 5.9 %collective-permute-start.16 = (f32[224,128]{1,0:T(8,128)S(1)}, f32[224,128]{1,0:T(8,128)S(1)}, u32[]{:S(2)}, u32[]{:S(2)}) collective-permute-start(f32[224,128]{1,0:T(8,128)S(1)} %get-tuple-element.106), channel_id=1, source_target_pairs={{4,8},{8,4},{12,16},{16,12},{20,24},{24,20},{5,9},{9,5},{13,17},{1... | collective-permute-start | bytes 344072 | tf_op jit(solution)/shard_map/ppermute | solution.py:75
  72.1 5.2 %collective-permute-start.17 = (f32[224,128]{1,0:T(8,128)S(1)}, f32[224,128]{1,0:T(8,128)S(1)}, u32[]{:S(2)}, u32[]{:S(2)}) collective-permute-start(f32[224,128]{1,0:T(8,128)S(1)} %get-tuple-element.104), channel_id=1, source_target_pairs={{0,4},{4,0},{8,12},{12,8},{16,20},{20,16},{24,28},{28,24},{1,5},{5... | collective-permute-start | bytes 344072 | tf_op jit(solution)/shard_map/ppermute | solution.py:75
  78.9 8.5 %collective-permute-start.18 = (f32[224,128]{1,0:T(8,128)S(1)}, f32[224,128]{1,0:T(8,128)S(1)}, u32[]{:S(2)}, u32[]{:S(2)}) collective-permute-start(f32[224,128]{1,0:T(8,128)S(1)} %get-tuple-element.101), channel_id=1, source_target_pairs={{1,2},{2,1},{5,6},{6,5},{9,10},{10,9},{13,14},{14,13},{17,18},{18,... | collective-permute-start | bytes 344072 | tf_op jit(solution)/shard_map/ppermute | solution.py:75
  79.5 8.6 %collective-permute-start.19 = (f32[224,128]{1,0:T(8,128)S(1)}, f32[224,128]{1,0:T(8,128)S(1)}, u32[]{:S(2)}, u32[]{:S(2)}) collective-permute-start(f32[224,128]{1,0:T(8,128)S(1)} %get-tuple-element.99), channel_id=1, source_target_pairs={{0,1},{1,0},{2,3},{3,2},{4,5},{5,4},{6,7},{7,6},{8,9},{9,8},{10,11... | collective-permute-start | bytes 344072 | tf_op jit(solution)/shard_map/ppermute | solution.py:75
  81.8 6.3 %collective-permute-start.20 = (f32[224,128]{1,0:T(8,128)S(1)}, f32[224,128]{1,0:T(8,128)S(1)}, u32[]{:S(2)}, u32[]{:S(2)}) collective-permute-start(f32[224,128]{1,0:T(8,128)S(1)} %get-tuple-element.100), channel_id=1, source_target_pairs={{4,8},{8,4},{12,16},{16,12},{20,24},{24,20},{5,9},{9,5},{13,17},{1... | collective-permute-start | bytes 344072 | tf_op jit(solution)/shard_map/ppermute | solution.py:75
  82.5 5.6 %collective-permute-start.21 = (f32[224,128]{1,0:T(8,128)S(1)}, f32[224,128]{1,0:T(8,128)S(1)}, u32[]{:S(2)}, u32[]{:S(2)}) collective-permute-start(f32[224,128]{1,0:T(8,128)S(1)} %get-tuple-element.98), channel_id=1, source_target_pairs={{0,4},{4,0},{8,12},{12,8},{16,20},{20,16},{24,28},{28,24},{1,5},{5... | collective-permute-start | bytes 344072 | tf_op jit(solution)/shard_map/ppermute | solution.py:75

commit v11 on v10

--- a/solution.py
+++ b/solution.py
@@ -143,15 +143,18 @@
     spill_place = jnp.where(
         slot_map[:, None] == spill_ids[None, :], slot_scale[:, None], 0.0
     ).astype(jnp.bfloat16)
-    spill_stack = jnp.concatenate(homed, axis=0)
-    spill_slots = slot_pieces(spill_stack, to_rows, spill_place)
+    spill_slots = [
+        slot_pieces(homed[slot_id], to_rows, spill_place[:, slot_id * tile_rows : (slot_id + 1) * tile_rows])
+        for slot_id in range(2)
+    ]
     own_high = own_slots[:, :order_max].astype(jnp.bfloat16)
     own_mid = own_slots[:, order_max:].astype(jnp.bfloat16)
-    op_high = (own_slots[:, :order_max] + spill_slots[:, :order_max]).astype(jnp.bfloat16)
-    op_mid = (own_slots[:, order_max:] + spill_slots[:, order_max:]).astype(jnp.bfloat16)
-    spill_high = lax.reduce_precision(spill_stack, exponent_bits=8, mantissa_bits=7)
-    spill_mid = (spill_stack - spill_high).astype(jnp.bfloat16)
-    spill_high = spill_high.astype(jnp.bfloat16)
+    full_slots = own_slots + (spill_slots[0] + spill_slots[1])
+    op_high = full_slots[:, :order_max].astype(jnp.bfloat16)
+    op_mid = full_slots[:, order_max:].astype(jnp.bfloat16)
+    spill_high = [lax.reduce_precision(block, exponent_bits=8, mantissa_bits=7) for block in homed]
+    spill_mid = [(block - high).astype(jnp.bfloat16) for block, high in zip(homed, spill_high)]
+    spill_high = [high.astype(jnp.bfloat16) for high in spill_high]
     centre = (high_bound + low_bound) / 2.0
     half_width = (high_bound - low_bound) / 2.0
     sigma_value = centre / half_width
@@ -168,17 +171,20 @@
             moved = jnp.dot(to_rows, dir_pair, preferred_element_type=jnp.float32).astype(
                 jnp.bfloat16
             )
-            spill_out = bf16x3_apply(spill_high, spill_mid, moved, cols)
-            out_high = lax.reduce_precision(spill_out, exponent_bits=8, mantissa_bits=7)
-            out_rest = spill_out - out_high
-            out_mid = lax.reduce_precision(out_rest, exponent_bits=8, mantissa_bits=7)
-            pieces = jnp.concatenate([out_high, out_mid, out_rest - out_mid], axis=1)
-            placed = jnp.dot(
-                spill_place, pieces.astype(jnp.bfloat16), preferred_element_type=jnp.float32
-            )
-            local = local + (
-                (placed[:, :cols] + placed[:, cols : 2 * cols]) + placed[:, 2 * cols :]
-            )
+            for slot_id in range(2):
+                spill_out = bf16x3_apply(spill_high[slot_id], spill_mid[slot_id], moved, cols)
+                out_high = lax.reduce_precision(spill_out, exponent_bits=8, mantissa_bits=7)
+                out_rest = spill_out - out_high
+                out_mid = lax.reduce_precision(out_rest, exponent_bits=8, mantissa_bits=7)
+                pieces = jnp.concatenate([out_high, out_mid, out_rest - out_mid], axis=1)
+                placed = jnp.dot(
+                    spill_place[:, slot_id * tile_rows : (slot_id + 1) * tile_rows],
+                    pieces.astype(jnp.bfloat16),
+                    preferred_element_type=jnp.float32,
+                )
+                local = local + (
+                    (placed[:, :cols] + placed[:, cols : 2 * cols]) + placed[:, 2 * cols :]
+                )
         else:
             local = bf16x3_apply(op_high, op_mid, dir_pair, cols)
         faces = [local[face_id * width : (face_id + 1) * width] for face_id in range(4)]

time: 90.4 us -> 90.5 us (level)
  waiting for transfers between devices: 15.5 us -> 17.9 us
  local copies, waits for them, and re-layouts: 5.11 us -> 3.53 us
    ppermute x2, waiting for transfers between devices: 4.81 us -> 7.11 us  [from_behind(): return lax.ppermute(value, axis, pairs)]
    dot_general x2 -> x3, matrix products: 5.4 us -> 3.98 us  [slot_pieces(): jnp.dot(stacked, to_rows, preferred_element_type=jnp.float32)]
    another operation x7 -> x9, other arithmetic: 2.38 us -> 0.98 us
    select_n x5, other arithmetic: 0.87 us -> 1.95 us  [face_sum_parts(): jnp.where(even, high, low)]
    concatenate x1 -> x0, local copies, waits for them, and re-layouts: 1.05 us -> none  [body(): spill_stack = jnp.concatenate(homed, axis=0)]
    dot_general x2 -> x3, matrix products: 3.87 us -> 4.68 us  [slot_pieces(): return jnp.dot(to_slots, side, preferred_element_type=jnp.float32)]
    dot_general x5 -> x6, matrix products: 2.65 us -> 2.9 us  [bf16x3_apply(): jnp.dot(op_mid, pair[:, :cols], preferred_element_type=jnp.float32)]
    dot_general x5 -> x6, matrix products: 2.93 us -> 3.05 us  [bf16x3_apply(): both = jnp.dot(op_high, pair, preferred_element_type=jnp.float32)]
  transfers between devices with their start and end apart: 22 -> 22, of which waited for: 5 -> 5; matrix products, arithmetic and copies ran while one was open for 19% -> 16% of each run, Pallas kernels for 0% -> 0%
where the time goes in v11:
time: 90.5 us; the launch traced here: 89.4 us
  starting transfers between devices  40.9 us (45%)
  waiting for transfers between devices  17.9 us (20%)
  matrix products  15.9 us (18%)
  other arithmetic  6.81 us (8%)
  between operations  4.32 us (5%)
  local copies, waits for them, and re-layouts  3.53 us (4%)
    ppermute x20, starting transfers between devices, face_sum_parts(): lax.ppermute(block, axis, pairs)  37.9 us
    ppermute x20, waiting for transfers between devices, face_sum_parts(): lax.ppermute(block, axis, pairs)  10.8 us
    ppermute x2, waiting for transfers between devices, from_behind(): return lax.ppermute(value, axis, pairs)  7.11 us
    dot_general x3, matrix products, slot_pieces(): return jnp.dot(to_slots, side, preferred_element_type=jnp.float32)  4.68 us
    dot_general x3, matrix products, slot_pieces(): jnp.dot(stacked, to_rows, preferred_element_type=jnp.float32)  3.98 us
    dot_general x6, matrix products, bf16x3_apply(): both = jnp.dot(op_high, pair, preferred_element_type=jnp.float32)  3.05 us
    ppermute x2, starting transfers between devices, from_behind(): return lax.ppermute(value, axis, pairs)  3.04 us
    dot_general x6, matrix products, bf16x3_apply(): jnp.dot(op_mid, pair[:, :cols], preferred_element_type=jnp.float32)  2.9 us
  transfers between devices with their start and end apart: 22, of which 5 were waited for; matrix products, arithmetic and copies ran while one was open for 16% of the time, Pallas kernels for 0%

profile of v11, /device:TPU:0, one launch (start us, length us, event | category | flops | bytes accessed | tf_op | source)
XLA Modules:
  0.0 89.4 jit_solution(14307246409589069729)
XLA Ops:
  0.7 2.3 %slice_bitcast_fusion = (f32[128,896]{1,0:T(8,128)}, f32[128,896]{1,0:T(8,128)}) fusion(f32[1,1,2,128,896]{4,3,2,1,0:T(8,128)} %param.8), kind=kLoop, calls=%fused_computation.125 | loop fusion | bytes 1835008 | tf_op jit(solution)/shard_map/squeeze | solution.py:117
  3.0 1.8 %slice_select_fusion.16 = (f32[224,128]{1,0:T(8,128)}, f32[224,128]{1,0:T(8,128)S(1)}, f32[224,128]{1,0:T(8,128)}, f32[224,128]{1,0:T(8,128)}) fusion(f32[896,128]{1,0:T(8,128)} %bitcast.60, pred[]{:T(512)S(6)} %eq.100, pred[]{:T(512)S(6)} %eq.101), kind=kLoop, calls=%fused_computation.175 | loop fusion | flops 114688 | bytes 917506 | tf_op jit(solution)/shard_map/jit(_where)/select_n | solution.py:64
  4.8 0.7 collective-permute-start
  5.4 4.4 %collective-permute-start.1 = (f32[224,128]{1,0:T(8,128)}, f32[224,128]{1,0:T(8,128)S(1)}, u32[]{:S(2)}, u32[]{:S(2)}) collective-permute-start(f32[224,128]{1,0:T(8,128)} %get-tuple-element.128), channel_id=1, source_target_pairs={{0,4},{4,0},{8,12},{12,8},{16,20},{20,16},{24,28},{28,24},{1,5},{5... | collective-permute-start | bytes 344072 | tf_op jit(solution)/shard_map/ppermute | solution.py:66
  9.9 2.0 %collective-permute-start.4 = (f32[128,896]{1,0:T(8,128)}, f32[128,896]{1,0:T(8,128)S(1)}, u32[]{:S(2)}, u32[]{:S(2)}) collective-permute-start(f32[128,896]{1,0:T(8,128)} %get-tuple-element.38), channel_id=1, source_target_pairs={{0,24},{4,28},{8,0},{12,4},{16,8},{20,12},{24,16},{28,20},{1,25},{... | collective-permute-start | bytes 1376264 | tf_op jit(solution)/shard_map/ppermute | solution.py:22
  11.9 1.1 %collective-permute-start.5 = (f32[128,896]{1,0:T(8,128)}, f32[128,896]{1,0:T(8,128)S(1)}, u32[]{:S(2)}, u32[]{:S(2)}) collective-permute-start(f32[128,896]{1,0:T(8,128)} %get-tuple-element.39), channel_id=1, source_target_pairs={{0,16},{4,20},{8,24},{12,28},{16,0},{20,4},{24,8},{28,12},{1,17},{... | collective-permute-start | bytes 1376264 | tf_op jit(solution)/shard_map/ppermute | solution.py:22
  12.9 0.6 fusion.151
  16.0 1.3 %reduce = s32[896]{0:T(1024)} reduce(s32[1,1,896]{2,1,0:T(1,128)} %param.11, s32[]{:T(128)} %constant.99.clone.1), dimensions={0,1}, to_apply=%param.11.reduce_sub_computation | reduce | bytes 7172 | tf_op args[5]
  18.7 2.6 %convolution_convert_fusion = bf16[1280,896]{0,1:T(8,128)(2,1)S(1)} fusion(bf16[640,896]{1,0:T(8,128)(2,1)S(1)} %get-tuple-element.69, bf16[640,896]{1,0:T(8,128)(2,1)S(1)} %get-tuple-element.68, bf16[896]{0:T(1024)(128)(2,1)S(1)} %select_select_fusion, s32[896]{0:T(1024)S(1)} %copy-done.3), kind=kOutput, calls=%fused_computation.1 | convolution fusion | flops 2062548992 | bytes 4592896 | tf_op jit(solution)/shard_map/dot_general | solution.py:92
  21.5 2.7 %fusion.152 = (bf16[896,1792]{1,0:T(8,128)(2,1)S(1)}, f32[896,1792]{1,0:T(8,128)S(1)}) fusion(bf16[640,896]{0,1:T(8,128)(2,1)S(1)} %get-tuple-element.67, bf16[640,896]{0,1:T(8,128)(2,1)S(1)} %get-tuple-element.66, bf16[896]{0:T(1024)(128)(2,1)S(1)} %select_select_fusion, s32[896]{0:T(1024)S(1)} %copy-done.3), kind=kOutput, calls=%fused_computation.242 | convolution fusion | flops 2063122432 | bytes 11932928 | tf_op jit(solution)/shard_map/dot_general | solution.py:94
  24.3 0.7 collective-permute-start.2
  25.0 4.3 %collective-permute-start.3 = (f32[224,128]{1,0:T(8,128)S(1)}, f32[224,128]{1,0:T(8,128)S(1)}, u32[]{:S(2)}, u32[]{:S(2)}) collective-permute-start(f32[224,128]{1,0:T(8,128)S(1)} %get-tuple-element.31), channel_id=1, source_target_pairs={{0,1},{1,0},{2,3},{3,2},{4,5},{5,4},{6,7},{7,6},{8,9},{9,8},{10,11... | collective-permute-start | bytes 344072 | tf_op jit(solution)/shard_map/ppermute | solution.py:69
  29.6 4.6 %collective-permute-done.3 = f32[224,128]{1,0:T(8,128)S(1)} collective-permute-done((f32[224,128]{1,0:T(8,128)S(1)}, f32[224,128]{1,0:T(8,128)S(1)}, u32[]{:S(2)}, u32[]{:S(2)}) %collective-permute-start.3) | collective-permute-done | bytes 114720 | tf_op jit(solution)/shard_map/ppermute | solution.py:69
  34.3 0.6 fusion.28
  34.9 0.6 fusion.14
  36.1 7.1 %collective-permute-done.5 = f32[128,896]{1,0:T(8,128)S(1)} collective-permute-done((f32[128,896]{1,0:T(8,128)}, f32[128,896]{1,0:T(8,128)S(1)}, u32[]{:S(2)}, u32[]{:S(2)}) %collective-permute-start.5) | collective-permute-done | bytes 458784 | tf_op jit(solution)/shard_map/ppermute | solution.py:22
  44.5 0.7 fusion.58
  45.2 0.7 collective-permute-start.6
  45.9 4.3 %collective-permute-start.7 = (f32[224,128]{1,0:T(8,128)S(1)}, f32[224,128]{1,0:T(8,128)S(1)}, u32[]{:S(2)}, u32[]{:S(2)}) collective-permute-start(f32[224,128]{1,0:T(8,128)S(1)} %get-tuple-element.121), channel_id=1, source_target_pairs={{0,1},{1,0},{2,3},{3,2},{4,5},{5,4},{6,7},{7,6},{8,9},{9,8},{10,11... | collective-permute-start | bytes 344072 | tf_op jit(solution)/shard_map/ppermute | solution.py:75
  50.2 0.8 collective-permute-start.8
  51.0 1.9 %collective-permute-start.9 = (f32[224,128]{1,0:T(8,128)S(1)}, f32[224,128]{1,0:T(8,128)S(1)}, u32[]{:S(2)}, u32[]{:S(2)}) collective-permute-start(f32[224,128]{1,0:T(8,128)S(1)} %get-tuple-element.120), channel_id=1, source_target_pairs={{0,4},{4,0},{8,12},{12,8},{16,20},{20,16},{24,28},{28,24},{1,5},{5... | collective-permute-start | bytes 344072 | tf_op jit(solution)/shard_map/ppermute | solution.py:75
  52.9 0.7 fusion.29
  53.6 0.7 fusion.30
  54.4 1.0 %fusion.72 = f32[896,1792]{1,0:T(8,128)S(1)} fusion(bf16[128,896]{1,0:T(8,128)(2,1)S(1)} %get-tuple-element.115, bf16[128,896]{1,0:T(8,128)(2,1)S(1)} %get-tuple-element.114, bf16[896,256]{1,0:T(8,128)(2,1)S(1)} %select_convert_fusion.13), kind=kOutput, calls=%fused_computation.93 | convolution fusion | flops 411959296 | bytes 7110656 | tf_op jit(solution)/shard_map/dot_general | solution.py:94
  55.4 1.0 %add_convert_fusion = bf16[896,1792]{1,0:T(8,128)(2,1)S(1)} fusion(f32[896,1792]{1,0:T(8,128)S(1)} %get-tuple-element.139, f32[896,1792]{1,0:T(8,128)S(1)} %fusion.72, bf16[128,896]{1,0:T(8,128)(2,1)S(1)} %get-tuple-element.111, bf16[128,896]{1,0:T(8,128)(2,1)S(1)} %get-tuple-element.110, bf16[896,256]{1,0:T(8,128)(2,1)S(1)} %select_convert_fusion.13), kind=kOutput, calls=%fused_computation | convolution fusion | flops 416776192 | bytes 16744448 | tf_op jit(solution)/shard_map/dot_general | solution.py:94
  56.6 0.6 fusion.41
  57.2 0.6 fusion.43
  57.9 0.7 collective-permute-start.10
  58.6 2.8 %collective-permute-start.11 = (f32[224,128]{1,0:T(8,128)S(1)}, f32[224,128]{1,0:T(8,128)S(1)}, u32[]{:S(2)}, u32[]{:S(2)}) collective-permute-start(f32[224,128]{1,0:T(8,128)S(1)} %get-tuple-element.107), channel_id=1, source_target_pairs={{0,1},{1,0},{2,3},{3,2},{4,5},{5,4},{6,7},{7,6},{8,9},{9,8},{10,11... | collective-permute-start | bytes 344072 | tf_op jit(solution)/shard_map/ppermute | solution.py:75
  61.3 0.7 collective-permute-start.12
  62.0 1.7 %collective-permute-start.13 = (f32[224,128]{1,0:T(8,128)S(1)}, f32[224,128]{1,0:T(8,128)S(1)}, u32[]{:S(2)}, u32[]{:S(2)}) collective-permute-start(f32[224,128]{1,0:T(8,128)S(1)} %get-tuple-element.106), channel_id=1, source_target_pairs={{0,4},{4,0},{8,12},{12,8},{16,20},{20,16},{24,28},{28,24},{1,5},{5... | collective-permute-start | bytes 344072 | tf_op jit(solution)/shard_map/ppermute | solution.py:75
  63.7 3.0 %collective-permute-done.11 = f32[224,128]{1,0:T(8,128)S(1)} collective-permute-done((f32[224,128]{1,0:T(8,128)S(1)}, f32[224,128]{1,0:T(8,128)S(1)}, u32[]{:S(2)}, u32[]{:S(2)}) %collective-permute-start.11) | collective-permute-done | bytes 114720 | tf_op jit(solution)/shard_map/ppermute | solution.py:75
  67.0 0.6 fusion.39
  67.7 0.6 fusion.46
  68.3 0.7 collective-permute-start.14
  69.0 2.7 %collective-permute-start.15 = (f32[224,128]{1,0:T(8,128)S(1)}, f32[224,128]{1,0:T(8,128)S(1)}, u32[]{:S(2)}, u32[]{:S(2)}) collective-permute-start(f32[224,128]{1,0:T(8,128)S(1)} %get-tuple-element.101), channel_id=1, source_target_pairs={{0,1},{1,0},{2,3},{3,2},{4,5},{5,4},{6,7},{7,6},{8,9},{9,8},{10,11... | collective-permute-start | bytes 344072 | tf_op jit(solution)/shard_map/ppermute | solution.py:75
  71.7 0.7 collective-permute-start.16
  72.4 3.0 %collective-permute-start.17 = (f32[224,128]{1,0:T(8,128)S(1)}, f32[224,128]{1,0:T(8,128)S(1)}, u32[]{:S(2)}, u32[]{:S(2)}) collective-permute-start(f32[224,128]{1,0:T(8,128)S(1)} %get-tuple-element.100), channel_id=1, source_target_pairs={{0,4},{4,0},{8,12},{12,8},{16,20},{20,16},{24,28},{28,24},{1,5},{5... | collective-permute-start | bytes 344072 | tf_op jit(solution)/shard_map/ppermute | solution.py:75
  75.4 2.2 %collective-permute-done.15 = f32[224,128]{1,0:T(8,128)S(1)} collective-permute-done((f32[224,128]{1,0:T(8,128)S(1)}, f32[224,128]{1,0:T(8,128)S(1)}, u32[]{:S(2)}, u32[]{:S(2)}) %collective-permute-start.15) | collective-permute-done | bytes 114720 | tf_op jit(solution)/shard_map/ppermute | solution.py:75
  77.9 0.6 fusion.37
  78.6 0.6 fusion.49
  79.2 0.7 collective-permute-start.18
  79.9 2.3 %collective-permute-start.19 = (f32[224,128]{1,0:T(8,128)S(1)}, f32[224,128]{1,0:T(8,128)S(1)}, u32[]{:S(2)}, u32[]{:S(2)}) collective-permute-start(f32[224,128]{1,0:T(8,128)S(1)} %get-tuple-element.95), channel_id=1, source_target_pairs={{0,1},{1,0},{2,3},{3,2},{4,5},{5,4},{6,7},{7,6},{8,9},{9,8},{10,11... | collective-permute-start | bytes 344072 | tf_op jit(solution)/shard_map/ppermute | solution.py:75
  82.2 0.7 collective-permute-start.20
  82.8 3.7 %collective-permute-start.21 = (f32[224,128]{1,0:T(8,128)S(1)}, f32[224,128]{1,0:T(8,128)S(1)}, u32[]{:S(2)}, u32[]{:S(2)}) collective-permute-start(f32[224,128]{1,0:T(8,128)S(1)} %get-tuple-element.94), channel_id=1, source_target_pairs={{0,4},{4,0},{8,12},{12,8},{16,20},{20,16},{24,28},{28,24},{1,5},{5... | collective-permute-start | bytes 344072 | tf_op jit(solution)/shard_map/ppermute | solution.py:75
  86.5 1.0 %add_add_fusion = f32[1,1,896,128]{3,2,1,0:T(8,128)} fusion(f32[1,1,224,128]{3,2,1,0:T(8,128)S(1)} %bitcast.48, f32[1,1,224,128]{3,2,1,0:T(8,128)S(1)} %bitcast.50, f32[1,1,224,128]{3,2,1,0:T(8,128)S(1)} %bitcast.46, f32[1,1,224,128]{3,2,1,0:T(8,128)S(1)} %bitcast.44, f32[1,1,224,128]{3,2,1,0:T(8,128)S(1)} %bitcast.56, f32[1,1,224,128]{3,2,1,0:T(8,128)S(1)} %bitcast.58, ...), kind=kLoop, calls=%fused_computation.120 | loop fusion | flops 3211264 | bytes 2293760 | tf_op jit(solution)/shard_map/add | solution.py:166
  87.5 0.9 %collective-permute-done.19 = f32[224,128]{1,0:T(8,128)S(1)} collective-permute-done((f32[224,128]{1,0:T(8,128)S(1)}, f32[224,128]{1,0:T(8,128)S(1)}, u32[]{:S(2)}, u32[]{:S(2)}) %collective-permute-start.19) | collective-permute-done | bytes 114720 | tf_op jit(solution)/shard_map/ppermute | solution.py:75
  88.5 0.9 maximum_subtract_fusion.6
  (61 shorter events, 4.1 us)
Async XLA Ops:
  0.6 17.3 %copy-start = (f32[1,1,640,896]{3,2,1,0:T(8,128)S(1)}, f32[1,1,640,896]{3,2,1,0:T(8,128)}, u32[]{:S(2)}) copy-start(f32[1,1,640,896]{3,2,1,0:T(8,128)} %param.7) | copy-start | bytes 6881284
  0.7 12.3 %copy-start.4 = (s32[1,1,2]{2,1,0:T(1,128)S(1)}, s32[1,1,2]{2,1,0:T(1,128)}, u32[]{:S(2)}) copy-start(s32[1,1,2]{2,1,0:T(1,128)} %param.9) | copy-start | bytes 28
  4.8 19.5 %collective-permute-start = (f32[224,128]{1,0:T(8,128)}, f32[224,128]{1,0:T(8,128)S(1)}, u32[]{:S(2)}, u32[]{:S(2)}) collective-permute-start(f32[224,128]{1,0:T(8,128)} %get-tuple-element.130), channel_id=1, source_target_pairs={{4,8},{8,4},{12,16},{16,12},{20,24},{24,20},{5,9},{9,5},{13,17},{1... | collective-permute-start | bytes 344072 | tf_op jit(solution)/shard_map/ppermute | solution.py:66
  5.4 18.8 %collective-permute-start.1 = (f32[224,128]{1,0:T(8,128)}, f32[224,128]{1,0:T(8,128)S(1)}, u32[]{:S(2)}, u32[]{:S(2)}) collective-permute-start(f32[224,128]{1,0:T(8,128)} %get-tuple-element.128), channel_id=1, source_target_pairs={{0,4},{4,0},{8,12},{12,8},{16,20},{20,16},{24,28},{28,24},{1,5},{5... | collective-permute-start | bytes 344072 | tf_op jit(solution)/shard_map/ppermute | solution.py:66
  9.9 25.7 %collective-permute-start.4 = (f32[128,896]{1,0:T(8,128)}, f32[128,896]{1,0:T(8,128)S(1)}, u32[]{:S(2)}, u32[]{:S(2)}) collective-permute-start(f32[128,896]{1,0:T(8,128)} %get-tuple-element.38), channel_id=1, source_target_pairs={{0,24},{4,28},{8,0},{12,4},{16,8},{20,12},{24,16},{28,20},{1,25},{... | collective-permute-start | bytes 1376264 | tf_op jit(solution)/shard_map/ppermute | solution.py:22
  11.9 31.4 %collective-permute-start.5 = (f32[128,896]{1,0:T(8,128)}, f32[128,896]{1,0:T(8,128)S(1)}, u32[]{:S(2)}, u32[]{:S(2)}) collective-permute-start(f32[128,896]{1,0:T(8,128)} %get-tuple-element.39), channel_id=1, source_target_pairs={{0,16},{4,20},{8,24},{12,28},{16,0},{20,4},{24,8},{28,12},{1,17},{... | collective-permute-start | bytes 1376264 | tf_op jit(solution)/shard_map/ppermute | solution.py:22
  18.0 0.7 copy-start.3
  21.5 2.8 %copy-start.2 = (f32[224,128]{1,0:T(8,128)S(1)}, f32[224,128]{1,0:T(8,128)}, u32[]{:S(2)}) copy-start(f32[224,128]{1,0:T(8,128)} %get-tuple-element.30) | copy-start | bytes 344068
  21.5 12.7 %copy-start.1 = (f32[1,1,896,128]{3,2,1,0:T(8,128)S(1)}, f32[1,1,896,128]{3,2,1,0:T(8,128)}, u32[]{:S(2)}) copy-start(f32[1,1,896,128]{3,2,1,0:T(8,128)} %param.6) | copy-start | bytes 1376260
  24.3 5.3 %collective-permute-start.2 = (f32[224,128]{1,0:T(8,128)S(1)}, f32[224,128]{1,0:T(8,128)S(1)}, u32[]{:S(2)}, u32[]{:S(2)}) collective-permute-start(f32[224,128]{1,0:T(8,128)S(1)} %copy-done.2), channel_id=1, source_target_pairs={{1,2},{2,1},{5,6},{6,5},{9,10},{10,9},{13,14},{14,13},{17,18},{18,... | collective-permute-start | bytes 344072 | tf_op jit(solution)/shard_map/ppermute | solution.py:69
  25.0 9.2 %collective-permute-start.3 = (f32[224,128]{1,0:T(8,128)S(1)}, f32[224,128]{1,0:T(8,128)S(1)}, u32[]{:S(2)}, u32[]{:S(2)}) collective-permute-start(f32[224,128]{1,0:T(8,128)S(1)} %get-tuple-element.31), channel_id=1, source_target_pairs={{0,1},{1,0},{2,3},{3,2},{4,5},{5,4},{6,7},{7,6},{8,9},{9,8},{10,11... | collective-permute-start | bytes 344072 | tf_op jit(solution)/shard_map/ppermute | solution.py:69
  45.2 11.1 %collective-permute-start.6 = (f32[224,128]{1,0:T(8,128)S(1)}, f32[224,128]{1,0:T(8,128)S(1)}, u32[]{:S(2)}, u32[]{:S(2)}) collective-permute-start(f32[224,128]{1,0:T(8,128)S(1)} %get-tuple-element.123), channel_id=1, source_target_pairs={{1,2},{2,1},{5,6},{6,5},{9,10},{10,9},{13,14},{14,13},{17,18},{18,... | collective-permute-start | bytes 344072 | tf_op jit(solution)/shard_map/ppermute | solution.py:75
  45.9 10.5 %collective-permute-start.7 = (f32[224,128]{1,0:T(8,128)S(1)}, f32[224,128]{1,0:T(8,128)S(1)}, u32[]{:S(2)}, u32[]{:S(2)}) collective-permute-start(f32[224,128]{1,0:T(8,128)S(1)} %get-tuple-element.121), channel_id=1, source_target_pairs={{0,1},{1,0},{2,3},{3,2},{4,5},{5,4},{6,7},{7,6},{8,9},{9,8},{10,11... | collective-permute-start | bytes 344072 | tf_op jit(solution)/shard_map/ppermute | solution.py:75
  50.2 6.2 %collective-permute-start.8 = (f32[224,128]{1,0:T(8,128)S(1)}, f32[224,128]{1,0:T(8,128)S(1)}, u32[]{:S(2)}, u32[]{:S(2)}) collective-permute-start(f32[224,128]{1,0:T(8,128)S(1)} %get-tuple-element.122), channel_id=1, source_target_pairs={{4,8},{8,4},{12,16},{16,12},{20,24},{24,20},{5,9},{9,5},{13,17},{1... | collective-permute-start | bytes 344072 | tf_op jit(solution)/shard_map/ppermute | solution.py:75
  51.0 5.4 %collective-permute-start.9 = (f32[224,128]{1,0:T(8,128)S(1)}, f32[224,128]{1,0:T(8,128)S(1)}, u32[]{:S(2)}, u32[]{:S(2)}) collective-permute-start(f32[224,128]{1,0:T(8,128)S(1)} %get-tuple-element.120), channel_id=1, source_target_pairs={{0,4},{4,0},{8,12},{12,8},{16,20},{20,16},{24,28},{28,24},{1,5},{5... | collective-permute-start | bytes 344072 | tf_op jit(solution)/shard_map/ppermute | solution.py:75
  57.9 5.8 %collective-permute-start.10 = (f32[224,128]{1,0:T(8,128)S(1)}, f32[224,128]{1,0:T(8,128)S(1)}, u32[]{:S(2)}, u32[]{:S(2)}) collective-permute-start(f32[224,128]{1,0:T(8,128)S(1)} %get-tuple-element.109), channel_id=1, source_target_pairs={{1,2},{2,1},{5,6},{6,5},{9,10},{10,9},{13,14},{14,13},{17,18},{18,... | collective-permute-start | bytes 344072 | tf_op jit(solution)/shard_map/ppermute | solution.py:75
  58.6 8.2 %collective-permute-start.11 = (f32[224,128]{1,0:T(8,128)S(1)}, f32[224,128]{1,0:T(8,128)S(1)}, u32[]{:S(2)}, u32[]{:S(2)}) collective-permute-start(f32[224,128]{1,0:T(8,128)S(1)} %get-tuple-element.107), channel_id=1, source_target_pairs={{0,1},{1,0},{2,3},{3,2},{4,5},{5,4},{6,7},{7,6},{8,9},{9,8},{10,11... | collective-permute-start | bytes 344072 | tf_op jit(solution)/shard_map/ppermute | solution.py:75
  61.3 5.4 %collective-permute-start.12 = (f32[224,128]{1,0:T(8,128)S(1)}, f32[224,128]{1,0:T(8,128)S(1)}, u32[]{:S(2)}, u32[]{:S(2)}) collective-permute-start(f32[224,128]{1,0:T(8,128)S(1)} %get-tuple-element.108), channel_id=1, source_target_pairs={{4,8},{8,4},{12,16},{16,12},{20,24},{24,20},{5,9},{9,5},{13,17},{1... | collective-permute-start | bytes 344072 | tf_op jit(solution)/shard_map/ppermute | solution.py:75
  62.0 4.8 %collective-permute-start.13 = (f32[224,128]{1,0:T(8,128)S(1)}, f32[224,128]{1,0:T(8,128)S(1)}, u32[]{:S(2)}, u32[]{:S(2)}) collective-permute-start(f32[224,128]{1,0:T(8,128)S(1)} %get-tuple-element.106), channel_id=1, source_target_pairs={{0,4},{4,0},{8,12},{12,8},{16,20},{20,16},{24,28},{28,24},{1,5},{5... | collective-permute-start | bytes 344072 | tf_op jit(solution)/shard_map/ppermute | solution.py:75
  68.3 7.1 %collective-permute-start.14 = (f32[224,128]{1,0:T(8,128)S(1)}, f32[224,128]{1,0:T(8,128)S(1)}, u32[]{:S(2)}, u32[]{:S(2)}) collective-permute-start(f32[224,128]{1,0:T(8,128)S(1)} %get-tuple-element.103), channel_id=1, source_target_pairs={{1,2},{2,1},{5,6},{6,5},{9,10},{10,9},{13,14},{14,13},{17,18},{18,... | collective-permute-start | bytes 344072 | tf_op jit(solution)/shard_map/ppermute | solution.py:75
  69.0 8.6 %collective-permute-start.15 = (f32[224,128]{1,0:T(8,128)S(1)}, f32[224,128]{1,0:T(8,128)S(1)}, u32[]{:S(2)}, u32[]{:S(2)}) collective-permute-start(f32[224,128]{1,0:T(8,128)S(1)} %get-tuple-element.101), channel_id=1, source_target_pairs={{0,1},{1,0},{2,3},{3,2},{4,5},{5,4},{6,7},{7,6},{8,9},{9,8},{10,11... | collective-permute-start | bytes 344072 | tf_op jit(solution)/shard_map/ppermute | solution.py:75
  71.7 5.9 %collective-permute-start.16 = (f32[224,128]{1,0:T(8,128)S(1)}, f32[224,128]{1,0:T(8,128)S(1)}, u32[]{:S(2)}, u32[]{:S(2)}) collective-permute-start(f32[224,128]{1,0:T(8,128)S(1)} %get-tuple-element.102), channel_id=1, source_target_pairs={{4,8},{8,4},{12,16},{16,12},{20,24},{24,20},{5,9},{9,5},{13,17},{1... | collective-permute-start | bytes 344072 | tf_op jit(solution)/shard_map/ppermute | solution.py:75
  72.4 5.3 %collective-permute-start.17 = (f32[224,128]{1,0:T(8,128)S(1)}, f32[224,128]{1,0:T(8,128)S(1)}, u32[]{:S(2)}, u32[]{:S(2)}) collective-permute-start(f32[224,128]{1,0:T(8,128)S(1)} %get-tuple-element.100), channel_id=1, source_target_pairs={{0,4},{4,0},{8,12},{12,8},{16,20},{20,16},{24,28},{28,24},{1,5},{5... | collective-permute-start | bytes 344072 | tf_op jit(solution)/shard_map/ppermute | solution.py:75
  79.2 8.3 %collective-permute-start.18 = (f32[224,128]{1,0:T(8,128)S(1)}, f32[224,128]{1,0:T(8,128)S(1)}, u32[]{:S(2)}, u32[]{:S(2)}) collective-permute-start(f32[224,128]{1,0:T(8,128)S(1)} %get-tuple-element.97), channel_id=1, source_target_pairs={{1,2},{2,1},{5,6},{6,5},{9,10},{10,9},{13,14},{14,13},{17,18},{18,... | collective-permute-start | bytes 344072 | tf_op jit(solution)/shard_map/ppermute | solution.py:75
  79.9 8.6 %collective-permute-start.19 = (f32[224,128]{1,0:T(8,128)S(1)}, f32[224,128]{1,0:T(8,128)S(1)}, u32[]{:S(2)}, u32[]{:S(2)}) collective-permute-start(f32[224,128]{1,0:T(8,128)S(1)} %get-tuple-element.95), channel_id=1, source_target_pairs={{0,1},{1,0},{2,3},{3,2},{4,5},{5,4},{6,7},{7,6},{8,9},{9,8},{10,11... | collective-permute-start | bytes 344072 | tf_op jit(solution)/shard_map/ppermute | solution.py:75
  82.2 6.3 %collective-permute-start.20 = (f32[224,128]{1,0:T(8,128)S(1)}, f32[224,128]{1,0:T(8,128)S(1)}, u32[]{:S(2)}, u32[]{:S(2)}) collective-permute-start(f32[224,128]{1,0:T(8,128)S(1)} %get-tuple-element.96), channel_id=1, source_target_pairs={{4,8},{8,4},{12,16},{16,12},{20,24},{24,20},{5,9},{9,5},{13,17},{1... | collective-permute-start | bytes 344072 | tf_op jit(solution)/shard_map/ppermute | solution.py:75
  82.8 5.6 %collective-permute-start.21 = (f32[224,128]{1,0:T(8,128)S(1)}, f32[224,128]{1,0:T(8,128)S(1)}, u32[]{:S(2)}, u32[]{:S(2)}) collective-permute-start(f32[224,128]{1,0:T(8,128)S(1)} %get-tuple-element.94), channel_id=1, source_target_pairs={{0,4},{4,0},{8,12},{12,8},{16,20},{20,16},{24,28},{28,24},{1,5},{5... | collective-permute-start | bytes 344072 | tf_op jit(solution)/shard_map/ppermute | solution.py:75

commit v12 on v11

--- a/solution.py
+++ b/solution.py
@@ -114,11 +114,11 @@
     row_ids = jnp.arange(order_max, dtype=jnp.int32)
     face_sign = jnp.where(row_ids // (order_max // 4) % 2 == 0, -1.0, 1.0).astype(jnp.float32)
     slot_scale = face_sign * (slot_map < order_now).astype(jnp.float32)
-    spill_parts = [spill_block[slot_id] for slot_id in range(2)]
-    gap_faces, spill_parts = lax.optimization_barrier((gap[0, 0], spill_parts))
+    spill_parts = lax.optimization_barrier([spill_block[slot_id] for slot_id in range(2)])
     homed = [
         from_behind(spill_parts[slot_id], "gx", -(slot_id + 1) * hop_span) for slot_id in range(2)
     ]
+    gap_faces, _ = lax.optimization_barrier((gap[0, 0], spill_parts))
     own_count = own_block.shape[0]
     cols = gap.shape[3]
     width = order_max // 4

time: 90.5 us -> 98.3 us (1.086)
  starting transfers between devices: 40.9 us -> 58.4 us
  waiting for transfers between devices: 17.9 us -> 7.24 us
    ppermute x20, starting transfers between devices: 37.9 us -> 53.4 us  [face_sum_parts(): lax.ppermute(block, axis, pairs)]
    ppermute x2, waiting for transfers between devices: 7.11 us -> 1.7 us  [from_behind(): return lax.ppermute(value, axis, pairs)]
    ppermute x20, waiting for transfers between devices: 10.8 us -> 5.54 us  [face_sum_parts(): lax.ppermute(block, axis, pairs)]
    ppermute x2, starting transfers between devices: 3.04 us -> 5.05 us  [from_behind(): return lax.ppermute(value, axis, pairs)]
  transfers between devices with their start and end apart: 22 -> 22, of which waited for: 5 -> 5; matrix products, arithmetic and copies ran while one was open for 16% -> 18% of each run, Pallas kernels for 0% -> 0%
where the time goes in v12:
time: 98.3 us; the launch traced here: 96.9 us
  starting transfers between devices  58.4 us (59%)
  matrix products  15.9 us (16%)
  waiting for transfers between devices  7.24 us (7%)
  other arithmetic  6.82 us (7%)
  between operations  4.27 us (4%)
  local copies, waits for them, and re-layouts  4.26 us (4%)
    ppermute x20, starting transfers between devices, face_sum_parts(): lax.ppermute(block, axis, pairs)  53.4 us
    ppermute x20, waiting for transfers between devices, face_sum_parts(): lax.ppermute(block, axis, pairs)  5.54 us
    ppermute x2, starting transfers between devices, from_behind(): return lax.ppermute(value, axis, pairs)  5.05 us
    dot_general x3, matrix products, slot_pieces(): return jnp.dot(to_slots, side, preferred_element_type=jnp.float32)  4.69 us
    dot_general x3, matrix products, slot_pieces(): jnp.dot(stacked, to_rows, preferred_element_type=jnp.float32)  3.98 us
    dot_general x6, matrix products, bf16x3_apply(): both = jnp.dot(op_high, pair, preferred_element_type=jnp.float32)  3.05 us
    dot_general x6, matrix products, bf16x3_apply(): jnp.dot(op_mid, pair[:, :cols], preferred_element_type=jnp.float32)  2.91 us
    squeeze x1, local copies, waits for them, and re-layouts, body(): spill_block[slot_id]  2.29 us
  transfers between devices with their start and end apart: 22, of which 5 were waited for; matrix products, arithmetic and copies ran while one was open for 18% of the time, Pallas kernels for 0%

profile of v12, /device:TPU:0, one launch (start us, length us, event | category | flops | bytes accessed | tf_op | source)
XLA Modules:
  0.0 96.9 jit_solution(24476313696392901)
XLA Ops:
  0.6 2.3 %slice_bitcast_fusion = (f32[128,896]{1,0:T(8,128)}, f32[128,896]{1,0:T(8,128)}) fusion(f32[1,1,2,128,896]{4,3,2,1,0:T(8,128)} %param.8), kind=kLoop, calls=%fused_computation.125 | loop fusion | bytes 1835008 | tf_op jit(solution)/shard_map/squeeze | solution.py:117
  2.9 5.0 %collective-permute-start.4 = (f32[128,896]{1,0:T(8,128)}, f32[128,896]{1,0:T(8,128)S(1)}, u32[]{:S(2)}, u32[]{:S(2)}) collective-permute-start(f32[128,896]{1,0:T(8,128)} %get-tuple-element.29), channel_id=1, source_target_pairs={{0,24},{4,28},{8,0},{12,4},{16,8},{20,12},{24,16},{28,20},{1,25},{... | collective-permute-start | bytes 1376264 | tf_op jit(solution)/shard_map/ppermute | solution.py:22
  8.0 1.8 %slice_select_fusion.16 = (f32[224,128]{1,0:T(8,128)}, f32[224,128]{1,0:T(8,128)S(1)}, f32[224,128]{1,0:T(8,128)}, f32[224,128]{1,0:T(8,128)}) fusion(f32[896,128]{1,0:T(8,128)} %bitcast.60, pred[]{:T(512)S(6)} %eq.100, pred[]{:T(512)S(6)} %eq.101), kind=kLoop, calls=%fused_computation.175 | loop fusion | flops 114688 | bytes 917506 | tf_op jit(solution)/shard_map/jit(_where)/select_n | solution.py:64
  9.8 0.7 collective-permute-start
  10.5 2.4 %collective-permute-start.1 = (f32[224,128]{1,0:T(8,128)}, f32[224,128]{1,0:T(8,128)S(1)}, u32[]{:S(2)}, u32[]{:S(2)}) collective-permute-start(f32[224,128]{1,0:T(8,128)} %get-tuple-element.128), channel_id=1, source_target_pairs={{0,4},{4,0},{8,12},{12,8},{16,20},{20,16},{24,28},{28,24},{1,5},{5... | collective-permute-start | bytes 344072 | tf_op jit(solution)/shard_map/ppermute | solution.py:66
  12.9 1.3 %fusion.151 = (s32[1,1,1]{2,1,0:T(1,128)}, s32[1,1,1]{2,1,0:T(1,128)}) fusion(s32[1,1,2]{2,1,0:T(1,128)} %param.9), kind=kLoop, calls=%fused_computation.241 | loop fusion | bytes 16 | tf_op jit(solution)/shard_map/slice | solution.py:138
  16.7 1.3 %reduce = s32[896]{0:T(1024)} reduce(s32[1,1,896]{2,1,0:T(1,128)} %param.11, s32[]{:T(128)} %constant.99.clone.1), dimensions={0,1}, to_apply=%param.11.reduce_sub_computation | reduce | bytes 7172 | tf_op args[5]
  19.0 0.3 copy-done.3
  19.3 2.6 %convolution_convert_fusion = bf16[1280,896]{0,1:T(8,128)(2,1)S(1)} fusion(bf16[640,896]{1,0:T(8,128)(2,1)S(1)} %get-tuple-element.69, bf16[640,896]{1,0:T(8,128)(2,1)S(1)} %get-tuple-element.68, bf16[896]{0:T(1024)(128)(2,1)S(1)} %select_select_fusion, s32[896]{0:T(1024)S(1)} %copy-done.3), kind=kOutput, calls=%fused_computation.1 | convolution fusion | flops 2062548992 | bytes 4592896 | tf_op jit(solution)/shard_map/dot_general | solution.py:92
  22.2 2.7 %fusion.152 = (bf16[896,1792]{1,0:T(8,128)(2,1)S(1)}, f32[896,1792]{1,0:T(8,128)S(1)}) fusion(bf16[640,896]{0,1:T(8,128)(2,1)S(1)} %get-tuple-element.67, bf16[640,896]{0,1:T(8,128)(2,1)S(1)} %get-tuple-element.66, bf16[896]{0:T(1024)(128)(2,1)S(1)} %select_select_fusion, s32[896]{0:T(1024)S(1)} %copy-done.3), kind=kOutput, calls=%fused_computation.242 | convolution fusion | flops 2063122432 | bytes 11932928 | tf_op jit(solution)/shard_map/dot_general | solution.py:94
  24.9 0.7 collective-permute-start.2
  25.6 4.3 %collective-permute-start.3 = (f32[224,128]{1,0:T(8,128)S(1)}, f32[224,128]{1,0:T(8,128)S(1)}, u32[]{:S(2)}, u32[]{:S(2)}) collective-permute-start(f32[224,128]{1,0:T(8,128)S(1)} %get-tuple-element.33), channel_id=1, source_target_pairs={{0,1},{1,0},{2,3},{3,2},{4,5},{5,4},{6,7},{7,6},{8,9},{9,8},{10,11... | collective-permute-start | bytes 344072 | tf_op jit(solution)/shard_map/ppermute | solution.py:69
  30.2 3.6 %collective-permute-done.3 = f32[224,128]{1,0:T(8,128)S(1)} collective-permute-done((f32[224,128]{1,0:T(8,128)S(1)}, f32[224,128]{1,0:T(8,128)S(1)}, u32[]{:S(2)}, u32[]{:S(2)}) %collective-permute-start.3) | collective-permute-done | bytes 114720 | tf_op jit(solution)/shard_map/ppermute | solution.py:69
  34.0 0.6 fusion.28
  34.6 0.6 fusion.14
  35.8 1.7 %collective-permute-done.5 = f32[128,896]{1,0:T(8,128)S(1)} collective-permute-done((f32[128,896]{1,0:T(8,128)}, f32[128,896]{1,0:T(8,128)S(1)}, u32[]{:S(2)}, u32[]{:S(2)}) %collective-permute-start.5) | collective-permute-done | bytes 458784 | tf_op jit(solution)/shard_map/ppermute | solution.py:22
  38.4 0.3 fusion.100
  38.7 0.7 fusion.58
  39.5 0.7 collective-permute-start.6
  40.1 4.3 %collective-permute-start.7 = (f32[224,128]{1,0:T(8,128)S(1)}, f32[224,128]{1,0:T(8,128)S(1)}, u32[]{:S(2)}, u32[]{:S(2)}) collective-permute-start(f32[224,128]{1,0:T(8,128)S(1)} %get-tuple-element.121), channel_id=1, source_target_pairs={{0,1},{1,0},{2,3},{3,2},{4,5},{5,4},{6,7},{7,6},{8,9},{9,8},{10,11... | collective-permute-start | bytes 344072 | tf_op jit(solution)/shard_map/ppermute | solution.py:75
  44.4 0.8 collective-permute-start.8
  45.3 5.7 %collective-permute-start.9 = (f32[224,128]{1,0:T(8,128)S(1)}, f32[224,128]{1,0:T(8,128)S(1)}, u32[]{:S(2)}, u32[]{:S(2)}) collective-permute-start(f32[224,128]{1,0:T(8,128)S(1)} %get-tuple-element.120), channel_id=1, source_target_pairs={{0,4},{4,0},{8,12},{12,8},{16,20},{20,16},{24,28},{28,24},{1,5},{5... | collective-permute-start | bytes 344072 | tf_op jit(solution)/shard_map/ppermute | solution.py:75
  51.0 0.7 fusion.29
  51.8 0.7 fusion.30
  52.5 1.0 %fusion.72 = f32[896,1792]{1,0:T(8,128)S(1)} fusion(bf16[128,896]{1,0:T(8,128)(2,1)S(1)} %get-tuple-element.115, bf16[128,896]{1,0:T(8,128)(2,1)S(1)} %get-tuple-element.114, bf16[896,256]{1,0:T(8,128)(2,1)S(1)} %select_convert_fusion.13), kind=kOutput, calls=%fused_computation.93 | convolution fusion | flops 411959296 | bytes 7110656 | tf_op jit(solution)/shard_map/dot_general | solution.py:94
  53.5 1.0 %add_convert_fusion = bf16[896,1792]{1,0:T(8,128)(2,1)S(1)} fusion(f32[896,1792]{1,0:T(8,128)S(1)} %get-tuple-element.139, f32[896,1792]{1,0:T(8,128)S(1)} %fusion.72, bf16[128,896]{1,0:T(8,128)(2,1)S(1)} %get-tuple-element.111, bf16[128,896]{1,0:T(8,128)(2,1)S(1)} %get-tuple-element.110, bf16[896,256]{1,0:T(8,128)(2,1)S(1)} %select_convert_fusion.13), kind=kOutput, calls=%fused_computation | convolution fusion | flops 416776192 | bytes 16744448 | tf_op jit(solution)/shard_map/dot_general | solution.py:94
  54.7 0.6 fusion.41
  55.4 0.6 fusion.43
  56.0 0.7 collective-permute-start.10
  56.7 2.8 %collective-permute-start.11 = (f32[224,128]{1,0:T(8,128)S(1)}, f32[224,128]{1,0:T(8,128)S(1)}, u32[]{:S(2)}, u32[]{:S(2)}) collective-permute-start(f32[224,128]{1,0:T(8,128)S(1)} %get-tuple-element.107), channel_id=1, source_target_pairs={{0,1},{1,0},{2,3},{3,2},{4,5},{5,4},{6,7},{7,6},{8,9},{9,8},{10,11... | collective-permute-start | bytes 344072 | tf_op jit(solution)/shard_map/ppermute | solution.py:75
  59.5 0.7 collective-permute-start.12
  60.2 12.5 %collective-permute-start.13 = (f32[224,128]{1,0:T(8,128)S(1)}, f32[224,128]{1,0:T(8,128)S(1)}, u32[]{:S(2)}, u32[]{:S(2)}) collective-permute-start(f32[224,128]{1,0:T(8,128)S(1)} %get-tuple-element.106), channel_id=1, source_target_pairs={{0,4},{4,0},{8,12},{12,8},{16,20},{20,16},{24,28},{28,24},{1,5},{5... | collective-permute-start | bytes 344072 | tf_op jit(solution)/shard_map/ppermute | solution.py:75
  72.7 1.0 collective-permute-done.13
  73.9 0.6 fusion.39
  74.6 0.6 fusion.46
  75.2 0.7 collective-permute-start.14
  75.9 2.8 %collective-permute-start.15 = (f32[224,128]{1,0:T(8,128)S(1)}, f32[224,128]{1,0:T(8,128)S(1)}, u32[]{:S(2)}, u32[]{:S(2)}) collective-permute-start(f32[224,128]{1,0:T(8,128)S(1)} %get-tuple-element.101), channel_id=1, source_target_pairs={{0,1},{1,0},{2,3},{3,2},{4,5},{5,4},{6,7},{7,6},{8,9},{9,8},{10,11... | collective-permute-start | bytes 344072 | tf_op jit(solution)/shard_map/ppermute | solution.py:75
  78.7 0.7 collective-permute-start.16
  79.4 4.5 %collective-permute-start.17 = (f32[224,128]{1,0:T(8,128)S(1)}, f32[224,128]{1,0:T(8,128)S(1)}, u32[]{:S(2)}, u32[]{:S(2)}) collective-permute-start(f32[224,128]{1,0:T(8,128)S(1)} %get-tuple-element.100), channel_id=1, source_target_pairs={{0,4},{4,0},{8,12},{12,8},{16,20},{20,16},{24,28},{28,24},{1,5},{5... | collective-permute-start | bytes 344072 | tf_op jit(solution)/shard_map/ppermute | solution.py:75
  83.9 0.8 collective-permute-done.15
  85.1 0.6 fusion.37
  85.7 0.6 fusion.49
  86.4 0.7 collective-permute-start.18
  87.1 2.7 %collective-permute-start.19 = (f32[224,128]{1,0:T(8,128)S(1)}, f32[224,128]{1,0:T(8,128)S(1)}, u32[]{:S(2)}, u32[]{:S(2)}) collective-permute-start(f32[224,128]{1,0:T(8,128)S(1)} %get-tuple-element.95), channel_id=1, source_target_pairs={{0,1},{1,0},{2,3},{3,2},{4,5},{5,4},{6,7},{7,6},{8,9},{9,8},{10,11... | collective-permute-start | bytes 344072 | tf_op jit(solution)/shard_map/ppermute | solution.py:75
  89.8 0.7 collective-permute-start.20
  90.5 4.5 %collective-permute-start.21 = (f32[224,128]{1,0:T(8,128)S(1)}, f32[224,128]{1,0:T(8,128)S(1)}, u32[]{:S(2)}, u32[]{:S(2)}) collective-permute-start(f32[224,128]{1,0:T(8,128)S(1)} %get-tuple-element.94), channel_id=1, source_target_pairs={{0,4},{4,0},{8,12},{12,8},{16,20},{20,16},{24,28},{28,24},{1,5},{5... | collective-permute-start | bytes 344072 | tf_op jit(solution)/shard_map/ppermute | solution.py:75
  94.9 1.0 %add_add_fusion = f32[1,1,896,128]{3,2,1,0:T(8,128)} fusion(f32[1,1,224,128]{3,2,1,0:T(8,128)S(1)} %bitcast.48, f32[1,1,224,128]{3,2,1,0:T(8,128)S(1)} %bitcast.50, f32[1,1,224,128]{3,2,1,0:T(8,128)S(1)} %bitcast.46, f32[1,1,224,128]{3,2,1,0:T(8,128)S(1)} %bitcast.44, f32[1,1,224,128]{3,2,1,0:T(8,128)S(1)} %bitcast.56, f32[1,1,224,128]{3,2,1,0:T(8,128)S(1)} %bitcast.58, ...), kind=kLoop, calls=%fused_computation.120 | loop fusion | flops 3211264 | bytes 2293760 | tf_op jit(solution)/shard_map/add | solution.py:166
  96.0 0.9 maximum_subtract_fusion.6
  (59 shorter events, 3.5 us)
Async XLA Ops:
  0.6 18.0 %copy-start = (f32[1,1,640,896]{3,2,1,0:T(8,128)S(1)}, f32[1,1,640,896]{3,2,1,0:T(8,128)}, u32[]{:S(2)}) copy-start(f32[1,1,640,896]{3,2,1,0:T(8,128)} %param.7) | copy-start | bytes 6881284
  2.9 32.3 %collective-permute-start.4 = (f32[128,896]{1,0:T(8,128)}, f32[128,896]{1,0:T(8,128)S(1)}, u32[]{:S(2)}, u32[]{:S(2)}) collective-permute-start(f32[128,896]{1,0:T(8,128)} %get-tuple-element.29), channel_id=1, source_target_pairs={{0,24},{4,28},{8,0},{12,4},{16,8},{20,12},{24,16},{28,20},{1,25},{... | collective-permute-start | bytes 1376264 | tf_op jit(solution)/shard_map/ppermute | solution.py:22
  8.0 29.5 %collective-permute-start.5 = (f32[128,896]{1,0:T(8,128)}, f32[128,896]{1,0:T(8,128)S(1)}, u32[]{:S(2)}, u32[]{:S(2)}) collective-permute-start(f32[128,896]{1,0:T(8,128)} %get-tuple-element.30), channel_id=1, source_target_pairs={{0,16},{4,20},{8,24},{12,28},{16,0},{20,4},{24,8},{28,12},{1,17},{... | collective-permute-start | bytes 1376264 | tf_op jit(solution)/shard_map/ppermute | solution.py:22
  9.8 15.1 %collective-permute-start = (f32[224,128]{1,0:T(8,128)}, f32[224,128]{1,0:T(8,128)S(1)}, u32[]{:S(2)}, u32[]{:S(2)}) collective-permute-start(f32[224,128]{1,0:T(8,128)} %get-tuple-element.130), channel_id=1, source_target_pairs={{4,8},{8,4},{12,16},{16,12},{20,24},{24,20},{5,9},{9,5},{13,17},{1... | collective-permute-start | bytes 344072 | tf_op jit(solution)/shard_map/ppermute | solution.py:66
  10.5 14.5 %collective-permute-start.1 = (f32[224,128]{1,0:T(8,128)}, f32[224,128]{1,0:T(8,128)S(1)}, u32[]{:S(2)}, u32[]{:S(2)}) collective-permute-start(f32[224,128]{1,0:T(8,128)} %get-tuple-element.128), channel_id=1, source_target_pairs={{0,4},{4,0},{8,12},{12,8},{16,20},{20,16},{24,28},{28,24},{1,5},{5... | collective-permute-start | bytes 344072 | tf_op jit(solution)/shard_map/ppermute | solution.py:66
  18.6 0.7 copy-start.3
  22.1 2.8 %copy-start.2 = (f32[224,128]{1,0:T(8,128)S(1)}, f32[224,128]{1,0:T(8,128)}, u32[]{:S(2)}) copy-start(f32[224,128]{1,0:T(8,128)} %get-tuple-element.32) | copy-start | bytes 344068
  22.1 11.7 %copy-start.1 = (f32[1,1,896,128]{3,2,1,0:T(8,128)S(1)}, f32[1,1,896,128]{3,2,1,0:T(8,128)}, u32[]{:S(2)}) copy-start(f32[1,1,896,128]{3,2,1,0:T(8,128)} %param.6) | copy-start | bytes 1376260
  24.9 5.3 %collective-permute-start.2 = (f32[224,128]{1,0:T(8,128)S(1)}, f32[224,128]{1,0:T(8,128)S(1)}, u32[]{:S(2)}, u32[]{:S(2)}) collective-permute-start(f32[224,128]{1,0:T(8,128)S(1)} %copy-done.2), channel_id=1, source_target_pairs={{1,2},{2,1},{5,6},{6,5},{9,10},{10,9},{13,14},{14,13},{17,18},{18,... | collective-permute-start | bytes 344072 | tf_op jit(solution)/shard_map/ppermute | solution.py:69
  25.6 8.2 %collective-permute-start.3 = (f32[224,128]{1,0:T(8,128)S(1)}, f32[224,128]{1,0:T(8,128)S(1)}, u32[]{:S(2)}, u32[]{:S(2)}) collective-permute-start(f32[224,128]{1,0:T(8,128)S(1)} %get-tuple-element.33), channel_id=1, source_target_pairs={{0,1},{1,0},{2,3},{3,2},{4,5},{5,4},{6,7},{7,6},{8,9},{9,8},{10,11... | collective-permute-start | bytes 344072 | tf_op jit(solution)/shard_map/ppermute | solution.py:69
  39.5 15.0 %collective-permute-start.6 = (f32[224,128]{1,0:T(8,128)S(1)}, f32[224,128]{1,0:T(8,128)S(1)}, u32[]{:S(2)}, u32[]{:S(2)}) collective-permute-start(f32[224,128]{1,0:T(8,128)S(1)} %get-tuple-element.123), channel_id=1, source_target_pairs={{1,2},{2,1},{5,6},{6,5},{9,10},{10,9},{13,14},{14,13},{17,18},{18,... | collective-permute-start | bytes 344072 | tf_op jit(solution)/shard_map/ppermute | solution.py:75
  40.1 14.4 %collective-permute-start.7 = (f32[224,128]{1,0:T(8,128)S(1)}, f32[224,128]{1,0:T(8,128)S(1)}, u32[]{:S(2)}, u32[]{:S(2)}) collective-permute-start(f32[224,128]{1,0:T(8,128)S(1)} %get-tuple-element.121), channel_id=1, source_target_pairs={{0,1},{1,0},{2,3},{3,2},{4,5},{5,4},{6,7},{7,6},{8,9},{9,8},{10,11... | collective-permute-start | bytes 344072 | tf_op jit(solution)/shard_map/ppermute | solution.py:75
  44.4 10.1 %collective-permute-start.8 = (f32[224,128]{1,0:T(8,128)S(1)}, f32[224,128]{1,0:T(8,128)S(1)}, u32[]{:S(2)}, u32[]{:S(2)}) collective-permute-start(f32[224,128]{1,0:T(8,128)S(1)} %get-tuple-element.122), channel_id=1, source_target_pairs={{4,8},{8,4},{12,16},{16,12},{20,24},{24,20},{5,9},{9,5},{13,17},{1... | collective-permute-start | bytes 344072 | tf_op jit(solution)/shard_map/ppermute | solution.py:75
  45.3 9.2 %collective-permute-start.9 = (f32[224,128]{1,0:T(8,128)S(1)}, f32[224,128]{1,0:T(8,128)S(1)}, u32[]{:S(2)}, u32[]{:S(2)}) collective-permute-start(f32[224,128]{1,0:T(8,128)S(1)} %get-tuple-element.120), channel_id=1, source_target_pairs={{0,4},{4,0},{8,12},{12,8},{16,20},{20,16},{24,28},{28,24},{1,5},{5... | collective-permute-start | bytes 344072 | tf_op jit(solution)/shard_map/ppermute | solution.py:75
  56.0 16.6 %collective-permute-start.10 = (f32[224,128]{1,0:T(8,128)S(1)}, f32[224,128]{1,0:T(8,128)S(1)}, u32[]{:S(2)}, u32[]{:S(2)}) collective-permute-start(f32[224,128]{1,0:T(8,128)S(1)} %get-tuple-element.109), channel_id=1, source_target_pairs={{1,2},{2,1},{5,6},{6,5},{9,10},{10,9},{13,14},{14,13},{17,18},{18,... | collective-permute-start | bytes 344072 | tf_op jit(solution)/shard_map/ppermute | solution.py:75
  56.7 16.0 %collective-permute-start.11 = (f32[224,128]{1,0:T(8,128)S(1)}, f32[224,128]{1,0:T(8,128)S(1)}, u32[]{:S(2)}, u32[]{:S(2)}) collective-permute-start(f32[224,128]{1,0:T(8,128)S(1)} %get-tuple-element.107), channel_id=1, source_target_pairs={{0,1},{1,0},{2,3},{3,2},{4,5},{5,4},{6,7},{7,6},{8,9},{9,8},{10,11... | collective-permute-start | bytes 344072 | tf_op jit(solution)/shard_map/ppermute | solution.py:75
  59.5 13.1 %collective-permute-start.12 = (f32[224,128]{1,0:T(8,128)S(1)}, f32[224,128]{1,0:T(8,128)S(1)}, u32[]{:S(2)}, u32[]{:S(2)}) collective-permute-start(f32[224,128]{1,0:T(8,128)S(1)} %get-tuple-element.108), channel_id=1, source_target_pairs={{4,8},{8,4},{12,16},{16,12},{20,24},{24,20},{5,9},{9,5},{13,17},{1... | collective-permute-start | bytes 344072 | tf_op jit(solution)/shard_map/ppermute | solution.py:75
  60.2 13.4 %collective-permute-start.13 = (f32[224,128]{1,0:T(8,128)S(1)}, f32[224,128]{1,0:T(8,128)S(1)}, u32[]{:S(2)}, u32[]{:S(2)}) collective-permute-start(f32[224,128]{1,0:T(8,128)S(1)} %get-tuple-element.106), channel_id=1, source_target_pairs={{0,4},{4,0},{8,12},{12,8},{16,20},{20,16},{24,28},{28,24},{1,5},{5... | collective-permute-start | bytes 344072 | tf_op jit(solution)/shard_map/ppermute | solution.py:75
  75.2 8.7 %collective-permute-start.14 = (f32[224,128]{1,0:T(8,128)S(1)}, f32[224,128]{1,0:T(8,128)S(1)}, u32[]{:S(2)}, u32[]{:S(2)}) collective-permute-start(f32[224,128]{1,0:T(8,128)S(1)} %get-tuple-element.103), channel_id=1, source_target_pairs={{1,2},{2,1},{5,6},{6,5},{9,10},{10,9},{13,14},{14,13},{17,18},{18,... | collective-permute-start | bytes 344072 | tf_op jit(solution)/shard_map/ppermute | solution.py:75
  75.9 8.8 %collective-permute-start.15 = (f32[224,128]{1,0:T(8,128)S(1)}, f32[224,128]{1,0:T(8,128)S(1)}, u32[]{:S(2)}, u32[]{:S(2)}) collective-permute-start(f32[224,128]{1,0:T(8,128)S(1)} %get-tuple-element.101), channel_id=1, source_target_pairs={{0,1},{1,0},{2,3},{3,2},{4,5},{5,4},{6,7},{7,6},{8,9},{9,8},{10,11... | collective-permute-start | bytes 344072 | tf_op jit(solution)/shard_map/ppermute | solution.py:75
  78.7 6.0 %collective-permute-start.16 = (f32[224,128]{1,0:T(8,128)S(1)}, f32[224,128]{1,0:T(8,128)S(1)}, u32[]{:S(2)}, u32[]{:S(2)}) collective-permute-start(f32[224,128]{1,0:T(8,128)S(1)} %get-tuple-element.102), channel_id=1, source_target_pairs={{4,8},{8,4},{12,16},{16,12},{20,24},{24,20},{5,9},{9,5},{13,17},{1... | collective-permute-start | bytes 344072 | tf_op jit(solution)/shard_map/ppermute | solution.py:75
  79.4 5.4 %collective-permute-start.17 = (f32[224,128]{1,0:T(8,128)S(1)}, f32[224,128]{1,0:T(8,128)S(1)}, u32[]{:S(2)}, u32[]{:S(2)}) collective-permute-start(f32[224,128]{1,0:T(8,128)S(1)} %get-tuple-element.100), channel_id=1, source_target_pairs={{0,4},{4,0},{8,12},{12,8},{16,20},{20,16},{24,28},{28,24},{1,5},{5... | collective-permute-start | bytes 344072 | tf_op jit(solution)/shard_map/ppermute | solution.py:75
  86.4 9.6 %collective-permute-start.18 = (f32[224,128]{1,0:T(8,128)S(1)}, f32[224,128]{1,0:T(8,128)S(1)}, u32[]{:S(2)}, u32[]{:S(2)}) collective-permute-start(f32[224,128]{1,0:T(8,128)S(1)} %get-tuple-element.97), channel_id=1, source_target_pairs={{1,2},{2,1},{5,6},{6,5},{9,10},{10,9},{13,14},{14,13},{17,18},{18,... | collective-permute-start | bytes 344072 | tf_op jit(solution)/shard_map/ppermute | solution.py:75
  87.1 8.9 %collective-permute-start.19 = (f32[224,128]{1,0:T(8,128)S(1)}, f32[224,128]{1,0:T(8,128)S(1)}, u32[]{:S(2)}, u32[]{:S(2)}) collective-permute-start(f32[224,128]{1,0:T(8,128)S(1)} %get-tuple-element.95), channel_id=1, source_target_pairs={{0,1},{1,0},{2,3},{3,2},{4,5},{5,4},{6,7},{7,6},{8,9},{9,8},{10,11... | collective-permute-start | bytes 344072 | tf_op jit(solution)/shard_map/ppermute | solution.py:75
  89.8 6.2 %collective-permute-start.20 = (f32[224,128]{1,0:T(8,128)S(1)}, f32[224,128]{1,0:T(8,128)S(1)}, u32[]{:S(2)}, u32[]{:S(2)}) collective-permute-start(f32[224,128]{1,0:T(8,128)S(1)} %get-tuple-element.96), channel_id=1, source_target_pairs={{4,8},{8,4},{12,16},{16,12},{20,24},{24,20},{5,9},{9,5},{13,17},{1... | collective-permute-start | bytes 344072 | tf_op jit(solution)/shard_map/ppermute | solution.py:75
  90.5 5.5 %collective-permute-start.21 = (f32[224,128]{1,0:T(8,128)S(1)}, f32[224,128]{1,0:T(8,128)S(1)}, u32[]{:S(2)}, u32[]{:S(2)}) collective-permute-start(f32[224,128]{1,0:T(8,128)S(1)} %get-tuple-element.94), channel_id=1, source_target_pairs={{0,4},{4,0},{8,12},{12,8},{16,20},{20,16},{24,28},{28,24},{1,5},{5... | collective-permute-start | bytes 344072 | tf_op jit(solution)/shard_map/ppermute | solution.py:75

commit v13 on v11

--- a/solution.py
+++ b/solution.py
@@ -63,13 +63,13 @@
         sends.append((jnp.where(even, low, high), swap_pairs(lax.axis_size(axis), 1), axis))
         sends.append((jnp.where(even, high, low), swap_pairs(lax.axis_size(axis), 0), axis))
     if one_axis_at_a_time:
-        first = [lax.ppermute(block, axis, pairs) for block, pairs, axis in sends[2:]]
-        later, first = lax.optimization_barrier(([block for block, _, _ in sends[:2]], first))
+        rest = [sends[0], sends[1], sends[3]]
+        first = lax.ppermute(sends[2][0], sends[2][2], sends[2][1])
+        later, first = lax.optimization_barrier(([block for block, _, _ in rest], first))
         second = [
-            lax.ppermute(block, axis, pairs)
-            for block, (_, pairs, axis) in zip(later, sends[:2])
+            lax.ppermute(block, axis, pairs) for block, (_, pairs, axis) in zip(later, rest)
         ]
-        received = lax.optimization_barrier(second + first)
+        received = lax.optimization_barrier([second[0], second[1], first, second[2]])
     else:
         received = lax.optimization_barrier(
             [lax.ppermute(block, axis, pairs) for block, pairs, axis in sends]

time: 90.5 us -> 91 us (level)
  starting transfers between devices: 40.9 us -> 44.3 us
  waiting for transfers between devices: 17.9 us -> 14.8 us
    ppermute x2, starting transfers between devices: 3.04 us -> 6.36 us  [from_behind(): return lax.ppermute(value, axis, pairs)]
    ppermute x20 -> x19, waiting for transfers between devices: 10.8 us -> 7.67 us  [face_sum_parts(): lax.ppermute(block, axis, pairs)]
    select_n x5 -> x4, other arithmetic: 1.95 us -> 0.14 us  [face_sum_parts(): jnp.where(even, high, low)]
    select_n x0 -> x1, other arithmetic: none -> 1.79 us  [face_sum_parts(): jnp.where(even, low, high)]
    ppermute x20 -> x19, starting transfers between devices: 37.9 us -> 37.3 us  [face_sum_parts(): lax.ppermute(block, axis, pairs)]
  transfers between devices with their start and end apart: 22 -> 22, of which waited for: 5 -> 6; matrix products, arithmetic and copies ran while one was open for 16% -> 16% of each run, Pallas kernels for 0% -> 0%
where the time goes in v13:
time: 91 us; the launch traced here: 89.6 us
  starting transfers between devices  44.3 us (49%)
  matrix products  15.9 us (17%)
  waiting for transfers between devices  14.8 us (16%)
  other arithmetic  6.8 us (7%)
  between operations  4.22 us (5%)
  local copies, waits for them, and re-layouts  3.51 us (4%)
    ppermute x19, starting transfers between devices, face_sum_parts(): lax.ppermute(block, axis, pairs)  37.3 us
    ppermute x19, waiting for transfers between devices, face_sum_parts(): lax.ppermute(block, axis, pairs)  7.67 us
    ppermute x2, waiting for transfers between devices, from_behind(): return lax.ppermute(value, axis, pairs)  7.17 us
    ppermute x2, starting transfers between devices, from_behind(): return lax.ppermute(value, axis, pairs)  6.36 us
    dot_general x3, matrix products, slot_pieces(): return jnp.dot(to_slots, side, preferred_element_type=jnp.float32)  4.69 us
    dot_general x3, matrix products, slot_pieces(): jnp.dot(stacked, to_rows, preferred_element_type=jnp.float32)  3.98 us
    dot_general x6, matrix products, bf16x3_apply(): both = jnp.dot(op_high, pair, preferred_element_type=jnp.float32)  3.04 us
    dot_general x6, matrix products, bf16x3_apply(): jnp.dot(op_mid, pair[:, :cols], preferred_element_type=jnp.float32)  2.91 us
  transfers between devices with their start and end apart: 22, of which 6 were waited for; matrix products, arithmetic and copies ran while one was open for 16% of the time, Pallas kernels for 0%

profile of v13, /device:TPU:0, one launch (start us, length us, event | category | flops | bytes accessed | tf_op | source)
XLA Modules:
  0.0 89.6 jit_solution(15548980248020587818)
XLA Ops:
  0.7 2.3 %slice_bitcast_fusion = (f32[128,896]{1,0:T(8,128)}, f32[128,896]{1,0:T(8,128)}) fusion(f32[1,1,2,128,896]{4,3,2,1,0:T(8,128)} %param.8), kind=kLoop, calls=%fused_computation.125 | loop fusion | bytes 1835008 | tf_op jit(solution)/shard_map/squeeze | solution.py:117
  3.0 1.8 %slice_select_fusion.16 = (f32[224,128]{1,0:T(8,128)}, f32[224,128]{1,0:T(8,128)S(1)}, f32[224,128]{1,0:T(8,128)S(1)}, f32[224,128]{1,0:T(8,128)}) fusion(f32[896,128]{1,0:T(8,128)} %bitcast.60, pred[]{:T(512)S(6)} %eq.100, pred[]{:T(512)S(6)} %eq.101), kind=kLoop, calls=%fused_computation.175 | loop fusion | flops 114688 | bytes 917506 | tf_op jit(solution)/shard_map/jit(_where)/select_n | solution.py:63
  4.8 0.7 collective-permute-start
  5.4 6.4 %collective-permute-start.4 = (f32[128,896]{1,0:T(8,128)}, f32[128,896]{1,0:T(8,128)S(1)}, u32[]{:S(2)}, u32[]{:S(2)}) collective-permute-start(f32[128,896]{1,0:T(8,128)} %get-tuple-element.38), channel_id=1, source_target_pairs={{0,24},{4,28},{8,0},{12,4},{16,8},{20,12},{24,16},{28,20},{1,25},{... | collective-permute-start | bytes 1376264 | tf_op jit(solution)/shard_map/ppermute | solution.py:22
  11.8 0.6 fusion.151
  14.8 1.3 %reduce = s32[896]{0:T(1024)} reduce(s32[1,1,896]{2,1,0:T(1,128)} %param.11, s32[]{:T(128)} %constant.99.clone.1), dimensions={0,1}, to_apply=%param.11.reduce_sub_computation | reduce | bytes 7172 | tf_op args[5]
  17.0 0.3 copy-done.3
  17.4 2.6 %convolution_convert_fusion = bf16[1280,896]{0,1:T(8,128)(2,1)S(1)} fusion(bf16[640,896]{1,0:T(8,128)(2,1)S(1)} %get-tuple-element.69, bf16[640,896]{1,0:T(8,128)(2,1)S(1)} %get-tuple-element.68, bf16[896]{0:T(1024)(128)(2,1)S(1)} %select_select_fusion, s32[896]{0:T(1024)S(1)} %copy-done.3), kind=kOutput, calls=%fused_computation.1 | convolution fusion | flops 2062548992 | bytes 4592896 | tf_op jit(solution)/shard_map/dot_general | solution.py:92
  20.2 2.7 %fusion.152 = (bf16[896,1792]{1,0:T(8,128)(2,1)S(1)}, f32[896,1792]{1,0:T(8,128)S(1)}) fusion(bf16[640,896]{0,1:T(8,128)(2,1)S(1)} %get-tuple-element.67, bf16[640,896]{0,1:T(8,128)(2,1)S(1)} %get-tuple-element.66, bf16[896]{0:T(1024)(128)(2,1)S(1)} %select_select_fusion, s32[896]{0:T(1024)S(1)} %copy-done.3), kind=kOutput, calls=%fused_computation.242 | convolution fusion | flops 2063122432 | bytes 11932928 | tf_op jit(solution)/shard_map/dot_general | solution.py:94
  23.0 0.7 collective-permute-start.1
  23.7 4.3 %collective-permute-start.2 = (f32[224,128]{1,0:T(8,128)S(1)}, f32[224,128]{1,0:T(8,128)S(1)}, u32[]{:S(2)}, u32[]{:S(2)}) collective-permute-start(f32[224,128]{1,0:T(8,128)S(1)} %get-tuple-element.31), channel_id=1, source_target_pairs={{0,1},{1,0},{2,3},{3,2},{4,5},{5,4},{6,7},{7,6},{8,9},{9,8},{10,11... | collective-permute-start | bytes 344072 | tf_op jit(solution)/shard_map/ppermute | solution.py:70
  28.3 5.6 %collective-permute-done.2 = f32[224,128]{1,0:T(8,128)S(1)} collective-permute-done((f32[224,128]{1,0:T(8,128)S(1)}, f32[224,128]{1,0:T(8,128)S(1)}, u32[]{:S(2)}, u32[]{:S(2)}) %collective-permute-start.2) | collective-permute-done | bytes 114720 | tf_op jit(solution)/shard_map/ppermute | solution.py:70
  34.1 0.6 fusion.28
  34.7 0.6 fusion.14
  35.9 7.2 %collective-permute-done.5 = f32[128,896]{1,0:T(8,128)S(1)} collective-permute-done((f32[128,896]{1,0:T(8,128)}, f32[128,896]{1,0:T(8,128)S(1)}, u32[]{:S(2)}, u32[]{:S(2)}) %collective-permute-start.5) | collective-permute-done | bytes 458784 | tf_op jit(solution)/shard_map/ppermute | solution.py:22
  43.7 0.3 fusion.105
  44.0 0.3 fusion.100
  44.3 0.7 fusion.58
  45.1 0.7 collective-permute-start.6
  45.7 4.3 %collective-permute-start.7 = (f32[224,128]{1,0:T(8,128)S(1)}, f32[224,128]{1,0:T(8,128)S(1)}, u32[]{:S(2)}, u32[]{:S(2)}) collective-permute-start(f32[224,128]{1,0:T(8,128)S(1)} %get-tuple-element.121), channel_id=1, source_target_pairs={{0,1},{1,0},{2,3},{3,2},{4,5},{5,4},{6,7},{7,6},{8,9},{9,8},{10,11... | collective-permute-start | bytes 344072 | tf_op jit(solution)/shard_map/ppermute | solution.py:75
  50.0 0.8 collective-permute-start.8
  50.9 1.1 %collective-permute-start.9 = (f32[224,128]{1,0:T(8,128)S(1)}, f32[224,128]{1,0:T(8,128)S(1)}, u32[]{:S(2)}, u32[]{:S(2)}) collective-permute-start(f32[224,128]{1,0:T(8,128)S(1)} %get-tuple-element.120), channel_id=1, source_target_pairs={{0,4},{4,0},{8,12},{12,8},{16,20},{20,16},{24,28},{28,24},{1,5},{5... | collective-permute-start | bytes 344072 | tf_op jit(solution)/shard_map/ppermute | solution.py:75
  52.0 0.7 fusion.29
  52.7 0.7 fusion.30
  53.5 1.0 %fusion.72 = f32[896,1792]{1,0:T(8,128)S(1)} fusion(bf16[128,896]{1,0:T(8,128)(2,1)S(1)} %get-tuple-element.115, bf16[128,896]{1,0:T(8,128)(2,1)S(1)} %get-tuple-element.114, bf16[896,256]{1,0:T(8,128)(2,1)S(1)} %select_convert_fusion.13), kind=kOutput, calls=%fused_computation.93 | convolution fusion | flops 411959296 | bytes 7110656 | tf_op jit(solution)/shard_map/dot_general | solution.py:94
  54.4 1.0 %add_convert_fusion = bf16[896,1792]{1,0:T(8,128)(2,1)S(1)} fusion(f32[896,1792]{1,0:T(8,128)S(1)} %get-tuple-element.139, f32[896,1792]{1,0:T(8,128)S(1)} %fusion.72, bf16[128,896]{1,0:T(8,128)(2,1)S(1)} %get-tuple-element.111, bf16[128,896]{1,0:T(8,128)(2,1)S(1)} %get-tuple-element.110, bf16[896,256]{1,0:T(8,128)(2,1)S(1)} %select_convert_fusion.13), kind=kOutput, calls=%fused_computation | convolution fusion | flops 416776192 | bytes 16744448 | tf_op jit(solution)/shard_map/dot_general | solution.py:94
  55.7 0.6 fusion.41
  56.4 0.6 fusion.43
  57.0 0.7 collective-permute-start.10
  57.7 2.8 %collective-permute-start.11 = (f32[224,128]{1,0:T(8,128)S(1)}, f32[224,128]{1,0:T(8,128)S(1)}, u32[]{:S(2)}, u32[]{:S(2)}) collective-permute-start(f32[224,128]{1,0:T(8,128)S(1)} %get-tuple-element.107), channel_id=1, source_target_pairs={{0,1},{1,0},{2,3},{3,2},{4,5},{5,4},{6,7},{7,6},{8,9},{9,8},{10,11... | collective-permute-start | bytes 344072 | tf_op jit(solution)/shard_map/ppermute | solution.py:75
  60.5 0.7 collective-permute-start.12
  61.1 4.2 %collective-permute-start.13 = (f32[224,128]{1,0:T(8,128)S(1)}, f32[224,128]{1,0:T(8,128)S(1)}, u32[]{:S(2)}, u32[]{:S(2)}) collective-permute-start(f32[224,128]{1,0:T(8,128)S(1)} %get-tuple-element.106), channel_id=1, source_target_pairs={{0,4},{4,0},{8,12},{12,8},{16,20},{20,16},{24,28},{28,24},{1,5},{5... | collective-permute-start | bytes 344072 | tf_op jit(solution)/shard_map/ppermute | solution.py:75
  65.3 1.0 %collective-permute-done.11 = f32[224,128]{1,0:T(8,128)S(1)} collective-permute-done((f32[224,128]{1,0:T(8,128)S(1)}, f32[224,128]{1,0:T(8,128)S(1)}, u32[]{:S(2)}, u32[]{:S(2)}) %collective-permute-start.11) | collective-permute-done | bytes 114720 | tf_op jit(solution)/shard_map/ppermute | solution.py:75
  66.6 0.6 fusion.39
  67.3 0.6 fusion.46
  67.9 0.7 collective-permute-start.14
  68.6 2.7 %collective-permute-start.15 = (f32[224,128]{1,0:T(8,128)S(1)}, f32[224,128]{1,0:T(8,128)S(1)}, u32[]{:S(2)}, u32[]{:S(2)}) collective-permute-start(f32[224,128]{1,0:T(8,128)S(1)} %get-tuple-element.101), channel_id=1, source_target_pairs={{0,1},{1,0},{2,3},{3,2},{4,5},{5,4},{6,7},{7,6},{8,9},{9,8},{10,11... | collective-permute-start | bytes 344072 | tf_op jit(solution)/shard_map/ppermute | solution.py:75
  71.3 0.7 collective-permute-start.16
  72.0 4.5 %collective-permute-start.17 = (f32[224,128]{1,0:T(8,128)S(1)}, f32[224,128]{1,0:T(8,128)S(1)}, u32[]{:S(2)}, u32[]{:S(2)}) collective-permute-start(f32[224,128]{1,0:T(8,128)S(1)} %get-tuple-element.100), channel_id=1, source_target_pairs={{0,4},{4,0},{8,12},{12,8},{16,20},{20,16},{24,28},{28,24},{1,5},{5... | collective-permute-start | bytes 344072 | tf_op jit(solution)/shard_map/ppermute | solution.py:75
  76.5 0.8 collective-permute-done.15
  77.7 0.6 fusion.37
  78.3 0.6 fusion.49
  79.0 0.7 collective-permute-start.18
  79.7 2.8 %collective-permute-start.19 = (f32[224,128]{1,0:T(8,128)S(1)}, f32[224,128]{1,0:T(8,128)S(1)}, u32[]{:S(2)}, u32[]{:S(2)}) collective-permute-start(f32[224,128]{1,0:T(8,128)S(1)} %get-tuple-element.95), channel_id=1, source_target_pairs={{0,1},{1,0},{2,3},{3,2},{4,5},{5,4},{6,7},{7,6},{8,9},{9,8},{10,11... | collective-permute-start | bytes 344072 | tf_op jit(solution)/shard_map/ppermute | solution.py:75
  82.5 0.7 collective-permute-start.20
  83.1 4.5 %collective-permute-start.21 = (f32[224,128]{1,0:T(8,128)S(1)}, f32[224,128]{1,0:T(8,128)S(1)}, u32[]{:S(2)}, u32[]{:S(2)}) collective-permute-start(f32[224,128]{1,0:T(8,128)S(1)} %get-tuple-element.94), channel_id=1, source_target_pairs={{0,4},{4,0},{8,12},{12,8},{16,20},{20,16},{24,28},{28,24},{1,5},{5... | collective-permute-start | bytes 344072 | tf_op jit(solution)/shard_map/ppermute | solution.py:75
  87.6 1.0 %add_add_fusion = f32[1,1,896,128]{3,2,1,0:T(8,128)} fusion(f32[1,1,224,128]{3,2,1,0:T(8,128)S(1)} %bitcast.48, f32[1,1,224,128]{3,2,1,0:T(8,128)S(1)} %bitcast.50, f32[1,1,224,128]{3,2,1,0:T(8,128)S(1)} %bitcast.46, f32[1,1,224,128]{3,2,1,0:T(8,128)S(1)} %bitcast.44, f32[1,1,224,128]{3,2,1,0:T(8,128)S(1)} %bitcast.56, f32[1,1,224,128]{3,2,1,0:T(8,128)S(1)} %bitcast.58, ...), kind=kLoop, calls=%fused_computation.120 | loop fusion | flops 3211264 | bytes 2293760 | tf_op jit(solution)/shard_map/add | solution.py:166
  88.7 0.9 maximum_subtract_fusion.6
  (61 shorter events, 3.3 us)
Async XLA Ops:
  0.6 16.1 %copy-start = (f32[1,1,640,896]{3,2,1,0:T(8,128)S(1)}, f32[1,1,640,896]{3,2,1,0:T(8,128)}, u32[]{:S(2)}) copy-start(f32[1,1,640,896]{3,2,1,0:T(8,128)} %param.7) | copy-start | bytes 6881284
  0.7 11.1 %copy-start.4 = (s32[1,1,2]{2,1,0:T(1,128)S(1)}, s32[1,1,2]{2,1,0:T(1,128)}, u32[]{:S(2)}) copy-start(s32[1,1,2]{2,1,0:T(1,128)} %param.9) | copy-start | bytes 28
  4.8 18.3 %collective-permute-start = (f32[224,128]{1,0:T(8,128)}, f32[224,128]{1,0:T(8,128)S(1)}, u32[]{:S(2)}, u32[]{:S(2)}) collective-permute-start(f32[224,128]{1,0:T(8,128)} %get-tuple-element.128), channel_id=1, source_target_pairs={{4,8},{8,4},{12,16},{16,12},{20,24},{24,20},{5,9},{9,5},{13,17},{1... | collective-permute-start | bytes 344072 | tf_op jit(solution)/shard_map/ppermute | solution.py:67
  5.4 30.0 %collective-permute-start.4 = (f32[128,896]{1,0:T(8,128)}, f32[128,896]{1,0:T(8,128)S(1)}, u32[]{:S(2)}, u32[]{:S(2)}) collective-permute-start(f32[128,896]{1,0:T(8,128)} %get-tuple-element.38), channel_id=1, source_target_pairs={{0,24},{4,28},{8,0},{12,4},{16,8},{20,12},{24,16},{28,20},{1,25},{... | collective-permute-start | bytes 1376264 | tf_op jit(solution)/shard_map/ppermute | solution.py:22
  11.8 31.3 %collective-permute-start.5 = (f32[128,896]{1,0:T(8,128)}, f32[128,896]{1,0:T(8,128)S(1)}, u32[]{:S(2)}, u32[]{:S(2)}) collective-permute-start(f32[128,896]{1,0:T(8,128)} %get-tuple-element.39), channel_id=1, source_target_pairs={{0,16},{4,20},{8,24},{12,28},{16,0},{20,4},{24,8},{28,12},{1,17},{... | collective-permute-start | bytes 1376264 | tf_op jit(solution)/shard_map/ppermute | solution.py:22
  16.7 0.7 copy-start.3
  20.2 2.8 %copy-start.2 = (f32[224,128]{1,0:T(8,128)S(1)}, f32[224,128]{1,0:T(8,128)}, u32[]{:S(2)}) copy-start(f32[224,128]{1,0:T(8,128)} %get-tuple-element.30) | copy-start | bytes 344068
  20.2 13.7 %copy-start.1 = (f32[1,1,896,128]{3,2,1,0:T(8,128)S(1)}, f32[1,1,896,128]{3,2,1,0:T(8,128)}, u32[]{:S(2)}) copy-start(f32[1,1,896,128]{3,2,1,0:T(8,128)} %param.6) | copy-start | bytes 1376260
  23.0 5.3 %collective-permute-start.1 = (f32[224,128]{1,0:T(8,128)S(1)}, f32[224,128]{1,0:T(8,128)S(1)}, u32[]{:S(2)}, u32[]{:S(2)}) collective-permute-start(f32[224,128]{1,0:T(8,128)S(1)} %copy-done.2), channel_id=1, source_target_pairs={{1,2},{2,1},{5,6},{6,5},{9,10},{10,9},{13,14},{14,13},{17,18},{18,... | collective-permute-start | bytes 344072 | tf_op jit(solution)/shard_map/ppermute | solution.py:70
  23.7 10.2 %collective-permute-start.2 = (f32[224,128]{1,0:T(8,128)S(1)}, f32[224,128]{1,0:T(8,128)S(1)}, u32[]{:S(2)}, u32[]{:S(2)}) collective-permute-start(f32[224,128]{1,0:T(8,128)S(1)} %get-tuple-element.31), channel_id=1, source_target_pairs={{0,1},{1,0},{2,3},{3,2},{4,5},{5,4},{6,7},{7,6},{8,9},{9,8},{10,11... | collective-permute-start | bytes 344072 | tf_op jit(solution)/shard_map/ppermute | solution.py:70
  28.0 5.9 %collective-permute-start.3 = (f32[224,128]{1,0:T(8,128)S(1)}, f32[224,128]{1,0:T(8,128)S(1)}, u32[]{:S(2)}, u32[]{:S(2)}) collective-permute-start(f32[224,128]{1,0:T(8,128)S(1)} %get-tuple-element.33), channel_id=1, source_target_pairs={{0,4},{4,0},{8,12},{12,8},{16,20},{20,16},{24,28},{28,24},{1,5},{5... | collective-permute-start | bytes 344072 | tf_op jit(solution)/shard_map/ppermute | solution.py:70
  45.1 10.4 %collective-permute-start.6 = (f32[224,128]{1,0:T(8,128)S(1)}, f32[224,128]{1,0:T(8,128)S(1)}, u32[]{:S(2)}, u32[]{:S(2)}) collective-permute-start(f32[224,128]{1,0:T(8,128)S(1)} %get-tuple-element.123), channel_id=1, source_target_pairs={{1,2},{2,1},{5,6},{6,5},{9,10},{10,9},{13,14},{14,13},{17,18},{18,... | collective-permute-start | bytes 344072 | tf_op jit(solution)/shard_map/ppermute | solution.py:75
  45.7 9.8 %collective-permute-start.7 = (f32[224,128]{1,0:T(8,128)S(1)}, f32[224,128]{1,0:T(8,128)S(1)}, u32[]{:S(2)}, u32[]{:S(2)}) collective-permute-start(f32[224,128]{1,0:T(8,128)S(1)} %get-tuple-element.121), channel_id=1, source_target_pairs={{0,1},{1,0},{2,3},{3,2},{4,5},{5,4},{6,7},{7,6},{8,9},{9,8},{10,11... | collective-permute-start | bytes 344072 | tf_op jit(solution)/shard_map/ppermute | solution.py:75
  50.0 5.5 %collective-permute-start.8 = (f32[224,128]{1,0:T(8,128)S(1)}, f32[224,128]{1,0:T(8,128)S(1)}, u32[]{:S(2)}, u32[]{:S(2)}) collective-permute-start(f32[224,128]{1,0:T(8,128)S(1)} %get-tuple-element.122), channel_id=1, source_target_pairs={{4,8},{8,4},{12,16},{16,12},{20,24},{24,20},{5,9},{9,5},{13,17},{1... | collective-permute-start | bytes 344072 | tf_op jit(solution)/shard_map/ppermute | solution.py:75
  50.9 4.7 %collective-permute-start.9 = (f32[224,128]{1,0:T(8,128)S(1)}, f32[224,128]{1,0:T(8,128)S(1)}, u32[]{:S(2)}, u32[]{:S(2)}) collective-permute-start(f32[224,128]{1,0:T(8,128)S(1)} %get-tuple-element.120), channel_id=1, source_target_pairs={{0,4},{4,0},{8,12},{12,8},{16,20},{20,16},{24,28},{28,24},{1,5},{5... | collective-permute-start | bytes 344072 | tf_op jit(solution)/shard_map/ppermute | solution.py:75
  57.0 8.3 %collective-permute-start.10 = (f32[224,128]{1,0:T(8,128)S(1)}, f32[224,128]{1,0:T(8,128)S(1)}, u32[]{:S(2)}, u32[]{:S(2)}) collective-permute-start(f32[224,128]{1,0:T(8,128)S(1)} %get-tuple-element.109), channel_id=1, source_target_pairs={{1,2},{2,1},{5,6},{6,5},{9,10},{10,9},{13,14},{14,13},{17,18},{18,... | collective-permute-start | bytes 344072 | tf_op jit(solution)/shard_map/ppermute | solution.py:75
  57.7 8.6 %collective-permute-start.11 = (f32[224,128]{1,0:T(8,128)S(1)}, f32[224,128]{1,0:T(8,128)S(1)}, u32[]{:S(2)}, u32[]{:S(2)}) collective-permute-start(f32[224,128]{1,0:T(8,128)S(1)} %get-tuple-element.107), channel_id=1, source_target_pairs={{0,1},{1,0},{2,3},{3,2},{4,5},{5,4},{6,7},{7,6},{8,9},{9,8},{10,11... | collective-permute-start | bytes 344072 | tf_op jit(solution)/shard_map/ppermute | solution.py:75
  60.5 5.8 %collective-permute-start.12 = (f32[224,128]{1,0:T(8,128)S(1)}, f32[224,128]{1,0:T(8,128)S(1)}, u32[]{:S(2)}, u32[]{:S(2)}) collective-permute-start(f32[224,128]{1,0:T(8,128)S(1)} %get-tuple-element.108), channel_id=1, source_target_pairs={{4,8},{8,4},{12,16},{16,12},{20,24},{24,20},{5,9},{9,5},{13,17},{1... | collective-permute-start | bytes 344072 | tf_op jit(solution)/shard_map/ppermute | solution.py:75
  61.1 5.2 %collective-permute-start.13 = (f32[224,128]{1,0:T(8,128)S(1)}, f32[224,128]{1,0:T(8,128)S(1)}, u32[]{:S(2)}, u32[]{:S(2)}) collective-permute-start(f32[224,128]{1,0:T(8,128)S(1)} %get-tuple-element.106), channel_id=1, source_target_pairs={{0,4},{4,0},{8,12},{12,8},{16,20},{20,16},{24,28},{28,24},{1,5},{5... | collective-permute-start | bytes 344072 | tf_op jit(solution)/shard_map/ppermute | solution.py:75
  67.9 8.6 %collective-permute-start.14 = (f32[224,128]{1,0:T(8,128)S(1)}, f32[224,128]{1,0:T(8,128)S(1)}, u32[]{:S(2)}, u32[]{:S(2)}) collective-permute-start(f32[224,128]{1,0:T(8,128)S(1)} %get-tuple-element.103), channel_id=1, source_target_pairs={{1,2},{2,1},{5,6},{6,5},{9,10},{10,9},{13,14},{14,13},{17,18},{18,... | collective-permute-start | bytes 344072 | tf_op jit(solution)/shard_map/ppermute | solution.py:75
  68.6 8.7 %collective-permute-start.15 = (f32[224,128]{1,0:T(8,128)S(1)}, f32[224,128]{1,0:T(8,128)S(1)}, u32[]{:S(2)}, u32[]{:S(2)}) collective-permute-start(f32[224,128]{1,0:T(8,128)S(1)} %get-tuple-element.101), channel_id=1, source_target_pairs={{0,1},{1,0},{2,3},{3,2},{4,5},{5,4},{6,7},{7,6},{8,9},{9,8},{10,11... | collective-permute-start | bytes 344072 | tf_op jit(solution)/shard_map/ppermute | solution.py:75
  71.3 6.0 %collective-permute-start.16 = (f32[224,128]{1,0:T(8,128)S(1)}, f32[224,128]{1,0:T(8,128)S(1)}, u32[]{:S(2)}, u32[]{:S(2)}) collective-permute-start(f32[224,128]{1,0:T(8,128)S(1)} %get-tuple-element.102), channel_id=1, source_target_pairs={{4,8},{8,4},{12,16},{16,12},{20,24},{24,20},{5,9},{9,5},{13,17},{1... | collective-permute-start | bytes 344072 | tf_op jit(solution)/shard_map/ppermute | solution.py:75
  72.0 5.4 %collective-permute-start.17 = (f32[224,128]{1,0:T(8,128)S(1)}, f32[224,128]{1,0:T(8,128)S(1)}, u32[]{:S(2)}, u32[]{:S(2)}) collective-permute-start(f32[224,128]{1,0:T(8,128)S(1)} %get-tuple-element.100), channel_id=1, source_target_pairs={{0,4},{4,0},{8,12},{12,8},{16,20},{20,16},{24,28},{28,24},{1,5},{5... | collective-permute-start | bytes 344072 | tf_op jit(solution)/shard_map/ppermute | solution.py:75
  79.0 9.7 %collective-permute-start.18 = (f32[224,128]{1,0:T(8,128)S(1)}, f32[224,128]{1,0:T(8,128)S(1)}, u32[]{:S(2)}, u32[]{:S(2)}) collective-permute-start(f32[224,128]{1,0:T(8,128)S(1)} %get-tuple-element.97), channel_id=1, source_target_pairs={{1,2},{2,1},{5,6},{6,5},{9,10},{10,9},{13,14},{14,13},{17,18},{18,... | collective-permute-start | bytes 344072 | tf_op jit(solution)/shard_map/ppermute | solution.py:75
  79.7 9.0 %collective-permute-start.19 = (f32[224,128]{1,0:T(8,128)S(1)}, f32[224,128]{1,0:T(8,128)S(1)}, u32[]{:S(2)}, u32[]{:S(2)}) collective-permute-start(f32[224,128]{1,0:T(8,128)S(1)} %get-tuple-element.95), channel_id=1, source_target_pairs={{0,1},{1,0},{2,3},{3,2},{4,5},{5,4},{6,7},{7,6},{8,9},{9,8},{10,11... | collective-permute-start | bytes 344072 | tf_op jit(solution)/shard_map/ppermute | solution.py:75
  82.5 6.2 %collective-permute-start.20 = (f32[224,128]{1,0:T(8,128)S(1)}, f32[224,128]{1,0:T(8,128)S(1)}, u32[]{:S(2)}, u32[]{:S(2)}) collective-permute-start(f32[224,128]{1,0:T(8,128)S(1)} %get-tuple-element.96), channel_id=1, source_target_pairs={{4,8},{8,4},{12,16},{16,12},{20,24},{24,20},{5,9},{9,5},{13,17},{1... | collective-permute-start | bytes 344072 | tf_op jit(solution)/shard_map/ppermute | solution.py:75
  83.1 5.5 %collective-permute-start.21 = (f32[224,128]{1,0:T(8,128)S(1)}, f32[224,128]{1,0:T(8,128)S(1)}, u32[]{:S(2)}, u32[]{:S(2)}) collective-permute-start(f32[224,128]{1,0:T(8,128)S(1)} %get-tuple-element.94), channel_id=1, source_target_pairs={{0,4},{4,0},{8,12},{12,8},{16,20},{20,16},{24,28},{28,24},{1,5},{5... | collective-permute-start | bytes 344072 | tf_op jit(solution)/shard_map/ppermute | solution.py:75

commit v14 on v11

--- a/solution.py
+++ b/solution.py
@@ -186,8 +186,13 @@
                     (placed[:, :cols] + placed[:, cols : 2 * cols]) + placed[:, 2 * cols :]
                 )
         else:
-            local = bf16x3_apply(op_high, op_mid, dir_pair, cols)
-        faces = [local[face_id * width : (face_id + 1) * width] for face_id in range(4)]
+            local = None
+        if local is None:
+            y_faces = bf16x3_apply(op_high[2 * width :], op_mid[2 * width :], dir_pair, cols)
+            x_faces = bf16x3_apply(op_high[: 2 * width], op_mid[: 2 * width], dir_pair, cols)
+            faces = [x_faces[:width], x_faces[width:], y_faces[:width], y_faces[width:]]
+        else:
+            faces = [local[face_id * width : (face_id + 1) * width] for face_id in range(4)]
         residual = residual - face_sum_parts(faces)
         if step_id + 1 < ITERS:
             rho_next = 1.0 / (2.0 * sigma_value - rho_value)

time: 90.5 us -> 100 us (1.10); the launches traced: 89.4 us -> 100 us
  waiting for transfers between devices: 17.9 us -> 26.9 us
    ppermute x20, waiting for transfers between devices: 10.8 us -> 19.8 us  [face_sum_parts(): lax.ppermute(block, axis, pairs)]
    dot_general x6 -> x9, matrix products: 2.9 us -> 3.41 us  [bf16x3_apply(): jnp.dot(op_mid, pair[:, :cols], preferred_element_type=jnp.float32)]
    dot_general x6 -> x9, matrix products: 3.05 us -> 3.54 us  [bf16x3_apply(): both = jnp.dot(op_high, pair, preferred_element_type=jnp.float32)]
where the time goes in v14:
time: 100 us
  starting transfers between devices  41.4 us (41%)
  waiting for transfers between devices  26.9 us (27%)
  matrix products  16.9 us (17%)
  other arithmetic  6.86 us (7%)
  between operations  4.44 us (4%)
  local copies, waits for them, and re-layouts  3.53 us (4%)
    ppermute x20, starting transfers between devices, face_sum_parts(): lax.ppermute(block, axis, pairs)  38.3 us
    ppermute x20, waiting for transfers between devices, face_sum_parts(): lax.ppermute(block, axis, pairs)  19.8 us
    ppermute x2, waiting for transfers between devices, from_behind(): return lax.ppermute(value, axis, pairs)  7.07 us
    dot_general x3, matrix products, slot_pieces(): return jnp.dot(to_slots, side, preferred_element_type=jnp.float32)  4.68 us
    dot_general x3, matrix products, slot_pieces(): jnp.dot(stacked, to_rows, preferred_element_type=jnp.float32)  3.98 us
    dot_general x9, matrix products, bf16x3_apply(): both = jnp.dot(op_high, pair, preferred_element_type=jnp.float32)  3.54 us
    dot_general x9, matrix products, bf16x3_apply(): jnp.dot(op_mid, pair[:, :cols], preferred_element_type=jnp.float32)  3.41 us
    ppermute x2, starting transfers between devices, from_behind(): return lax.ppermute(value, axis, pairs)  3.04 us
  transfers between devices with their start and end apart: 22, of which 5 were waited for; matrix products, arithmetic and copies ran while one was open for 16% of the time, Pallas kernels for 0%

profile of v14, /device:TPU:0, one launch (start us, length us, event | category | flops | bytes accessed | tf_op | source)
XLA Modules:
  0.0 100.0 jit_solution(2173029775714201521)
XLA Ops:
  0.7 2.3 %slice_bitcast_fusion = (f32[128,896]{1,0:T(8,128)}, f32[128,896]{1,0:T(8,128)}) fusion(f32[1,1,2,128,896]{4,3,2,1,0:T(8,128)} %param.8), kind=kLoop, calls=%fused_computation.125 | loop fusion | bytes 1835008 | tf_op jit(solution)/shard_map/squeeze | solution.py:117
  3.0 1.8 %slice_select_fusion.16 = (f32[224,128]{1,0:T(8,128)}, f32[224,128]{1,0:T(8,128)S(1)}, f32[224,128]{1,0:T(8,128)}, f32[224,128]{1,0:T(8,128)}) fusion(f32[896,128]{1,0:T(8,128)} %bitcast.63, pred[]{:T(512)S(6)} %eq.100, pred[]{:T(512)S(6)} %eq.101), kind=kLoop, calls=%fused_computation.181 | loop fusion | flops 114688 | bytes 917506 | tf_op jit(solution)/shard_map/jit(_where)/select_n | solution.py:64
  4.8 0.7 collective-permute-start
  5.5 4.4 %collective-permute-start.1 = (f32[224,128]{1,0:T(8,128)}, f32[224,128]{1,0:T(8,128)S(1)}, u32[]{:S(2)}, u32[]{:S(2)}) collective-permute-start(f32[224,128]{1,0:T(8,128)} %get-tuple-element.110), channel_id=1, source_target_pairs={{0,4},{4,0},{8,12},{12,8},{16,20},{20,16},{24,28},{28,24},{1,5},{5... | collective-permute-start | bytes 344072 | tf_op jit(solution)/shard_map/ppermute | solution.py:66
  9.9 2.0 %collective-permute-start.4 = (f32[128,896]{1,0:T(8,128)}, f32[128,896]{1,0:T(8,128)S(1)}, u32[]{:S(2)}, u32[]{:S(2)}) collective-permute-start(f32[128,896]{1,0:T(8,128)} %get-tuple-element.38), channel_id=1, source_target_pairs={{0,24},{4,28},{8,0},{12,4},{16,8},{20,12},{24,16},{28,20},{1,25},{... | collective-permute-start | bytes 1376264 | tf_op jit(solution)/shard_map/ppermute | solution.py:22
  11.9 1.1 %collective-permute-start.5 = (f32[128,896]{1,0:T(8,128)}, f32[128,896]{1,0:T(8,128)S(1)}, u32[]{:S(2)}, u32[]{:S(2)}) collective-permute-start(f32[128,896]{1,0:T(8,128)} %get-tuple-element.39), channel_id=1, source_target_pairs={{0,16},{4,20},{8,24},{12,28},{16,0},{20,4},{24,8},{28,12},{1,17},{... | collective-permute-start | bytes 1376264 | tf_op jit(solution)/shard_map/ppermute | solution.py:22
  12.9 0.6 fusion.142
  16.1 1.3 %reduce = s32[896]{0:T(1024)} reduce(s32[1,1,896]{2,1,0:T(1,128)} %param.11, s32[]{:T(128)} %constant.99.clone.1), dimensions={0,1}, to_apply=%param.11.reduce_sub_computation | reduce | bytes 7172 | tf_op args[5]
  18.7 2.6 %convolution_convert_fusion = bf16[1280,896]{0,1:T(8,128)(2,1)S(1)} fusion(bf16[640,896]{1,0:T(8,128)(2,1)S(1)} %get-tuple-element.69, bf16[640,896]{1,0:T(8,128)(2,1)S(1)} %get-tuple-element.68, bf16[896]{0:T(1024)(128)(2,1)S(1)} %select_select_fusion, s32[896]{0:T(1024)S(1)} %copy-done.3), kind=kOutput, calls=%fused_computation.1 | convolution fusion | flops 2062548992 | bytes 4592896 | tf_op jit(solution)/shard_map/dot_general | solution.py:92
  21.5 2.7 %fusion.143 = (bf16[896,1792]{1,0:T(8,128)(2,1)S(1)}, f32[896,1792]{1,0:T(8,128)S(1)}) fusion(bf16[640,896]{0,1:T(8,128)(2,1)S(1)} %get-tuple-element.67, bf16[640,896]{0,1:T(8,128)(2,1)S(1)} %get-tuple-element.66, bf16[896]{0:T(1024)(128)(2,1)S(1)} %select_select_fusion, s32[896]{0:T(1024)S(1)} %copy-done.3), kind=kOutput, calls=%fused_computation.251 | convolution fusion | flops 2063122432 | bytes 11932928 | tf_op jit(solution)/shard_map/dot_general | solution.py:94
  24.3 0.7 collective-permute-start.2
  25.0 4.3 %collective-permute-start.3 = (f32[224,128]{1,0:T(8,128)S(1)}, f32[224,128]{1,0:T(8,128)S(1)}, u32[]{:S(2)}, u32[]{:S(2)}) collective-permute-start(f32[224,128]{1,0:T(8,128)S(1)} %get-tuple-element.31), channel_id=1, source_target_pairs={{0,1},{1,0},{2,3},{3,2},{4,5},{5,4},{6,7},{7,6},{8,9},{9,8},{10,11... | collective-permute-start | bytes 344072 | tf_op jit(solution)/shard_map/ppermute | solution.py:69
  29.6 4.6 %collective-permute-done.3 = f32[224,128]{1,0:T(8,128)S(1)} collective-permute-done((f32[224,128]{1,0:T(8,128)S(1)}, f32[224,128]{1,0:T(8,128)S(1)}, u32[]{:S(2)}, u32[]{:S(2)}) %collective-permute-start.3) | collective-permute-done | bytes 114720 | tf_op jit(solution)/shard_map/ppermute | solution.py:69
  34.3 0.6 fusion.28
  35.0 0.6 fusion.14
  36.2 7.1 %collective-permute-done.5 = f32[128,896]{1,0:T(8,128)S(1)} collective-permute-done((f32[128,896]{1,0:T(8,128)}, f32[128,896]{1,0:T(8,128)S(1)}, u32[]{:S(2)}, u32[]{:S(2)}) %collective-permute-start.5) | collective-permute-done | bytes 458784 | tf_op jit(solution)/shard_map/ppermute | solution.py:22
  44.5 0.7 fusion.37
  45.2 0.7 collective-permute-start.6
  45.9 4.3 %collective-permute-start.7 = (f32[224,128]{1,0:T(8,128)S(1)}, f32[224,128]{1,0:T(8,128)S(1)}, u32[]{:S(2)}, u32[]{:S(2)}) collective-permute-start(f32[224,128]{1,0:T(8,128)S(1)} %get-tuple-element.103), channel_id=1, source_target_pairs={{0,1},{1,0},{2,3},{3,2},{4,5},{5,4},{6,7},{7,6},{8,9},{9,8},{10,11... | collective-permute-start | bytes 344072 | tf_op jit(solution)/shard_map/ppermute | solution.py:75
  50.2 0.8 collective-permute-start.8
  51.0 1.9 %collective-permute-start.9 = (f32[224,128]{1,0:T(8,128)S(1)}, f32[224,128]{1,0:T(8,128)S(1)}, u32[]{:S(2)}, u32[]{:S(2)}) collective-permute-start(f32[224,128]{1,0:T(8,128)S(1)} %get-tuple-element.102), channel_id=1, source_target_pairs={{0,4},{4,0},{8,12},{12,8},{16,20},{20,16},{24,28},{28,24},{1,5},{5... | collective-permute-start | bytes 344072 | tf_op jit(solution)/shard_map/ppermute | solution.py:75
  52.9 0.7 fusion.29
  53.6 0.7 fusion.30
  54.4 1.0 fusion.69
  55.4 1.0 add_convert_fusion
  56.6 0.4 fusion.60
  57.0 0.4 fusion.51
  57.8 0.7 collective-permute-start.12
  58.5 1.7 %collective-permute-start.13 = (f32[224,128]{1,0:T(8,128)S(1)}, f32[224,128]{1,0:T(8,128)S(1)}, u32[]{:S(2)}, u32[]{:S(2)}) collective-permute-start(f32[224,128]{1,0:T(8,128)S(1)} %get-tuple-element.122), channel_id=1, source_target_pairs={{0,4},{4,0},{8,12},{12,8},{16,20},{20,16},{24,28},{28,24},{1,5},{5... | collective-permute-start | bytes 344072 | tf_op jit(solution)/shard_map/ppermute | solution.py:75
  60.7 0.7 collective-permute-start.10
  61.4 2.8 %collective-permute-start.11 = (f32[224,128]{1,0:T(8,128)S(1)}, f32[224,128]{1,0:T(8,128)S(1)}, u32[]{:S(2)}, u32[]{:S(2)}) collective-permute-start(f32[224,128]{1,0:T(8,128)S(1)} %get-tuple-element.124), channel_id=1, source_target_pairs={{0,1},{1,0},{2,3},{3,2},{4,5},{5,4},{6,7},{7,6},{8,9},{9,8},{10,11... | collective-permute-start | bytes 344072 | tf_op jit(solution)/shard_map/ppermute | solution.py:75
  64.1 5.4 %collective-permute-done.11 = f32[224,128]{1,0:T(8,128)S(1)} collective-permute-done((f32[224,128]{1,0:T(8,128)S(1)}, f32[224,128]{1,0:T(8,128)S(1)}, u32[]{:S(2)}, u32[]{:S(2)}) %collective-permute-start.11) | collective-permute-done | bytes 114720 | tf_op jit(solution)/shard_map/ppermute | solution.py:75
  69.8 0.4 fusion.58
  70.3 0.4 fusion.49
  71.1 0.7 collective-permute-start.16
  71.8 4.9 %collective-permute-start.17 = (f32[224,128]{1,0:T(8,128)S(1)}, f32[224,128]{1,0:T(8,128)S(1)}, u32[]{:S(2)}, u32[]{:S(2)}) collective-permute-start(f32[224,128]{1,0:T(8,128)S(1)} %get-tuple-element.118), channel_id=1, source_target_pairs={{0,4},{4,0},{8,12},{12,8},{16,20},{20,16},{24,28},{28,24},{1,5},{5... | collective-permute-start | bytes 344072 | tf_op jit(solution)/shard_map/ppermute | solution.py:75
  77.1 0.7 collective-permute-start.14
  77.8 2.7 %collective-permute-start.15 = (f32[224,128]{1,0:T(8,128)S(1)}, f32[224,128]{1,0:T(8,128)S(1)}, u32[]{:S(2)}, u32[]{:S(2)}) collective-permute-start(f32[224,128]{1,0:T(8,128)S(1)} %get-tuple-element.120), channel_id=1, source_target_pairs={{0,1},{1,0},{2,3},{3,2},{4,5},{5,4},{6,7},{7,6},{8,9},{9,8},{10,11... | collective-permute-start | bytes 344072 | tf_op jit(solution)/shard_map/ppermute | solution.py:75
  80.5 5.4 %collective-permute-done.15 = f32[224,128]{1,0:T(8,128)S(1)} collective-permute-done((f32[224,128]{1,0:T(8,128)S(1)}, f32[224,128]{1,0:T(8,128)S(1)}, u32[]{:S(2)}, u32[]{:S(2)}) %collective-permute-start.15) | collective-permute-done | bytes 114720 | tf_op jit(solution)/shard_map/ppermute | solution.py:75
  86.2 0.4 fusion.56
  86.6 0.4 fusion.47
  87.4 0.7 collective-permute-start.20
  88.1 1.8 %collective-permute-start.21 = (f32[224,128]{1,0:T(8,128)S(1)}, f32[224,128]{1,0:T(8,128)S(1)}, u32[]{:S(2)}, u32[]{:S(2)}) collective-permute-start(f32[224,128]{1,0:T(8,128)S(1)} %get-tuple-element.114), channel_id=1, source_target_pairs={{0,4},{4,0},{8,12},{12,8},{16,20},{20,16},{24,28},{28,24},{1,5},{5... | collective-permute-start | bytes 344072 | tf_op jit(solution)/shard_map/ppermute | solution.py:75
  90.3 0.7 collective-permute-start.18
  91.0 2.6 %collective-permute-start.19 = (f32[224,128]{1,0:T(8,128)S(1)}, f32[224,128]{1,0:T(8,128)S(1)}, u32[]{:S(2)}, u32[]{:S(2)}) collective-permute-start(f32[224,128]{1,0:T(8,128)S(1)} %get-tuple-element.116), channel_id=1, source_target_pairs={{0,1},{1,0},{2,3},{3,2},{4,5},{5,4},{6,7},{7,6},{8,9},{9,8},{10,11... | collective-permute-start | bytes 344072 | tf_op jit(solution)/shard_map/ppermute | solution.py:75
  93.6 1.0 %add_add_fusion = f32[1,1,896,128]{3,2,1,0:T(8,128)} fusion(f32[1,1,224,128]{3,2,1,0:T(8,128)S(1)} %bitcast.51, f32[1,1,224,128]{3,2,1,0:T(8,128)S(1)} %bitcast.53, f32[1,1,224,128]{3,2,1,0:T(8,128)S(1)} %bitcast.49, f32[1,1,224,128]{3,2,1,0:T(8,128)S(1)} %bitcast.47, f32[1,1,224,128]{3,2,1,0:T(8,128)S(1)} %bitcast.59, f32[1,1,224,128]{3,2,1,0:T(8,128)S(1)} %bitcast.61, ...), kind=kLoop, calls=%fused_computation.120 | loop fusion | flops 3211264 | bytes 2293760 | tf_op jit(solution)/shard_map/add | solution.py:166
  94.6 4.4 %collective-permute-done.19 = f32[224,128]{1,0:T(8,128)S(1)} collective-permute-done((f32[224,128]{1,0:T(8,128)S(1)}, f32[224,128]{1,0:T(8,128)S(1)}, u32[]{:S(2)}, u32[]{:S(2)}) %collective-permute-start.19) | collective-permute-done | bytes 114720 | tf_op jit(solution)/shard_map/ppermute | solution.py:75
  99.1 0.9 maximum_subtract_fusion.6
  (73 shorter events, 6.4 us)
Async XLA Ops:
  0.6 17.4 %copy-start = (f32[1,1,640,896]{3,2,1,0:T(8,128)S(1)}, f32[1,1,640,896]{3,2,1,0:T(8,128)}, u32[]{:S(2)}) copy-start(f32[1,1,640,896]{3,2,1,0:T(8,128)} %param.7) | copy-start | bytes 6881284
  0.7 12.3 %copy-start.4 = (s32[1,1,2]{2,1,0:T(1,128)S(1)}, s32[1,1,2]{2,1,0:T(1,128)}, u32[]{:S(2)}) copy-start(s32[1,1,2]{2,1,0:T(1,128)} %param.9) | copy-start | bytes 28
  4.8 19.5 %collective-permute-start = (f32[224,128]{1,0:T(8,128)}, f32[224,128]{1,0:T(8,128)S(1)}, u32[]{:S(2)}, u32[]{:S(2)}) collective-permute-start(f32[224,128]{1,0:T(8,128)} %get-tuple-element.112), channel_id=1, source_target_pairs={{4,8},{8,4},{12,16},{16,12},{20,24},{24,20},{5,9},{9,5},{13,17},{1... | collective-permute-start | bytes 344072 | tf_op jit(solution)/shard_map/ppermute | solution.py:66
  5.5 18.9 %collective-permute-start.1 = (f32[224,128]{1,0:T(8,128)}, f32[224,128]{1,0:T(8,128)S(1)}, u32[]{:S(2)}, u32[]{:S(2)}) collective-permute-start(f32[224,128]{1,0:T(8,128)} %get-tuple-element.110), channel_id=1, source_target_pairs={{0,4},{4,0},{8,12},{12,8},{16,20},{20,16},{24,28},{28,24},{1,5},{5... | collective-permute-start | bytes 344072 | tf_op jit(solution)/shard_map/ppermute | solution.py:66
  9.9 25.7 %collective-permute-start.4 = (f32[128,896]{1,0:T(8,128)}, f32[128,896]{1,0:T(8,128)S(1)}, u32[]{:S(2)}, u32[]{:S(2)}) collective-permute-start(f32[128,896]{1,0:T(8,128)} %get-tuple-element.38), channel_id=1, source_target_pairs={{0,24},{4,28},{8,0},{12,4},{16,8},{20,12},{24,16},{28,20},{1,25},{... | collective-permute-start | bytes 1376264 | tf_op jit(solution)/shard_map/ppermute | solution.py:22
  11.9 31.4 %collective-permute-start.5 = (f32[128,896]{1,0:T(8,128)}, f32[128,896]{1,0:T(8,128)S(1)}, u32[]{:S(2)}, u32[]{:S(2)}) collective-permute-start(f32[128,896]{1,0:T(8,128)} %get-tuple-element.39), channel_id=1, source_target_pairs={{0,16},{4,20},{8,24},{12,28},{16,0},{20,4},{24,8},{28,12},{1,17},{... | collective-permute-start | bytes 1376264 | tf_op jit(solution)/shard_map/ppermute | solution.py:22
  18.0 0.7 copy-start.3
  21.5 2.8 %copy-start.2 = (f32[224,128]{1,0:T(8,128)S(1)}, f32[224,128]{1,0:T(8,128)}, u32[]{:S(2)}) copy-start(f32[224,128]{1,0:T(8,128)} %get-tuple-element.30) | copy-start | bytes 344068
  21.5 12.7 %copy-start.1 = (f32[1,1,896,128]{3,2,1,0:T(8,128)S(1)}, f32[1,1,896,128]{3,2,1,0:T(8,128)}, u32[]{:S(2)}) copy-start(f32[1,1,896,128]{3,2,1,0:T(8,128)} %param.6) | copy-start | bytes 1376260
  24.3 5.3 %collective-permute-start.2 = (f32[224,128]{1,0:T(8,128)S(1)}, f32[224,128]{1,0:T(8,128)S(1)}, u32[]{:S(2)}, u32[]{:S(2)}) collective-permute-start(f32[224,128]{1,0:T(8,128)S(1)} %copy-done.2), channel_id=1, source_target_pairs={{1,2},{2,1},{5,6},{6,5},{9,10},{10,9},{13,14},{14,13},{17,18},{18,... | collective-permute-start | bytes 344072 | tf_op jit(solution)/shard_map/ppermute | solution.py:69
  25.0 9.2 %collective-permute-start.3 = (f32[224,128]{1,0:T(8,128)S(1)}, f32[224,128]{1,0:T(8,128)S(1)}, u32[]{:S(2)}, u32[]{:S(2)}) collective-permute-start(f32[224,128]{1,0:T(8,128)S(1)} %get-tuple-element.31), channel_id=1, source_target_pairs={{0,1},{1,0},{2,3},{3,2},{4,5},{5,4},{6,7},{7,6},{8,9},{9,8},{10,11... | collective-permute-start | bytes 344072 | tf_op jit(solution)/shard_map/ppermute | solution.py:69
  45.2 11.1 %collective-permute-start.6 = (f32[224,128]{1,0:T(8,128)S(1)}, f32[224,128]{1,0:T(8,128)S(1)}, u32[]{:S(2)}, u32[]{:S(2)}) collective-permute-start(f32[224,128]{1,0:T(8,128)S(1)} %get-tuple-element.105), channel_id=1, source_target_pairs={{1,2},{2,1},{5,6},{6,5},{9,10},{10,9},{13,14},{14,13},{17,18},{18,... | collective-permute-start | bytes 344072 | tf_op jit(solution)/shard_map/ppermute | solution.py:75
  45.9 10.5 %collective-permute-start.7 = (f32[224,128]{1,0:T(8,128)S(1)}, f32[224,128]{1,0:T(8,128)S(1)}, u32[]{:S(2)}, u32[]{:S(2)}) collective-permute-start(f32[224,128]{1,0:T(8,128)S(1)} %get-tuple-element.103), channel_id=1, source_target_pairs={{0,1},{1,0},{2,3},{3,2},{4,5},{5,4},{6,7},{7,6},{8,9},{9,8},{10,11... | collective-permute-start | bytes 344072 | tf_op jit(solution)/shard_map/ppermute | solution.py:75
  50.2 6.2 %collective-permute-start.8 = (f32[224,128]{1,0:T(8,128)S(1)}, f32[224,128]{1,0:T(8,128)S(1)}, u32[]{:S(2)}, u32[]{:S(2)}) collective-permute-start(f32[224,128]{1,0:T(8,128)S(1)} %get-tuple-element.104), channel_id=1, source_target_pairs={{4,8},{8,4},{12,16},{16,12},{20,24},{24,20},{5,9},{9,5},{13,17},{1... | collective-permute-start | bytes 344072 | tf_op jit(solution)/shard_map/ppermute | solution.py:75
  51.0 5.4 %collective-permute-start.9 = (f32[224,128]{1,0:T(8,128)S(1)}, f32[224,128]{1,0:T(8,128)S(1)}, u32[]{:S(2)}, u32[]{:S(2)}) collective-permute-start(f32[224,128]{1,0:T(8,128)S(1)} %get-tuple-element.102), channel_id=1, source_target_pairs={{0,4},{4,0},{8,12},{12,8},{16,20},{20,16},{24,28},{28,24},{1,5},{5... | collective-permute-start | bytes 344072 | tf_op jit(solution)/shard_map/ppermute | solution.py:75
  57.8 6.3 %collective-permute-start.12 = (f32[224,128]{1,0:T(8,128)S(1)}, f32[224,128]{1,0:T(8,128)S(1)}, u32[]{:S(2)}, u32[]{:S(2)}) collective-permute-start(f32[224,128]{1,0:T(8,128)S(1)} %get-tuple-element.123), channel_id=1, source_target_pairs={{4,8},{8,4},{12,16},{16,12},{20,24},{24,20},{5,9},{9,5},{13,17},{1... | collective-permute-start | bytes 344072 | tf_op jit(solution)/shard_map/ppermute | solution.py:75
  58.5 5.6 %collective-permute-start.13 = (f32[224,128]{1,0:T(8,128)S(1)}, f32[224,128]{1,0:T(8,128)S(1)}, u32[]{:S(2)}, u32[]{:S(2)}) collective-permute-start(f32[224,128]{1,0:T(8,128)S(1)} %get-tuple-element.122), channel_id=1, source_target_pairs={{0,4},{4,0},{8,12},{12,8},{16,20},{20,16},{24,28},{28,24},{1,5},{5... | collective-permute-start | bytes 344072 | tf_op jit(solution)/shard_map/ppermute | solution.py:75
  60.7 3.5 %collective-permute-start.10 = (f32[224,128]{1,0:T(8,128)S(1)}, f32[224,128]{1,0:T(8,128)S(1)}, u32[]{:S(2)}, u32[]{:S(2)}) collective-permute-start(f32[224,128]{1,0:T(8,128)S(1)} %get-tuple-element.125), channel_id=1, source_target_pairs={{1,2},{2,1},{5,6},{6,5},{9,10},{10,9},{13,14},{14,13},{17,18},{18,... | collective-permute-start | bytes 344072 | tf_op jit(solution)/shard_map/ppermute | solution.py:75
  61.4 8.2 %collective-permute-start.11 = (f32[224,128]{1,0:T(8,128)S(1)}, f32[224,128]{1,0:T(8,128)S(1)}, u32[]{:S(2)}, u32[]{:S(2)}) collective-permute-start(f32[224,128]{1,0:T(8,128)S(1)} %get-tuple-element.124), channel_id=1, source_target_pairs={{0,1},{1,0},{2,3},{3,2},{4,5},{5,4},{6,7},{7,6},{8,9},{9,8},{10,11... | collective-permute-start | bytes 344072 | tf_op jit(solution)/shard_map/ppermute | solution.py:75
  71.1 9.4 %collective-permute-start.16 = (f32[224,128]{1,0:T(8,128)S(1)}, f32[224,128]{1,0:T(8,128)S(1)}, u32[]{:S(2)}, u32[]{:S(2)}) collective-permute-start(f32[224,128]{1,0:T(8,128)S(1)} %get-tuple-element.119), channel_id=1, source_target_pairs={{4,8},{8,4},{12,16},{16,12},{20,24},{24,20},{5,9},{9,5},{13,17},{1... | collective-permute-start | bytes 344072 | tf_op jit(solution)/shard_map/ppermute | solution.py:75
  71.8 8.8 %collective-permute-start.17 = (f32[224,128]{1,0:T(8,128)S(1)}, f32[224,128]{1,0:T(8,128)S(1)}, u32[]{:S(2)}, u32[]{:S(2)}) collective-permute-start(f32[224,128]{1,0:T(8,128)S(1)} %get-tuple-element.118), channel_id=1, source_target_pairs={{0,4},{4,0},{8,12},{12,8},{16,20},{20,16},{24,28},{28,24},{1,5},{5... | collective-permute-start | bytes 344072 | tf_op jit(solution)/shard_map/ppermute | solution.py:75
  77.1 3.4 %collective-permute-start.14 = (f32[224,128]{1,0:T(8,128)S(1)}, f32[224,128]{1,0:T(8,128)S(1)}, u32[]{:S(2)}, u32[]{:S(2)}) collective-permute-start(f32[224,128]{1,0:T(8,128)S(1)} %get-tuple-element.121), channel_id=1, source_target_pairs={{1,2},{2,1},{5,6},{6,5},{9,10},{10,9},{13,14},{14,13},{17,18},{18,... | collective-permute-start | bytes 344072 | tf_op jit(solution)/shard_map/ppermute | solution.py:75
  77.8 8.1 %collective-permute-start.15 = (f32[224,128]{1,0:T(8,128)S(1)}, f32[224,128]{1,0:T(8,128)S(1)}, u32[]{:S(2)}, u32[]{:S(2)}) collective-permute-start(f32[224,128]{1,0:T(8,128)S(1)} %get-tuple-element.120), channel_id=1, source_target_pairs={{0,1},{1,0},{2,3},{3,2},{4,5},{5,4},{6,7},{7,6},{8,9},{9,8},{10,11... | collective-permute-start | bytes 344072 | tf_op jit(solution)/shard_map/ppermute | solution.py:75
  87.4 7.2 %collective-permute-start.20 = (f32[224,128]{1,0:T(8,128)S(1)}, f32[224,128]{1,0:T(8,128)S(1)}, u32[]{:S(2)}, u32[]{:S(2)}) collective-permute-start(f32[224,128]{1,0:T(8,128)S(1)} %get-tuple-element.115), channel_id=1, source_target_pairs={{4,8},{8,4},{12,16},{16,12},{20,24},{24,20},{5,9},{9,5},{13,17},{1... | collective-permute-start | bytes 344072 | tf_op jit(solution)/shard_map/ppermute | solution.py:75
  88.1 6.5 %collective-permute-start.21 = (f32[224,128]{1,0:T(8,128)S(1)}, f32[224,128]{1,0:T(8,128)S(1)}, u32[]{:S(2)}, u32[]{:S(2)}) collective-permute-start(f32[224,128]{1,0:T(8,128)S(1)} %get-tuple-element.114), channel_id=1, source_target_pairs={{0,4},{4,0},{8,12},{12,8},{16,20},{20,16},{24,28},{28,24},{1,5},{5... | collective-permute-start | bytes 344072 | tf_op jit(solution)/shard_map/ppermute | solution.py:75
  90.3 4.3 %collective-permute-start.18 = (f32[224,128]{1,0:T(8,128)S(1)}, f32[224,128]{1,0:T(8,128)S(1)}, u32[]{:S(2)}, u32[]{:S(2)}) collective-permute-start(f32[224,128]{1,0:T(8,128)S(1)} %get-tuple-element.117), channel_id=1, source_target_pairs={{1,2},{2,1},{5,6},{6,5},{9,10},{10,9},{13,14},{14,13},{17,18},{18,... | collective-permute-start | bytes 344072 | tf_op jit(solution)/shard_map/ppermute | solution.py:75
  91.0 8.0 %collective-permute-start.19 = (f32[224,128]{1,0:T(8,128)S(1)}, f32[224,128]{1,0:T(8,128)S(1)}, u32[]{:S(2)}, u32[]{:S(2)}) collective-permute-start(f32[224,128]{1,0:T(8,128)S(1)} %get-tuple-element.116), channel_id=1, source_target_pairs={{0,1},{1,0},{2,3},{3,2},{4,5},{5,4},{6,7},{7,6},{8,9},{9,8},{10,11... | collective-permute-start | bytes 344072 | tf_op jit(solution)/shard_map/ppermute | solution.py:75

commit v15 on v10

--- a/solution.py
+++ b/solution.py
@@ -145,10 +145,13 @@
     ).astype(jnp.bfloat16)
     spill_stack = jnp.concatenate(homed, axis=0)
     spill_slots = slot_pieces(spill_stack, to_rows, spill_place)
-    own_high = own_slots[:, :order_max].astype(jnp.bfloat16)
-    own_mid = own_slots[:, order_max:].astype(jnp.bfloat16)
-    op_high = (own_slots[:, :order_max] + spill_slots[:, :order_max]).astype(jnp.bfloat16)
-    op_mid = (own_slots[:, order_max:] + spill_slots[:, order_max:]).astype(jnp.bfloat16)
+    own_cat = jnp.concatenate(
+        [own_slots[:, :order_max], own_slots[:, :order_max], own_slots[:, order_max:]], axis=1
+    ).astype(jnp.bfloat16)
+    full_slots = own_slots + spill_slots
+    op_cat = jnp.concatenate(
+        [full_slots[:, :order_max], full_slots[:, :order_max], full_slots[:, order_max:]], axis=1
+    ).astype(jnp.bfloat16)
     spill_high = lax.reduce_precision(spill_stack, exponent_bits=8, mantissa_bits=7)
     spill_mid = (spill_stack - spill_high).astype(jnp.bfloat16)
     spill_high = spill_high.astype(jnp.bfloat16)
@@ -163,8 +166,11 @@
         solution = solution + direction
         dir_high = lax.reduce_precision(direction, exponent_bits=8, mantissa_bits=7)
         dir_pair = jnp.concatenate([dir_high, direction - dir_high], axis=1).astype(jnp.bfloat16)
+        dir_stack = jnp.concatenate(
+            [dir_high, direction - dir_high, dir_high], axis=0
+        ).astype(jnp.bfloat16)
         if step_id == 0:
-            local = bf16x3_apply(own_high, own_mid, dir_pair, cols)
+            local = jnp.dot(own_cat, dir_stack, preferred_element_type=jnp.float32)
             moved = jnp.dot(to_rows, dir_pair, preferred_element_type=jnp.float32).astype(
                 jnp.bfloat16
             )
@@ -180,7 +186,7 @@
                 (placed[:, :cols] + placed[:, cols : 2 * cols]) + placed[:, 2 * cols :]
             )
         else:
-            local = bf16x3_apply(op_high, op_mid, dir_pair, cols)
+            local = jnp.dot(op_cat, dir_stack, preferred_element_type=jnp.float32)
         faces = [local[face_id * width : (face_id + 1) * width] for face_id in range(4)]
         residual = residual - face_sum_parts(faces)
         if step_id + 1 < ITERS:

time: 90.4 us -> 92.4 us (1.022)
  starting transfers between devices: 41.1 us -> 42.3 us
    dot_general x0 -> x4, matrix products: none -> 5.73 us  [the longest x3 4.28 us: body(): local = jnp.dot(op_cat, dir_stack, preferred_element_type=jnp.float32)]
    dot_general x5 -> x1, matrix products: 2.93 us -> 0.35 us  [bf16x3_apply(): both = jnp.dot(op_high, pair, preferred_element_type=jnp.float32)]
    dot_general x5 -> x1, matrix products: 2.65 us -> 0.31 us  [bf16x3_apply(): jnp.dot(op_mid, pair[:, :cols], preferred_element_type=jnp.float32)]
    ppermute x20, starting transfers between devices: 38 us -> 39.3 us  [face_sum_parts(): lax.ppermute(block, axis, pairs)]
    ppermute x20, waiting for transfers between devices: 10.7 us -> 9.49 us  [face_sum_parts(): lax.ppermute(block, axis, pairs)]
    select_n x5, other arithmetic: 0.87 us -> 2 us  [face_sum_parts(): jnp.where(even, high, low)]
    convert_element_type x1 -> x0, other arithmetic: 1.01 us -> none  [body(): (own_slots[:, :order_max] + spill_slots[:, :order_max]).astype(jnp.bfloat16)]
    another operation x7 -> x10, other arithmetic: 2.38 us -> 2.11 us
  transfers between devices with their start and end apart: 22 -> 22, of which waited for: 5 -> 5; matrix products, arithmetic and copies ran while one was open for 19% -> 17% of each run, Pallas kernels for 0% -> 0%
where the time goes in v15:
time: 92.4 us; the launch traced here: 91.1 us
  starting transfers between devices  42.3 us (46%)
  matrix products  16.5 us (18%)
  waiting for transfers between devices  14.7 us (16%)
  other arithmetic  7.94 us (9%)
  local copies, waits for them, and re-layouts  5.55 us (6%)
  between operations  4.12 us (4%)
    ppermute x20, starting transfers between devices, face_sum_parts(): lax.ppermute(block, axis, pairs)  39.3 us
    ppermute x20, waiting for transfers between devices, face_sum_parts(): lax.ppermute(block, axis, pairs)  9.49 us
    ppermute x2, waiting for transfers between devices, from_behind(): return lax.ppermute(value, axis, pairs)  5.24 us
    dot_general x2, matrix products, slot_pieces(): jnp.dot(stacked, to_rows, preferred_element_type=jnp.float32)  5.06 us
    dot_general x3, matrix products, body(): local = jnp.dot(op_cat, dir_stack, preferred_element_type=jnp.float32)  4.28 us
    dot_general x2, matrix products, slot_pieces(): return jnp.dot(to_slots, side, preferred_element_type=jnp.float32)  3.91 us
    ppermute x2, starting transfers between devices, from_behind(): return lax.ppermute(value, axis, pairs)  3.04 us
    squeeze x1, local copies, waits for them, and re-layouts, body(): spill_parts = [spill_block[slot_id] for slot_id in range(2)]  2.29 us
  transfers between devices with their start and end apart: 22, of which 5 were waited for; matrix products, arithmetic and copies ran while one was open for 17% of the time, Pallas kernels for 0%

profile of v15, /device:TPU:0, one launch (start us, length us, event | category | flops | bytes accessed | tf_op | source)
XLA Modules:
  0.0 91.1 jit_solution(9591002964507355973)
XLA Ops:
  0.7 2.3 %slice_bitcast_fusion = (f32[128,896]{1,0:T(8,128)}, f32[128,896]{1,0:T(8,128)}) fusion(f32[1,1,2,128,896]{4,3,2,1,0:T(8,128)} %param.8), kind=kLoop, calls=%fused_computation.113 | loop fusion | bytes 1835008 | tf_op jit(solution)/shard_map/squeeze | solution.py:117
  2.9 1.9 %slice_select_fusion.16 = (f32[224,128]{1,0:T(8,128)}, f32[224,128]{1,0:T(8,128)}, f32[224,128]{1,0:T(8,128)}, f32[224,128]{1,0:T(8,128)}) fusion(f32[896,128]{1,0:T(8,128)} %bitcast.54, pred[]{:T(512)S(6)} %eq.100, pred[]{:T(512)S(6)} %eq.101), kind=kLoop, calls=%fused_computation.166 | loop fusion | flops 114688 | bytes 917506 | tf_op jit(solution)/shard_map/jit(_where)/select_n | solution.py:64
  4.8 0.7 collective-permute-start
  5.5 4.4 %collective-permute-start.1 = (f32[224,128]{1,0:T(8,128)}, f32[224,128]{1,0:T(8,128)}, u32[]{:S(2)}, u32[]{:S(2)}) collective-permute-start(f32[224,128]{1,0:T(8,128)} %get-tuple-element.122), channel_id=1, source_target_pairs={{0,4},{4,0},{8,12},{12,8},{16,20},{20,16},{24,28},{28,24},{1,5},{5... | collective-permute-start | bytes 344072 | tf_op jit(solution)/shard_map/ppermute | solution.py:66
  9.9 2.0 %collective-permute-start.4 = (f32[128,896]{1,0:T(8,128)}, f32[128,896]{1,0:T(8,128)}, u32[]{:S(2)}, u32[]{:S(2)}) collective-permute-start(f32[128,896]{1,0:T(8,128)} %get-tuple-element.38), channel_id=1, source_target_pairs={{0,24},{4,28},{8,0},{12,4},{16,8},{20,12},{24,16},{28,20},{1,25},{... | collective-permute-start | bytes 1376264 | tf_op jit(solution)/shard_map/ppermute | solution.py:22
  11.9 1.0 %collective-permute-start.5 = (f32[128,896]{1,0:T(8,128)}, f32[128,896]{1,0:T(8,128)}, u32[]{:S(2)}, u32[]{:S(2)}) collective-permute-start(f32[128,896]{1,0:T(8,128)} %get-tuple-element.39), channel_id=1, source_target_pairs={{0,16},{4,20},{8,24},{12,28},{16,0},{20,4},{24,8},{28,12},{1,17},{... | collective-permute-start | bytes 1376264 | tf_op jit(solution)/shard_map/ppermute | solution.py:22
  12.9 1.3 %reduce-precision_convert_fusion = (bf16[640,896]{1,0:T(8,128)(2,1)S(1)}, bf16[640,896]{1,0:T(8,128)(2,1)}) fusion(f32[1,1,640,896]{3,2,1,0:T(8,128)S(1)} %copy-done), kind=kLoop, calls=%fused_computation.8 | loop fusion | flops 2867200 | bytes 4587520 | tf_op jit(solution)/shard_map/convert.25
  14.3 0.7 reduce
  15.7 3.8 %convolution_convert_fusion = bf16[1280,896]{0,1:T(8,128)(2,1)S(1)} fusion(bf16[640,896]{1,0:T(8,128)(2,1)} %get-tuple-element.67, bf16[640,896]{1,0:T(8,128)(2,1)S(1)} %get-tuple-element.66, bf16[896]{0:T(1024)(128)(2,1)S(1)} %select_select_fusion, s32[896]{0:T(1024)S(1)} %reduce), kind=kOutput, calls=%fused_computation.6 | convolution fusion | flops 2062548992 | bytes 4592896 | tf_op jit(solution)/shard_map/dot_general | solution.py:92
  19.8 2.7 %fusion.118 = (bf16[896,1792]{1,0:T(8,128)(2,1)S(1)}, f32[896,1792]{1,0:T(8,128)S(1)}) fusion(bf16[640,896]{0,1:T(8,128)(2,1)S(1)} %get-tuple-element.65, bf16[640,896]{0,1:T(8,128)(2,1)S(1)} %get-tuple-element.64, bf16[896]{0:T(1024)(128)(2,1)S(1)} %select_select_fusion, s32[896]{0:T(1024)S(1)} %reduce), kind=kOutput, calls=%fused_computation.208 | convolution fusion | flops 2063122432 | bytes 11932928 | tf_op jit(solution)/shard_map/dot_general | solution.py:94
  22.5 0.6 fusion.117
  25.5 0.7 collective-permute-start.2
  26.2 4.3 %collective-permute-start.3 = (f32[224,128]{1,0:T(8,128)S(1)}, f32[224,128]{1,0:T(8,128)S(1)}, u32[]{:S(2)}, u32[]{:S(2)}) collective-permute-start(f32[224,128]{1,0:T(8,128)S(1)} %copy-done.2), channel_id=1, source_target_pairs={{0,1},{1,0},{2,3},{3,2},{4,5},{5,4},{6,7},{7,6},{8,9},{9,8},{10,11... | collective-permute-start | bytes 344072 | tf_op jit(solution)/shard_map/ppermute | solution.py:69
  30.7 4.7 %collective-permute-done.3 = f32[224,128]{1,0:T(8,128)S(1)} collective-permute-done((f32[224,128]{1,0:T(8,128)S(1)}, f32[224,128]{1,0:T(8,128)S(1)}, u32[]{:S(2)}, u32[]{:S(2)}) %collective-permute-start.3) | collective-permute-done | bytes 114720 | tf_op jit(solution)/shard_map/ppermute | solution.py:69
  35.4 1.0 %select_add_fusion.15 = (f32[224,128]{1,0:T(8,128)S(1)}, f32[224,128]{1,0:T(8,128)S(1)}, f32[224,128]{1,0:T(8,128)S(1)}, f32[224,128]{1,0:T(8,128)S(1)}) fusion(f32[224,128]{1,0:T(8,128)S(1)} %collective-permute-done, f32[224,128]{1,0:T(8,128)} %collective-permute-done.1, f32[896,128]{1,0:T(8,128)S(1)} %bitcast.55, pred[]{:T(512)S(6)} %eq.100, ...), kind=kLoop, calls=%fused_computation.149 | loop fusion | flops 229376 | bytes 1376258 | tf_op jit(solution)/shard_map/add | solution.py:81
  36.4 0.6 fusion.28
  37.1 1.0 %constant_dynamic-update-slice_fusion.1 = f32[256,896]{1,0:T(8,128)S(1)} fusion(f32[128,896]{1,0:T(8,128)} %collective-permute-done.4), kind=kLoop, calls=%fused_computation.183 | loop fusion | bytes 917504
  38.2 5.2 %collective-permute-done.5 = f32[128,896]{1,0:T(8,128)} collective-permute-done((f32[128,896]{1,0:T(8,128)}, f32[128,896]{1,0:T(8,128)}, u32[]{:S(2)}, u32[]{:S(2)}) %collective-permute-start.5) | collective-permute-done | bytes 458784 | tf_op jit(solution)/shard_map/ppermute | solution.py:22
  43.4 1.0 %constant_dynamic-update-slice_fusion = f32[256,896]{1,0:T(8,128)S(1)} fusion(f32[256,896]{1,0:T(8,128)S(1)} %constant_dynamic-update-slice_fusion.1, f32[128,896]{1,0:T(8,128)} %collective-permute-done.5), kind=kLoop, calls=%fused_computation.181 | loop fusion | bytes 917504 | tf_op jit(solution)/shard_map/concatenate | solution.py:146
  44.6 0.4 fusion.119
  45.3 0.5 fusion.63
  45.7 1.4 %fusion.29 = f32[896,128]{1,0:T(8,128)S(1)} fusion(bf16[896,1792]{1,0:T(8,128)(2,1)S(1)} %get-tuple-element.130, bf16[896,896]{1,0:T(8,128)(2,1)S(1)} %slice.164, bf16[896,128]{1,0:T(8,128)(2,1)S(1)} %get-tuple-element.119, bf16[896,128]{1,0:T(8,128)(2,1)S(1)} %get-tuple-element.118, f32[896,384]{1,0:T(8,128)S(1)} %fusion.63), kind=kOutput, calls=%fused_computation.40 | convolution fusion | flops 628604928 | bytes 7110656 | tf_op jit(solution)/shard_map/dot_general | solution.py:173
  47.2 0.7 collective-permute-start.6
  47.9 4.3 %collective-permute-start.7 = (f32[224,128]{1,0:T(8,128)S(1)}, f32[224,128]{1,0:T(8,128)S(1)}, u32[]{:S(2)}, u32[]{:S(2)}) collective-permute-start(f32[224,128]{1,0:T(8,128)S(1)} %get-tuple-element.115), channel_id=1, source_target_pairs={{0,1},{1,0},{2,3},{3,2},{4,5},{5,4},{6,7},{7,6},{8,9},{9,8},{10,11... | collective-permute-start | bytes 344072 | tf_op jit(solution)/shard_map/ppermute | solution.py:75
  52.2 0.8 collective-permute-start.8
  53.0 1.7 %collective-permute-start.9 = (f32[224,128]{1,0:T(8,128)S(1)}, f32[224,128]{1,0:T(8,128)S(1)}, u32[]{:S(2)}, u32[]{:S(2)}) collective-permute-start(f32[224,128]{1,0:T(8,128)S(1)} %get-tuple-element.114), channel_id=1, source_target_pairs={{0,4},{4,0},{8,12},{12,8},{16,20},{20,16},{24,28},{28,24},{1,5},{5... | collective-permute-start | bytes 344072 | tf_op jit(solution)/shard_map/ppermute | solution.py:75
  54.8 1.2 %fusion.24 = bf16[512,896]{1,0:T(8,128)(2,1)S(1)} fusion(bf16[896]{0:T(1024)(128)(2,1)S(1)} %select_select_fusion, s32[896]{0:T(1024)S(1)} %reduce, bf16[256,896]{1,0:T(8,128)(2,1)S(1)} %get-tuple-element.70, bf16[256,896]{1,0:T(8,128)(2,1)S(1)} %get-tuple-element.71), kind=kOutput, calls=%fused_computation.33 | convolution fusion | flops 825982976 | bytes 1840384 | tf_op jit(solution)/shard_map/dot_general | solution.py:92
  56.1 1.2 %add_convert_fusion = bf16[896,1792]{1,0:T(8,128)(2,1)S(1)} fusion(f32[896,1792]{1,0:T(8,128)S(1)} %get-tuple-element.131, bf16[256,896]{1,0:T(8,128)(2,1)S(1)} %get-tuple-element.69, bf16[256,896]{1,0:T(8,128)(2,1)S(1)} %get-tuple-element.68, bf16[896]{0:T(1024)(128)(2,1)S(1)} %select_select_fusion, s32[256]{0:T(256)S(1)} %pad_add_fusion, s32[896]{0:T(1024)S(1)} %reduce), kind=kOutput, calls=%fused_computation | convolution fusion | flops 827588608 | bytes 10557696 | tf_op jit(solution)/shard_map/dot_general | solution.py:94
  57.7 1.4 %fusion.27 = f32[896,128]{1,0:T(8,128)S(1)} fusion(bf16[896,1792]{1,0:T(8,128)(2,1)S(1)} %add_convert_fusion, bf16[896,896]{1,0:T(8,128)(2,1)S(1)} %slice.177, bf16[896,128]{1,0:T(8,128)(2,1)S(1)} %reduce-precision_convert_fusion.5, bf16[896,128]{1,0:T(8,128)(2,1)S(1)} %get-tuple-element.60), kind=kOutput, calls=%fused_computation.36 | convolution fusion | flops 628260864 | bytes 5734400 | tf_op jit(solution)/shard_map/dot_general | solution.py:189
  59.1 0.7 collective-permute-start.10
  59.8 2.8 %collective-permute-start.11 = (f32[224,128]{1,0:T(8,128)S(1)}, f32[224,128]{1,0:T(8,128)S(1)}, u32[]{:S(2)}, u32[]{:S(2)}) collective-permute-start(f32[224,128]{1,0:T(8,128)S(1)} %get-tuple-element.109), channel_id=1, source_target_pairs={{0,1},{1,0},{2,3},{3,2},{4,5},{5,4},{6,7},{7,6},{8,9},{9,8},{10,11... | collective-permute-start | bytes 344072 | tf_op jit(solution)/shard_map/ppermute | solution.py:75
  62.6 0.7 collective-permute-start.12
  63.3 2.6 %collective-permute-start.13 = (f32[224,128]{1,0:T(8,128)S(1)}, f32[224,128]{1,0:T(8,128)S(1)}, u32[]{:S(2)}, u32[]{:S(2)}) collective-permute-start(f32[224,128]{1,0:T(8,128)S(1)} %get-tuple-element.108), channel_id=1, source_target_pairs={{0,4},{4,0},{8,12},{12,8},{16,20},{20,16},{24,28},{28,24},{1,5},{5... | collective-permute-start | bytes 344072 | tf_op jit(solution)/shard_map/ppermute | solution.py:75
  65.8 2.2 %collective-permute-done.11 = f32[224,128]{1,0:T(8,128)S(1)} collective-permute-done((f32[224,128]{1,0:T(8,128)S(1)}, f32[224,128]{1,0:T(8,128)S(1)}, u32[]{:S(2)}, u32[]{:S(2)}) %collective-permute-start.11) | collective-permute-done | bytes 114720 | tf_op jit(solution)/shard_map/ppermute | solution.py:75
  68.3 1.4 %fusion.26 = f32[896,128]{1,0:T(8,128)S(1)} fusion(bf16[896,1792]{1,0:T(8,128)(2,1)S(1)} %add_convert_fusion, bf16[896,896]{1,0:T(8,128)(2,1)S(1)} %slice.177, bf16[896,128]{1,0:T(8,128)(2,1)S(1)} %reduce-precision_convert_fusion.4, bf16[896,128]{1,0:T(8,128)(2,1)S(1)} %get-tuple-element.58), kind=kOutput, calls=%fused_computation.35 | convolution fusion | flops 628260864 | bytes 5734400 | tf_op jit(solution)/shard_map/dot_general | solution.py:189
  69.8 0.7 collective-permute-start.14
  70.4 2.7 %collective-permute-start.15 = (f32[224,128]{1,0:T(8,128)S(1)}, f32[224,128]{1,0:T(8,128)S(1)}, u32[]{:S(2)}, u32[]{:S(2)}) collective-permute-start(f32[224,128]{1,0:T(8,128)S(1)} %get-tuple-element.103), channel_id=1, source_target_pairs={{0,1},{1,0},{2,3},{3,2},{4,5},{5,4},{6,7},{7,6},{8,9},{9,8},{10,11... | collective-permute-start | bytes 344072 | tf_op jit(solution)/shard_map/ppermute | solution.py:75
  73.2 0.7 collective-permute-start.16
  73.8 3.4 %collective-permute-start.17 = (f32[224,128]{1,0:T(8,128)S(1)}, f32[224,128]{1,0:T(8,128)S(1)}, u32[]{:S(2)}, u32[]{:S(2)}) collective-permute-start(f32[224,128]{1,0:T(8,128)S(1)} %get-tuple-element.102), channel_id=1, source_target_pairs={{0,4},{4,0},{8,12},{12,8},{16,20},{20,16},{24,28},{28,24},{1,5},{5... | collective-permute-start | bytes 344072 | tf_op jit(solution)/shard_map/ppermute | solution.py:75
  77.2 1.9 %collective-permute-done.15 = f32[224,128]{1,0:T(8,128)S(1)} collective-permute-done((f32[224,128]{1,0:T(8,128)S(1)}, f32[224,128]{1,0:T(8,128)S(1)}, u32[]{:S(2)}, u32[]{:S(2)}) %collective-permute-start.15) | collective-permute-done | bytes 114720 | tf_op jit(solution)/shard_map/ppermute | solution.py:75
  79.3 1.4 %fusion.25 = f32[896,128]{1,0:T(8,128)S(1)} fusion(bf16[896,1792]{1,0:T(8,128)(2,1)S(1)} %add_convert_fusion, bf16[896,896]{1,0:T(8,128)(2,1)S(1)} %slice.177, bf16[896,128]{1,0:T(8,128)(2,1)S(1)} %reduce-precision_convert_fusion.3, bf16[896,128]{1,0:T(8,128)(2,1)S(1)} %get-tuple-element.56), kind=kOutput, calls=%fused_computation.34 | convolution fusion | flops 628260864 | bytes 5734400 | tf_op jit(solution)/shard_map/dot_general | solution.py:189
  80.8 0.7 collective-permute-start.18
  81.5 2.3 %collective-permute-start.19 = (f32[224,128]{1,0:T(8,128)S(1)}, f32[224,128]{1,0:T(8,128)S(1)}, u32[]{:S(2)}, u32[]{:S(2)}) collective-permute-start(f32[224,128]{1,0:T(8,128)S(1)} %get-tuple-element.97), channel_id=1, source_target_pairs={{0,1},{1,0},{2,3},{3,2},{4,5},{5,4},{6,7},{7,6},{8,9},{9,8},{10,11... | collective-permute-start | bytes 344072 | tf_op jit(solution)/shard_map/ppermute | solution.py:75
  83.8 0.7 collective-permute-start.20
  84.4 4.0 %collective-permute-start.21 = (f32[224,128]{1,0:T(8,128)S(1)}, f32[224,128]{1,0:T(8,128)S(1)}, u32[]{:S(2)}, u32[]{:S(2)}) collective-permute-start(f32[224,128]{1,0:T(8,128)S(1)} %get-tuple-element.96), channel_id=1, source_target_pairs={{0,4},{4,0},{8,12},{12,8},{16,20},{20,16},{24,28},{28,24},{1,5},{5... | collective-permute-start | bytes 344072 | tf_op jit(solution)/shard_map/ppermute | solution.py:75
  88.5 1.0 %add_add_fusion = f32[1,1,896,128]{3,2,1,0:T(8,128)} fusion(f32[1,1,224,128]{3,2,1,0:T(8,128)S(1)} %bitcast.42, f32[1,1,224,128]{3,2,1,0:T(8,128)S(1)} %bitcast.44, f32[1,1,224,128]{3,2,1,0:T(8,128)S(1)} %bitcast.40, f32[1,1,224,128]{3,2,1,0:T(8,128)S(1)} %bitcast.38, f32[1,1,224,128]{3,2,1,0:T(8,128)S(1)} %bitcast.50, f32[1,1,224,128]{3,2,1,0:T(8,128)S(1)} %bitcast.52, ...), kind=kLoop, calls=%fused_computation.104 | loop fusion | flops 3211264 | bytes 2293760 | tf_op jit(solution)/shard_map/add | solution.py:166
  89.5 0.7 collective-permute-done.19
  90.2 0.9 %maximum_subtract_fusion.6 = f32[1,1,896,128]{3,2,1,0:T(8,128)} fusion(f32[1,1,224,128]{3,2,1,0:T(8,128)S(1)} %get-tuple-element.94, f32[1,1,224,128]{3,2,1,0:T(8,128)S(1)} %get-tuple-element.95, f32[1,1,224,128]{3,2,1,0:T(8,128)S(1)} %get-tuple-element.75, f32[1,1,224,128]{3,2,1,0:T(8,128)S(1)} %get-tuple-element.74, f32[1,1,224,128]{3,2,1,0:T(8,128)S(1)} %bitcast.69, ...), kind=kLoop, calls=%fused_computation.103 | loop fusion | flops 2179072 | bytes 2752512 | tf_op jit(solution)/shard_map/sub | solution.py:191
  (52 shorter events, 2.1 us)
Async XLA Ops:
  0.6 12.3 %copy-start = (f32[1,1,640,896]{3,2,1,0:T(8,128)S(1)}, f32[1,1,640,896]{3,2,1,0:T(8,128)}, u32[]{:S(2)}) copy-start(f32[1,1,640,896]{3,2,1,0:T(8,128)} %param.7) | copy-start | bytes 6881284
  4.8 20.7 %collective-permute-start = (f32[224,128]{1,0:T(8,128)}, f32[224,128]{1,0:T(8,128)S(1)}, u32[]{:S(2)}, u32[]{:S(2)}) collective-permute-start(f32[224,128]{1,0:T(8,128)} %get-tuple-element.124), channel_id=1, source_target_pairs={{4,8},{8,4},{12,16},{16,12},{20,24},{24,20},{5,9},{9,5},{13,17},{1... | collective-permute-start | bytes 344072 | tf_op jit(solution)/shard_map/ppermute | solution.py:66
  5.5 20.0 %collective-permute-start.1 = (f32[224,128]{1,0:T(8,128)}, f32[224,128]{1,0:T(8,128)}, u32[]{:S(2)}, u32[]{:S(2)}) collective-permute-start(f32[224,128]{1,0:T(8,128)} %get-tuple-element.122), channel_id=1, source_target_pairs={{0,4},{4,0},{8,12},{12,8},{16,20},{20,16},{24,28},{28,24},{1,5},{5... | collective-permute-start | bytes 344072 | tf_op jit(solution)/shard_map/ppermute | solution.py:66
  9.9 27.2 %collective-permute-start.4 = (f32[128,896]{1,0:T(8,128)}, f32[128,896]{1,0:T(8,128)}, u32[]{:S(2)}, u32[]{:S(2)}) collective-permute-start(f32[128,896]{1,0:T(8,128)} %get-tuple-element.38), channel_id=1, source_target_pairs={{0,24},{4,28},{8,0},{12,4},{16,8},{20,12},{24,16},{28,20},{1,25},{... | collective-permute-start | bytes 1376264 | tf_op jit(solution)/shard_map/ppermute | solution.py:22
  11.9 31.5 %collective-permute-start.5 = (f32[128,896]{1,0:T(8,128)}, f32[128,896]{1,0:T(8,128)}, u32[]{:S(2)}, u32[]{:S(2)}) collective-permute-start(f32[128,896]{1,0:T(8,128)} %get-tuple-element.39), channel_id=1, source_target_pairs={{0,16},{4,20},{8,24},{12,28},{16,0},{20,4},{24,8},{28,12},{1,17},{... | collective-permute-start | bytes 1376264 | tf_op jit(solution)/shard_map/ppermute | solution.py:22
  19.7 2.8 %copy-start.4 = (s32[1,1,2]{2,1,0:T(1,128)S(1)}, s32[1,1,2]{2,1,0:T(1,128)}, u32[]{:S(2)}) copy-start(s32[1,1,2]{2,1,0:T(1,128)} %param.9) | copy-start | bytes 28
  19.7 5.8 %copy-start.3 = (f32[224,128]{1,0:T(8,128)S(1)}, f32[224,128]{1,0:T(8,128)}, u32[]{:S(2)}) copy-start(f32[224,128]{1,0:T(8,128)} %get-tuple-element.30) | copy-start | bytes 344068
  19.7 6.5 %copy-start.2 = (f32[224,128]{1,0:T(8,128)S(1)}, f32[224,128]{1,0:T(8,128)}, u32[]{:S(2)}) copy-start(f32[224,128]{1,0:T(8,128)} %get-tuple-element.31) | copy-start | bytes 344068
  22.5 12.9 %copy-start.1 = (f32[1,1,896,128]{3,2,1,0:T(8,128)S(1)}, f32[1,1,896,128]{3,2,1,0:T(8,128)}, u32[]{:S(2)}) copy-start(f32[1,1,896,128]{3,2,1,0:T(8,128)} %param.6) | copy-start | bytes 1376260
  25.5 5.1 %collective-permute-start.2 = (f32[224,128]{1,0:T(8,128)S(1)}, f32[224,128]{1,0:T(8,128)S(1)}, u32[]{:S(2)}, u32[]{:S(2)}) collective-permute-start(f32[224,128]{1,0:T(8,128)S(1)} %copy-done.3), channel_id=1, source_target_pairs={{1,2},{2,1},{5,6},{6,5},{9,10},{10,9},{13,14},{14,13},{17,18},{18,... | collective-permute-start | bytes 344072 | tf_op jit(solution)/shard_map/ppermute | solution.py:69
  26.2 9.2 %collective-permute-start.3 = (f32[224,128]{1,0:T(8,128)S(1)}, f32[224,128]{1,0:T(8,128)S(1)}, u32[]{:S(2)}, u32[]{:S(2)}) collective-permute-start(f32[224,128]{1,0:T(8,128)S(1)} %copy-done.2), channel_id=1, source_target_pairs={{0,1},{1,0},{2,3},{3,2},{4,5},{5,4},{6,7},{7,6},{8,9},{9,8},{10,11... | collective-permute-start | bytes 344072 | tf_op jit(solution)/shard_map/ppermute | solution.py:69
  47.2 10.2 %collective-permute-start.6 = (f32[224,128]{1,0:T(8,128)S(1)}, f32[224,128]{1,0:T(8,128)S(1)}, u32[]{:S(2)}, u32[]{:S(2)}) collective-permute-start(f32[224,128]{1,0:T(8,128)S(1)} %get-tuple-element.117), channel_id=1, source_target_pairs={{1,2},{2,1},{5,6},{6,5},{9,10},{10,9},{13,14},{14,13},{17,18},{18,... | collective-permute-start | bytes 344072 | tf_op jit(solution)/shard_map/ppermute | solution.py:75
  47.9 9.5 %collective-permute-start.7 = (f32[224,128]{1,0:T(8,128)S(1)}, f32[224,128]{1,0:T(8,128)S(1)}, u32[]{:S(2)}, u32[]{:S(2)}) collective-permute-start(f32[224,128]{1,0:T(8,128)S(1)} %get-tuple-element.115), channel_id=1, source_target_pairs={{0,1},{1,0},{2,3},{3,2},{4,5},{5,4},{6,7},{7,6},{8,9},{9,8},{10,11... | collective-permute-start | bytes 344072 | tf_op jit(solution)/shard_map/ppermute | solution.py:75
  52.2 5.3 %collective-permute-start.8 = (f32[224,128]{1,0:T(8,128)S(1)}, f32[224,128]{1,0:T(8,128)S(1)}, u32[]{:S(2)}, u32[]{:S(2)}) collective-permute-start(f32[224,128]{1,0:T(8,128)S(1)} %get-tuple-element.116), channel_id=1, source_target_pairs={{4,8},{8,4},{12,16},{16,12},{20,24},{24,20},{5,9},{9,5},{13,17},{1... | collective-permute-start | bytes 344072 | tf_op jit(solution)/shard_map/ppermute | solution.py:75
  53.0 4.4 %collective-permute-start.9 = (f32[224,128]{1,0:T(8,128)S(1)}, f32[224,128]{1,0:T(8,128)S(1)}, u32[]{:S(2)}, u32[]{:S(2)}) collective-permute-start(f32[224,128]{1,0:T(8,128)S(1)} %get-tuple-element.114), channel_id=1, source_target_pairs={{0,4},{4,0},{8,12},{12,8},{16,20},{20,16},{24,28},{28,24},{1,5},{5... | collective-permute-start | bytes 344072 | tf_op jit(solution)/shard_map/ppermute | solution.py:75
  59.1 6.7 %collective-permute-start.10 = (f32[224,128]{1,0:T(8,128)S(1)}, f32[224,128]{1,0:T(8,128)S(1)}, u32[]{:S(2)}, u32[]{:S(2)}) collective-permute-start(f32[224,128]{1,0:T(8,128)S(1)} %get-tuple-element.111), channel_id=1, source_target_pairs={{1,2},{2,1},{5,6},{6,5},{9,10},{10,9},{13,14},{14,13},{17,18},{18,... | collective-permute-start | bytes 344072 | tf_op jit(solution)/shard_map/ppermute | solution.py:75
  59.8 8.2 %collective-permute-start.11 = (f32[224,128]{1,0:T(8,128)S(1)}, f32[224,128]{1,0:T(8,128)S(1)}, u32[]{:S(2)}, u32[]{:S(2)}) collective-permute-start(f32[224,128]{1,0:T(8,128)S(1)} %get-tuple-element.109), channel_id=1, source_target_pairs={{0,1},{1,0},{2,3},{3,2},{4,5},{5,4},{6,7},{7,6},{8,9},{9,8},{10,11... | collective-permute-start | bytes 344072 | tf_op jit(solution)/shard_map/ppermute | solution.py:75
  62.6 5.4 %collective-permute-start.12 = (f32[224,128]{1,0:T(8,128)S(1)}, f32[224,128]{1,0:T(8,128)S(1)}, u32[]{:S(2)}, u32[]{:S(2)}) collective-permute-start(f32[224,128]{1,0:T(8,128)S(1)} %get-tuple-element.110), channel_id=1, source_target_pairs={{4,8},{8,4},{12,16},{16,12},{20,24},{24,20},{5,9},{9,5},{13,17},{1... | collective-permute-start | bytes 344072 | tf_op jit(solution)/shard_map/ppermute | solution.py:75
  63.3 4.8 %collective-permute-start.13 = (f32[224,128]{1,0:T(8,128)S(1)}, f32[224,128]{1,0:T(8,128)S(1)}, u32[]{:S(2)}, u32[]{:S(2)}) collective-permute-start(f32[224,128]{1,0:T(8,128)S(1)} %get-tuple-element.108), channel_id=1, source_target_pairs={{0,4},{4,0},{8,12},{12,8},{16,20},{20,16},{24,28},{28,24},{1,5},{5... | collective-permute-start | bytes 344072 | tf_op jit(solution)/shard_map/ppermute | solution.py:75
  69.8 7.4 %collective-permute-start.14 = (f32[224,128]{1,0:T(8,128)S(1)}, f32[224,128]{1,0:T(8,128)S(1)}, u32[]{:S(2)}, u32[]{:S(2)}) collective-permute-start(f32[224,128]{1,0:T(8,128)S(1)} %get-tuple-element.105), channel_id=1, source_target_pairs={{1,2},{2,1},{5,6},{6,5},{9,10},{10,9},{13,14},{14,13},{17,18},{18,... | collective-permute-start | bytes 344072 | tf_op jit(solution)/shard_map/ppermute | solution.py:75
  70.4 8.6 %collective-permute-start.15 = (f32[224,128]{1,0:T(8,128)S(1)}, f32[224,128]{1,0:T(8,128)S(1)}, u32[]{:S(2)}, u32[]{:S(2)}) collective-permute-start(f32[224,128]{1,0:T(8,128)S(1)} %get-tuple-element.103), channel_id=1, source_target_pairs={{0,1},{1,0},{2,3},{3,2},{4,5},{5,4},{6,7},{7,6},{8,9},{9,8},{10,11... | collective-permute-start | bytes 344072 | tf_op jit(solution)/shard_map/ppermute | solution.py:75
  73.2 5.9 %collective-permute-start.16 = (f32[224,128]{1,0:T(8,128)S(1)}, f32[224,128]{1,0:T(8,128)S(1)}, u32[]{:S(2)}, u32[]{:S(2)}) collective-permute-start(f32[224,128]{1,0:T(8,128)S(1)} %get-tuple-element.104), channel_id=1, source_target_pairs={{4,8},{8,4},{12,16},{16,12},{20,24},{24,20},{5,9},{9,5},{13,17},{1... | collective-permute-start | bytes 344072 | tf_op jit(solution)/shard_map/ppermute | solution.py:75
  73.8 5.3 %collective-permute-start.17 = (f32[224,128]{1,0:T(8,128)S(1)}, f32[224,128]{1,0:T(8,128)S(1)}, u32[]{:S(2)}, u32[]{:S(2)}) collective-permute-start(f32[224,128]{1,0:T(8,128)S(1)} %get-tuple-element.102), channel_id=1, source_target_pairs={{0,4},{4,0},{8,12},{12,8},{16,20},{20,16},{24,28},{28,24},{1,5},{5... | collective-permute-start | bytes 344072 | tf_op jit(solution)/shard_map/ppermute | solution.py:75
  80.8 8.7 %collective-permute-start.18 = (f32[224,128]{1,0:T(8,128)S(1)}, f32[224,128]{1,0:T(8,128)S(1)}, u32[]{:S(2)}, u32[]{:S(2)}) collective-permute-start(f32[224,128]{1,0:T(8,128)S(1)} %get-tuple-element.99), channel_id=1, source_target_pairs={{1,2},{2,1},{5,6},{6,5},{9,10},{10,9},{13,14},{14,13},{17,18},{18,... | collective-permute-start | bytes 344072 | tf_op jit(solution)/shard_map/ppermute | solution.py:75
  81.5 8.6 %collective-permute-start.19 = (f32[224,128]{1,0:T(8,128)S(1)}, f32[224,128]{1,0:T(8,128)S(1)}, u32[]{:S(2)}, u32[]{:S(2)}) collective-permute-start(f32[224,128]{1,0:T(8,128)S(1)} %get-tuple-element.97), channel_id=1, source_target_pairs={{0,1},{1,0},{2,3},{3,2},{4,5},{5,4},{6,7},{7,6},{8,9},{9,8},{10,11... | collective-permute-start | bytes 344072 | tf_op jit(solution)/shard_map/ppermute | solution.py:75
  83.8 6.4 %collective-permute-start.20 = (f32[224,128]{1,0:T(8,128)S(1)}, f32[224,128]{1,0:T(8,128)S(1)}, u32[]{:S(2)}, u32[]{:S(2)}) collective-permute-start(f32[224,128]{1,0:T(8,128)S(1)} %get-tuple-element.98), channel_id=1, source_target_pairs={{4,8},{8,4},{12,16},{16,12},{20,24},{24,20},{5,9},{9,5},{13,17},{1... | collective-permute-start | bytes 344072 | tf_op jit(solution)/shard_map/ppermute | solution.py:75
  84.4 5.7 %collective-permute-start.21 = (f32[224,128]{1,0:T(8,128)S(1)}, f32[224,128]{1,0:T(8,128)S(1)}, u32[]{:S(2)}, u32[]{:S(2)}) collective-permute-start(f32[224,128]{1,0:T(8,128)S(1)} %get-tuple-element.96), channel_id=1, source_target_pairs={{0,4},{4,0},{8,12},{12,8},{16,20},{20,16},{24,28},{28,24},{1,5},{5... | collective-permute-start | bytes 344072 | tf_op jit(solution)/shard_map/ppermute | solution.py:75

commit v16 on v10

--- a/solution.py
+++ b/solution.py
@@ -115,7 +115,7 @@
     face_sign = jnp.where(row_ids // (order_max // 4) % 2 == 0, -1.0, 1.0).astype(jnp.float32)
     slot_scale = face_sign * (slot_map < order_now).astype(jnp.float32)
     spill_parts = [spill_block[slot_id] for slot_id in range(2)]
-    gap_faces, spill_parts = lax.optimization_barrier((gap[0, 0], spill_parts))
+    gap_faces = gap[0, 0]
     homed = [
         from_behind(spill_parts[slot_id], "gx", -(slot_id + 1) * hop_span) for slot_id in range(2)
     ]

time: 90.4 us -> 91.8 us (1.015)
  other arithmetic: 7.28 us -> 9.06 us
    select_n x5, other arithmetic: 0.87 us -> 2.15 us  [face_sum_parts(): jnp.where(even, high, low)]
  transfers between devices with their start and end apart: 22 -> 22, of which waited for: 5 -> 5; matrix products, arithmetic and copies ran while one was open for 19% -> 21% of each run, Pallas kernels for 0% -> 0%
where the time goes in v16:
time: 91.8 us; the launch traced here: 90.5 us
  starting transfers between devices  41 us (45%)
  matrix products  15.7 us (17%)
  waiting for transfers between devices  15.5 us (17%)
  other arithmetic  9.06 us (10%)
  local copies, waits for them, and re-layouts  5.14 us (6%)
  between operations  4.14 us (5%)
    ppermute x20, starting transfers between devices, face_sum_parts(): lax.ppermute(block, axis, pairs)  38 us
    ppermute x20, waiting for transfers between devices, face_sum_parts(): lax.ppermute(block, axis, pairs)  10.9 us
    dot_general x2, matrix products, slot_pieces(): jnp.dot(stacked, to_rows, preferred_element_type=jnp.float32)  5.06 us
    ppermute x2, waiting for transfers between devices, from_behind(): return lax.ppermute(value, axis, pairs)  4.6 us
    dot_general x2, matrix products, slot_pieces(): return jnp.dot(to_slots, side, preferred_element_type=jnp.float32)  3.87 us
    ppermute x2, starting transfers between devices, from_behind(): return lax.ppermute(value, axis, pairs)  3.04 us
    dot_general x5, matrix products, bf16x3_apply(): both = jnp.dot(op_high, pair, preferred_element_type=jnp.float32)  2.92 us
    dot_general x5, matrix products, bf16x3_apply(): jnp.dot(op_mid, pair[:, :cols], preferred_element_type=jnp.float32)  2.72 us
  transfers between devices with their start and end apart: 22, of which 5 were waited for; matrix products, arithmetic and copies ran while one was open for 21% of the time, Pallas kernels for 0%

profile of v16, /device:TPU:0, one launch (start us, length us, event | category | flops | bytes accessed | tf_op | source)
XLA Modules:
  0.0 90.5 jit_solution(17906696591239540117)
XLA Ops:
  0.7 2.0 %bitcast_select_fusion = (f32[224,128]{1,0:T(8,128)}, f32[224,128]{1,0:T(8,128)}, f32[224,128]{1,0:T(8,128)}, f32[224,128]{1,0:T(8,128)}) fusion(f32[1,1,896,128]{3,2,1,0:T(8,128)} %param.6, pred[]{:T(512)S(6)} %eq.100, pred[]{:T(512)S(6)} %eq.101), kind=kLoop, calls=%fused_computation.129 | loop fusion | flops 114688 | bytes 917506 | tf_op jit(solution)/shard_map/jit(_where)/select_n | solution.py:64
  2.7 0.7 collective-permute-start
  3.3 4.4 %collective-permute-start.1 = (f32[224,128]{1,0:T(8,128)}, f32[224,128]{1,0:T(8,128)}, u32[]{:S(2)}, u32[]{:S(2)}) collective-permute-start(f32[224,128]{1,0:T(8,128)} %get-tuple-element.118), channel_id=1, source_target_pairs={{0,4},{4,0},{8,12},{12,8},{16,20},{20,16},{24,28},{28,24},{1,5},{5... | collective-permute-start | bytes 344072 | tf_op jit(solution)/shard_map/ppermute | solution.py:66
  7.8 2.1 %slice_bitcast_fusion = (f32[128,896]{1,0:T(8,128)}, f32[128,896]{1,0:T(8,128)}) fusion(f32[1,1,2,128,896]{4,3,2,1,0:T(8,128)} %param.8), kind=kLoop, calls=%fused_computation.105 | loop fusion | bytes 1835008 | tf_op jit(solution)/shard_map/squeeze | solution.py:117
  9.9 1.9 %collective-permute-start.4 = (f32[128,896]{1,0:T(8,128)}, f32[128,896]{1,0:T(8,128)}, u32[]{:S(2)}, u32[]{:S(2)}) collective-permute-start(f32[128,896]{1,0:T(8,128)} %get-tuple-element.69), channel_id=1, source_target_pairs={{0,24},{4,28},{8,0},{12,4},{16,8},{20,12},{24,16},{28,20},{1,25},{... | collective-permute-start | bytes 1376264 | tf_op jit(solution)/shard_map/ppermute | solution.py:22
  11.9 1.1 %collective-permute-start.5 = (f32[128,896]{1,0:T(8,128)}, f32[128,896]{1,0:T(8,128)}, u32[]{:S(2)}, u32[]{:S(2)}) collective-permute-start(f32[128,896]{1,0:T(8,128)} %get-tuple-element.68), channel_id=1, source_target_pairs={{0,16},{4,20},{8,24},{12,28},{16,0},{20,4},{24,8},{28,12},{1,17},{... | collective-permute-start | bytes 1376264 | tf_op jit(solution)/shard_map/ppermute | solution.py:22
  13.0 1.3 %reduce-precision_convert_fusion = (bf16[640,896]{1,0:T(8,128)(2,1)S(1)}, bf16[640,896]{1,0:T(8,128)(2,1)}) fusion(f32[1,1,640,896]{3,2,1,0:T(8,128)S(1)} %copy-done), kind=kLoop, calls=%fused_computation.2 | loop fusion | flops 2867200 | bytes 4587520 | tf_op jit(solution)/shard_map/convert.13
  14.3 0.7 reduce
  15.7 3.9 %convolution_convert_fusion = bf16[1280,896]{0,1:T(8,128)(2,1)S(1)} fusion(bf16[640,896]{1,0:T(8,128)(2,1)} %get-tuple-element.63, bf16[640,896]{1,0:T(8,128)(2,1)S(1)} %get-tuple-element.62, bf16[896]{0:T(1024)(128)(2,1)S(1)} %select_select_fusion, s32[896]{0:T(1024)S(1)} %reduce), kind=kOutput, calls=%fused_computation | convolution fusion | flops 2062548992 | bytes 4592896 | tf_op jit(solution)/shard_map/dot_general | solution.py:92
  19.8 2.7 %fusion.9 = f32[896,1792]{1,0:T(8,128)S(1)} fusion(bf16[640,896]{0,1:T(8,128)(2,1)S(1)} %get-tuple-element.61, bf16[640,896]{0,1:T(8,128)(2,1)S(1)} %get-tuple-element.60, bf16[896]{0:T(1024)(128)(2,1)S(1)} %select_select_fusion, s32[896]{0:T(1024)S(1)} %reduce), kind=kOutput, calls=%fused_computation.19 | convolution fusion | flops 2061516800 | bytes 8721664 | tf_op jit(solution)/shard_map/dot_general | solution.py:94
  22.5 0.6 fusion.103
  25.5 0.7 collective-permute-start.2
  26.2 4.3 %collective-permute-start.3 = (f32[224,128]{1,0:T(8,128)S(1)}, f32[224,128]{1,0:T(8,128)S(1)}, u32[]{:S(2)}, u32[]{:S(2)}) collective-permute-start(f32[224,128]{1,0:T(8,128)S(1)} %copy-done.2), channel_id=1, source_target_pairs={{0,1},{1,0},{2,3},{3,2},{4,5},{5,4},{6,7},{7,6},{8,9},{9,8},{10,11... | collective-permute-start | bytes 344072 | tf_op jit(solution)/shard_map/ppermute | solution.py:69
  30.5 4.8 %collective-permute-done.3 = f32[224,128]{1,0:T(8,128)S(1)} collective-permute-done((f32[224,128]{1,0:T(8,128)S(1)}, f32[224,128]{1,0:T(8,128)S(1)}, u32[]{:S(2)}, u32[]{:S(2)}) %collective-permute-start.3) | collective-permute-done | bytes 114720 | tf_op jit(solution)/shard_map/ppermute | solution.py:69
  35.3 1.0 %bitcast_add_fusion.3 = (f32[224,128]{1,0:T(8,128)S(1)}, f32[224,128]{1,0:T(8,128)S(1)}, f32[224,128]{1,0:T(8,128)S(1)}, f32[224,128]{1,0:T(8,128)S(1)}) fusion(f32[224,128]{1,0:T(8,128)S(1)} %collective-permute-done, f32[224,128]{1,0:T(8,128)} %collective-permute-done.1, f32[1,1,896,128]{3,2,1,0:T(8,128)S(1)} %copy-done.1, pred[]{:T(512)S(6)} %eq.100, ...), kind=kLoop, calls=%fused_computation.135 | loop fusion | flops 229376 | bytes 1376258 | tf_op jit(solution)/shard_map/add | solution.py:81
  36.4 0.6 fusion.25
  37.0 0.6 fusion.13
  37.7 1.0 %constant_dynamic-update-slice_fusion.1 = f32[256,896]{1,0:T(8,128)S(1)} fusion(f32[128,896]{1,0:T(8,128)} %collective-permute-done.4), kind=kLoop, calls=%fused_computation.181 | loop fusion | bytes 917504
  38.8 4.6 %collective-permute-done.5 = f32[128,896]{1,0:T(8,128)} collective-permute-done((f32[128,896]{1,0:T(8,128)}, f32[128,896]{1,0:T(8,128)}, u32[]{:S(2)}, u32[]{:S(2)}) %collective-permute-start.5) | collective-permute-done | bytes 458784 | tf_op jit(solution)/shard_map/ppermute | solution.py:22
  43.4 1.0 %constant_dynamic-update-slice_fusion = f32[256,896]{1,0:T(8,128)S(1)} fusion(f32[256,896]{1,0:T(8,128)S(1)} %constant_dynamic-update-slice_fusion.1, f32[128,896]{1,0:T(8,128)} %collective-permute-done.5), kind=kLoop, calls=%fused_computation.179 | loop fusion | bytes 917504 | tf_op jit(solution)/shard_map/concatenate | solution.py:146
  45.7 0.7 fusion.27
  46.4 0.7 collective-permute-start.6
  47.1 4.3 %collective-permute-start.7 = (f32[224,128]{1,0:T(8,128)S(1)}, f32[224,128]{1,0:T(8,128)S(1)}, u32[]{:S(2)}, u32[]{:S(2)}) collective-permute-start(f32[224,128]{1,0:T(8,128)S(1)} %get-tuple-element.111), channel_id=1, source_target_pairs={{0,1},{1,0},{2,3},{3,2},{4,5},{5,4},{6,7},{7,6},{8,9},{9,8},{10,11... | collective-permute-start | bytes 344072 | tf_op jit(solution)/shard_map/ppermute | solution.py:75
  51.4 0.8 collective-permute-start.8
  52.2 1.8 %collective-permute-start.9 = (f32[224,128]{1,0:T(8,128)S(1)}, f32[224,128]{1,0:T(8,128)S(1)}, u32[]{:S(2)}, u32[]{:S(2)}) collective-permute-start(f32[224,128]{1,0:T(8,128)S(1)} %get-tuple-element.110), channel_id=1, source_target_pairs={{0,4},{4,0},{8,12},{12,8},{16,20},{20,16},{24,28},{28,24},{1,5},{5... | collective-permute-start | bytes 344072 | tf_op jit(solution)/shard_map/ppermute | solution.py:75
  54.0 1.2 %fusion.24 = bf16[512,896]{1,0:T(8,128)(2,1)S(1)} fusion(bf16[896]{0:T(1024)(128)(2,1)S(1)} %select_select_fusion, s32[896]{0:T(1024)S(1)} %reduce, bf16[256,896]{1,0:T(8,128)(2,1)S(1)} %get-tuple-element.66, bf16[256,896]{1,0:T(8,128)(2,1)S(1)} %get-tuple-element.67), kind=kOutput, calls=%fused_computation.35 | convolution fusion | flops 825982976 | bytes 1840384 | tf_op jit(solution)/shard_map/dot_general | solution.py:92
  55.3 1.1 %fusion.35 = f32[896,1792]{1,0:T(8,128)S(1)} fusion(bf16[256,896]{1,0:T(8,128)(2,1)S(1)} %get-tuple-element.65, bf16[256,896]{1,0:T(8,128)(2,1)S(1)} %get-tuple-element.64, bf16[896]{0:T(1024)(128)(2,1)S(1)} %select_select_fusion, s32[256]{0:T(256)S(1)} %pad_add_fusion, s32[896]{0:T(1024)S(1)} %reduce), kind=kOutput, calls=%fused_computation.51 | convolution fusion | flops 824377344 | bytes 7346432 | tf_op jit(solution)/shard_map/dot_general | solution.py:94
  56.5 1.0 %fusion.1 = (bf16[896,896]{1,0:T(8,128)(2,1)S(1)}, bf16[896,896]{1,0:T(8,128)(2,1)S(1)}) fusion(f32[896,1792]{1,0:T(8,128)S(1)} %fusion.35, f32[896,1792]{1,0:T(8,128)S(1)} %fusion.9), kind=kLoop, calls=%fused_computation.6 | loop fusion | flops 3211264 | bytes 16056320 | tf_op jit(solution)/shard_map/convert_element_type | solution.py:150
  57.7 0.6 fusion.47
  59.0 0.7 collective-permute-start.10
  59.7 2.8 %collective-permute-start.11 = (f32[224,128]{1,0:T(8,128)S(1)}, f32[224,128]{1,0:T(8,128)S(1)}, u32[]{:S(2)}, u32[]{:S(2)}) collective-permute-start(f32[224,128]{1,0:T(8,128)S(1)} %get-tuple-element.105), channel_id=1, source_target_pairs={{0,1},{1,0},{2,3},{3,2},{4,5},{5,4},{6,7},{7,6},{8,9},{9,8},{10,11... | collective-permute-start | bytes 344072 | tf_op jit(solution)/shard_map/ppermute | solution.py:75
  62.5 0.7 collective-permute-start.12
  63.1 1.7 %collective-permute-start.13 = (f32[224,128]{1,0:T(8,128)S(1)}, f32[224,128]{1,0:T(8,128)S(1)}, u32[]{:S(2)}, u32[]{:S(2)}) collective-permute-start(f32[224,128]{1,0:T(8,128)S(1)} %get-tuple-element.104), channel_id=1, source_target_pairs={{0,4},{4,0},{8,12},{12,8},{16,20},{20,16},{24,28},{28,24},{1,5},{5... | collective-permute-start | bytes 344072 | tf_op jit(solution)/shard_map/ppermute | solution.py:75
  64.9 3.0 %collective-permute-done.11 = f32[224,128]{1,0:T(8,128)S(1)} collective-permute-done((f32[224,128]{1,0:T(8,128)S(1)}, f32[224,128]{1,0:T(8,128)S(1)}, u32[]{:S(2)}, u32[]{:S(2)}) %collective-permute-start.11) | collective-permute-done | bytes 114720 | tf_op jit(solution)/shard_map/ppermute | solution.py:75
  68.2 0.6 fusion.51
  69.5 0.7 collective-permute-start.14
  70.1 2.7 %collective-permute-start.15 = (f32[224,128]{1,0:T(8,128)S(1)}, f32[224,128]{1,0:T(8,128)S(1)}, u32[]{:S(2)}, u32[]{:S(2)}) collective-permute-start(f32[224,128]{1,0:T(8,128)S(1)} %get-tuple-element.99), channel_id=1, source_target_pairs={{0,1},{1,0},{2,3},{3,2},{4,5},{5,4},{6,7},{7,6},{8,9},{9,8},{10,11... | collective-permute-start | bytes 344072 | tf_op jit(solution)/shard_map/ppermute | solution.py:75
  72.9 0.7 collective-permute-start.16
  73.5 3.1 %collective-permute-start.17 = (f32[224,128]{1,0:T(8,128)S(1)}, f32[224,128]{1,0:T(8,128)S(1)}, u32[]{:S(2)}, u32[]{:S(2)}) collective-permute-start(f32[224,128]{1,0:T(8,128)S(1)} %get-tuple-element.98), channel_id=1, source_target_pairs={{0,4},{4,0},{8,12},{12,8},{16,20},{20,16},{24,28},{28,24},{1,5},{5... | collective-permute-start | bytes 344072 | tf_op jit(solution)/shard_map/ppermute | solution.py:75
  76.6 2.2 %collective-permute-done.15 = f32[224,128]{1,0:T(8,128)S(1)} collective-permute-done((f32[224,128]{1,0:T(8,128)S(1)}, f32[224,128]{1,0:T(8,128)S(1)}, u32[]{:S(2)}, u32[]{:S(2)}) %collective-permute-start.15) | collective-permute-done | bytes 114720 | tf_op jit(solution)/shard_map/ppermute | solution.py:75
  79.0 0.6 fusion.57
  80.3 0.7 collective-permute-start.18
  81.0 2.3 %collective-permute-start.19 = (f32[224,128]{1,0:T(8,128)S(1)}, f32[224,128]{1,0:T(8,128)S(1)}, u32[]{:S(2)}, u32[]{:S(2)}) collective-permute-start(f32[224,128]{1,0:T(8,128)S(1)} %get-tuple-element.93), channel_id=1, source_target_pairs={{0,1},{1,0},{2,3},{3,2},{4,5},{5,4},{6,7},{7,6},{8,9},{9,8},{10,11... | collective-permute-start | bytes 344072 | tf_op jit(solution)/shard_map/ppermute | solution.py:75
  83.3 0.7 collective-permute-start.20
  84.0 3.7 %collective-permute-start.21 = (f32[224,128]{1,0:T(8,128)S(1)}, f32[224,128]{1,0:T(8,128)S(1)}, u32[]{:S(2)}, u32[]{:S(2)}) collective-permute-start(f32[224,128]{1,0:T(8,128)S(1)} %get-tuple-element.92), channel_id=1, source_target_pairs={{0,4},{4,0},{8,12},{12,8},{16,20},{20,16},{24,28},{28,24},{1,5},{5... | collective-permute-start | bytes 344072 | tf_op jit(solution)/shard_map/ppermute | solution.py:75
  87.7 1.0 %add_add_fusion = f32[1,1,896,128]{3,2,1,0:T(8,128)} fusion(f32[1,1,224,128]{3,2,1,0:T(8,128)S(1)} %bitcast.67, f32[1,1,224,128]{3,2,1,0:T(8,128)S(1)} %bitcast.69, f32[1,1,224,128]{3,2,1,0:T(8,128)S(1)} %bitcast.65, f32[1,1,224,128]{3,2,1,0:T(8,128)S(1)} %bitcast.63, f32[1,1,224,128]{3,2,1,0:T(8,128)S(1)} %bitcast.75, f32[1,1,224,128]{3,2,1,0:T(8,128)S(1)} %bitcast.77, ...), kind=kLoop, calls=%fused_computation.102 | loop fusion | flops 3211264 | bytes 2293760 | tf_op jit(solution)/shard_map/add | solution.py:163
  88.7 0.9 collective-permute-done.19
  89.7 0.9 maximum_subtract_fusion.6
  (55 shorter events, 4.4 us)
Async XLA Ops:
  0.6 12.3 %copy-start = (f32[1,1,640,896]{3,2,1,0:T(8,128)S(1)}, f32[1,1,640,896]{3,2,1,0:T(8,128)}, u32[]{:S(2)}) copy-start(f32[1,1,640,896]{3,2,1,0:T(8,128)} %param.7) | copy-start | bytes 6881284
  2.7 22.8 %collective-permute-start = (f32[224,128]{1,0:T(8,128)}, f32[224,128]{1,0:T(8,128)S(1)}, u32[]{:S(2)}, u32[]{:S(2)}) collective-permute-start(f32[224,128]{1,0:T(8,128)} %get-tuple-element.120), channel_id=1, source_target_pairs={{4,8},{8,4},{12,16},{16,12},{20,24},{24,20},{5,9},{9,5},{13,17},{1... | collective-permute-start | bytes 344072 | tf_op jit(solution)/shard_map/ppermute | solution.py:66
  3.3 22.2 %collective-permute-start.1 = (f32[224,128]{1,0:T(8,128)}, f32[224,128]{1,0:T(8,128)}, u32[]{:S(2)}, u32[]{:S(2)}) collective-permute-start(f32[224,128]{1,0:T(8,128)} %get-tuple-element.118), channel_id=1, source_target_pairs={{0,4},{4,0},{8,12},{12,8},{16,20},{20,16},{24,28},{28,24},{1,5},{5... | collective-permute-start | bytes 344072 | tf_op jit(solution)/shard_map/ppermute | solution.py:66
  9.9 27.8 %collective-permute-start.4 = (f32[128,896]{1,0:T(8,128)}, f32[128,896]{1,0:T(8,128)}, u32[]{:S(2)}, u32[]{:S(2)}) collective-permute-start(f32[128,896]{1,0:T(8,128)} %get-tuple-element.69), channel_id=1, source_target_pairs={{0,24},{4,28},{8,0},{12,4},{16,8},{20,12},{24,16},{28,20},{1,25},{... | collective-permute-start | bytes 1376264 | tf_op jit(solution)/shard_map/ppermute | solution.py:22
  11.9 31.5 %collective-permute-start.5 = (f32[128,896]{1,0:T(8,128)}, f32[128,896]{1,0:T(8,128)}, u32[]{:S(2)}, u32[]{:S(2)}) collective-permute-start(f32[128,896]{1,0:T(8,128)} %get-tuple-element.68), channel_id=1, source_target_pairs={{0,16},{4,20},{8,24},{12,28},{16,0},{20,4},{24,8},{28,12},{1,17},{... | collective-permute-start | bytes 1376264 | tf_op jit(solution)/shard_map/ppermute | solution.py:22
  19.7 2.8 %copy-start.4 = (s32[1,1,2]{2,1,0:T(1,128)S(1)}, s32[1,1,2]{2,1,0:T(1,128)}, u32[]{:S(2)}) copy-start(s32[1,1,2]{2,1,0:T(1,128)} %param.9) | copy-start | bytes 28
  19.7 5.8 %copy-start.3 = (f32[224,128]{1,0:T(8,128)S(1)}, f32[224,128]{1,0:T(8,128)}, u32[]{:S(2)}) copy-start(f32[224,128]{1,0:T(8,128)} %get-tuple-element.26) | copy-start | bytes 344068
  19.8 6.4 %copy-start.2 = (f32[224,128]{1,0:T(8,128)S(1)}, f32[224,128]{1,0:T(8,128)}, u32[]{:S(2)}) copy-start(f32[224,128]{1,0:T(8,128)} %get-tuple-element.27) | copy-start | bytes 344068
  19.8 15.6 %copy-start.1 = (f32[1,1,896,128]{3,2,1,0:T(8,128)S(1)}, f32[1,1,896,128]{3,2,1,0:T(8,128)}, u32[]{:S(2)}) copy-start(f32[1,1,896,128]{3,2,1,0:T(8,128)} %param.6) | copy-start | bytes 1376260
  25.5 5.0 %collective-permute-start.2 = (f32[224,128]{1,0:T(8,128)S(1)}, f32[224,128]{1,0:T(8,128)S(1)}, u32[]{:S(2)}, u32[]{:S(2)}) collective-permute-start(f32[224,128]{1,0:T(8,128)S(1)} %copy-done.3), channel_id=1, source_target_pairs={{1,2},{2,1},{5,6},{6,5},{9,10},{10,9},{13,14},{14,13},{17,18},{18,... | collective-permute-start | bytes 344072 | tf_op jit(solution)/shard_map/ppermute | solution.py:69
  26.2 9.1 %collective-permute-start.3 = (f32[224,128]{1,0:T(8,128)S(1)}, f32[224,128]{1,0:T(8,128)S(1)}, u32[]{:S(2)}, u32[]{:S(2)}) collective-permute-start(f32[224,128]{1,0:T(8,128)S(1)} %copy-done.2), channel_id=1, source_target_pairs={{0,1},{1,0},{2,3},{3,2},{4,5},{5,4},{6,7},{7,6},{8,9},{9,8},{10,11... | collective-permute-start | bytes 344072 | tf_op jit(solution)/shard_map/ppermute | solution.py:69
  46.4 11.1 %collective-permute-start.6 = (f32[224,128]{1,0:T(8,128)S(1)}, f32[224,128]{1,0:T(8,128)S(1)}, u32[]{:S(2)}, u32[]{:S(2)}) collective-permute-start(f32[224,128]{1,0:T(8,128)S(1)} %get-tuple-element.113), channel_id=1, source_target_pairs={{1,2},{2,1},{5,6},{6,5},{9,10},{10,9},{13,14},{14,13},{17,18},{18,... | collective-permute-start | bytes 344072 | tf_op jit(solution)/shard_map/ppermute | solution.py:75
  47.1 10.4 %collective-permute-start.7 = (f32[224,128]{1,0:T(8,128)S(1)}, f32[224,128]{1,0:T(8,128)S(1)}, u32[]{:S(2)}, u32[]{:S(2)}) collective-permute-start(f32[224,128]{1,0:T(8,128)S(1)} %get-tuple-element.111), channel_id=1, source_target_pairs={{0,1},{1,0},{2,3},{3,2},{4,5},{5,4},{6,7},{7,6},{8,9},{9,8},{10,11... | collective-permute-start | bytes 344072 | tf_op jit(solution)/shard_map/ppermute | solution.py:75
  51.4 6.2 %collective-permute-start.8 = (f32[224,128]{1,0:T(8,128)S(1)}, f32[224,128]{1,0:T(8,128)S(1)}, u32[]{:S(2)}, u32[]{:S(2)}) collective-permute-start(f32[224,128]{1,0:T(8,128)S(1)} %get-tuple-element.112), channel_id=1, source_target_pairs={{4,8},{8,4},{12,16},{16,12},{20,24},{24,20},{5,9},{9,5},{13,17},{1... | collective-permute-start | bytes 344072 | tf_op jit(solution)/shard_map/ppermute | solution.py:75
  52.2 5.3 %collective-permute-start.9 = (f32[224,128]{1,0:T(8,128)S(1)}, f32[224,128]{1,0:T(8,128)S(1)}, u32[]{:S(2)}, u32[]{:S(2)}) collective-permute-start(f32[224,128]{1,0:T(8,128)S(1)} %get-tuple-element.110), channel_id=1, source_target_pairs={{0,4},{4,0},{8,12},{12,8},{16,20},{20,16},{24,28},{28,24},{1,5},{5... | collective-permute-start | bytes 344072 | tf_op jit(solution)/shard_map/ppermute | solution.py:75
  59.0 5.9 %collective-permute-start.10 = (f32[224,128]{1,0:T(8,128)S(1)}, f32[224,128]{1,0:T(8,128)S(1)}, u32[]{:S(2)}, u32[]{:S(2)}) collective-permute-start(f32[224,128]{1,0:T(8,128)S(1)} %get-tuple-element.107), channel_id=1, source_target_pairs={{1,2},{2,1},{5,6},{6,5},{9,10},{10,9},{13,14},{14,13},{17,18},{18,... | collective-permute-start | bytes 344072 | tf_op jit(solution)/shard_map/ppermute | solution.py:75
  59.7 8.2 %collective-permute-start.11 = (f32[224,128]{1,0:T(8,128)S(1)}, f32[224,128]{1,0:T(8,128)S(1)}, u32[]{:S(2)}, u32[]{:S(2)}) collective-permute-start(f32[224,128]{1,0:T(8,128)S(1)} %get-tuple-element.105), channel_id=1, source_target_pairs={{0,1},{1,0},{2,3},{3,2},{4,5},{5,4},{6,7},{7,6},{8,9},{9,8},{10,11... | collective-permute-start | bytes 344072 | tf_op jit(solution)/shard_map/ppermute | solution.py:75
  62.5 5.4 %collective-permute-start.12 = (f32[224,128]{1,0:T(8,128)S(1)}, f32[224,128]{1,0:T(8,128)S(1)}, u32[]{:S(2)}, u32[]{:S(2)}) collective-permute-start(f32[224,128]{1,0:T(8,128)S(1)} %get-tuple-element.106), channel_id=1, source_target_pairs={{4,8},{8,4},{12,16},{16,12},{20,24},{24,20},{5,9},{9,5},{13,17},{1... | collective-permute-start | bytes 344072 | tf_op jit(solution)/shard_map/ppermute | solution.py:75
  63.1 4.8 %collective-permute-start.13 = (f32[224,128]{1,0:T(8,128)S(1)}, f32[224,128]{1,0:T(8,128)S(1)}, u32[]{:S(2)}, u32[]{:S(2)}) collective-permute-start(f32[224,128]{1,0:T(8,128)S(1)} %get-tuple-element.104), channel_id=1, source_target_pairs={{0,4},{4,0},{8,12},{12,8},{16,20},{20,16},{24,28},{28,24},{1,5},{5... | collective-permute-start | bytes 344072 | tf_op jit(solution)/shard_map/ppermute | solution.py:75
  69.5 7.1 %collective-permute-start.14 = (f32[224,128]{1,0:T(8,128)S(1)}, f32[224,128]{1,0:T(8,128)S(1)}, u32[]{:S(2)}, u32[]{:S(2)}) collective-permute-start(f32[224,128]{1,0:T(8,128)S(1)} %get-tuple-element.101), channel_id=1, source_target_pairs={{1,2},{2,1},{5,6},{6,5},{9,10},{10,9},{13,14},{14,13},{17,18},{18,... | collective-permute-start | bytes 344072 | tf_op jit(solution)/shard_map/ppermute | solution.py:75
  70.1 8.6 %collective-permute-start.15 = (f32[224,128]{1,0:T(8,128)S(1)}, f32[224,128]{1,0:T(8,128)S(1)}, u32[]{:S(2)}, u32[]{:S(2)}) collective-permute-start(f32[224,128]{1,0:T(8,128)S(1)} %get-tuple-element.99), channel_id=1, source_target_pairs={{0,1},{1,0},{2,3},{3,2},{4,5},{5,4},{6,7},{7,6},{8,9},{9,8},{10,11... | collective-permute-start | bytes 344072 | tf_op jit(solution)/shard_map/ppermute | solution.py:75
  72.9 5.9 %collective-permute-start.16 = (f32[224,128]{1,0:T(8,128)S(1)}, f32[224,128]{1,0:T(8,128)S(1)}, u32[]{:S(2)}, u32[]{:S(2)}) collective-permute-start(f32[224,128]{1,0:T(8,128)S(1)} %get-tuple-element.100), channel_id=1, source_target_pairs={{4,8},{8,4},{12,16},{16,12},{20,24},{24,20},{5,9},{9,5},{13,17},{1... | collective-permute-start | bytes 344072 | tf_op jit(solution)/shard_map/ppermute | solution.py:75
  73.5 5.2 %collective-permute-start.17 = (f32[224,128]{1,0:T(8,128)S(1)}, f32[224,128]{1,0:T(8,128)S(1)}, u32[]{:S(2)}, u32[]{:S(2)}) collective-permute-start(f32[224,128]{1,0:T(8,128)S(1)} %get-tuple-element.98), channel_id=1, source_target_pairs={{0,4},{4,0},{8,12},{12,8},{16,20},{20,16},{24,28},{28,24},{1,5},{5... | collective-permute-start | bytes 344072 | tf_op jit(solution)/shard_map/ppermute | solution.py:75
  80.3 8.4 %collective-permute-start.18 = (f32[224,128]{1,0:T(8,128)S(1)}, f32[224,128]{1,0:T(8,128)S(1)}, u32[]{:S(2)}, u32[]{:S(2)}) collective-permute-start(f32[224,128]{1,0:T(8,128)S(1)} %get-tuple-element.95), channel_id=1, source_target_pairs={{1,2},{2,1},{5,6},{6,5},{9,10},{10,9},{13,14},{14,13},{17,18},{18,... | collective-permute-start | bytes 344072 | tf_op jit(solution)/shard_map/ppermute | solution.py:75
  81.0 8.6 %collective-permute-start.19 = (f32[224,128]{1,0:T(8,128)S(1)}, f32[224,128]{1,0:T(8,128)S(1)}, u32[]{:S(2)}, u32[]{:S(2)}) collective-permute-start(f32[224,128]{1,0:T(8,128)S(1)} %get-tuple-element.93), channel_id=1, source_target_pairs={{0,1},{1,0},{2,3},{3,2},{4,5},{5,4},{6,7},{7,6},{8,9},{9,8},{10,11... | collective-permute-start | bytes 344072 | tf_op jit(solution)/shard_map/ppermute | solution.py:75
  83.3 6.3 %collective-permute-start.20 = (f32[224,128]{1,0:T(8,128)S(1)}, f32[224,128]{1,0:T(8,128)S(1)}, u32[]{:S(2)}, u32[]{:S(2)}) collective-permute-start(f32[224,128]{1,0:T(8,128)S(1)} %get-tuple-element.94), channel_id=1, source_target_pairs={{4,8},{8,4},{12,16},{16,12},{20,24},{24,20},{5,9},{9,5},{13,17},{1... | collective-permute-start | bytes 344072 | tf_op jit(solution)/shard_map/ppermute | solution.py:75
  84.0 5.6 %collective-permute-start.21 = (f32[224,128]{1,0:T(8,128)S(1)}, f32[224,128]{1,0:T(8,128)S(1)}, u32[]{:S(2)}, u32[]{:S(2)}) collective-permute-start(f32[224,128]{1,0:T(8,128)S(1)} %get-tuple-element.92), channel_id=1, source_target_pairs={{0,4},{4,0},{8,12},{12,8},{16,20},{20,16},{24,28},{28,24},{1,5},{5... | collective-permute-start | bytes 344072 | tf_op jit(solution)/shard_map/ppermute | solution.py:75

commit v17 on v10

--- a/solution.py
+++ b/solution.py
@@ -54,7 +54,7 @@
     return pairs
 
 
-def face_sum_parts(faces, one_axis_at_a_time=False):
+def face_arrivals(faces, one_axis_at_a_time=False):
     low_x, high_x, low_y, high_y = faces
     sides = [(low_y, high_y, "gy"), (low_x, high_x, "gx")]
     sends = []
@@ -74,14 +74,14 @@
         received = lax.optimization_barrier(
             [lax.ppermute(block, axis, pairs) for block, pairs, axis in sends]
         )
-    summed = []
+    arrived = []
     for side_id, (low, high, axis) in enumerate(sides):
         even = lax.axis_index(axis) % 2 == 0
         odd_recv, even_recv = received[2 * side_id], received[2 * side_id + 1]
-        summed.append(low + jnp.where(even, odd_recv, even_recv))
-        summed.append(high + jnp.where(even, even_recv, odd_recv))
-    new_low_y, new_high_y, new_low_x, new_high_x = summed
-    return jnp.concatenate([new_low_x, new_high_x, new_low_y, new_high_y], axis=0)
+        arrived.append(jnp.where(even, odd_recv, even_recv))
+        arrived.append(jnp.where(even, even_recv, odd_recv))
+    from_low_y, from_high_y, from_low_x, from_high_x = arrived
+    return jnp.concatenate([from_low_x, from_high_x, from_low_y, from_high_y], axis=0)
 
 
 def slot_pieces(rows, to_rows, to_slots):
@@ -122,7 +122,7 @@
     own_count = own_block.shape[0]
     cols = gap.shape[3]
     width = order_max // 4
-    load = face_sum_parts(
+    load = gap_faces + face_arrivals(
         [gap_faces[face_id * width : (face_id + 1) * width] for face_id in range(4)],
         one_axis_at_a_time=True,
     )
@@ -182,7 +182,7 @@
         else:
             local = bf16x3_apply(op_high, op_mid, dir_pair, cols)
         faces = [local[face_id * width : (face_id + 1) * width] for face_id in range(4)]
-        residual = residual - face_sum_parts(faces)
+        residual = (residual - local) - face_arrivals(faces)
         if step_id + 1 < ITERS:
             rho_next = 1.0 / (2.0 * sigma_value - rho_value)
             direction = rho_next * rho_value * direction + 2.0 * rho_next / half_width * residual

time: 90.4 us -> 91.2 us (level)
  waiting for transfers between devices: 15.5 us -> 16.5 us
    add x5 -> x0, other arithmetic: 1.23 us -> none  [the longest x1 1.01 us: body(): solution = solution + direction]
    ppermute x20, waiting for transfers between devices: 10.7 us -> 11.7 us  [face_arrivals(): lax.ppermute(block, axis, pairs)]
  transfers between devices with their start and end apart: 22 -> 22, of which waited for: 5 -> 5; matrix products, arithmetic and copies ran while one was open for 19% -> 18% of each run, Pallas kernels for 0% -> 0%
where the time goes in v17:
time: 91.2 us; the launch traced here: 89.9 us
  starting transfers between devices  41.1 us (45%)
  waiting for transfers between devices  16.5 us (18%)
  matrix products  15.9 us (17%)
  other arithmetic  7.06 us (8%)
  local copies, waits for them, and re-layouts  5.1 us (6%)
  between operations  4.14 us (5%)
    ppermute x20, starting transfers between devices, face_arrivals(): lax.ppermute(block, axis, pairs)  38.1 us
    ppermute x20, waiting for transfers between devices, face_arrivals(): lax.ppermute(block, axis, pairs)  11.7 us
    dot_general x2, matrix products, slot_pieces(): jnp.dot(stacked, to_rows, preferred_element_type=jnp.float32)  5.4 us
    ppermute x2, waiting for transfers between devices, from_behind(): return lax.ppermute(value, axis, pairs)  4.8 us
    dot_general x2, matrix products, slot_pieces(): return jnp.dot(to_slots, side, preferred_element_type=jnp.float32)  3.87 us
    ppermute x2, starting transfers between devices, from_behind(): return lax.ppermute(value, axis, pairs)  3.04 us
    dot_general x5, matrix products, bf16x3_apply(): both = jnp.dot(op_high, pair, preferred_element_type=jnp.float32)  2.91 us
    dot_general x5, matrix products, bf16x3_apply(): jnp.dot(op_mid, pair[:, :cols], preferred_element_type=jnp.float32)  2.65 us
  transfers between devices with their start and end apart: 22, of which 5 were waited for; matrix products, arithmetic and copies ran while one was open for 18% of the time, Pallas kernels for 0%

profile of v17, /device:TPU:0, one launch (start us, length us, event | category | flops | bytes accessed | tf_op | source)
XLA Modules:
  0.0 89.9 jit_solution(16921523677913563236)
XLA Ops:
  0.7 2.1 %slice_bitcast_fusion = (f32[128,896]{1,0:T(8,128)S(1)}, f32[128,896]{1,0:T(8,128)}) fusion(f32[1,1,2,128,896]{4,3,2,1,0:T(8,128)} %param.8), kind=kLoop, calls=%fused_computation.107 | loop fusion | bytes 1835008 | tf_op jit(solution)/shard_map/squeeze | solution.py:117
  2.8 0.7 slice_select_fusion.16
  3.5 0.7 collective-permute-start
  4.2 4.4 %collective-permute-start.1 = (f32[224,128]{1,0:T(8,128)}, f32[224,128]{1,0:T(8,128)S(1)}, u32[]{:S(2)}, u32[]{:S(2)}) collective-permute-start(f32[224,128]{1,0:T(8,128)} %get-tuple-element.97), channel_id=1, source_target_pairs={{0,4},{4,0},{8,12},{12,8},{16,20},{20,16},{24,28},{28,24},{1,5},{5... | collective-permute-start | bytes 344072 | tf_op jit(solution)/shard_map/ppermute | solution.py:66
  8.6 2.0 %collective-permute-start.4 = (f32[128,896]{1,0:T(8,128)}, f32[128,896]{1,0:T(8,128)}, u32[]{:S(2)}, u32[]{:S(2)}) collective-permute-start(f32[128,896]{1,0:T(8,128)} %get-tuple-element.38), channel_id=1, source_target_pairs={{0,24},{4,28},{8,0},{12,4},{16,8},{20,12},{24,16},{28,20},{1,25},{... | collective-permute-start | bytes 1376264 | tf_op jit(solution)/shard_map/ppermute | solution.py:22
  10.6 1.1 %collective-permute-start.5 = (f32[128,896]{1,0:T(8,128)S(1)}, f32[128,896]{1,0:T(8,128)}, u32[]{:S(2)}, u32[]{:S(2)}) collective-permute-start(f32[128,896]{1,0:T(8,128)S(1)} %get-tuple-element.39), channel_id=1, source_target_pairs={{0,16},{4,20},{8,24},{12,28},{16,0},{20,4},{24,8},{28,12},{1,17},{... | collective-permute-start | bytes 1376264 | tf_op jit(solution)/shard_map/ppermute | solution.py:22
  11.7 1.7 %reduce-precision_convert_fusion = (bf16[640,896]{1,0:T(8,128)(2,1)}, bf16[640,896]{1,0:T(8,128)(2,1)}) fusion(f32[1,1,640,896]{3,2,1,0:T(8,128)S(1)} %copy-done), kind=kLoop, calls=%fused_computation.2 | loop fusion | flops 2867200 | bytes 4587520 | tf_op jit(solution)/shard_map/convert.13
  13.4 0.7 reduce
  14.8 4.2 %convolution_convert_fusion = bf16[1280,896]{0,1:T(8,128)(2,1)S(1)} fusion(bf16[640,896]{1,0:T(8,128)(2,1)} %get-tuple-element.72, bf16[640,896]{1,0:T(8,128)(2,1)} %get-tuple-element.71, bf16[896]{0:T(1024)(128)(2,1)S(1)} %select_select_fusion, s32[896]{0:T(1024)S(1)} %reduce), kind=kOutput, calls=%fused_computation | convolution fusion | flops 2062548992 | bytes 4592896 | tf_op jit(solution)/shard_map/dot_general | solution.py:92
  19.2 2.7 %fusion.9 = f32[896,1792]{1,0:T(8,128)S(1)} fusion(bf16[640,896]{0,1:T(8,128)(2,1)S(1)} %get-tuple-element.70, bf16[640,896]{0,1:T(8,128)(2,1)S(1)} %get-tuple-element.69, bf16[896]{0:T(1024)(128)(2,1)S(1)} %select_select_fusion, s32[896]{0:T(1024)S(1)} %reduce), kind=kOutput, calls=%fused_computation.19 | convolution fusion | flops 2061516800 | bytes 8721664 | tf_op jit(solution)/shard_map/dot_general | solution.py:94
  24.9 0.7 collective-permute-start.2
  25.6 4.3 %collective-permute-start.3 = (f32[224,128]{1,0:T(8,128)S(1)}, f32[224,128]{1,0:T(8,128)S(1)}, u32[]{:S(2)}, u32[]{:S(2)}) collective-permute-start(f32[224,128]{1,0:T(8,128)S(1)} %get-tuple-element.31), channel_id=1, source_target_pairs={{0,1},{1,0},{2,3},{3,2},{4,5},{5,4},{6,7},{7,6},{8,9},{9,8},{10,11... | collective-permute-start | bytes 344072 | tf_op jit(solution)/shard_map/ppermute | solution.py:69
  29.9 4.9 %collective-permute-done.3 = f32[224,128]{1,0:T(8,128)S(1)} collective-permute-done((f32[224,128]{1,0:T(8,128)S(1)}, f32[224,128]{1,0:T(8,128)S(1)}, u32[]{:S(2)}, u32[]{:S(2)}) %collective-permute-start.3) | collective-permute-done | bytes 114720 | tf_op jit(solution)/shard_map/ppermute | solution.py:69
  35.0 0.6 fusion.25
  35.6 0.6 fusion.13
  36.3 1.0 %constant_dynamic-update-slice_fusion.1 = f32[256,896]{1,0:T(8,128)S(1)} fusion(f32[128,896]{1,0:T(8,128)} %collective-permute-done.4), kind=kLoop, calls=%fused_computation.177 | loop fusion | bytes 917504
  37.3 4.8 %collective-permute-done.5 = f32[128,896]{1,0:T(8,128)} collective-permute-done((f32[128,896]{1,0:T(8,128)S(1)}, f32[128,896]{1,0:T(8,128)}, u32[]{:S(2)}, u32[]{:S(2)}) %collective-permute-start.5) | collective-permute-done | bytes 458784 | tf_op jit(solution)/shard_map/ppermute | solution.py:22
  42.1 1.0 %constant_dynamic-update-slice_fusion = f32[256,896]{1,0:T(8,128)S(1)} fusion(f32[256,896]{1,0:T(8,128)S(1)} %constant_dynamic-update-slice_fusion.1, f32[128,896]{1,0:T(8,128)} %collective-permute-done.5), kind=kLoop, calls=%fused_computation.175 | loop fusion | bytes 917504 | tf_op jit(solution)/shard_map/concatenate | solution.py:146
  44.4 0.6 fusion.27
  45.1 0.7 collective-permute-start.6
  45.8 4.3 %collective-permute-start.7 = (f32[224,128]{1,0:T(8,128)S(1)}, f32[224,128]{1,0:T(8,128)S(1)}, u32[]{:S(2)}, u32[]{:S(2)}) collective-permute-start(f32[224,128]{1,0:T(8,128)S(1)} %get-tuple-element.96), channel_id=1, source_target_pairs={{0,1},{1,0},{2,3},{3,2},{4,5},{5,4},{6,7},{7,6},{8,9},{9,8},{10,11... | collective-permute-start | bytes 344072 | tf_op jit(solution)/shard_map/ppermute | solution.py:75
  50.1 0.8 collective-permute-start.8
  50.9 1.7 %collective-permute-start.9 = (f32[224,128]{1,0:T(8,128)S(1)}, f32[224,128]{1,0:T(8,128)S(1)}, u32[]{:S(2)}, u32[]{:S(2)}) collective-permute-start(f32[224,128]{1,0:T(8,128)S(1)} %get-tuple-element.93), channel_id=1, source_target_pairs={{0,4},{4,0},{8,12},{12,8},{16,20},{20,16},{24,28},{28,24},{1,5},{5... | collective-permute-start | bytes 344072 | tf_op jit(solution)/shard_map/ppermute | solution.py:75
  52.6 1.2 %fusion.24 = bf16[512,896]{1,0:T(8,128)(2,1)S(1)} fusion(bf16[896]{0:T(1024)(128)(2,1)S(1)} %select_select_fusion, s32[896]{0:T(1024)S(1)} %reduce, bf16[256,896]{1,0:T(8,128)(2,1)S(1)} %get-tuple-element.77, bf16[256,896]{1,0:T(8,128)(2,1)S(1)} %get-tuple-element.78), kind=kOutput, calls=%fused_computation.35 | convolution fusion | flops 825982976 | bytes 1840384 | tf_op jit(solution)/shard_map/dot_general | solution.py:92
  53.9 1.1 %fusion.35 = f32[896,1792]{1,0:T(8,128)S(1)} fusion(bf16[256,896]{1,0:T(8,128)(2,1)S(1)} %get-tuple-element.76, bf16[256,896]{1,0:T(8,128)(2,1)S(1)} %get-tuple-element.75, bf16[896]{0:T(1024)(128)(2,1)S(1)} %select_select_fusion, s32[256]{0:T(256)S(1)} %pad_add_fusion, s32[896]{0:T(1024)S(1)} %reduce), kind=kOutput, calls=%fused_computation.51 | convolution fusion | flops 824377344 | bytes 7346432 | tf_op jit(solution)/shard_map/dot_general | solution.py:94
  55.0 1.0 %fusion.1 = (bf16[896,896]{1,0:T(8,128)(2,1)S(1)}, bf16[896,896]{1,0:T(8,128)(2,1)S(1)}) fusion(f32[896,1792]{1,0:T(8,128)S(1)} %fusion.35, f32[896,1792]{1,0:T(8,128)S(1)} %fusion.9), kind=kLoop, calls=%fused_computation.6 | loop fusion | flops 3211264 | bytes 16056320 | tf_op jit(solution)/shard_map/convert_element_type | solution.py:150
  56.3 0.6 fusion.47
  56.9 0.6 convolution_add_fusion.2
  57.6 0.7 collective-permute-start.10
  58.3 2.8 %collective-permute-start.11 = (f32[224,128]{1,0:T(8,128)S(1)}, f32[224,128]{1,0:T(8,128)S(1)}, u32[]{:S(2)}, u32[]{:S(2)}) collective-permute-start(f32[224,128]{1,0:T(8,128)S(1)} %get-tuple-element.92), channel_id=1, source_target_pairs={{0,1},{1,0},{2,3},{3,2},{4,5},{5,4},{6,7},{7,6},{8,9},{9,8},{10,11... | collective-permute-start | bytes 344072 | tf_op jit(solution)/shard_map/ppermute | solution.py:75
  61.0 0.7 collective-permute-start.12
  61.7 1.7 %collective-permute-start.13 = (f32[224,128]{1,0:T(8,128)S(1)}, f32[224,128]{1,0:T(8,128)S(1)}, u32[]{:S(2)}, u32[]{:S(2)}) collective-permute-start(f32[224,128]{1,0:T(8,128)S(1)} %get-tuple-element.89), channel_id=1, source_target_pairs={{0,4},{4,0},{8,12},{12,8},{16,20},{20,16},{24,28},{28,24},{1,5},{5... | collective-permute-start | bytes 344072 | tf_op jit(solution)/shard_map/ppermute | solution.py:75
  63.4 3.0 %collective-permute-done.11 = f32[224,128]{1,0:T(8,128)S(1)} collective-permute-done((f32[224,128]{1,0:T(8,128)S(1)}, f32[224,128]{1,0:T(8,128)S(1)}, u32[]{:S(2)}, u32[]{:S(2)}) %collective-permute-start.11) | collective-permute-done | bytes 114720 | tf_op jit(solution)/shard_map/ppermute | solution.py:75
  66.7 0.6 fusion.51
  68.0 0.7 collective-permute-start.14
  68.6 2.7 %collective-permute-start.15 = (f32[224,128]{1,0:T(8,128)S(1)}, f32[224,128]{1,0:T(8,128)S(1)}, u32[]{:S(2)}, u32[]{:S(2)}) collective-permute-start(f32[224,128]{1,0:T(8,128)S(1)} %get-tuple-element.88), channel_id=1, source_target_pairs={{0,1},{1,0},{2,3},{3,2},{4,5},{5,4},{6,7},{7,6},{8,9},{9,8},{10,11... | collective-permute-start | bytes 344072 | tf_op jit(solution)/shard_map/ppermute | solution.py:75
  71.4 0.7 collective-permute-start.16
  72.0 3.2 %collective-permute-start.17 = (f32[224,128]{1,0:T(8,128)S(1)}, f32[224,128]{1,0:T(8,128)S(1)}, u32[]{:S(2)}, u32[]{:S(2)}) collective-permute-start(f32[224,128]{1,0:T(8,128)S(1)} %get-tuple-element.85), channel_id=1, source_target_pairs={{0,4},{4,0},{8,12},{12,8},{16,20},{20,16},{24,28},{28,24},{1,5},{5... | collective-permute-start | bytes 344072 | tf_op jit(solution)/shard_map/ppermute | solution.py:75
  75.2 2.0 %collective-permute-done.15 = f32[224,128]{1,0:T(8,128)S(1)} collective-permute-done((f32[224,128]{1,0:T(8,128)S(1)}, f32[224,128]{1,0:T(8,128)S(1)}, u32[]{:S(2)}, u32[]{:S(2)}) %collective-permute-start.15) | collective-permute-done | bytes 114720 | tf_op jit(solution)/shard_map/ppermute | solution.py:75
  77.5 0.9 %reduce-precision_convert_fusion.3 = (bf16[896,128]{1,0:T(8,128)(2,1)S(1)}, f32[1,1,896,128]{3,2,1,0:T(8,128)}) fusion(f32[896,128]{1,0:T(8,128)S(1)} %get-tuple-element.57, f32[896,128]{1,0:T(8,128)S(1)} %get-tuple-element.59, f32[896,128]{1,0:T(8,128)S(1)} %get-tuple-element.62, f32[896,128]{1,0:T(8,128)S(1)} %get-tuple-element.66), kind=kLoop, calls=%fused_computation.59 | loop fusion | flops 1032192 | bytes 2523136 | tf_op jit(solution)/shard_map/slice | solution.py:100
  78.4 0.6 fusion.55
  79.1 0.6 convolution_add_fusion
  79.7 0.7 collective-permute-start.18
  80.4 2.3 %collective-permute-start.19 = (f32[224,128]{1,0:T(8,128)S(1)}, f32[224,128]{1,0:T(8,128)S(1)}, u32[]{:S(2)}, u32[]{:S(2)}) collective-permute-start(f32[224,128]{1,0:T(8,128)S(1)} %get-tuple-element.84), channel_id=1, source_target_pairs={{0,1},{1,0},{2,3},{3,2},{4,5},{5,4},{6,7},{7,6},{8,9},{9,8},{10,11... | collective-permute-start | bytes 344072 | tf_op jit(solution)/shard_map/ppermute | solution.py:75
  82.7 0.7 collective-permute-start.20
  83.3 3.9 %collective-permute-start.21 = (f32[224,128]{1,0:T(8,128)S(1)}, f32[224,128]{1,0:T(8,128)S(1)}, u32[]{:S(2)}, u32[]{:S(2)}) collective-permute-start(f32[224,128]{1,0:T(8,128)S(1)} %get-tuple-element.81), channel_id=1, source_target_pairs={{0,4},{4,0},{8,12},{12,8},{16,20},{20,16},{24,28},{28,24},{1,5},{5... | collective-permute-start | bytes 344072 | tf_op jit(solution)/shard_map/ppermute | solution.py:75
  87.2 1.8 %collective-permute-done.19 = f32[224,128]{1,0:T(8,128)S(1)} collective-permute-done((f32[224,128]{1,0:T(8,128)S(1)}, f32[224,128]{1,0:T(8,128)S(1)}, u32[]{:S(2)}, u32[]{:S(2)}) %collective-permute-start.19) | collective-permute-done | bytes 114720 | tf_op jit(solution)/shard_map/ppermute | solution.py:75
  89.0 0.8 fusion.59
  (57 shorter events, 3.7 us)
Async XLA Ops:
  0.6 2.2 %copy-start.1 = (f32[1,1,896,128]{3,2,1,0:T(8,128)S(1)}, f32[1,1,896,128]{3,2,1,0:T(8,128)}, u32[]{:S(2)}) copy-start(f32[1,1,896,128]{3,2,1,0:T(8,128)} %param.6) | copy-start | bytes 1376260
  0.6 11.0 %copy-start = (f32[1,1,640,896]{3,2,1,0:T(8,128)S(1)}, f32[1,1,640,896]{3,2,1,0:T(8,128)}, u32[]{:S(2)}) copy-start(f32[1,1,640,896]{3,2,1,0:T(8,128)} %param.7) | copy-start | bytes 6881284
  3.5 21.4 %collective-permute-start = (f32[224,128]{1,0:T(8,128)}, f32[224,128]{1,0:T(8,128)S(1)}, u32[]{:S(2)}, u32[]{:S(2)}) collective-permute-start(f32[224,128]{1,0:T(8,128)} %get-tuple-element.98), channel_id=1, source_target_pairs={{4,8},{8,4},{12,16},{16,12},{20,24},{24,20},{5,9},{9,5},{13,17},{1... | collective-permute-start | bytes 344072 | tf_op jit(solution)/shard_map/ppermute | solution.py:66
  4.2 20.7 %collective-permute-start.1 = (f32[224,128]{1,0:T(8,128)}, f32[224,128]{1,0:T(8,128)S(1)}, u32[]{:S(2)}, u32[]{:S(2)}) collective-permute-start(f32[224,128]{1,0:T(8,128)} %get-tuple-element.97), channel_id=1, source_target_pairs={{0,4},{4,0},{8,12},{12,8},{16,20},{20,16},{24,28},{28,24},{1,5},{5... | collective-permute-start | bytes 344072 | tf_op jit(solution)/shard_map/ppermute | solution.py:66
  8.6 27.6 %collective-permute-start.4 = (f32[128,896]{1,0:T(8,128)}, f32[128,896]{1,0:T(8,128)}, u32[]{:S(2)}, u32[]{:S(2)}) collective-permute-start(f32[128,896]{1,0:T(8,128)} %get-tuple-element.38), channel_id=1, source_target_pairs={{0,24},{4,28},{8,0},{12,4},{16,8},{20,12},{24,16},{28,20},{1,25},{... | collective-permute-start | bytes 1376264 | tf_op jit(solution)/shard_map/ppermute | solution.py:22
  10.6 31.5 %collective-permute-start.5 = (f32[128,896]{1,0:T(8,128)S(1)}, f32[128,896]{1,0:T(8,128)}, u32[]{:S(2)}, u32[]{:S(2)}) collective-permute-start(f32[128,896]{1,0:T(8,128)S(1)} %get-tuple-element.39), channel_id=1, source_target_pairs={{0,16},{4,20},{8,24},{12,28},{16,0},{20,4},{24,8},{28,12},{1,17},{... | collective-permute-start | bytes 1376264 | tf_op jit(solution)/shard_map/ppermute | solution.py:22
  19.2 2.8 %copy-start.3 = (s32[1,1,2]{2,1,0:T(1,128)S(1)}, s32[1,1,2]{2,1,0:T(1,128)}, u32[]{:S(2)}) copy-start(s32[1,1,2]{2,1,0:T(1,128)} %param.9) | copy-start | bytes 28
  19.2 5.7 %copy-start.2 = (f32[224,128]{1,0:T(8,128)S(1)}, f32[224,128]{1,0:T(8,128)}, u32[]{:S(2)}) copy-start(f32[224,128]{1,0:T(8,128)} %get-tuple-element.30) | copy-start | bytes 344068
  24.9 5.0 %collective-permute-start.2 = (f32[224,128]{1,0:T(8,128)S(1)}, f32[224,128]{1,0:T(8,128)S(1)}, u32[]{:S(2)}, u32[]{:S(2)}) collective-permute-start(f32[224,128]{1,0:T(8,128)S(1)} %copy-done.2), channel_id=1, source_target_pairs={{1,2},{2,1},{5,6},{6,5},{9,10},{10,9},{13,14},{14,13},{17,18},{18,... | collective-permute-start | bytes 344072 | tf_op jit(solution)/shard_map/ppermute | solution.py:69
  25.6 9.2 %collective-permute-start.3 = (f32[224,128]{1,0:T(8,128)S(1)}, f32[224,128]{1,0:T(8,128)S(1)}, u32[]{:S(2)}, u32[]{:S(2)}) collective-permute-start(f32[224,128]{1,0:T(8,128)S(1)} %get-tuple-element.31), channel_id=1, source_target_pairs={{0,1},{1,0},{2,3},{3,2},{4,5},{5,4},{6,7},{7,6},{8,9},{9,8},{10,11... | collective-permute-start | bytes 344072 | tf_op jit(solution)/shard_map/ppermute | solution.py:69
  45.1 10.9 %collective-permute-start.6 = (f32[224,128]{1,0:T(8,128)S(1)}, f32[224,128]{1,0:T(8,128)S(1)}, u32[]{:S(2)}, u32[]{:S(2)}) collective-permute-start(f32[224,128]{1,0:T(8,128)S(1)} %get-tuple-element.95), channel_id=1, source_target_pairs={{1,2},{2,1},{5,6},{6,5},{9,10},{10,9},{13,14},{14,13},{17,18},{18,... | collective-permute-start | bytes 344072 | tf_op jit(solution)/shard_map/ppermute | solution.py:75
  45.8 10.3 %collective-permute-start.7 = (f32[224,128]{1,0:T(8,128)S(1)}, f32[224,128]{1,0:T(8,128)S(1)}, u32[]{:S(2)}, u32[]{:S(2)}) collective-permute-start(f32[224,128]{1,0:T(8,128)S(1)} %get-tuple-element.96), channel_id=1, source_target_pairs={{0,1},{1,0},{2,3},{3,2},{4,5},{5,4},{6,7},{7,6},{8,9},{9,8},{10,11... | collective-permute-start | bytes 344072 | tf_op jit(solution)/shard_map/ppermute | solution.py:75
  50.1 6.0 %collective-permute-start.8 = (f32[224,128]{1,0:T(8,128)S(1)}, f32[224,128]{1,0:T(8,128)S(1)}, u32[]{:S(2)}, u32[]{:S(2)}) collective-permute-start(f32[224,128]{1,0:T(8,128)S(1)} %get-tuple-element.94), channel_id=1, source_target_pairs={{4,8},{8,4},{12,16},{16,12},{20,24},{24,20},{5,9},{9,5},{13,17},{1... | collective-permute-start | bytes 344072 | tf_op jit(solution)/shard_map/ppermute | solution.py:75
  50.9 5.2 %collective-permute-start.9 = (f32[224,128]{1,0:T(8,128)S(1)}, f32[224,128]{1,0:T(8,128)S(1)}, u32[]{:S(2)}, u32[]{:S(2)}) collective-permute-start(f32[224,128]{1,0:T(8,128)S(1)} %get-tuple-element.93), channel_id=1, source_target_pairs={{0,4},{4,0},{8,12},{12,8},{16,20},{20,16},{24,28},{28,24},{1,5},{5... | collective-permute-start | bytes 344072 | tf_op jit(solution)/shard_map/ppermute | solution.py:75
  57.6 5.8 %collective-permute-start.10 = (f32[224,128]{1,0:T(8,128)S(1)}, f32[224,128]{1,0:T(8,128)S(1)}, u32[]{:S(2)}, u32[]{:S(2)}) collective-permute-start(f32[224,128]{1,0:T(8,128)S(1)} %get-tuple-element.91), channel_id=1, source_target_pairs={{1,2},{2,1},{5,6},{6,5},{9,10},{10,9},{13,14},{14,13},{17,18},{18,... | collective-permute-start | bytes 344072 | tf_op jit(solution)/shard_map/ppermute | solution.py:75
  58.3 8.2 %collective-permute-start.11 = (f32[224,128]{1,0:T(8,128)S(1)}, f32[224,128]{1,0:T(8,128)S(1)}, u32[]{:S(2)}, u32[]{:S(2)}) collective-permute-start(f32[224,128]{1,0:T(8,128)S(1)} %get-tuple-element.92), channel_id=1, source_target_pairs={{0,1},{1,0},{2,3},{3,2},{4,5},{5,4},{6,7},{7,6},{8,9},{9,8},{10,11... | collective-permute-start | bytes 344072 | tf_op jit(solution)/shard_map/ppermute | solution.py:75
  61.0 5.4 %collective-permute-start.12 = (f32[224,128]{1,0:T(8,128)S(1)}, f32[224,128]{1,0:T(8,128)S(1)}, u32[]{:S(2)}, u32[]{:S(2)}) collective-permute-start(f32[224,128]{1,0:T(8,128)S(1)} %get-tuple-element.90), channel_id=1, source_target_pairs={{4,8},{8,4},{12,16},{16,12},{20,24},{24,20},{5,9},{9,5},{13,17},{1... | collective-permute-start | bytes 344072 | tf_op jit(solution)/shard_map/ppermute | solution.py:75
  61.7 4.8 %collective-permute-start.13 = (f32[224,128]{1,0:T(8,128)S(1)}, f32[224,128]{1,0:T(8,128)S(1)}, u32[]{:S(2)}, u32[]{:S(2)}) collective-permute-start(f32[224,128]{1,0:T(8,128)S(1)} %get-tuple-element.89), channel_id=1, source_target_pairs={{0,4},{4,0},{8,12},{12,8},{16,20},{20,16},{24,28},{28,24},{1,5},{5... | collective-permute-start | bytes 344072 | tf_op jit(solution)/shard_map/ppermute | solution.py:75
  68.0 7.3 %collective-permute-start.14 = (f32[224,128]{1,0:T(8,128)S(1)}, f32[224,128]{1,0:T(8,128)S(1)}, u32[]{:S(2)}, u32[]{:S(2)}) collective-permute-start(f32[224,128]{1,0:T(8,128)S(1)} %get-tuple-element.87), channel_id=1, source_target_pairs={{1,2},{2,1},{5,6},{6,5},{9,10},{10,9},{13,14},{14,13},{17,18},{18,... | collective-permute-start | bytes 344072 | tf_op jit(solution)/shard_map/ppermute | solution.py:75
  68.6 8.6 %collective-permute-start.15 = (f32[224,128]{1,0:T(8,128)S(1)}, f32[224,128]{1,0:T(8,128)S(1)}, u32[]{:S(2)}, u32[]{:S(2)}) collective-permute-start(f32[224,128]{1,0:T(8,128)S(1)} %get-tuple-element.88), channel_id=1, source_target_pairs={{0,1},{1,0},{2,3},{3,2},{4,5},{5,4},{6,7},{7,6},{8,9},{9,8},{10,11... | collective-permute-start | bytes 344072 | tf_op jit(solution)/shard_map/ppermute | solution.py:75
  71.4 5.9 %collective-permute-start.16 = (f32[224,128]{1,0:T(8,128)S(1)}, f32[224,128]{1,0:T(8,128)S(1)}, u32[]{:S(2)}, u32[]{:S(2)}) collective-permute-start(f32[224,128]{1,0:T(8,128)S(1)} %get-tuple-element.86), channel_id=1, source_target_pairs={{4,8},{8,4},{12,16},{16,12},{20,24},{24,20},{5,9},{9,5},{13,17},{1... | collective-permute-start | bytes 344072 | tf_op jit(solution)/shard_map/ppermute | solution.py:75
  72.0 5.3 %collective-permute-start.17 = (f32[224,128]{1,0:T(8,128)S(1)}, f32[224,128]{1,0:T(8,128)S(1)}, u32[]{:S(2)}, u32[]{:S(2)}) collective-permute-start(f32[224,128]{1,0:T(8,128)S(1)} %get-tuple-element.85), channel_id=1, source_target_pairs={{0,4},{4,0},{8,12},{12,8},{16,20},{20,16},{24,28},{28,24},{1,5},{5... | collective-permute-start | bytes 344072 | tf_op jit(solution)/shard_map/ppermute | solution.py:75
  79.7 7.5 %collective-permute-start.18 = (f32[224,128]{1,0:T(8,128)S(1)}, f32[224,128]{1,0:T(8,128)S(1)}, u32[]{:S(2)}, u32[]{:S(2)}) collective-permute-start(f32[224,128]{1,0:T(8,128)S(1)} %get-tuple-element.83), channel_id=1, source_target_pairs={{1,2},{2,1},{5,6},{6,5},{9,10},{10,9},{13,14},{14,13},{17,18},{18,... | collective-permute-start | bytes 344072 | tf_op jit(solution)/shard_map/ppermute | solution.py:75
  80.4 8.6 %collective-permute-start.19 = (f32[224,128]{1,0:T(8,128)S(1)}, f32[224,128]{1,0:T(8,128)S(1)}, u32[]{:S(2)}, u32[]{:S(2)}) collective-permute-start(f32[224,128]{1,0:T(8,128)S(1)} %get-tuple-element.84), channel_id=1, source_target_pairs={{0,1},{1,0},{2,3},{3,2},{4,5},{5,4},{6,7},{7,6},{8,9},{9,8},{10,11... | collective-permute-start | bytes 344072 | tf_op jit(solution)/shard_map/ppermute | solution.py:75
  82.7 6.3 %collective-permute-start.20 = (f32[224,128]{1,0:T(8,128)S(1)}, f32[224,128]{1,0:T(8,128)S(1)}, u32[]{:S(2)}, u32[]{:S(2)}) collective-permute-start(f32[224,128]{1,0:T(8,128)S(1)} %get-tuple-element.82), channel_id=1, source_target_pairs={{4,8},{8,4},{12,16},{16,12},{20,24},{24,20},{5,9},{9,5},{13,17},{1... | collective-permute-start | bytes 344072 | tf_op jit(solution)/shard_map/ppermute | solution.py:75
  83.3 5.6 %collective-permute-start.21 = (f32[224,128]{1,0:T(8,128)S(1)}, f32[224,128]{1,0:T(8,128)S(1)}, u32[]{:S(2)}, u32[]{:S(2)}) collective-permute-start(f32[224,128]{1,0:T(8,128)S(1)} %get-tuple-element.81), channel_id=1, source_target_pairs={{0,4},{4,0},{8,12},{12,8},{16,20},{20,16},{24,28},{28,24},{1,5},{5... | collective-permute-start | bytes 344072 | tf_op jit(solution)/shard_map/ppermute | solution.py:75

commit v18 on v10

--- a/solution.py
+++ b/solution.py
@@ -147,8 +147,10 @@
     spill_slots = slot_pieces(spill_stack, to_rows, spill_place)
     own_high = own_slots[:, :order_max].astype(jnp.bfloat16)
     own_mid = own_slots[:, order_max:].astype(jnp.bfloat16)
-    op_high = (own_slots[:, :order_max] + spill_slots[:, :order_max]).astype(jnp.bfloat16)
-    op_mid = (own_slots[:, order_max:] + spill_slots[:, order_max:]).astype(jnp.bfloat16)
+    full_slots = own_slots + spill_slots
+    op_stack = jnp.concatenate(
+        [full_slots[:, :order_max], full_slots[:, order_max:]], axis=0
+    ).astype(jnp.bfloat16)
     spill_high = lax.reduce_precision(spill_stack, exponent_bits=8, mantissa_bits=7)
     spill_mid = (spill_stack - spill_high).astype(jnp.bfloat16)
     spill_high = spill_high.astype(jnp.bfloat16)
@@ -180,7 +182,10 @@
                 (placed[:, :cols] + placed[:, cols : 2 * cols]) + placed[:, 2 * cols :]
             )
         else:
-            local = bf16x3_apply(op_high, op_mid, dir_pair, cols)
+            stacked_out = jnp.dot(op_stack, dir_pair, preferred_element_type=jnp.float32)
+            local = (
+                stacked_out[:order_max, :cols] + stacked_out[:order_max, cols:]
+            ) + stacked_out[order_max:, :cols]
         faces = [local[face_id * width : (face_id + 1) * width] for face_id in range(4)]
         residual = residual - face_sum_parts(faces)
         if step_id + 1 < ITERS:

time: 90.4 us -> 89.9 us (level)
  matrix products: 16 us -> 14.2 us
    dot_general x0 -> x3, matrix products: none -> 3.41 us  [body(): jnp.dot(op_stack, dir_pair, preferred_element_type=jnp.float32)]
    dot_general x5 -> x2, matrix products: 2.93 us -> 1 us  [bf16x3_apply(): both = jnp.dot(op_high, pair, preferred_element_type=jnp.float32)]
    dot_general x5 -> x2, matrix products: 2.65 us -> 0.95 us  [bf16x3_apply(): jnp.dot(op_mid, pair[:, :cols], preferred_element_type=jnp.float32)]
    dot_general x2, matrix products: 5.4 us -> 3.8 us  [slot_pieces(): jnp.dot(stacked, to_rows, preferred_element_type=jnp.float32)]
    ppermute x2, waiting for transfers between devices: 4.81 us -> 6.32 us  [from_behind(): return lax.ppermute(value, axis, pairs)]
    another operation x7 -> x10, other arithmetic: 2.38 us -> 1.12 us
    select_n x5, other arithmetic: 0.87 us -> 1.96 us  [face_sum_parts(): jnp.where(even, high, low)]
    convert_element_type x1 -> x0, other arithmetic: 1.01 us -> none  [body(): (own_slots[:, :order_max] + spill_slots[:, :order_max]).astype(jnp.bfloat16)]
  transfers between devices with their start and end apart: 22 -> 22, of which waited for: 5 -> 5; matrix products, arithmetic and copies ran while one was open for 19% -> 16% of each run, Pallas kernels for 0% -> 0%
where the time goes in v18:
time: 89.9 us; the launch traced here: 88.5 us
  starting transfers between devices  41.7 us (46%)
  waiting for transfers between devices  16.3 us (18%)
  matrix products  14.2 us (16%)
  other arithmetic  6.74 us (7%)
  local copies, waits for them, and re-layouts  5.02 us (6%)
  between operations  4.55 us (5%)
    ppermute x20, starting transfers between devices, face_sum_parts(): lax.ppermute(block, axis, pairs)  38.7 us
    ppermute x20, waiting for transfers between devices, face_sum_parts(): lax.ppermute(block, axis, pairs)  9.96 us
    ppermute x2, waiting for transfers between devices, from_behind(): return lax.ppermute(value, axis, pairs)  6.32 us
    dot_general x2, matrix products, slot_pieces(): return jnp.dot(to_slots, side, preferred_element_type=jnp.float32)  3.91 us
    dot_general x2, matrix products, slot_pieces(): jnp.dot(stacked, to_rows, preferred_element_type=jnp.float32)  3.8 us
    dot_general x3, matrix products, body(): jnp.dot(op_stack, dir_pair, preferred_element_type=jnp.float32)  3.41 us
    ppermute x2, starting transfers between devices, from_behind(): return lax.ppermute(value, axis, pairs)  3.04 us
    select_n x5, other arithmetic, face_sum_parts(): jnp.where(even, high, low)  1.96 us
  transfers between devices with their start and end apart: 22, of which 5 were waited for; matrix products, arithmetic and copies ran while one was open for 16% of the time, Pallas kernels for 0%

profile of v18, /device:TPU:0, one launch (start us, length us, event | category | flops | bytes accessed | tf_op | source)
XLA Modules:
  0.0 88.5 jit_solution(3267910891456865801)
XLA Ops:
  0.7 1.4 %slice_bitcast_fusion = (f32[128,896]{1,0:T(8,128)S(1)}, f32[128,896]{1,0:T(8,128)S(1)}) fusion(f32[1,1,2,128,896]{4,3,2,1,0:T(8,128)} %param.8), kind=kLoop, calls=%fused_computation.108 | loop fusion | bytes 1835008 | tf_op jit(solution)/shard_map/squeeze | solution.py:117
  2.0 1.8 %slice_select_fusion.16 = (f32[224,128]{1,0:T(8,128)}, f32[224,128]{1,0:T(8,128)S(1)}, f32[224,128]{1,0:T(8,128)}, f32[224,128]{1,0:T(8,128)}) fusion(f32[896,128]{1,0:T(8,128)} %bitcast.55, pred[]{:T(512)S(6)} %eq.100, pred[]{:T(512)S(6)} %eq.101), kind=kLoop, calls=%fused_computation.161 | loop fusion | flops 114688 | bytes 917506 | tf_op jit(solution)/shard_map/jit(_where)/select_n | solution.py:64
  3.9 0.7 collective-permute-start
  4.5 4.4 %collective-permute-start.1 = (f32[224,128]{1,0:T(8,128)}, f32[224,128]{1,0:T(8,128)S(1)}, u32[]{:S(2)}, u32[]{:S(2)}) collective-permute-start(f32[224,128]{1,0:T(8,128)} %get-tuple-element.124), channel_id=1, source_target_pairs={{0,4},{4,0},{8,12},{12,8},{16,20},{20,16},{24,28},{28,24},{1,5},{5... | collective-permute-start | bytes 344072 | tf_op jit(solution)/shard_map/ppermute | solution.py:66
  9.0 2.0 %collective-permute-start.4 = (f32[128,896]{1,0:T(8,128)S(1)}, f32[128,896]{1,0:T(8,128)}, u32[]{:S(2)}, u32[]{:S(2)}) collective-permute-start(f32[128,896]{1,0:T(8,128)S(1)} %get-tuple-element.38), channel_id=1, source_target_pairs={{0,24},{4,28},{8,0},{12,4},{16,8},{20,12},{24,16},{28,20},{1,25},{... | collective-permute-start | bytes 1376264 | tf_op jit(solution)/shard_map/ppermute | solution.py:22
  10.9 1.1 %collective-permute-start.5 = (f32[128,896]{1,0:T(8,128)S(1)}, f32[128,896]{1,0:T(8,128)}, u32[]{:S(2)}, u32[]{:S(2)}) collective-permute-start(f32[128,896]{1,0:T(8,128)S(1)} %get-tuple-element.39), channel_id=1, source_target_pairs={{0,16},{4,20},{8,24},{12,28},{16,0},{20,4},{24,8},{28,12},{1,17},{... | collective-permute-start | bytes 1376264 | tf_op jit(solution)/shard_map/ppermute | solution.py:22
  12.0 1.3 %reduce = s32[896]{0:T(1024)} reduce(s32[1,1,896]{2,1,0:T(1,128)} %param.11, s32[]{:T(128)} %constant.99.clone.1), dimensions={0,1}, to_apply=%param.11.reduce_sub_computation | reduce | bytes 7172 | tf_op args[5]
  14.3 0.3 copy-done.3
  14.6 2.6 %convolution_convert_fusion = bf16[1280,896]{0,1:T(8,128)(2,1)S(1)} fusion(bf16[640,896]{1,0:T(8,128)(2,1)S(1)} %get-tuple-element.69, bf16[640,896]{1,0:T(8,128)(2,1)S(1)} %get-tuple-element.68, bf16[896]{0:T(1024)(128)(2,1)S(1)} %select_select_fusion, s32[896]{0:T(1024)S(1)} %copy-done.3), kind=kOutput, calls=%fused_computation.1 | convolution fusion | flops 2062548992 | bytes 4592896 | tf_op jit(solution)/shard_map/dot_general | solution.py:92
  17.5 2.7 %fusion.108 = (bf16[896,1792]{1,0:T(8,128)(2,1)S(1)}, f32[896,1792]{1,0:T(8,128)S(1)}) fusion(bf16[640,896]{0,1:T(8,128)(2,1)S(1)} %get-tuple-element.67, bf16[640,896]{0,1:T(8,128)(2,1)S(1)} %get-tuple-element.66, bf16[896]{0:T(1024)(128)(2,1)S(1)} %select_select_fusion, s32[896]{0:T(1024)S(1)} %copy-done.3), kind=kOutput, calls=%fused_computation.204 | convolution fusion | flops 2063122432 | bytes 11932928 | tf_op jit(solution)/shard_map/dot_general | solution.py:94
  20.2 0.7 fusion.107
  23.7 0.7 collective-permute-start.2
  24.3 4.3 %collective-permute-start.3 = (f32[224,128]{1,0:T(8,128)S(1)}, f32[224,128]{1,0:T(8,128)S(1)}, u32[]{:S(2)}, u32[]{:S(2)}) collective-permute-start(f32[224,128]{1,0:T(8,128)S(1)} %get-tuple-element.31), channel_id=1, source_target_pairs={{0,1},{1,0},{2,3},{3,2},{4,5},{5,4},{6,7},{7,6},{8,9},{9,8},{10,11... | collective-permute-start | bytes 344072 | tf_op jit(solution)/shard_map/ppermute | solution.py:69
  28.7 4.9 %collective-permute-done.3 = f32[224,128]{1,0:T(8,128)S(1)} collective-permute-done((f32[224,128]{1,0:T(8,128)S(1)}, f32[224,128]{1,0:T(8,128)S(1)}, u32[]{:S(2)}, u32[]{:S(2)}) %collective-permute-start.3) | collective-permute-done | bytes 114720 | tf_op jit(solution)/shard_map/ppermute | solution.py:69
  33.7 0.6 fusion.25
  34.3 0.6 fusion.13
  35.0 1.0 %constant_dynamic-update-slice_fusion.1 = f32[256,896]{1,0:T(8,128)S(1)} fusion(f32[128,896]{1,0:T(8,128)} %collective-permute-done.4), kind=kLoop, calls=%fused_computation.178 | loop fusion | bytes 917504
  36.0 6.3 %collective-permute-done.5 = f32[128,896]{1,0:T(8,128)} collective-permute-done((f32[128,896]{1,0:T(8,128)S(1)}, f32[128,896]{1,0:T(8,128)}, u32[]{:S(2)}, u32[]{:S(2)}) %collective-permute-start.5) | collective-permute-done | bytes 458784 | tf_op jit(solution)/shard_map/ppermute | solution.py:22
  42.4 1.0 %constant_dynamic-update-slice_fusion = f32[256,896]{1,0:T(8,128)S(1)} fusion(f32[256,896]{1,0:T(8,128)S(1)} %constant_dynamic-update-slice_fusion.1, f32[128,896]{1,0:T(8,128)} %collective-permute-done.5), kind=kLoop, calls=%fused_computation.176 | loop fusion | bytes 917504 | tf_op jit(solution)/shard_map/concatenate | solution.py:146
  43.5 0.4 fusion.109
  44.2 0.5 fusion.46
  44.7 0.7 fusion.29
  45.4 0.7 collective-permute-start.6
  46.1 4.3 %collective-permute-start.7 = (f32[224,128]{1,0:T(8,128)S(1)}, f32[224,128]{1,0:T(8,128)S(1)}, u32[]{:S(2)}, u32[]{:S(2)}) collective-permute-start(f32[224,128]{1,0:T(8,128)S(1)} %get-tuple-element.117), channel_id=1, source_target_pairs={{0,1},{1,0},{2,3},{3,2},{4,5},{5,4},{6,7},{7,6},{8,9},{9,8},{10,11... | collective-permute-start | bytes 344072 | tf_op jit(solution)/shard_map/ppermute | solution.py:75
  50.4 0.8 collective-permute-start.8
  51.2 1.5 %collective-permute-start.9 = (f32[224,128]{1,0:T(8,128)S(1)}, f32[224,128]{1,0:T(8,128)S(1)}, u32[]{:S(2)}, u32[]{:S(2)}) collective-permute-start(f32[224,128]{1,0:T(8,128)S(1)} %get-tuple-element.116), channel_id=1, source_target_pairs={{0,4},{4,0},{8,12},{12,8},{16,20},{20,16},{24,28},{28,24},{1,5},{5... | collective-permute-start | bytes 344072 | tf_op jit(solution)/shard_map/ppermute | solution.py:75
  52.7 1.2 %fusion.24 = bf16[512,896]{1,0:T(8,128)(2,1)S(1)} fusion(bf16[896]{0:T(1024)(128)(2,1)S(1)} %select_select_fusion, s32[896]{0:T(1024)S(1)} %copy-done.3, bf16[256,896]{1,0:T(8,128)(2,1)S(1)} %get-tuple-element.72, bf16[256,896]{1,0:T(8,128)(2,1)S(1)} %get-tuple-element.73), kind=kOutput, calls=%fused_computation.33 | convolution fusion | flops 825982976 | bytes 1840384 | tf_op jit(solution)/shard_map/dot_general | solution.py:92
  54.0 1.2 %add_convert_fusion = bf16[896,1792]{1,0:T(8,128)(2,1)S(1)} fusion(f32[896,1792]{1,0:T(8,128)S(1)} %get-tuple-element.133, bf16[256,896]{1,0:T(8,128)(2,1)S(1)} %get-tuple-element.71, bf16[256,896]{1,0:T(8,128)(2,1)S(1)} %get-tuple-element.70, bf16[896]{0:T(1024)(128)(2,1)S(1)} %select_select_fusion, s32[256]{0:T(256)S(1)} %pad_add_fusion, s32[896]{0:T(1024)S(1)} %copy-done.3), kind=kOutput, calls=%fused_computation | convolution fusion | flops 827588608 | bytes 10557696 | tf_op jit(solution)/shard_map/dot_general | solution.py:94
  55.8 1.1 %fusion.38 = f32[1792,256]{1,0:T(8,128)S(1)} fusion(bf16[896,896]{1,0:T(8,128)(2,1)S(1)} %get-tuple-element.65, bf16[896,896]{1,0:T(8,128)(2,1)S(1)} %get-tuple-element.64, bf16[896,128]{1,0:T(8,128)(2,1)S(1)} %fusion.48, bf16[896,128]{1,0:T(8,128)(2,1)S(1)} %get-tuple-element.60), kind=kOutput, calls=%fused_computation.45 | convolution fusion | flops 829423616 | bytes 5505024 | tf_op jit(solution)/shard_map/dot_general | solution.py:185
  57.0 0.7 collective-permute-start.10
  57.7 2.8 %collective-permute-start.11 = (f32[224,128]{1,0:T(8,128)S(1)}, f32[224,128]{1,0:T(8,128)S(1)}, u32[]{:S(2)}, u32[]{:S(2)}) collective-permute-start(f32[224,128]{1,0:T(8,128)S(1)} %get-tuple-element.111), channel_id=1, source_target_pairs={{0,1},{1,0},{2,3},{3,2},{4,5},{5,4},{6,7},{7,6},{8,9},{9,8},{10,11... | collective-permute-start | bytes 344072 | tf_op jit(solution)/shard_map/ppermute | solution.py:75
  60.5 0.7 collective-permute-start.12
  61.1 2.4 %collective-permute-start.13 = (f32[224,128]{1,0:T(8,128)S(1)}, f32[224,128]{1,0:T(8,128)S(1)}, u32[]{:S(2)}, u32[]{:S(2)}) collective-permute-start(f32[224,128]{1,0:T(8,128)S(1)} %get-tuple-element.110), channel_id=1, source_target_pairs={{0,4},{4,0},{8,12},{12,8},{16,20},{20,16},{24,28},{28,24},{1,5},{5... | collective-permute-start | bytes 344072 | tf_op jit(solution)/shard_map/ppermute | solution.py:75
  63.6 2.3 %collective-permute-done.11 = f32[224,128]{1,0:T(8,128)S(1)} collective-permute-done((f32[224,128]{1,0:T(8,128)S(1)}, f32[224,128]{1,0:T(8,128)S(1)}, u32[]{:S(2)}, u32[]{:S(2)}) %collective-permute-start.11) | collective-permute-done | bytes 114720 | tf_op jit(solution)/shard_map/ppermute | solution.py:75
  66.2 1.1 %fusion.37 = f32[1792,256]{1,0:T(8,128)S(1)} fusion(bf16[896,896]{1,0:T(8,128)(2,1)S(1)} %get-tuple-element.65, bf16[896,896]{1,0:T(8,128)(2,1)S(1)} %get-tuple-element.64, bf16[896,128]{1,0:T(8,128)(2,1)S(1)} %fusion.49, bf16[896,128]{1,0:T(8,128)(2,1)S(1)} %get-tuple-element.58), kind=kOutput, calls=%fused_computation.44 | convolution fusion | flops 829423616 | bytes 5505024 | tf_op jit(solution)/shard_map/dot_general | solution.py:185
  67.4 0.7 collective-permute-start.14
  68.1 2.7 %collective-permute-start.15 = (f32[224,128]{1,0:T(8,128)S(1)}, f32[224,128]{1,0:T(8,128)S(1)}, u32[]{:S(2)}, u32[]{:S(2)}) collective-permute-start(f32[224,128]{1,0:T(8,128)S(1)} %get-tuple-element.105), channel_id=1, source_target_pairs={{0,1},{1,0},{2,3},{3,2},{4,5},{5,4},{6,7},{7,6},{8,9},{9,8},{10,11... | collective-permute-start | bytes 344072 | tf_op jit(solution)/shard_map/ppermute | solution.py:75
  70.8 0.7 collective-permute-start.16
  71.5 3.2 %collective-permute-start.17 = (f32[224,128]{1,0:T(8,128)S(1)}, f32[224,128]{1,0:T(8,128)S(1)}, u32[]{:S(2)}, u32[]{:S(2)}) collective-permute-start(f32[224,128]{1,0:T(8,128)S(1)} %get-tuple-element.104), channel_id=1, source_target_pairs={{0,4},{4,0},{8,12},{12,8},{16,20},{20,16},{24,28},{28,24},{1,5},{5... | collective-permute-start | bytes 344072 | tf_op jit(solution)/shard_map/ppermute | solution.py:75
  74.7 2.0 %collective-permute-done.15 = f32[224,128]{1,0:T(8,128)S(1)} collective-permute-done((f32[224,128]{1,0:T(8,128)S(1)}, f32[224,128]{1,0:T(8,128)S(1)}, u32[]{:S(2)}, u32[]{:S(2)}) %collective-permute-start.15) | collective-permute-done | bytes 114720 | tf_op jit(solution)/shard_map/ppermute | solution.py:75
  77.0 1.1 %fusion.36 = f32[1792,256]{1,0:T(8,128)S(1)} fusion(bf16[896,896]{1,0:T(8,128)(2,1)S(1)} %get-tuple-element.65, bf16[896,896]{1,0:T(8,128)(2,1)S(1)} %get-tuple-element.64, bf16[896,128]{1,0:T(8,128)(2,1)S(1)} %fusion.50, bf16[896,128]{1,0:T(8,128)(2,1)S(1)} %get-tuple-element.56), kind=kOutput, calls=%fused_computation.43 | convolution fusion | flops 829423616 | bytes 5505024 | tf_op jit(solution)/shard_map/dot_general | solution.py:185
  78.3 0.7 collective-permute-start.18
  79.0 2.3 %collective-permute-start.19 = (f32[224,128]{1,0:T(8,128)S(1)}, f32[224,128]{1,0:T(8,128)S(1)}, u32[]{:S(2)}, u32[]{:S(2)}) collective-permute-start(f32[224,128]{1,0:T(8,128)S(1)} %get-tuple-element.99), channel_id=1, source_target_pairs={{0,1},{1,0},{2,3},{3,2},{4,5},{5,4},{6,7},{7,6},{8,9},{9,8},{10,11... | collective-permute-start | bytes 344072 | tf_op jit(solution)/shard_map/ppermute | solution.py:75
  81.2 0.7 collective-permute-start.20
  81.9 3.9 %collective-permute-start.21 = (f32[224,128]{1,0:T(8,128)S(1)}, f32[224,128]{1,0:T(8,128)S(1)}, u32[]{:S(2)}, u32[]{:S(2)}) collective-permute-start(f32[224,128]{1,0:T(8,128)S(1)} %get-tuple-element.98), channel_id=1, source_target_pairs={{0,4},{4,0},{8,12},{12,8},{16,20},{20,16},{24,28},{28,24},{1,5},{5... | collective-permute-start | bytes 344072 | tf_op jit(solution)/shard_map/ppermute | solution.py:75
  85.8 1.0 %add_add_fusion = f32[1,1,896,128]{3,2,1,0:T(8,128)} fusion(f32[1,1,224,128]{3,2,1,0:T(8,128)S(1)} %bitcast.43, f32[1,1,224,128]{3,2,1,0:T(8,128)S(1)} %bitcast.45, f32[1,1,224,128]{3,2,1,0:T(8,128)S(1)} %bitcast.41, f32[1,1,224,128]{3,2,1,0:T(8,128)S(1)} %bitcast.39, f32[1,1,224,128]{3,2,1,0:T(8,128)S(1)} %bitcast.51, f32[1,1,224,128]{3,2,1,0:T(8,128)S(1)} %bitcast.53, ...), kind=kLoop, calls=%fused_computation.99 | loop fusion | flops 3211264 | bytes 2293760 | tf_op jit(solution)/shard_map/add | solution.py:165
  86.8 0.7 collective-permute-done.19
  87.6 0.9 maximum_subtract_fusion.6
  (55 shorter events, 2.6 us)
Async XLA Ops:
  0.6 13.3 %copy-start = (f32[1,1,640,896]{3,2,1,0:T(8,128)S(1)}, f32[1,1,640,896]{3,2,1,0:T(8,128)}, u32[]{:S(2)}) copy-start(f32[1,1,640,896]{3,2,1,0:T(8,128)} %param.7) | copy-start | bytes 6881284
  3.9 19.8 %collective-permute-start = (f32[224,128]{1,0:T(8,128)}, f32[224,128]{1,0:T(8,128)S(1)}, u32[]{:S(2)}, u32[]{:S(2)}) collective-permute-start(f32[224,128]{1,0:T(8,128)} %get-tuple-element.126), channel_id=1, source_target_pairs={{4,8},{8,4},{12,16},{16,12},{20,24},{24,20},{5,9},{9,5},{13,17},{1... | collective-permute-start | bytes 344072 | tf_op jit(solution)/shard_map/ppermute | solution.py:66
  4.5 19.1 %collective-permute-start.1 = (f32[224,128]{1,0:T(8,128)}, f32[224,128]{1,0:T(8,128)S(1)}, u32[]{:S(2)}, u32[]{:S(2)}) collective-permute-start(f32[224,128]{1,0:T(8,128)} %get-tuple-element.124), channel_id=1, source_target_pairs={{0,4},{4,0},{8,12},{12,8},{16,20},{20,16},{24,28},{28,24},{1,5},{5... | collective-permute-start | bytes 344072 | tf_op jit(solution)/shard_map/ppermute | solution.py:66
  9.0 26.0 %collective-permute-start.4 = (f32[128,896]{1,0:T(8,128)S(1)}, f32[128,896]{1,0:T(8,128)}, u32[]{:S(2)}, u32[]{:S(2)}) collective-permute-start(f32[128,896]{1,0:T(8,128)S(1)} %get-tuple-element.38), channel_id=1, source_target_pairs={{0,24},{4,28},{8,0},{12,4},{16,8},{20,12},{24,16},{28,20},{1,25},{... | collective-permute-start | bytes 1376264 | tf_op jit(solution)/shard_map/ppermute | solution.py:22
  10.9 31.4 %collective-permute-start.5 = (f32[128,896]{1,0:T(8,128)S(1)}, f32[128,896]{1,0:T(8,128)}, u32[]{:S(2)}, u32[]{:S(2)}) collective-permute-start(f32[128,896]{1,0:T(8,128)S(1)} %get-tuple-element.39), channel_id=1, source_target_pairs={{0,16},{4,20},{8,24},{12,28},{16,0},{20,4},{24,8},{28,12},{1,17},{... | collective-permute-start | bytes 1376264 | tf_op jit(solution)/shard_map/ppermute | solution.py:22
  13.9 0.7 copy-start.3
  17.4 2.8 %copy-start.4 = (s32[1,1,2]{2,1,0:T(1,128)S(1)}, s32[1,1,2]{2,1,0:T(1,128)}, u32[]{:S(2)}) copy-start(s32[1,1,2]{2,1,0:T(1,128)} %param.9) | copy-start | bytes 28
  17.5 6.2 %copy-start.2 = (f32[224,128]{1,0:T(8,128)S(1)}, f32[224,128]{1,0:T(8,128)}, u32[]{:S(2)}) copy-start(f32[224,128]{1,0:T(8,128)} %get-tuple-element.30) | copy-start | bytes 344068
  17.5 16.1 %copy-start.1 = (f32[1,1,896,128]{3,2,1,0:T(8,128)S(1)}, f32[1,1,896,128]{3,2,1,0:T(8,128)}, u32[]{:S(2)}) copy-start(f32[1,1,896,128]{3,2,1,0:T(8,128)} %param.6) | copy-start | bytes 1376260
  23.7 5.0 %collective-permute-start.2 = (f32[224,128]{1,0:T(8,128)S(1)}, f32[224,128]{1,0:T(8,128)S(1)}, u32[]{:S(2)}, u32[]{:S(2)}) collective-permute-start(f32[224,128]{1,0:T(8,128)S(1)} %copy-done.2), channel_id=1, source_target_pairs={{1,2},{2,1},{5,6},{6,5},{9,10},{10,9},{13,14},{14,13},{17,18},{18,... | collective-permute-start | bytes 344072 | tf_op jit(solution)/shard_map/ppermute | solution.py:69
  24.3 9.2 %collective-permute-start.3 = (f32[224,128]{1,0:T(8,128)S(1)}, f32[224,128]{1,0:T(8,128)S(1)}, u32[]{:S(2)}, u32[]{:S(2)}) collective-permute-start(f32[224,128]{1,0:T(8,128)S(1)} %get-tuple-element.31), channel_id=1, source_target_pairs={{0,1},{1,0},{2,3},{3,2},{4,5},{5,4},{6,7},{7,6},{8,9},{9,8},{10,11... | collective-permute-start | bytes 344072 | tf_op jit(solution)/shard_map/ppermute | solution.py:69
  45.4 10.1 %collective-permute-start.6 = (f32[224,128]{1,0:T(8,128)S(1)}, f32[224,128]{1,0:T(8,128)S(1)}, u32[]{:S(2)}, u32[]{:S(2)}) collective-permute-start(f32[224,128]{1,0:T(8,128)S(1)} %get-tuple-element.119), channel_id=1, source_target_pairs={{1,2},{2,1},{5,6},{6,5},{9,10},{10,9},{13,14},{14,13},{17,18},{18,... | collective-permute-start | bytes 344072 | tf_op jit(solution)/shard_map/ppermute | solution.py:75
  46.1 9.4 %collective-permute-start.7 = (f32[224,128]{1,0:T(8,128)S(1)}, f32[224,128]{1,0:T(8,128)S(1)}, u32[]{:S(2)}, u32[]{:S(2)}) collective-permute-start(f32[224,128]{1,0:T(8,128)S(1)} %get-tuple-element.117), channel_id=1, source_target_pairs={{0,1},{1,0},{2,3},{3,2},{4,5},{5,4},{6,7},{7,6},{8,9},{9,8},{10,11... | collective-permute-start | bytes 344072 | tf_op jit(solution)/shard_map/ppermute | solution.py:75
  50.4 5.2 %collective-permute-start.8 = (f32[224,128]{1,0:T(8,128)S(1)}, f32[224,128]{1,0:T(8,128)S(1)}, u32[]{:S(2)}, u32[]{:S(2)}) collective-permute-start(f32[224,128]{1,0:T(8,128)S(1)} %get-tuple-element.118), channel_id=1, source_target_pairs={{4,8},{8,4},{12,16},{16,12},{20,24},{24,20},{5,9},{9,5},{13,17},{1... | collective-permute-start | bytes 344072 | tf_op jit(solution)/shard_map/ppermute | solution.py:75
  51.2 4.3 %collective-permute-start.9 = (f32[224,128]{1,0:T(8,128)S(1)}, f32[224,128]{1,0:T(8,128)S(1)}, u32[]{:S(2)}, u32[]{:S(2)}) collective-permute-start(f32[224,128]{1,0:T(8,128)S(1)} %get-tuple-element.116), channel_id=1, source_target_pairs={{0,4},{4,0},{8,12},{12,8},{16,20},{20,16},{24,28},{28,24},{1,5},{5... | collective-permute-start | bytes 344072 | tf_op jit(solution)/shard_map/ppermute | solution.py:75
  57.0 6.6 %collective-permute-start.10 = (f32[224,128]{1,0:T(8,128)S(1)}, f32[224,128]{1,0:T(8,128)S(1)}, u32[]{:S(2)}, u32[]{:S(2)}) collective-permute-start(f32[224,128]{1,0:T(8,128)S(1)} %get-tuple-element.113), channel_id=1, source_target_pairs={{1,2},{2,1},{5,6},{6,5},{9,10},{10,9},{13,14},{14,13},{17,18},{18,... | collective-permute-start | bytes 344072 | tf_op jit(solution)/shard_map/ppermute | solution.py:75
  57.7 8.2 %collective-permute-start.11 = (f32[224,128]{1,0:T(8,128)S(1)}, f32[224,128]{1,0:T(8,128)S(1)}, u32[]{:S(2)}, u32[]{:S(2)}) collective-permute-start(f32[224,128]{1,0:T(8,128)S(1)} %get-tuple-element.111), channel_id=1, source_target_pairs={{0,1},{1,0},{2,3},{3,2},{4,5},{5,4},{6,7},{7,6},{8,9},{9,8},{10,11... | collective-permute-start | bytes 344072 | tf_op jit(solution)/shard_map/ppermute | solution.py:75
  60.5 5.4 %collective-permute-start.12 = (f32[224,128]{1,0:T(8,128)S(1)}, f32[224,128]{1,0:T(8,128)S(1)}, u32[]{:S(2)}, u32[]{:S(2)}) collective-permute-start(f32[224,128]{1,0:T(8,128)S(1)} %get-tuple-element.112), channel_id=1, source_target_pairs={{4,8},{8,4},{12,16},{16,12},{20,24},{24,20},{5,9},{9,5},{13,17},{1... | collective-permute-start | bytes 344072 | tf_op jit(solution)/shard_map/ppermute | solution.py:75
  61.1 4.8 %collective-permute-start.13 = (f32[224,128]{1,0:T(8,128)S(1)}, f32[224,128]{1,0:T(8,128)S(1)}, u32[]{:S(2)}, u32[]{:S(2)}) collective-permute-start(f32[224,128]{1,0:T(8,128)S(1)} %get-tuple-element.110), channel_id=1, source_target_pairs={{0,4},{4,0},{8,12},{12,8},{16,20},{20,16},{24,28},{28,24},{1,5},{5... | collective-permute-start | bytes 344072 | tf_op jit(solution)/shard_map/ppermute | solution.py:75
  67.4 7.3 %collective-permute-start.14 = (f32[224,128]{1,0:T(8,128)S(1)}, f32[224,128]{1,0:T(8,128)S(1)}, u32[]{:S(2)}, u32[]{:S(2)}) collective-permute-start(f32[224,128]{1,0:T(8,128)S(1)} %get-tuple-element.107), channel_id=1, source_target_pairs={{1,2},{2,1},{5,6},{6,5},{9,10},{10,9},{13,14},{14,13},{17,18},{18,... | collective-permute-start | bytes 344072 | tf_op jit(solution)/shard_map/ppermute | solution.py:75
  68.1 8.6 %collective-permute-start.15 = (f32[224,128]{1,0:T(8,128)S(1)}, f32[224,128]{1,0:T(8,128)S(1)}, u32[]{:S(2)}, u32[]{:S(2)}) collective-permute-start(f32[224,128]{1,0:T(8,128)S(1)} %get-tuple-element.105), channel_id=1, source_target_pairs={{0,1},{1,0},{2,3},{3,2},{4,5},{5,4},{6,7},{7,6},{8,9},{9,8},{10,11... | collective-permute-start | bytes 344072 | tf_op jit(solution)/shard_map/ppermute | solution.py:75
  70.8 5.9 %collective-permute-start.16 = (f32[224,128]{1,0:T(8,128)S(1)}, f32[224,128]{1,0:T(8,128)S(1)}, u32[]{:S(2)}, u32[]{:S(2)}) collective-permute-start(f32[224,128]{1,0:T(8,128)S(1)} %get-tuple-element.106), channel_id=1, source_target_pairs={{4,8},{8,4},{12,16},{16,12},{20,24},{24,20},{5,9},{9,5},{13,17},{1... | collective-permute-start | bytes 344072 | tf_op jit(solution)/shard_map/ppermute | solution.py:75
  71.5 5.3 %collective-permute-start.17 = (f32[224,128]{1,0:T(8,128)S(1)}, f32[224,128]{1,0:T(8,128)S(1)}, u32[]{:S(2)}, u32[]{:S(2)}) collective-permute-start(f32[224,128]{1,0:T(8,128)S(1)} %get-tuple-element.104), channel_id=1, source_target_pairs={{0,4},{4,0},{8,12},{12,8},{16,20},{20,16},{24,28},{28,24},{1,5},{5... | collective-permute-start | bytes 344072 | tf_op jit(solution)/shard_map/ppermute | solution.py:75
  78.3 8.5 %collective-permute-start.18 = (f32[224,128]{1,0:T(8,128)S(1)}, f32[224,128]{1,0:T(8,128)S(1)}, u32[]{:S(2)}, u32[]{:S(2)}) collective-permute-start(f32[224,128]{1,0:T(8,128)S(1)} %get-tuple-element.101), channel_id=1, source_target_pairs={{1,2},{2,1},{5,6},{6,5},{9,10},{10,9},{13,14},{14,13},{17,18},{18,... | collective-permute-start | bytes 344072 | tf_op jit(solution)/shard_map/ppermute | solution.py:75
  79.0 8.6 %collective-permute-start.19 = (f32[224,128]{1,0:T(8,128)S(1)}, f32[224,128]{1,0:T(8,128)S(1)}, u32[]{:S(2)}, u32[]{:S(2)}) collective-permute-start(f32[224,128]{1,0:T(8,128)S(1)} %get-tuple-element.99), channel_id=1, source_target_pairs={{0,1},{1,0},{2,3},{3,2},{4,5},{5,4},{6,7},{7,6},{8,9},{9,8},{10,11... | collective-permute-start | bytes 344072 | tf_op jit(solution)/shard_map/ppermute | solution.py:75
  81.2 6.3 %collective-permute-start.20 = (f32[224,128]{1,0:T(8,128)S(1)}, f32[224,128]{1,0:T(8,128)S(1)}, u32[]{:S(2)}, u32[]{:S(2)}) collective-permute-start(f32[224,128]{1,0:T(8,128)S(1)} %get-tuple-element.100), channel_id=1, source_target_pairs={{4,8},{8,4},{12,16},{16,12},{20,24},{24,20},{5,9},{9,5},{13,17},{1... | collective-permute-start | bytes 344072 | tf_op jit(solution)/shard_map/ppermute | solution.py:75
  81.9 5.6 %collective-permute-start.21 = (f32[224,128]{1,0:T(8,128)S(1)}, f32[224,128]{1,0:T(8,128)S(1)}, u32[]{:S(2)}, u32[]{:S(2)}) collective-permute-start(f32[224,128]{1,0:T(8,128)S(1)} %get-tuple-element.98), channel_id=1, source_target_pairs={{0,4},{4,0},{8,12},{12,8},{16,20},{20,16},{24,28},{28,24},{1,5},{5... | collective-permute-start | bytes 344072 | tf_op jit(solution)/shard_map/ppermute | solution.py:75

commit v19 on v18

--- a/solution.py
+++ b/solution.py
@@ -152,8 +152,10 @@
         [full_slots[:, :order_max], full_slots[:, order_max:]], axis=0
     ).astype(jnp.bfloat16)
     spill_high = lax.reduce_precision(spill_stack, exponent_bits=8, mantissa_bits=7)
-    spill_mid = (spill_stack - spill_high).astype(jnp.bfloat16)
-    spill_high = spill_high.astype(jnp.bfloat16)
+    spill_both = jnp.concatenate([spill_high, spill_stack - spill_high], axis=0).astype(
+        jnp.bfloat16
+    )
+    spill_count = spill_stack.shape[0]
     centre = (high_bound + low_bound) / 2.0
     half_width = (high_bound - low_bound) / 2.0
     sigma_value = centre / half_width
@@ -170,7 +172,10 @@
             moved = jnp.dot(to_rows, dir_pair, preferred_element_type=jnp.float32).astype(
                 jnp.bfloat16
             )
-            spill_out = bf16x3_apply(spill_high, spill_mid, moved, cols)
+            spill_prod = jnp.dot(spill_both, moved, preferred_element_type=jnp.float32)
+            spill_out = (
+                spill_prod[:spill_count, :cols] + spill_prod[:spill_count, cols:]
+            ) + spill_prod[spill_count:, :cols]
             out_high = lax.reduce_precision(spill_out, exponent_bits=8, mantissa_bits=7)
             out_rest = spill_out - out_high
             out_mid = lax.reduce_precision(out_rest, exponent_bits=8, mantissa_bits=7)

time: 89.9 us -> 93.6 us (1.041)
  matrix products: 14.2 us -> 19.6 us
  waiting for transfers between devices: 16.3 us -> 13.2 us
  local copies, waits for them, and re-layouts: 5.02 us -> 6.06 us
    ppermute x2, waiting for transfers between devices: 6.32 us -> 3.44 us  [from_behind(): return lax.ppermute(value, axis, pairs)]
    dot_general x2, matrix products: 3.91 us -> 6.57 us  [slot_pieces(): return jnp.dot(to_slots, side, preferred_element_type=jnp.float32)]
    dot_general x2 -> x1, matrix products: 0.95 us -> 2.2 us  [bf16x3_apply(): jnp.dot(op_mid, pair[:, :cols], preferred_element_type=jnp.float32)]
    unnamed x11 -> x31, local copies, waits for them, and re-layouts: 1.41 us -> 2.4 us
    dot_general x1, matrix products: 0.64 us -> 1.58 us  [body(): spill_prod = jnp.dot(spill_both, moved, preferred_element_type=jnp.float32)]
  transfers between devices with their start and end apart: 22 -> 22, of which waited for: 5 -> 5; matrix products, arithmetic and copies ran while one was open for 16% -> 19% of each run, Pallas kernels for 0% -> 0%
where the time goes in v19:
time: 93.6 us; the launch traced here: 92.1 us
  starting transfers between devices  41.3 us (44%)
  matrix products  19.6 us (21%)
  waiting for transfers between devices  13.2 us (14%)
  other arithmetic  7.4 us (8%)
  local copies, waits for them, and re-layouts  6.06 us (6%)
  between operations  4.5 us (5%)
    ppermute x20, starting transfers between devices, face_sum_parts(): lax.ppermute(block, axis, pairs)  38.3 us
    ppermute x20, waiting for transfers between devices, face_sum_parts(): lax.ppermute(block, axis, pairs)  9.78 us
    dot_general x2, matrix products, slot_pieces(): return jnp.dot(to_slots, side, preferred_element_type=jnp.float32)  6.57 us
    dot_general x2, matrix products, slot_pieces(): jnp.dot(stacked, to_rows, preferred_element_type=jnp.float32)  3.8 us
    ppermute x2, waiting for transfers between devices, from_behind(): return lax.ppermute(value, axis, pairs)  3.44 us
    dot_general x3, matrix products, body(): jnp.dot(op_stack, dir_pair, preferred_element_type=jnp.float32)  3.41 us
    ppermute x2, starting transfers between devices, from_behind(): return lax.ppermute(value, axis, pairs)  3.04 us
    unnamed x31, local copies, waits for them, and re-layouts  2.4 us
  transfers between devices with their start and end apart: 22, of which 5 were waited for; matrix products, arithmetic and copies ran while one was open for 19% of the time, Pallas kernels for 0%

profile of v19, /device:TPU:0, one launch (start us, length us, event | category | flops | bytes accessed | tf_op | source)
XLA Modules:
  0.0 92.1 jit_solution(11416340400185205478)
XLA Ops:
  0.7 1.4 %slice_bitcast_fusion = (f32[128,896]{1,0:T(8,128)S(1)}, f32[128,896]{1,0:T(8,128)S(1)}) fusion(f32[1,1,2,128,896]{4,3,2,1,0:T(8,128)} %param.8), kind=kLoop, calls=%fused_computation.109 | loop fusion | bytes 1835008 | tf_op jit(solution)/shard_map/squeeze | solution.py:117
  2.0 1.8 %slice_select_fusion.16 = (f32[224,128]{1,0:T(8,128)}, f32[224,128]{1,0:T(8,128)S(1)}, f32[224,128]{1,0:T(8,128)}, f32[224,128]{1,0:T(8,128)}) fusion(f32[896,128]{1,0:T(8,128)} %bitcast.55, pred[]{:T(512)S(6)} %eq.100, pred[]{:T(512)S(6)} %eq.101), kind=kLoop, calls=%fused_computation.161 | loop fusion | flops 114688 | bytes 917506 | tf_op jit(solution)/shard_map/jit(_where)/select_n | solution.py:64
  3.8 0.7 collective-permute-start
  4.5 4.4 %collective-permute-start.1 = (f32[224,128]{1,0:T(8,128)}, f32[224,128]{1,0:T(8,128)S(1)}, u32[]{:S(2)}, u32[]{:S(2)}) collective-permute-start(f32[224,128]{1,0:T(8,128)} %get-tuple-element.125), channel_id=1, source_target_pairs={{0,4},{4,0},{8,12},{12,8},{16,20},{20,16},{24,28},{28,24},{1,5},{5... | collective-permute-start | bytes 344072 | tf_op jit(solution)/shard_map/ppermute | solution.py:66
  9.0 2.0 %collective-permute-start.4 = (f32[128,896]{1,0:T(8,128)S(1)}, f32[128,896]{1,0:T(8,128)}, u32[]{:S(2)}, u32[]{:S(2)}) collective-permute-start(f32[128,896]{1,0:T(8,128)S(1)} %get-tuple-element.38), channel_id=1, source_target_pairs={{0,24},{4,28},{8,0},{12,4},{16,8},{20,12},{24,16},{28,20},{1,25},{... | collective-permute-start | bytes 1376264 | tf_op jit(solution)/shard_map/ppermute | solution.py:22
  10.9 1.1 %collective-permute-start.5 = (f32[128,896]{1,0:T(8,128)S(1)}, f32[128,896]{1,0:T(8,128)}, u32[]{:S(2)}, u32[]{:S(2)}) collective-permute-start(f32[128,896]{1,0:T(8,128)S(1)} %get-tuple-element.39), channel_id=1, source_target_pairs={{0,16},{4,20},{8,24},{12,28},{16,0},{20,4},{24,8},{28,12},{1,17},{... | collective-permute-start | bytes 1376264 | tf_op jit(solution)/shard_map/ppermute | solution.py:22
  12.0 1.3 %reduce = s32[896]{0:T(1024)} reduce(s32[1,1,896]{2,1,0:T(1,128)} %param.11, s32[]{:T(128)} %constant.99.clone.1), dimensions={0,1}, to_apply=%param.11.reduce_sub_computation | reduce | bytes 7172 | tf_op args[5]
  14.7 2.6 %convolution_convert_fusion = bf16[1280,896]{0,1:T(8,128)(2,1)S(1)} fusion(bf16[640,896]{1,0:T(8,128)(2,1)S(1)} %get-tuple-element.69, bf16[640,896]{1,0:T(8,128)(2,1)S(1)} %get-tuple-element.68, bf16[896]{0:T(1024)(128)(2,1)S(1)} %select_select_fusion, s32[896]{0:T(1024)S(1)} %copy-done.5), kind=kOutput, calls=%fused_computation.1 | convolution fusion | flops 2062548992 | bytes 4592896 | tf_op jit(solution)/shard_map/dot_general | solution.py:92
  17.5 5.4 %fusion.105 = (bf16[896,1792]{1,0:T(8,128)(2,1)S(1)}, f32[896,1792]{1,0:T(8,128)}) fusion(bf16[640,896]{0,1:T(8,128)(2,1)S(1)} %get-tuple-element.67, bf16[640,896]{0,1:T(8,128)(2,1)S(1)} %get-tuple-element.66, bf16[896]{0:T(1024)(128)(2,1)S(1)} %select_select_fusion, s32[896]{0:T(1024)S(1)} %copy-done.5), kind=kOutput, calls=%fused_computation.204 | convolution fusion | flops 2063122432 | bytes 11932928 | tf_op jit(solution)/shard_map/dot_general | solution.py:94
  22.9 0.7 fusion.104
  26.2 0.7 collective-permute-start.2
  26.9 4.3 %collective-permute-start.3 = (f32[224,128]{1,0:T(8,128)S(1)}, f32[224,128]{1,0:T(8,128)S(1)}, u32[]{:S(2)}, u32[]{:S(2)}) collective-permute-start(f32[224,128]{1,0:T(8,128)S(1)} %get-tuple-element.31), channel_id=1, source_target_pairs={{0,1},{1,0},{2,3},{3,2},{4,5},{5,4},{6,7},{7,6},{8,9},{9,8},{10,11... | collective-permute-start | bytes 344072 | tf_op jit(solution)/shard_map/ppermute | solution.py:69
  31.2 0.6 pad_add_fusion
  31.8 4.3 %collective-permute-done.3 = f32[224,128]{1,0:T(8,128)S(1)} collective-permute-done((f32[224,128]{1,0:T(8,128)S(1)}, f32[224,128]{1,0:T(8,128)S(1)}, u32[]{:S(2)}, u32[]{:S(2)}) %collective-permute-start.3) | collective-permute-done | bytes 114720 | tf_op jit(solution)/shard_map/ppermute | solution.py:69
  36.3 1.6 %fusion.13 = f32[896,256]{1,0:T(8,128)} fusion(bf16[896,1792]{1,0:T(8,128)(2,1)S(1)} %get-tuple-element.133, bf16[896,128]{1,0:T(8,128)(2,1)S(1)} %get-tuple-element.121, bf16[896,128]{1,0:T(8,128)(2,1)S(1)} %get-tuple-element.122), kind=kOutput, calls=%fused_computation.22 | convolution fusion | flops 411959296 | bytes 2981888 | tf_op jit(solution)/shard_map/dot_general | solution.py:98
  37.9 1.0 %constant_dynamic-update-slice_fusion.1 = f32[256,896]{1,0:T(8,128)S(1)} fusion(f32[128,896]{1,0:T(8,128)} %collective-permute-done.4), kind=kLoop, calls=%fused_computation.178 | loop fusion | bytes 917504
  38.9 3.4 %collective-permute-done.5 = f32[128,896]{1,0:T(8,128)} collective-permute-done((f32[128,896]{1,0:T(8,128)S(1)}, f32[128,896]{1,0:T(8,128)}, u32[]{:S(2)}, u32[]{:S(2)}) %collective-permute-start.5) | collective-permute-done | bytes 458784 | tf_op jit(solution)/shard_map/ppermute | solution.py:22
  42.4 1.1 %constant_dynamic-update-slice_fusion = f32[256,896]{1,0:T(8,128)S(1)} fusion(f32[256,896]{1,0:T(8,128)S(1)} %constant_dynamic-update-slice_fusion.1, f32[128,896]{1,0:T(8,128)} %collective-permute-done.5), kind=kLoop, calls=%fused_computation.176 | loop fusion | bytes 917504 | tf_op jit(solution)/shard_map/concatenate | solution.py:146
  43.6 1.6 %fusion.26 = f32[512,256]{0,1:T(8,128)S(1)} fusion(bf16[896]{0:T(1024)(128)(2,1)S(1)} %copy-done.8, s32[896]{0:T(1024)S(1)} %copy-done.6, bf16[256,896]{1,0:T(8,128)(2,1)S(1)} %get-tuple-element.74, bf16[256,896]{1,0:T(8,128)(2,1)S(1)} %get-tuple-element.73, bf16[896,128]{1,0:T(8,128)(2,1)S(1)} %copy-done.3, bf16[896,128]{1,0:T(8,128)(2,1)S(1)} %get-tuple-element.122), kind=kOutput, calls=%fused_computation.37 | convolution fusion | flops 650510336 | bytes 1905920 | tf_op jit(solution)/shard_map/dot_general | solution.py:175
  45.3 0.5 fusion.46
  45.8 0.6 copy-done.12
  46.4 2.2 %fusion.30 = f32[896,128]{1,0:T(8,128)S(1)} fusion(bf16[896,128]{1,0:T(8,128)(2,1)S(1)} %get-tuple-element.122, bf16[896,1792]{1,0:T(8,128)(2,1)} %copy-done.11, f32[896,384]{1,0:T(8,128)S(1)} %fusion.46, f32[896,256]{1,0:T(8,128)S(1)} %copy-done.12), kind=kOutput, calls=%fused_computation.39 | convolution fusion | flops 206094336 | bytes 4587520 | tf_op jit(solution)/shard_map/dot_general | solution.py:99
  48.7 0.7 collective-permute-start.6
  49.3 4.3 %collective-permute-start.7 = (f32[224,128]{1,0:T(8,128)S(1)}, f32[224,128]{1,0:T(8,128)S(1)}, u32[]{:S(2)}, u32[]{:S(2)}) collective-permute-start(f32[224,128]{1,0:T(8,128)S(1)} %get-tuple-element.118), channel_id=1, source_target_pairs={{0,1},{1,0},{2,3},{3,2},{4,5},{5,4},{6,7},{7,6},{8,9},{9,8},{10,11... | collective-permute-start | bytes 344072 | tf_op jit(solution)/shard_map/ppermute | solution.py:75
  53.6 0.8 collective-permute-start.8
  54.5 1.5 %collective-permute-start.9 = (f32[224,128]{1,0:T(8,128)S(1)}, f32[224,128]{1,0:T(8,128)S(1)}, u32[]{:S(2)}, u32[]{:S(2)}) collective-permute-start(f32[224,128]{1,0:T(8,128)S(1)} %get-tuple-element.117), channel_id=1, source_target_pairs={{0,4},{4,0},{8,12},{12,8},{16,20},{20,16},{24,28},{28,24},{1,5},{5... | collective-permute-start | bytes 344072 | tf_op jit(solution)/shard_map/ppermute | solution.py:75
  56.0 1.2 %fusion.24 = bf16[512,896]{1,0:T(8,128)(2,1)S(1)} fusion(bf16[896]{0:T(1024)(128)(2,1)S(1)} %copy-done.8, s32[896]{0:T(1024)S(1)} %copy-done.6, bf16[256,896]{1,0:T(8,128)(2,1)S(1)} %get-tuple-element.74, bf16[256,896]{1,0:T(8,128)(2,1)S(1)} %get-tuple-element.72), kind=kOutput, calls=%fused_computation.33 | convolution fusion | flops 825982976 | bytes 1840384 | tf_op jit(solution)/shard_map/dot_general | solution.py:92
  57.6 1.2 %add_convert_fusion = bf16[896,1792]{1,0:T(8,128)(2,1)S(1)} fusion(f32[896,1792]{1,0:T(8,128)S(1)} %bitcast.38, bf16[256,896]{1,0:T(8,128)(2,1)S(1)} %get-tuple-element.71, bf16[256,896]{1,0:T(8,128)(2,1)S(1)} %get-tuple-element.70, bf16[896]{0:T(1024)(128)(2,1)S(1)} %copy-done.8, s32[256]{0:T(256)S(1)} %copy-done.9, s32[896]{0:T(1024)S(1)} %copy-done.6), kind=kOutput, calls=%fused_computation | convolution fusion | flops 827588608 | bytes 10557696 | tf_op jit(solution)/shard_map/dot_general | solution.py:94
  59.4 1.1 %fusion.39 = f32[1792,256]{1,0:T(8,128)S(1)} fusion(bf16[896,896]{1,0:T(8,128)(2,1)S(1)} %get-tuple-element.65, bf16[896,896]{1,0:T(8,128)(2,1)S(1)} %get-tuple-element.64, bf16[896,128]{1,0:T(8,128)(2,1)S(1)} %fusion.48, bf16[896,128]{1,0:T(8,128)(2,1)S(1)} %get-tuple-element.60), kind=kOutput, calls=%fused_computation.48 | convolution fusion | flops 829423616 | bytes 5505024 | tf_op jit(solution)/shard_map/dot_general | solution.py:190
  60.6 0.7 collective-permute-start.10
  61.3 2.8 %collective-permute-start.11 = (f32[224,128]{1,0:T(8,128)S(1)}, f32[224,128]{1,0:T(8,128)S(1)}, u32[]{:S(2)}, u32[]{:S(2)}) collective-permute-start(f32[224,128]{1,0:T(8,128)S(1)} %get-tuple-element.112), channel_id=1, source_target_pairs={{0,1},{1,0},{2,3},{3,2},{4,5},{5,4},{6,7},{7,6},{8,9},{9,8},{10,11... | collective-permute-start | bytes 344072 | tf_op jit(solution)/shard_map/ppermute | solution.py:75
  64.1 0.7 collective-permute-start.12
  64.7 2.1 %collective-permute-start.13 = (f32[224,128]{1,0:T(8,128)S(1)}, f32[224,128]{1,0:T(8,128)S(1)}, u32[]{:S(2)}, u32[]{:S(2)}) collective-permute-start(f32[224,128]{1,0:T(8,128)S(1)} %get-tuple-element.111), channel_id=1, source_target_pairs={{0,4},{4,0},{8,12},{12,8},{16,20},{20,16},{24,28},{28,24},{1,5},{5... | collective-permute-start | bytes 344072 | tf_op jit(solution)/shard_map/ppermute | solution.py:75
  66.8 2.6 %collective-permute-done.11 = f32[224,128]{1,0:T(8,128)S(1)} collective-permute-done((f32[224,128]{1,0:T(8,128)S(1)}, f32[224,128]{1,0:T(8,128)S(1)}, u32[]{:S(2)}, u32[]{:S(2)}) %collective-permute-start.11) | collective-permute-done | bytes 114720 | tf_op jit(solution)/shard_map/ppermute | solution.py:75
  69.8 1.1 %fusion.38 = f32[1792,256]{1,0:T(8,128)S(1)} fusion(bf16[896,896]{1,0:T(8,128)(2,1)S(1)} %get-tuple-element.65, bf16[896,896]{1,0:T(8,128)(2,1)S(1)} %get-tuple-element.64, bf16[896,128]{1,0:T(8,128)(2,1)S(1)} %fusion.49, bf16[896,128]{1,0:T(8,128)(2,1)S(1)} %get-tuple-element.58), kind=kOutput, calls=%fused_computation.47 | convolution fusion | flops 829423616 | bytes 5505024 | tf_op jit(solution)/shard_map/dot_general | solution.py:190
  71.0 0.7 collective-permute-start.14
  71.7 2.7 %collective-permute-start.15 = (f32[224,128]{1,0:T(8,128)S(1)}, f32[224,128]{1,0:T(8,128)S(1)}, u32[]{:S(2)}, u32[]{:S(2)}) collective-permute-start(f32[224,128]{1,0:T(8,128)S(1)} %get-tuple-element.106), channel_id=1, source_target_pairs={{0,1},{1,0},{2,3},{3,2},{4,5},{5,4},{6,7},{7,6},{8,9},{9,8},{10,11... | collective-permute-start | bytes 344072 | tf_op jit(solution)/shard_map/ppermute | solution.py:75
  74.4 0.7 collective-permute-start.16
  75.1 3.2 %collective-permute-start.17 = (f32[224,128]{1,0:T(8,128)S(1)}, f32[224,128]{1,0:T(8,128)S(1)}, u32[]{:S(2)}, u32[]{:S(2)}) collective-permute-start(f32[224,128]{1,0:T(8,128)S(1)} %get-tuple-element.105), channel_id=1, source_target_pairs={{0,4},{4,0},{8,12},{12,8},{16,20},{20,16},{24,28},{28,24},{1,5},{5... | collective-permute-start | bytes 344072 | tf_op jit(solution)/shard_map/ppermute | solution.py:75
  78.3 2.0 %collective-permute-done.15 = f32[224,128]{1,0:T(8,128)S(1)} collective-permute-done((f32[224,128]{1,0:T(8,128)S(1)}, f32[224,128]{1,0:T(8,128)S(1)}, u32[]{:S(2)}, u32[]{:S(2)}) %collective-permute-start.15) | collective-permute-done | bytes 114720 | tf_op jit(solution)/shard_map/ppermute | solution.py:75
  80.6 1.1 %fusion.37 = f32[1792,256]{1,0:T(8,128)S(1)} fusion(bf16[896,896]{1,0:T(8,128)(2,1)S(1)} %get-tuple-element.65, bf16[896,896]{1,0:T(8,128)(2,1)S(1)} %get-tuple-element.64, bf16[896,128]{1,0:T(8,128)(2,1)S(1)} %fusion.50, bf16[896,128]{1,0:T(8,128)(2,1)S(1)} %get-tuple-element.56), kind=kOutput, calls=%fused_computation.46 | convolution fusion | flops 829423616 | bytes 5505024 | tf_op jit(solution)/shard_map/dot_general | solution.py:190
  81.9 0.7 collective-permute-start.18
  82.6 2.3 %collective-permute-start.19 = (f32[224,128]{1,0:T(8,128)S(1)}, f32[224,128]{1,0:T(8,128)S(1)}, u32[]{:S(2)}, u32[]{:S(2)}) collective-permute-start(f32[224,128]{1,0:T(8,128)S(1)} %get-tuple-element.100), channel_id=1, source_target_pairs={{0,1},{1,0},{2,3},{3,2},{4,5},{5,4},{6,7},{7,6},{8,9},{9,8},{10,11... | collective-permute-start | bytes 344072 | tf_op jit(solution)/shard_map/ppermute | solution.py:75
  84.9 0.7 collective-permute-start.20
  85.5 3.9 %collective-permute-start.21 = (f32[224,128]{1,0:T(8,128)S(1)}, f32[224,128]{1,0:T(8,128)S(1)}, u32[]{:S(2)}, u32[]{:S(2)}) collective-permute-start(f32[224,128]{1,0:T(8,128)S(1)} %get-tuple-element.99), channel_id=1, source_target_pairs={{0,4},{4,0},{8,12},{12,8},{16,20},{20,16},{24,28},{28,24},{1,5},{5... | collective-permute-start | bytes 344072 | tf_op jit(solution)/shard_map/ppermute | solution.py:75
  89.4 1.0 %add_add_fusion = f32[1,1,896,128]{3,2,1,0:T(8,128)} fusion(f32[1,1,224,128]{3,2,1,0:T(8,128)S(1)} %bitcast.43, f32[1,1,224,128]{3,2,1,0:T(8,128)S(1)} %bitcast.45, f32[1,1,224,128]{3,2,1,0:T(8,128)S(1)} %bitcast.41, f32[1,1,224,128]{3,2,1,0:T(8,128)S(1)} %bitcast.39, f32[1,1,224,128]{3,2,1,0:T(8,128)S(1)} %bitcast.51, f32[1,1,224,128]{3,2,1,0:T(8,128)S(1)} %bitcast.53, ...), kind=kLoop, calls=%fused_computation.100 | loop fusion | flops 3211264 | bytes 2293760 | tf_op jit(solution)/shard_map/add | solution.py:167
  90.4 0.8 collective-permute-done.19
  91.2 0.9 %maximum_subtract_fusion.6 = f32[1,1,896,128]{3,2,1,0:T(8,128)} fusion(f32[1,1,224,128]{3,2,1,0:T(8,128)S(1)} %get-tuple-element.97, f32[1,1,224,128]{3,2,1,0:T(8,128)S(1)} %get-tuple-element.98, f32[1,1,224,128]{3,2,1,0:T(8,128)S(1)} %get-tuple-element.78, f32[1,1,224,128]{3,2,1,0:T(8,128)S(1)} %get-tuple-element.77, f32[1,1,224,128]{3,2,1,0:T(8,128)S(1)} %bitcast.70, ...), kind=kLoop, calls=%fused_computation.99 | loop fusion | flops 2179072 | bytes 2752512 | tf_op jit(solution)/shard_map/sub | solution.py:195
  (75 shorter events, 3.1 us)
Async XLA Ops:
  0.6 13.3 %copy-start = (f32[1,1,640,896]{3,2,1,0:T(8,128)S(1)}, f32[1,1,640,896]{3,2,1,0:T(8,128)}, u32[]{:S(2)}) copy-start(f32[1,1,640,896]{3,2,1,0:T(8,128)} %param.7) | copy-start | bytes 6881284
  3.8 22.4 %collective-permute-start = (f32[224,128]{1,0:T(8,128)}, f32[224,128]{1,0:T(8,128)S(1)}, u32[]{:S(2)}, u32[]{:S(2)}) collective-permute-start(f32[224,128]{1,0:T(8,128)} %get-tuple-element.127), channel_id=1, source_target_pairs={{4,8},{8,4},{12,16},{16,12},{20,24},{24,20},{5,9},{9,5},{13,17},{1... | collective-permute-start | bytes 344072 | tf_op jit(solution)/shard_map/ppermute | solution.py:66
  4.5 21.7 %collective-permute-start.1 = (f32[224,128]{1,0:T(8,128)}, f32[224,128]{1,0:T(8,128)S(1)}, u32[]{:S(2)}, u32[]{:S(2)}) collective-permute-start(f32[224,128]{1,0:T(8,128)} %get-tuple-element.125), channel_id=1, source_target_pairs={{0,4},{4,0},{8,12},{12,8},{16,20},{20,16},{24,28},{28,24},{1,5},{5... | collective-permute-start | bytes 344072 | tf_op jit(solution)/shard_map/ppermute | solution.py:66
  9.0 28.9 %collective-permute-start.4 = (f32[128,896]{1,0:T(8,128)S(1)}, f32[128,896]{1,0:T(8,128)}, u32[]{:S(2)}, u32[]{:S(2)}) collective-permute-start(f32[128,896]{1,0:T(8,128)S(1)} %get-tuple-element.38), channel_id=1, source_target_pairs={{0,24},{4,28},{8,0},{12,4},{16,8},{20,12},{24,16},{28,20},{1,25},{... | collective-permute-start | bytes 1376264 | tf_op jit(solution)/shard_map/ppermute | solution.py:22
  10.9 31.4 %collective-permute-start.5 = (f32[128,896]{1,0:T(8,128)S(1)}, f32[128,896]{1,0:T(8,128)}, u32[]{:S(2)}, u32[]{:S(2)}) collective-permute-start(f32[128,896]{1,0:T(8,128)S(1)} %get-tuple-element.39), channel_id=1, source_target_pairs={{0,16},{4,20},{8,24},{12,28},{16,0},{20,4},{24,8},{28,12},{1,17},{... | collective-permute-start | bytes 1376264 | tf_op jit(solution)/shard_map/ppermute | solution.py:22
  13.9 0.7 copy-start.5
  14.6 2.8 %copy-start.7 = (bf16[896]{0:T(1024)(128)(2,1)}, bf16[896]{0:T(1024)(128)(2,1)S(1)}, u32[]{:S(2)}) copy-start(bf16[896]{0:T(1024)(128)(2,1)S(1)} %select_select_fusion) | copy-start | bytes 5380
  17.5 5.4 %copy-start.10 = (s32[1,1,2]{2,1,0:T(1,128)S(1)}, s32[1,1,2]{2,1,0:T(1,128)}, u32[]{:S(2)}) copy-start(s32[1,1,2]{2,1,0:T(1,128)} %param.9) | copy-start | bytes 28
  17.5 8.7 %copy-start.4 = (f32[224,128]{1,0:T(8,128)S(1)}, f32[224,128]{1,0:T(8,128)}, u32[]{:S(2)}) copy-start(f32[224,128]{1,0:T(8,128)} %get-tuple-element.30) | copy-start | bytes 344068
  17.5 18.6 %copy-start.1 = (f32[1,1,896,128]{3,2,1,0:T(8,128)S(1)}, f32[1,1,896,128]{3,2,1,0:T(8,128)}, u32[]{:S(2)}) copy-start(f32[1,1,896,128]{3,2,1,0:T(8,128)} %param.6) | copy-start | bytes 1376260
  22.9 20.7 %copy-start.11 = (bf16[896,1792]{1,0:T(8,128)(2,1)}, bf16[896,1792]{1,0:T(8,128)(2,1)S(1)}, u32[]{:S(2)}) copy-start(bf16[896,1792]{1,0:T(8,128)(2,1)S(1)} %get-tuple-element.133) | copy-start | bytes 9633796
  26.2 5.5 %collective-permute-start.2 = (f32[224,128]{1,0:T(8,128)S(1)}, f32[224,128]{1,0:T(8,128)S(1)}, u32[]{:S(2)}, u32[]{:S(2)}) collective-permute-start(f32[224,128]{1,0:T(8,128)S(1)} %copy-done.4), channel_id=1, source_target_pairs={{1,2},{2,1},{5,6},{6,5},{9,10},{10,9},{13,14},{14,13},{17,18},{18,... | collective-permute-start | bytes 344072 | tf_op jit(solution)/shard_map/ppermute | solution.py:69
  26.9 9.2 %collective-permute-start.3 = (f32[224,128]{1,0:T(8,128)S(1)}, f32[224,128]{1,0:T(8,128)S(1)}, u32[]{:S(2)}, u32[]{:S(2)}) collective-permute-start(f32[224,128]{1,0:T(8,128)S(1)} %get-tuple-element.31), channel_id=1, source_target_pairs={{0,1},{1,0},{2,3},{3,2},{4,5},{5,4},{6,7},{7,6},{8,9},{9,8},{10,11... | collective-permute-start | bytes 344072 | tf_op jit(solution)/shard_map/ppermute | solution.py:69
  36.2 2.7 %copy-start.2 = (bf16[896,128]{1,0:T(8,128)(2,1)}, bf16[896,128]{1,0:T(8,128)(2,1)S(1)}, u32[]{:S(2)}) copy-start(bf16[896,128]{1,0:T(8,128)(2,1)S(1)} %get-tuple-element.121) | copy-start | bytes 688132
  37.8 5.8 %copy-start.6 = (s32[896]{0:T(1024)S(1)}, s32[896]{0:T(1024)}, u32[]{:S(2)}) copy-start(s32[896]{0:T(1024)} %reduce) | copy-start | bytes 10756
  37.8 5.8 %copy-start.8 = (bf16[896]{0:T(1024)(128)(2,1)S(1)}, bf16[896]{0:T(1024)(128)(2,1)}, u32[]{:S(2)}) copy-start(bf16[896]{0:T(1024)(128)(2,1)} %copy-done.7) | copy-start | bytes 5380
  42.4 1.3 %copy-start.3 = (bf16[896,128]{1,0:T(8,128)(2,1)S(1)}, bf16[896,128]{1,0:T(8,128)(2,1)}, u32[]{:S(2)}) copy-start(bf16[896,128]{1,0:T(8,128)(2,1)} %copy-done.2) | copy-start | bytes 688132
  43.6 1.7 %copy-start.9 = (s32[256]{0:T(256)S(1)}, s32[256]{0:T(256)}, u32[]{:S(2)}) copy-start(s32[256]{0:T(256)} %pad_add_fusion) | copy-start | bytes 3076
  45.2 1.2 %copy-start.12 = (f32[896,256]{1,0:T(8,128)S(1)}, f32[896,256]{1,0:T(8,128)}, u32[]{:S(2)}) copy-start(f32[896,256]{1,0:T(8,128)} %fusion.13) | copy-start | bytes 2752516
  46.4 10.9 %slice-start = ((s8[6422528]{0:T(1024)(128)(4,1)}), s8[4194304]{0:T(1024)(128)(4,1)S(1)}, s32[]{:S(2)}) async-start(s8[6422528]{0:T(1024)(128)(4,1)} %bitcast.37), calls=%async_computation | async-start | bytes 8388608
  48.7 10.4 %collective-permute-start.6 = (f32[224,128]{1,0:T(8,128)S(1)}, f32[224,128]{1,0:T(8,128)S(1)}, u32[]{:S(2)}, u32[]{:S(2)}) collective-permute-start(f32[224,128]{1,0:T(8,128)S(1)} %get-tuple-element.120), channel_id=1, source_target_pairs={{1,2},{2,1},{5,6},{6,5},{9,10},{10,9},{13,14},{14,13},{17,18},{18,... | collective-permute-start | bytes 344072 | tf_op jit(solution)/shard_map/ppermute | solution.py:75
  49.3 9.8 %collective-permute-start.7 = (f32[224,128]{1,0:T(8,128)S(1)}, f32[224,128]{1,0:T(8,128)S(1)}, u32[]{:S(2)}, u32[]{:S(2)}) collective-permute-start(f32[224,128]{1,0:T(8,128)S(1)} %get-tuple-element.118), channel_id=1, source_target_pairs={{0,1},{1,0},{2,3},{3,2},{4,5},{5,4},{6,7},{7,6},{8,9},{9,8},{10,11... | collective-permute-start | bytes 344072 | tf_op jit(solution)/shard_map/ppermute | solution.py:75
  53.6 5.5 %collective-permute-start.8 = (f32[224,128]{1,0:T(8,128)S(1)}, f32[224,128]{1,0:T(8,128)S(1)}, u32[]{:S(2)}, u32[]{:S(2)}) collective-permute-start(f32[224,128]{1,0:T(8,128)S(1)} %get-tuple-element.119), channel_id=1, source_target_pairs={{4,8},{8,4},{12,16},{16,12},{20,24},{24,20},{5,9},{9,5},{13,17},{1... | collective-permute-start | bytes 344072 | tf_op jit(solution)/shard_map/ppermute | solution.py:75
  54.5 4.6 %collective-permute-start.9 = (f32[224,128]{1,0:T(8,128)S(1)}, f32[224,128]{1,0:T(8,128)S(1)}, u32[]{:S(2)}, u32[]{:S(2)}) collective-permute-start(f32[224,128]{1,0:T(8,128)S(1)} %get-tuple-element.117), channel_id=1, source_target_pairs={{0,4},{4,0},{8,12},{12,8},{16,20},{20,16},{24,28},{28,24},{1,5},{5... | collective-permute-start | bytes 344072 | tf_op jit(solution)/shard_map/ppermute | solution.py:75
  56.0 1.6 %slice-start.1 = ((s8[6422528]{0:T(1024)(128)(4,1)}), s8[2228224]{0:T(1024)(128)(4,1)S(1)}, s32[]{:S(2)}) async-start(s8[6422528]{0:T(1024)(128)(4,1)} %bitcast.37), calls=%async_computation.1 | async-start | bytes 4456448
  60.6 6.2 %collective-permute-start.10 = (f32[224,128]{1,0:T(8,128)S(1)}, f32[224,128]{1,0:T(8,128)S(1)}, u32[]{:S(2)}, u32[]{:S(2)}) collective-permute-start(f32[224,128]{1,0:T(8,128)S(1)} %get-tuple-element.114), channel_id=1, source_target_pairs={{1,2},{2,1},{5,6},{6,5},{9,10},{10,9},{13,14},{14,13},{17,18},{18,... | collective-permute-start | bytes 344072 | tf_op jit(solution)/shard_map/ppermute | solution.py:75
  61.3 8.2 %collective-permute-start.11 = (f32[224,128]{1,0:T(8,128)S(1)}, f32[224,128]{1,0:T(8,128)S(1)}, u32[]{:S(2)}, u32[]{:S(2)}) collective-permute-start(f32[224,128]{1,0:T(8,128)S(1)} %get-tuple-element.112), channel_id=1, source_target_pairs={{0,1},{1,0},{2,3},{3,2},{4,5},{5,4},{6,7},{7,6},{8,9},{9,8},{10,11... | collective-permute-start | bytes 344072 | tf_op jit(solution)/shard_map/ppermute | solution.py:75
  64.1 5.4 %collective-permute-start.12 = (f32[224,128]{1,0:T(8,128)S(1)}, f32[224,128]{1,0:T(8,128)S(1)}, u32[]{:S(2)}, u32[]{:S(2)}) collective-permute-start(f32[224,128]{1,0:T(8,128)S(1)} %get-tuple-element.113), channel_id=1, source_target_pairs={{4,8},{8,4},{12,16},{16,12},{20,24},{24,20},{5,9},{9,5},{13,17},{1... | collective-permute-start | bytes 344072 | tf_op jit(solution)/shard_map/ppermute | solution.py:75
  64.7 4.8 %collective-permute-start.13 = (f32[224,128]{1,0:T(8,128)S(1)}, f32[224,128]{1,0:T(8,128)S(1)}, u32[]{:S(2)}, u32[]{:S(2)}) collective-permute-start(f32[224,128]{1,0:T(8,128)S(1)} %get-tuple-element.111), channel_id=1, source_target_pairs={{0,4},{4,0},{8,12},{12,8},{16,20},{20,16},{24,28},{28,24},{1,5},{5... | collective-permute-start | bytes 344072 | tf_op jit(solution)/shard_map/ppermute | solution.py:75
  71.0 7.3 %collective-permute-start.14 = (f32[224,128]{1,0:T(8,128)S(1)}, f32[224,128]{1,0:T(8,128)S(1)}, u32[]{:S(2)}, u32[]{:S(2)}) collective-permute-start(f32[224,128]{1,0:T(8,128)S(1)} %get-tuple-element.108), channel_id=1, source_target_pairs={{1,2},{2,1},{5,6},{6,5},{9,10},{10,9},{13,14},{14,13},{17,18},{18,... | collective-permute-start | bytes 344072 | tf_op jit(solution)/shard_map/ppermute | solution.py:75
  71.7 8.6 %collective-permute-start.15 = (f32[224,128]{1,0:T(8,128)S(1)}, f32[224,128]{1,0:T(8,128)S(1)}, u32[]{:S(2)}, u32[]{:S(2)}) collective-permute-start(f32[224,128]{1,0:T(8,128)S(1)} %get-tuple-element.106), channel_id=1, source_target_pairs={{0,1},{1,0},{2,3},{3,2},{4,5},{5,4},{6,7},{7,6},{8,9},{9,8},{10,11... | collective-permute-start | bytes 344072 | tf_op jit(solution)/shard_map/ppermute | solution.py:75
  74.4 5.9 %collective-permute-start.16 = (f32[224,128]{1,0:T(8,128)S(1)}, f32[224,128]{1,0:T(8,128)S(1)}, u32[]{:S(2)}, u32[]{:S(2)}) collective-permute-start(f32[224,128]{1,0:T(8,128)S(1)} %get-tuple-element.107), channel_id=1, source_target_pairs={{4,8},{8,4},{12,16},{16,12},{20,24},{24,20},{5,9},{9,5},{13,17},{1... | collective-permute-start | bytes 344072 | tf_op jit(solution)/shard_map/ppermute | solution.py:75
  75.1 5.3 %collective-permute-start.17 = (f32[224,128]{1,0:T(8,128)S(1)}, f32[224,128]{1,0:T(8,128)S(1)}, u32[]{:S(2)}, u32[]{:S(2)}) collective-permute-start(f32[224,128]{1,0:T(8,128)S(1)} %get-tuple-element.105), channel_id=1, source_target_pairs={{0,4},{4,0},{8,12},{12,8},{16,20},{20,16},{24,28},{28,24},{1,5},{5... | collective-permute-start | bytes 344072 | tf_op jit(solution)/shard_map/ppermute | solution.py:75
  81.9 8.5 %collective-permute-start.18 = (f32[224,128]{1,0:T(8,128)S(1)}, f32[224,128]{1,0:T(8,128)S(1)}, u32[]{:S(2)}, u32[]{:S(2)}) collective-permute-start(f32[224,128]{1,0:T(8,128)S(1)} %get-tuple-element.102), channel_id=1, source_target_pairs={{1,2},{2,1},{5,6},{6,5},{9,10},{10,9},{13,14},{14,13},{17,18},{18,... | collective-permute-start | bytes 344072 | tf_op jit(solution)/shard_map/ppermute | solution.py:75
  82.6 8.6 %collective-permute-start.19 = (f32[224,128]{1,0:T(8,128)S(1)}, f32[224,128]{1,0:T(8,128)S(1)}, u32[]{:S(2)}, u32[]{:S(2)}) collective-permute-start(f32[224,128]{1,0:T(8,128)S(1)} %get-tuple-element.100), channel_id=1, source_target_pairs={{0,1},{1,0},{2,3},{3,2},{4,5},{5,4},{6,7},{7,6},{8,9},{9,8},{10,11... | collective-permute-start | bytes 344072 | tf_op jit(solution)/shard_map/ppermute | solution.py:75
  84.9 6.3 %collective-permute-start.20 = (f32[224,128]{1,0:T(8,128)S(1)}, f32[224,128]{1,0:T(8,128)S(1)}, u32[]{:S(2)}, u32[]{:S(2)}) collective-permute-start(f32[224,128]{1,0:T(8,128)S(1)} %get-tuple-element.101), channel_id=1, source_target_pairs={{4,8},{8,4},{12,16},{16,12},{20,24},{24,20},{5,9},{9,5},{13,17},{1... | collective-permute-start | bytes 344072 | tf_op jit(solution)/shard_map/ppermute | solution.py:75
  85.5 5.6 %collective-permute-start.21 = (f32[224,128]{1,0:T(8,128)S(1)}, f32[224,128]{1,0:T(8,128)S(1)}, u32[]{:S(2)}, u32[]{:S(2)}) collective-permute-start(f32[224,128]{1,0:T(8,128)S(1)} %get-tuple-element.99), channel_id=1, source_target_pairs={{0,4},{4,0},{8,12},{12,8},{16,20},{20,16},{24,28},{28,24},{1,5},{5... | collective-permute-start | bytes 344072 | tf_op jit(solution)/shard_map/ppermute | solution.py:75

commit v20 on v18

--- a/solution.py
+++ b/solution.py
@@ -162,6 +162,8 @@
     residual = load
     direction = residual / centre
     for step_id in range(ITERS):
+        if step_id + 1 == ITERS:
+            residual = lax.optimization_barrier(residual)
         solution = solution + direction
         dir_high = lax.reduce_precision(direction, exponent_bits=8, mantissa_bits=7)
         dir_pair = jnp.concatenate([dir_high, direction - dir_high], axis=1).astype(jnp.bfloat16)

time: 89.9 us -> 89.8 us (level)
  no operation moved by 1% of the time
where the time goes in v20:
time: 89.8 us; the launch traced here: 88.4 us
  starting transfers between devices  41.7 us (46%)
  waiting for transfers between devices  16.3 us (18%)
  matrix products  14.2 us (16%)
  other arithmetic  6.68 us (7%)
  local copies, waits for them, and re-layouts  5.02 us (6%)
  between operations  4.54 us (5%)
    ppermute x20, starting transfers between devices, face_sum_parts(): lax.ppermute(block, axis, pairs)  38.7 us
    ppermute x20, waiting for transfers between devices, face_sum_parts(): lax.ppermute(block, axis, pairs)  9.95 us
    ppermute x2, waiting for transfers between devices, from_behind(): return lax.ppermute(value, axis, pairs)  6.32 us
    dot_general x2, matrix products, slot_pieces(): return jnp.dot(to_slots, side, preferred_element_type=jnp.float32)  3.91 us
    dot_general x2, matrix products, slot_pieces(): jnp.dot(stacked, to_rows, preferred_element_type=jnp.float32)  3.8 us
    dot_general x3, matrix products, body(): jnp.dot(op_stack, dir_pair, preferred_element_type=jnp.float32)  3.41 us
    ppermute x2, starting transfers between devices, from_behind(): return lax.ppermute(value, axis, pairs)  3.04 us
    select_n x5, other arithmetic, face_sum_parts(): jnp.where(even, high, low)  1.96 us
  transfers between devices with their start and end apart: 22, of which 5 were waited for; matrix products, arithmetic and copies ran while one was open for 16% of the time, Pallas kernels for 0%

profile of v20, /device:TPU:0, one launch (start us, length us, event | category | flops | bytes accessed | tf_op | source)
XLA Modules:
  0.0 88.4 jit_solution(18283392554527060224)
XLA Ops:
  0.7 1.4 %slice_bitcast_fusion = (f32[128,896]{1,0:T(8,128)S(1)}, f32[128,896]{1,0:T(8,128)S(1)}) fusion(f32[1,1,2,128,896]{4,3,2,1,0:T(8,128)} %param.8), kind=kLoop, calls=%fused_computation.110 | loop fusion | bytes 1835008 | tf_op jit(solution)/shard_map/squeeze | solution.py:117
  2.0 1.8 %slice_select_fusion.16 = (f32[224,128]{1,0:T(8,128)}, f32[224,128]{1,0:T(8,128)S(1)}, f32[224,128]{1,0:T(8,128)}, f32[224,128]{1,0:T(8,128)}) fusion(f32[896,128]{1,0:T(8,128)} %bitcast.41, pred[]{:T(512)S(6)} %eq.100, pred[]{:T(512)S(6)} %eq.101), kind=kLoop, calls=%fused_computation.163 | loop fusion | flops 114688 | bytes 917506 | tf_op jit(solution)/shard_map/jit(_where)/select_n | solution.py:64
  3.9 0.7 collective-permute-start
  4.5 4.4 %collective-permute-start.1 = (f32[224,128]{1,0:T(8,128)}, f32[224,128]{1,0:T(8,128)S(1)}, u32[]{:S(2)}, u32[]{:S(2)}) collective-permute-start(f32[224,128]{1,0:T(8,128)} %get-tuple-element.124), channel_id=1, source_target_pairs={{0,4},{4,0},{8,12},{12,8},{16,20},{20,16},{24,28},{28,24},{1,5},{5... | collective-permute-start | bytes 344072 | tf_op jit(solution)/shard_map/ppermute | solution.py:66
  9.0 2.0 %collective-permute-start.4 = (f32[128,896]{1,0:T(8,128)S(1)}, f32[128,896]{1,0:T(8,128)}, u32[]{:S(2)}, u32[]{:S(2)}) collective-permute-start(f32[128,896]{1,0:T(8,128)S(1)} %get-tuple-element.38), channel_id=1, source_target_pairs={{0,24},{4,28},{8,0},{12,4},{16,8},{20,12},{24,16},{28,20},{1,25},{... | collective-permute-start | bytes 1376264 | tf_op jit(solution)/shard_map/ppermute | solution.py:22
  10.9 1.1 %collective-permute-start.5 = (f32[128,896]{1,0:T(8,128)S(1)}, f32[128,896]{1,0:T(8,128)}, u32[]{:S(2)}, u32[]{:S(2)}) collective-permute-start(f32[128,896]{1,0:T(8,128)S(1)} %get-tuple-element.39), channel_id=1, source_target_pairs={{0,16},{4,20},{8,24},{12,28},{16,0},{20,4},{24,8},{28,12},{1,17},{... | collective-permute-start | bytes 1376264 | tf_op jit(solution)/shard_map/ppermute | solution.py:22
  12.0 1.3 %reduce = s32[896]{0:T(1024)} reduce(s32[1,1,896]{2,1,0:T(1,128)} %param.11, s32[]{:T(128)} %constant.99.clone.1), dimensions={0,1}, to_apply=%param.11.reduce_sub_computation | reduce | bytes 7172 | tf_op args[5]
  14.3 0.3 copy-done.3
  14.6 2.6 %convolution_convert_fusion = bf16[1280,896]{0,1:T(8,128)(2,1)S(1)} fusion(bf16[640,896]{1,0:T(8,128)(2,1)S(1)} %get-tuple-element.67, bf16[640,896]{1,0:T(8,128)(2,1)S(1)} %get-tuple-element.66, bf16[896]{0:T(1024)(128)(2,1)S(1)} %select_select_fusion, s32[896]{0:T(1024)S(1)} %copy-done.3), kind=kOutput, calls=%fused_computation.1 | convolution fusion | flops 2062548992 | bytes 4592896 | tf_op jit(solution)/shard_map/dot_general | solution.py:92
  17.5 2.7 %fusion.109 = (bf16[896,1792]{1,0:T(8,128)(2,1)S(1)}, f32[896,1792]{1,0:T(8,128)S(1)}) fusion(bf16[640,896]{0,1:T(8,128)(2,1)S(1)} %get-tuple-element.65, bf16[640,896]{0,1:T(8,128)(2,1)S(1)} %get-tuple-element.64, bf16[896]{0:T(1024)(128)(2,1)S(1)} %select_select_fusion, s32[896]{0:T(1024)S(1)} %copy-done.3), kind=kOutput, calls=%fused_computation.206 | convolution fusion | flops 2063122432 | bytes 11932928 | tf_op jit(solution)/shard_map/dot_general | solution.py:94
  20.2 0.7 fusion.108
  23.7 0.7 collective-permute-start.2
  24.3 4.3 %collective-permute-start.3 = (f32[224,128]{1,0:T(8,128)S(1)}, f32[224,128]{1,0:T(8,128)S(1)}, u32[]{:S(2)}, u32[]{:S(2)}) collective-permute-start(f32[224,128]{1,0:T(8,128)S(1)} %get-tuple-element.31), channel_id=1, source_target_pairs={{0,1},{1,0},{2,3},{3,2},{4,5},{5,4},{6,7},{7,6},{8,9},{9,8},{10,11... | collective-permute-start | bytes 344072 | tf_op jit(solution)/shard_map/ppermute | solution.py:69
  28.7 4.9 %collective-permute-done.3 = f32[224,128]{1,0:T(8,128)S(1)} collective-permute-done((f32[224,128]{1,0:T(8,128)S(1)}, f32[224,128]{1,0:T(8,128)S(1)}, u32[]{:S(2)}, u32[]{:S(2)}) %collective-permute-start.3) | collective-permute-done | bytes 114720 | tf_op jit(solution)/shard_map/ppermute | solution.py:69
  33.7 0.6 fusion.25
  34.3 0.6 fusion.13
  35.0 1.0 %constant_dynamic-update-slice_fusion.1 = f32[256,896]{1,0:T(8,128)S(1)} fusion(f32[128,896]{1,0:T(8,128)} %collective-permute-done.4), kind=kLoop, calls=%fused_computation.180 | loop fusion | bytes 917504
  36.0 6.3 %collective-permute-done.5 = f32[128,896]{1,0:T(8,128)} collective-permute-done((f32[128,896]{1,0:T(8,128)S(1)}, f32[128,896]{1,0:T(8,128)}, u32[]{:S(2)}, u32[]{:S(2)}) %collective-permute-start.5) | collective-permute-done | bytes 458784 | tf_op jit(solution)/shard_map/ppermute | solution.py:22
  42.4 1.0 %constant_dynamic-update-slice_fusion = f32[256,896]{1,0:T(8,128)S(1)} fusion(f32[256,896]{1,0:T(8,128)S(1)} %constant_dynamic-update-slice_fusion.1, f32[128,896]{1,0:T(8,128)} %collective-permute-done.5), kind=kLoop, calls=%fused_computation.178 | loop fusion | bytes 917504 | tf_op jit(solution)/shard_map/concatenate | solution.py:146
  43.5 0.4 fusion.110
  44.2 0.5 fusion.46
  44.7 0.7 fusion.29
  45.4 0.7 collective-permute-start.6
  46.1 4.3 %collective-permute-start.7 = (f32[224,128]{1,0:T(8,128)S(1)}, f32[224,128]{1,0:T(8,128)S(1)}, u32[]{:S(2)}, u32[]{:S(2)}) collective-permute-start(f32[224,128]{1,0:T(8,128)S(1)} %get-tuple-element.117), channel_id=1, source_target_pairs={{0,1},{1,0},{2,3},{3,2},{4,5},{5,4},{6,7},{7,6},{8,9},{9,8},{10,11... | collective-permute-start | bytes 344072 | tf_op jit(solution)/shard_map/ppermute | solution.py:75
  50.4 0.8 collective-permute-start.8
  51.2 1.5 %collective-permute-start.9 = (f32[224,128]{1,0:T(8,128)S(1)}, f32[224,128]{1,0:T(8,128)S(1)}, u32[]{:S(2)}, u32[]{:S(2)}) collective-permute-start(f32[224,128]{1,0:T(8,128)S(1)} %get-tuple-element.116), channel_id=1, source_target_pairs={{0,4},{4,0},{8,12},{12,8},{16,20},{20,16},{24,28},{28,24},{1,5},{5... | collective-permute-start | bytes 344072 | tf_op jit(solution)/shard_map/ppermute | solution.py:75
  52.7 1.2 %fusion.24 = bf16[512,896]{1,0:T(8,128)(2,1)S(1)} fusion(bf16[896]{0:T(1024)(128)(2,1)S(1)} %select_select_fusion, s32[896]{0:T(1024)S(1)} %copy-done.3, bf16[256,896]{1,0:T(8,128)(2,1)S(1)} %get-tuple-element.73, bf16[256,896]{1,0:T(8,128)(2,1)S(1)} %get-tuple-element.72), kind=kOutput, calls=%fused_computation.33 | convolution fusion | flops 825982976 | bytes 1840384 | tf_op jit(solution)/shard_map/dot_general | solution.py:92
  54.0 1.2 %add_convert_fusion = bf16[896,1792]{1,0:T(8,128)(2,1)S(1)} fusion(f32[896,1792]{1,0:T(8,128)S(1)} %get-tuple-element.133, bf16[256,896]{1,0:T(8,128)(2,1)S(1)} %get-tuple-element.71, bf16[256,896]{1,0:T(8,128)(2,1)S(1)} %get-tuple-element.70, bf16[896]{0:T(1024)(128)(2,1)S(1)} %select_select_fusion, s32[256]{0:T(256)S(1)} %pad_add_fusion, s32[896]{0:T(1024)S(1)} %copy-done.3), kind=kOutput, calls=%fused_computation | convolution fusion | flops 827588608 | bytes 10557696 | tf_op jit(solution)/shard_map/dot_general | solution.py:94
  55.7 1.1 %fusion.38 = f32[1792,256]{1,0:T(8,128)S(1)} fusion(bf16[896,896]{1,0:T(8,128)(2,1)S(1)} %get-tuple-element.63, bf16[896,896]{1,0:T(8,128)(2,1)S(1)} %get-tuple-element.62, bf16[896,128]{1,0:T(8,128)(2,1)S(1)} %get-tuple-element.69, bf16[896,128]{1,0:T(8,128)(2,1)S(1)} %get-tuple-element.68), kind=kOutput, calls=%fused_computation.45 | convolution fusion | flops 829423616 | bytes 5505024 | tf_op jit(solution)/shard_map/dot_general | solution.py:187
  57.0 0.7 collective-permute-start.10
  57.7 2.8 %collective-permute-start.11 = (f32[224,128]{1,0:T(8,128)S(1)}, f32[224,128]{1,0:T(8,128)S(1)}, u32[]{:S(2)}, u32[]{:S(2)}) collective-permute-start(f32[224,128]{1,0:T(8,128)S(1)} %get-tuple-element.111), channel_id=1, source_target_pairs={{0,1},{1,0},{2,3},{3,2},{4,5},{5,4},{6,7},{7,6},{8,9},{9,8},{10,11... | collective-permute-start | bytes 344072 | tf_op jit(solution)/shard_map/ppermute | solution.py:75
  60.4 0.7 collective-permute-start.12
  61.1 2.4 %collective-permute-start.13 = (f32[224,128]{1,0:T(8,128)S(1)}, f32[224,128]{1,0:T(8,128)S(1)}, u32[]{:S(2)}, u32[]{:S(2)}) collective-permute-start(f32[224,128]{1,0:T(8,128)S(1)} %get-tuple-element.110), channel_id=1, source_target_pairs={{0,4},{4,0},{8,12},{12,8},{16,20},{20,16},{24,28},{28,24},{1,5},{5... | collective-permute-start | bytes 344072 | tf_op jit(solution)/shard_map/ppermute | solution.py:75
  63.5 2.3 %collective-permute-done.11 = f32[224,128]{1,0:T(8,128)S(1)} collective-permute-done((f32[224,128]{1,0:T(8,128)S(1)}, f32[224,128]{1,0:T(8,128)S(1)}, u32[]{:S(2)}, u32[]{:S(2)}) %collective-permute-start.11) | collective-permute-done | bytes 114720 | tf_op jit(solution)/shard_map/ppermute | solution.py:75
  66.1 1.1 %fusion.37 = f32[1792,256]{1,0:T(8,128)S(1)} fusion(bf16[896,896]{1,0:T(8,128)(2,1)S(1)} %get-tuple-element.63, bf16[896,896]{1,0:T(8,128)(2,1)S(1)} %get-tuple-element.62, bf16[896,128]{1,0:T(8,128)(2,1)S(1)} %fusion.49, bf16[896,128]{1,0:T(8,128)(2,1)S(1)} %get-tuple-element.58), kind=kOutput, calls=%fused_computation.44 | convolution fusion | flops 829423616 | bytes 5505024 | tf_op jit(solution)/shard_map/dot_general | solution.py:187
  67.4 0.7 collective-permute-start.14
  68.1 2.7 %collective-permute-start.15 = (f32[224,128]{1,0:T(8,128)S(1)}, f32[224,128]{1,0:T(8,128)S(1)}, u32[]{:S(2)}, u32[]{:S(2)}) collective-permute-start(f32[224,128]{1,0:T(8,128)S(1)} %get-tuple-element.105), channel_id=1, source_target_pairs={{0,1},{1,0},{2,3},{3,2},{4,5},{5,4},{6,7},{7,6},{8,9},{9,8},{10,11... | collective-permute-start | bytes 344072 | tf_op jit(solution)/shard_map/ppermute | solution.py:75
  70.8 0.7 collective-permute-start.16
  71.5 3.2 %collective-permute-start.17 = (f32[224,128]{1,0:T(8,128)S(1)}, f32[224,128]{1,0:T(8,128)S(1)}, u32[]{:S(2)}, u32[]{:S(2)}) collective-permute-start(f32[224,128]{1,0:T(8,128)S(1)} %get-tuple-element.104), channel_id=1, source_target_pairs={{0,4},{4,0},{8,12},{12,8},{16,20},{20,16},{24,28},{28,24},{1,5},{5... | collective-permute-start | bytes 344072 | tf_op jit(solution)/shard_map/ppermute | solution.py:75
  74.7 2.0 %collective-permute-done.15 = f32[224,128]{1,0:T(8,128)S(1)} collective-permute-done((f32[224,128]{1,0:T(8,128)S(1)}, f32[224,128]{1,0:T(8,128)S(1)}, u32[]{:S(2)}, u32[]{:S(2)}) %collective-permute-start.15) | collective-permute-done | bytes 114720 | tf_op jit(solution)/shard_map/ppermute | solution.py:75
  77.0 1.1 %fusion.36 = f32[1792,256]{1,0:T(8,128)S(1)} fusion(bf16[896,896]{1,0:T(8,128)(2,1)S(1)} %get-tuple-element.63, bf16[896,896]{1,0:T(8,128)(2,1)S(1)} %get-tuple-element.62, bf16[896,128]{1,0:T(8,128)(2,1)S(1)} %fusion.50, bf16[896,128]{1,0:T(8,128)(2,1)S(1)} %get-tuple-element.56), kind=kOutput, calls=%fused_computation.43 | convolution fusion | flops 829423616 | bytes 5505024 | tf_op jit(solution)/shard_map/dot_general | solution.py:187
  78.3 0.7 collective-permute-start.18
  79.0 2.3 %collective-permute-start.19 = (f32[224,128]{1,0:T(8,128)S(1)}, f32[224,128]{1,0:T(8,128)S(1)}, u32[]{:S(2)}, u32[]{:S(2)}) collective-permute-start(f32[224,128]{1,0:T(8,128)S(1)} %get-tuple-element.99), channel_id=1, source_target_pairs={{0,1},{1,0},{2,3},{3,2},{4,5},{5,4},{6,7},{7,6},{8,9},{9,8},{10,11... | collective-permute-start | bytes 344072 | tf_op jit(solution)/shard_map/ppermute | solution.py:75
  81.2 0.7 collective-permute-start.20
  81.9 3.9 %collective-permute-start.21 = (f32[224,128]{1,0:T(8,128)S(1)}, f32[224,128]{1,0:T(8,128)S(1)}, u32[]{:S(2)}, u32[]{:S(2)}) collective-permute-start(f32[224,128]{1,0:T(8,128)S(1)} %get-tuple-element.98), channel_id=1, source_target_pairs={{0,4},{4,0},{8,12},{12,8},{16,20},{20,16},{24,28},{28,24},{1,5},{5... | collective-permute-start | bytes 344072 | tf_op jit(solution)/shard_map/ppermute | solution.py:75
  85.8 1.0 %fusion.61 = f32[1,1,896,128]{3,2,1,0:T(8,128)} fusion(f32[1,1,224,128]{3,2,1,0:T(8,128)S(1)} %bitcast.49, f32[1,1,224,128]{3,2,1,0:T(8,128)S(1)} %bitcast.50, f32[1,1,224,128]{3,2,1,0:T(8,128)S(1)} %bitcast.48, f32[1,1,224,128]{3,2,1,0:T(8,128)S(1)} %bitcast.47, f32[1,1,224,128]{3,2,1,0:T(8,128)S(1)} %bitcast.45, f32[1,1,224,128]{3,2,1,0:T(8,128)S(1)} %bitcast.46, ...), kind=kLoop, calls=%fused_computation.94 | loop fusion | flops 3211264 | bytes 2293760 | tf_op jit(solution)/shard_map/add | solution.py:167
  86.8 0.7 collective-permute-done.19
  87.6 0.8 fusion.65
  (54 shorter events, 2.7 us)
Async XLA Ops:
  0.6 13.3 %copy-start = (f32[1,1,640,896]{3,2,1,0:T(8,128)S(1)}, f32[1,1,640,896]{3,2,1,0:T(8,128)}, u32[]{:S(2)}) copy-start(f32[1,1,640,896]{3,2,1,0:T(8,128)} %param.7) | copy-start | bytes 6881284
  3.9 19.8 %collective-permute-start = (f32[224,128]{1,0:T(8,128)}, f32[224,128]{1,0:T(8,128)S(1)}, u32[]{:S(2)}, u32[]{:S(2)}) collective-permute-start(f32[224,128]{1,0:T(8,128)} %get-tuple-element.126), channel_id=1, source_target_pairs={{4,8},{8,4},{12,16},{16,12},{20,24},{24,20},{5,9},{9,5},{13,17},{1... | collective-permute-start | bytes 344072 | tf_op jit(solution)/shard_map/ppermute | solution.py:66
  4.5 19.1 %collective-permute-start.1 = (f32[224,128]{1,0:T(8,128)}, f32[224,128]{1,0:T(8,128)S(1)}, u32[]{:S(2)}, u32[]{:S(2)}) collective-permute-start(f32[224,128]{1,0:T(8,128)} %get-tuple-element.124), channel_id=1, source_target_pairs={{0,4},{4,0},{8,12},{12,8},{16,20},{20,16},{24,28},{28,24},{1,5},{5... | collective-permute-start | bytes 344072 | tf_op jit(solution)/shard_map/ppermute | solution.py:66
  9.0 26.0 %collective-permute-start.4 = (f32[128,896]{1,0:T(8,128)S(1)}, f32[128,896]{1,0:T(8,128)}, u32[]{:S(2)}, u32[]{:S(2)}) collective-permute-start(f32[128,896]{1,0:T(8,128)S(1)} %get-tuple-element.38), channel_id=1, source_target_pairs={{0,24},{4,28},{8,0},{12,4},{16,8},{20,12},{24,16},{28,20},{1,25},{... | collective-permute-start | bytes 1376264 | tf_op jit(solution)/shard_map/ppermute | solution.py:22
  10.9 31.4 %collective-permute-start.5 = (f32[128,896]{1,0:T(8,128)S(1)}, f32[128,896]{1,0:T(8,128)}, u32[]{:S(2)}, u32[]{:S(2)}) collective-permute-start(f32[128,896]{1,0:T(8,128)S(1)} %get-tuple-element.39), channel_id=1, source_target_pairs={{0,16},{4,20},{8,24},{12,28},{16,0},{20,4},{24,8},{28,12},{1,17},{... | collective-permute-start | bytes 1376264 | tf_op jit(solution)/shard_map/ppermute | solution.py:22
  13.9 0.7 copy-start.3
  17.4 2.8 %copy-start.4 = (s32[1,1,2]{2,1,0:T(1,128)S(1)}, s32[1,1,2]{2,1,0:T(1,128)}, u32[]{:S(2)}) copy-start(s32[1,1,2]{2,1,0:T(1,128)} %param.9) | copy-start | bytes 28
  17.5 6.2 %copy-start.2 = (f32[224,128]{1,0:T(8,128)S(1)}, f32[224,128]{1,0:T(8,128)}, u32[]{:S(2)}) copy-start(f32[224,128]{1,0:T(8,128)} %get-tuple-element.30) | copy-start | bytes 344068
  17.5 16.1 %copy-start.1 = (f32[1,1,896,128]{3,2,1,0:T(8,128)S(1)}, f32[1,1,896,128]{3,2,1,0:T(8,128)}, u32[]{:S(2)}) copy-start(f32[1,1,896,128]{3,2,1,0:T(8,128)} %param.6) | copy-start | bytes 1376260
  23.7 5.0 %collective-permute-start.2 = (f32[224,128]{1,0:T(8,128)S(1)}, f32[224,128]{1,0:T(8,128)S(1)}, u32[]{:S(2)}, u32[]{:S(2)}) collective-permute-start(f32[224,128]{1,0:T(8,128)S(1)} %copy-done.2), channel_id=1, source_target_pairs={{1,2},{2,1},{5,6},{6,5},{9,10},{10,9},{13,14},{14,13},{17,18},{18,... | collective-permute-start | bytes 344072 | tf_op jit(solution)/shard_map/ppermute | solution.py:69
  24.3 9.2 %collective-permute-start.3 = (f32[224,128]{1,0:T(8,128)S(1)}, f32[224,128]{1,0:T(8,128)S(1)}, u32[]{:S(2)}, u32[]{:S(2)}) collective-permute-start(f32[224,128]{1,0:T(8,128)S(1)} %get-tuple-element.31), channel_id=1, source_target_pairs={{0,1},{1,0},{2,3},{3,2},{4,5},{5,4},{6,7},{7,6},{8,9},{9,8},{10,11... | collective-permute-start | bytes 344072 | tf_op jit(solution)/shard_map/ppermute | solution.py:69
  45.4 10.1 %collective-permute-start.6 = (f32[224,128]{1,0:T(8,128)S(1)}, f32[224,128]{1,0:T(8,128)S(1)}, u32[]{:S(2)}, u32[]{:S(2)}) collective-permute-start(f32[224,128]{1,0:T(8,128)S(1)} %get-tuple-element.119), channel_id=1, source_target_pairs={{1,2},{2,1},{5,6},{6,5},{9,10},{10,9},{13,14},{14,13},{17,18},{18,... | collective-permute-start | bytes 344072 | tf_op jit(solution)/shard_map/ppermute | solution.py:75
  46.1 9.4 %collective-permute-start.7 = (f32[224,128]{1,0:T(8,128)S(1)}, f32[224,128]{1,0:T(8,128)S(1)}, u32[]{:S(2)}, u32[]{:S(2)}) collective-permute-start(f32[224,128]{1,0:T(8,128)S(1)} %get-tuple-element.117), channel_id=1, source_target_pairs={{0,1},{1,0},{2,3},{3,2},{4,5},{5,4},{6,7},{7,6},{8,9},{9,8},{10,11... | collective-permute-start | bytes 344072 | tf_op jit(solution)/shard_map/ppermute | solution.py:75
  50.4 5.2 %collective-permute-start.8 = (f32[224,128]{1,0:T(8,128)S(1)}, f32[224,128]{1,0:T(8,128)S(1)}, u32[]{:S(2)}, u32[]{:S(2)}) collective-permute-start(f32[224,128]{1,0:T(8,128)S(1)} %get-tuple-element.118), channel_id=1, source_target_pairs={{4,8},{8,4},{12,16},{16,12},{20,24},{24,20},{5,9},{9,5},{13,17},{1... | collective-permute-start | bytes 344072 | tf_op jit(solution)/shard_map/ppermute | solution.py:75
  51.2 4.3 %collective-permute-start.9 = (f32[224,128]{1,0:T(8,128)S(1)}, f32[224,128]{1,0:T(8,128)S(1)}, u32[]{:S(2)}, u32[]{:S(2)}) collective-permute-start(f32[224,128]{1,0:T(8,128)S(1)} %get-tuple-element.116), channel_id=1, source_target_pairs={{0,4},{4,0},{8,12},{12,8},{16,20},{20,16},{24,28},{28,24},{1,5},{5... | collective-permute-start | bytes 344072 | tf_op jit(solution)/shard_map/ppermute | solution.py:75
  57.0 6.6 %collective-permute-start.10 = (f32[224,128]{1,0:T(8,128)S(1)}, f32[224,128]{1,0:T(8,128)S(1)}, u32[]{:S(2)}, u32[]{:S(2)}) collective-permute-start(f32[224,128]{1,0:T(8,128)S(1)} %get-tuple-element.113), channel_id=1, source_target_pairs={{1,2},{2,1},{5,6},{6,5},{9,10},{10,9},{13,14},{14,13},{17,18},{18,... | collective-permute-start | bytes 344072 | tf_op jit(solution)/shard_map/ppermute | solution.py:75
  57.7 8.2 %collective-permute-start.11 = (f32[224,128]{1,0:T(8,128)S(1)}, f32[224,128]{1,0:T(8,128)S(1)}, u32[]{:S(2)}, u32[]{:S(2)}) collective-permute-start(f32[224,128]{1,0:T(8,128)S(1)} %get-tuple-element.111), channel_id=1, source_target_pairs={{0,1},{1,0},{2,3},{3,2},{4,5},{5,4},{6,7},{7,6},{8,9},{9,8},{10,11... | collective-permute-start | bytes 344072 | tf_op jit(solution)/shard_map/ppermute | solution.py:75
  60.4 5.4 %collective-permute-start.12 = (f32[224,128]{1,0:T(8,128)S(1)}, f32[224,128]{1,0:T(8,128)S(1)}, u32[]{:S(2)}, u32[]{:S(2)}) collective-permute-start(f32[224,128]{1,0:T(8,128)S(1)} %get-tuple-element.112), channel_id=1, source_target_pairs={{4,8},{8,4},{12,16},{16,12},{20,24},{24,20},{5,9},{9,5},{13,17},{1... | collective-permute-start | bytes 344072 | tf_op jit(solution)/shard_map/ppermute | solution.py:75
  61.1 4.8 %collective-permute-start.13 = (f32[224,128]{1,0:T(8,128)S(1)}, f32[224,128]{1,0:T(8,128)S(1)}, u32[]{:S(2)}, u32[]{:S(2)}) collective-permute-start(f32[224,128]{1,0:T(8,128)S(1)} %get-tuple-element.110), channel_id=1, source_target_pairs={{0,4},{4,0},{8,12},{12,8},{16,20},{20,16},{24,28},{28,24},{1,5},{5... | collective-permute-start | bytes 344072 | tf_op jit(solution)/shard_map/ppermute | solution.py:75
  67.4 7.3 %collective-permute-start.14 = (f32[224,128]{1,0:T(8,128)S(1)}, f32[224,128]{1,0:T(8,128)S(1)}, u32[]{:S(2)}, u32[]{:S(2)}) collective-permute-start(f32[224,128]{1,0:T(8,128)S(1)} %get-tuple-element.107), channel_id=1, source_target_pairs={{1,2},{2,1},{5,6},{6,5},{9,10},{10,9},{13,14},{14,13},{17,18},{18,... | collective-permute-start | bytes 344072 | tf_op jit(solution)/shard_map/ppermute | solution.py:75
  68.1 8.6 %collective-permute-start.15 = (f32[224,128]{1,0:T(8,128)S(1)}, f32[224,128]{1,0:T(8,128)S(1)}, u32[]{:S(2)}, u32[]{:S(2)}) collective-permute-start(f32[224,128]{1,0:T(8,128)S(1)} %get-tuple-element.105), channel_id=1, source_target_pairs={{0,1},{1,0},{2,3},{3,2},{4,5},{5,4},{6,7},{7,6},{8,9},{9,8},{10,11... | collective-permute-start | bytes 344072 | tf_op jit(solution)/shard_map/ppermute | solution.py:75
  70.8 5.9 %collective-permute-start.16 = (f32[224,128]{1,0:T(8,128)S(1)}, f32[224,128]{1,0:T(8,128)S(1)}, u32[]{:S(2)}, u32[]{:S(2)}) collective-permute-start(f32[224,128]{1,0:T(8,128)S(1)} %get-tuple-element.106), channel_id=1, source_target_pairs={{4,8},{8,4},{12,16},{16,12},{20,24},{24,20},{5,9},{9,5},{13,17},{1... | collective-permute-start | bytes 344072 | tf_op jit(solution)/shard_map/ppermute | solution.py:75
  71.5 5.3 %collective-permute-start.17 = (f32[224,128]{1,0:T(8,128)S(1)}, f32[224,128]{1,0:T(8,128)S(1)}, u32[]{:S(2)}, u32[]{:S(2)}) collective-permute-start(f32[224,128]{1,0:T(8,128)S(1)} %get-tuple-element.104), channel_id=1, source_target_pairs={{0,4},{4,0},{8,12},{12,8},{16,20},{20,16},{24,28},{28,24},{1,5},{5... | collective-permute-start | bytes 344072 | tf_op jit(solution)/shard_map/ppermute | solution.py:75
  78.3 8.5 %collective-permute-start.18 = (f32[224,128]{1,0:T(8,128)S(1)}, f32[224,128]{1,0:T(8,128)S(1)}, u32[]{:S(2)}, u32[]{:S(2)}) collective-permute-start(f32[224,128]{1,0:T(8,128)S(1)} %get-tuple-element.101), channel_id=1, source_target_pairs={{1,2},{2,1},{5,6},{6,5},{9,10},{10,9},{13,14},{14,13},{17,18},{18,... | collective-permute-start | bytes 344072 | tf_op jit(solution)/shard_map/ppermute | solution.py:75
  79.0 8.6 %collective-permute-start.19 = (f32[224,128]{1,0:T(8,128)S(1)}, f32[224,128]{1,0:T(8,128)S(1)}, u32[]{:S(2)}, u32[]{:S(2)}) collective-permute-start(f32[224,128]{1,0:T(8,128)S(1)} %get-tuple-element.99), channel_id=1, source_target_pairs={{0,1},{1,0},{2,3},{3,2},{4,5},{5,4},{6,7},{7,6},{8,9},{9,8},{10,11... | collective-permute-start | bytes 344072 | tf_op jit(solution)/shard_map/ppermute | solution.py:75
  81.2 6.3 %collective-permute-start.20 = (f32[224,128]{1,0:T(8,128)S(1)}, f32[224,128]{1,0:T(8,128)S(1)}, u32[]{:S(2)}, u32[]{:S(2)}) collective-permute-start(f32[224,128]{1,0:T(8,128)S(1)} %get-tuple-element.100), channel_id=1, source_target_pairs={{4,8},{8,4},{12,16},{16,12},{20,24},{24,20},{5,9},{9,5},{13,17},{1... | collective-permute-start | bytes 344072 | tf_op jit(solution)/shard_map/ppermute | solution.py:75
  81.9 5.6 %collective-permute-start.21 = (f32[224,128]{1,0:T(8,128)S(1)}, f32[224,128]{1,0:T(8,128)S(1)}, u32[]{:S(2)}, u32[]{:S(2)}) collective-permute-start(f32[224,128]{1,0:T(8,128)S(1)} %get-tuple-element.98), channel_id=1, source_target_pairs={{0,4},{4,0},{8,12},{12,8},{16,20},{20,16},{24,28},{28,24},{1,5},{5... | collective-permute-start | bytes 344072 | tf_op jit(solution)/shard_map/ppermute | solution.py:75

commit v21 on v11

--- a/solution.py
+++ b/solution.py
@@ -150,8 +150,9 @@
     own_high = own_slots[:, :order_max].astype(jnp.bfloat16)
     own_mid = own_slots[:, order_max:].astype(jnp.bfloat16)
     full_slots = own_slots + (spill_slots[0] + spill_slots[1])
-    op_high = full_slots[:, :order_max].astype(jnp.bfloat16)
-    op_mid = full_slots[:, order_max:].astype(jnp.bfloat16)
+    op_stack = jnp.concatenate(
+        [full_slots[:, :order_max], full_slots[:, order_max:]], axis=0
+    ).astype(jnp.bfloat16)
     spill_high = [lax.reduce_precision(block, exponent_bits=8, mantissa_bits=7) for block in homed]
     spill_mid = [(block - high).astype(jnp.bfloat16) for block, high in zip(homed, spill_high)]
     spill_high = [high.astype(jnp.bfloat16) for high in spill_high]
@@ -186,7 +187,10 @@
                     (placed[:, :cols] + placed[:, cols : 2 * cols]) + placed[:, 2 * cols :]
                 )
         else:
-            local = bf16x3_apply(op_high, op_mid, dir_pair, cols)
+            stacked_out = jnp.dot(op_stack, dir_pair, preferred_element_type=jnp.float32)
+            local = (
+                stacked_out[:order_max, :cols] + stacked_out[:order_max, cols:]
+            ) + stacked_out[order_max:, :cols]
         faces = [local[face_id * width : (face_id + 1) * width] for face_id in range(4)]
         residual = residual - face_sum_parts(faces)
         if step_id + 1 < ITERS:

time: 90.5 us -> 90.4 us (level)
  waiting for transfers between devices: 17.9 us -> 11.8 us
  starting transfers between devices: 40.9 us -> 44.2 us
  matrix products: 15.9 us -> 17.2 us
  other arithmetic: 6.81 us -> 7.86 us
    ppermute x2, waiting for transfers between devices: 7.11 us -> 0.01 us  [from_behind(): return lax.ppermute(value, axis, pairs)]
    dot_general x0 -> x3, matrix products: none -> 3.37 us  [body(): jnp.dot(op_stack, dir_pair, preferred_element_type=jnp.float32)]
    ppermute x20, starting transfers between devices: 37.9 us -> 40.2 us  [face_sum_parts(): lax.ppermute(block, axis, pairs)]
    dot_general x6 -> x3, matrix products: 3.05 us -> 1.11 us  [bf16x3_apply(): both = jnp.dot(op_high, pair, preferred_element_type=jnp.float32)]
    dot_general x6 -> x3, matrix products: 2.9 us -> 1.18 us  [bf16x3_apply(): jnp.dot(op_mid, pair[:, :cols], preferred_element_type=jnp.float32)]
    dot_general x3, matrix products: 3.98 us -> 5.59 us  [slot_pieces(): jnp.dot(stacked, to_rows, preferred_element_type=jnp.float32)]
    another operation x9 -> x12, other arithmetic: 0.98 us -> 2.53 us
    ppermute x20, waiting for transfers between devices: 10.8 us -> 11.8 us  [face_sum_parts(): lax.ppermute(block, axis, pairs)]
  transfers between devices with their start and end apart: 22 -> 22, of which waited for: 5 -> 4; matrix products, arithmetic and copies ran while one was open for 16% -> 20% of each run, Pallas kernels for 0% -> 0%
where the time goes in v21:
time: 90.4 us; the launch traced here: 89.7 us
  starting transfers between devices  44.2 us (49%)
  matrix products  17.2 us (19%)
  waiting for transfers between devices  11.8 us (13%)
  other arithmetic  7.86 us (9%)
  between operations  4.35 us (5%)
  local copies, waits for them, and re-layouts  4.2 us (5%)
    ppermute x20, starting transfers between devices, face_sum_parts(): lax.ppermute(block, axis, pairs)  40.2 us
    ppermute x20, waiting for transfers between devices, face_sum_parts(): lax.ppermute(block, axis, pairs)  11.8 us
    dot_general x3, matrix products, slot_pieces(): jnp.dot(stacked, to_rows, preferred_element_type=jnp.float32)  5.59 us
    dot_general x3, matrix products, slot_pieces(): return jnp.dot(to_slots, side, preferred_element_type=jnp.float32)  4.7 us
    ppermute x2, starting transfers between devices, from_behind(): return lax.ppermute(value, axis, pairs)  3.94 us
    dot_general x3, matrix products, body(): jnp.dot(op_stack, dir_pair, preferred_element_type=jnp.float32)  3.37 us
    another operation x12, other arithmetic  2.53 us
    squeeze x1, local copies, waits for them, and re-layouts, body(): spill_parts = [spill_block[slot_id] for slot_id in range(2)]  2.29 us
  transfers between devices with their start and end apart: 22, of which 4 were waited for; matrix products, arithmetic and copies ran while one was open for 20% of the time, Pallas kernels for 0%

profile of v21, /device:TPU:0, one launch (start us, length us, event | category | flops | bytes accessed | tf_op | source)
XLA Modules:
  0.0 89.7 jit_solution(11879338784319845246)
XLA Ops:
  0.7 2.3 %slice_bitcast_fusion = (f32[128,896]{1,0:T(8,128)}, f32[128,896]{1,0:T(8,128)}) fusion(f32[1,1,2,128,896]{4,3,2,1,0:T(8,128)} %param.8), kind=kLoop, calls=%fused_computation.117 | loop fusion | bytes 1835008 | tf_op jit(solution)/shard_map/squeeze | solution.py:117
  2.9 1.8 %slice_select_fusion.16 = (f32[224,128]{1,0:T(8,128)}, f32[224,128]{1,0:T(8,128)S(1)}, f32[224,128]{1,0:T(8,128)}, f32[224,128]{1,0:T(8,128)}) fusion(f32[896,128]{1,0:T(8,128)} %bitcast.57, pred[]{:T(512)S(6)} %eq.100, pred[]{:T(512)S(6)} %eq.101), kind=kLoop, calls=%fused_computation.167 | loop fusion | flops 114688 | bytes 917506 | tf_op jit(solution)/shard_map/jit(_where)/select_n | solution.py:64
  4.8 0.7 collective-permute-start
  5.4 4.4 %collective-permute-start.1 = (f32[224,128]{1,0:T(8,128)}, f32[224,128]{1,0:T(8,128)S(1)}, u32[]{:S(2)}, u32[]{:S(2)}) collective-permute-start(f32[224,128]{1,0:T(8,128)} %get-tuple-element.130), channel_id=1, source_target_pairs={{0,4},{4,0},{8,12},{12,8},{16,20},{20,16},{24,28},{28,24},{1,5},{5... | collective-permute-start | bytes 344072 | tf_op jit(solution)/shard_map/ppermute | solution.py:66
  9.9 2.6 %collective-permute-start.5 = (f32[128,896]{1,0:T(8,128)}, f32[128,896]{1,0:T(8,128)S(1)}, u32[]{:S(2)}, u32[]{:S(2)}) collective-permute-start(f32[128,896]{1,0:T(8,128)} %get-tuple-element.39), channel_id=1, source_target_pairs={{0,16},{4,20},{8,24},{12,28},{16,0},{20,4},{24,8},{28,12},{1,17},{... | collective-permute-start | bytes 1376264 | tf_op jit(solution)/shard_map/ppermute | solution.py:22
  12.4 1.3 %collective-permute-start.4 = (f32[128,896]{1,0:T(8,128)}, f32[128,896]{1,0:T(8,128)S(1)}, u32[]{:S(2)}, u32[]{:S(2)}) collective-permute-start(f32[128,896]{1,0:T(8,128)} %get-tuple-element.38), channel_id=1, source_target_pairs={{0,24},{4,28},{8,0},{12,4},{16,8},{20,12},{24,16},{28,20},{1,25},{... | collective-permute-start | bytes 1376264 | tf_op jit(solution)/shard_map/ppermute | solution.py:22
  13.8 1.4 %fusion.134 = (s32[1,1,1]{2,1,0:T(1,128)}, s32[1,1,1]{2,1,0:T(1,128)}) fusion(s32[1,1,2]{2,1,0:T(1,128)} %param.9), kind=kLoop, calls=%fused_computation.234 | loop fusion | bytes 16 | tf_op jit(solution)/shard_map/slice | solution.py:138
  17.7 1.7 %reduce-precision_convert_fusion = (bf16[640,896]{1,0:T(8,128)(2,1)}, bf16[640,896]{1,0:T(8,128)(2,1)}) fusion(f32[1,1,640,896]{3,2,1,0:T(8,128)S(1)} %copy-done), kind=kLoop, calls=%fused_computation.3 | loop fusion | flops 2867200 | bytes 4587520 | tf_op jit(solution)/shard_map/convert.24
  19.4 0.7 reduce
  20.8 4.2 %convolution_convert_fusion = bf16[1280,896]{0,1:T(8,128)(2,1)S(1)} fusion(bf16[640,896]{1,0:T(8,128)(2,1)} %get-tuple-element.71, bf16[640,896]{1,0:T(8,128)(2,1)} %get-tuple-element.70, bf16[896]{0:T(1024)(128)(2,1)S(1)} %select_select_fusion, s32[896]{0:T(1024)S(1)} %reduce), kind=kOutput, calls=%fused_computation.1 | convolution fusion | flops 2062548992 | bytes 4592896 | tf_op jit(solution)/shard_map/dot_general | solution.py:92
  25.2 2.7 %fusion.135 = (bf16[896,1792]{1,0:T(8,128)(2,1)S(1)}, f32[896,1792]{1,0:T(8,128)S(1)}) fusion(bf16[640,896]{0,1:T(8,128)(2,1)S(1)} %get-tuple-element.69, bf16[640,896]{0,1:T(8,128)(2,1)S(1)} %get-tuple-element.68, bf16[896]{0:T(1024)(128)(2,1)S(1)} %select_select_fusion, s32[896]{0:T(1024)S(1)} %reduce), kind=kOutput, calls=%fused_computation.235 | convolution fusion | flops 2063122432 | bytes 11932928 | tf_op jit(solution)/shard_map/dot_general | solution.py:94
  28.0 0.7 collective-permute-start.2
  28.7 4.3 %collective-permute-start.3 = (f32[224,128]{1,0:T(8,128)S(1)}, f32[224,128]{1,0:T(8,128)S(1)}, u32[]{:S(2)}, u32[]{:S(2)}) collective-permute-start(f32[224,128]{1,0:T(8,128)S(1)} %get-tuple-element.31), channel_id=1, source_target_pairs={{0,1},{1,0},{2,3},{3,2},{4,5},{5,4},{6,7},{7,6},{8,9},{9,8},{10,11... | collective-permute-start | bytes 344072 | tf_op jit(solution)/shard_map/ppermute | solution.py:69
  33.0 0.3 select_convert_fusion.13
  33.3 4.6 %collective-permute-done.3 = f32[224,128]{1,0:T(8,128)S(1)} collective-permute-done((f32[224,128]{1,0:T(8,128)S(1)}, f32[224,128]{1,0:T(8,128)S(1)}, u32[]{:S(2)}, u32[]{:S(2)}) %collective-permute-start.3) | collective-permute-done | bytes 114720 | tf_op jit(solution)/shard_map/ppermute | solution.py:69
  38.1 0.6 fusion.28
  38.7 0.6 fusion.14
  40.5 0.3 fusion.82
  40.8 0.3 fusion.87
  41.1 0.7 fusion.37
  41.9 0.7 collective-permute-start.6
  42.6 3.0 %collective-permute-start.7 = (f32[224,128]{1,0:T(8,128)S(1)}, f32[224,128]{1,0:T(8,128)S(1)}, u32[]{:S(2)}, u32[]{:S(2)}) collective-permute-start(f32[224,128]{1,0:T(8,128)S(1)} %get-tuple-element.123), channel_id=1, source_target_pairs={{0,1},{1,0},{2,3},{3,2},{4,5},{5,4},{6,7},{7,6},{8,9},{9,8},{10,11... | collective-permute-start | bytes 344072 | tf_op jit(solution)/shard_map/ppermute | solution.py:75
  45.6 0.8 collective-permute-start.8
  46.5 6.5 %collective-permute-start.9 = (f32[224,128]{1,0:T(8,128)S(1)}, f32[224,128]{1,0:T(8,128)S(1)}, u32[]{:S(2)}, u32[]{:S(2)}) collective-permute-start(f32[224,128]{1,0:T(8,128)S(1)} %get-tuple-element.122), channel_id=1, source_target_pairs={{0,4},{4,0},{8,12},{12,8},{16,20},{20,16},{24,28},{28,24},{1,5},{5... | collective-permute-start | bytes 344072 | tf_op jit(solution)/shard_map/ppermute | solution.py:75
  53.0 0.7 fusion.29
  53.7 0.7 fusion.30
  54.5 1.0 %fusion.54 = f32[896,1792]{1,0:T(8,128)S(1)} fusion(bf16[128,896]{1,0:T(8,128)(2,1)S(1)} %get-tuple-element.117, bf16[128,896]{1,0:T(8,128)(2,1)S(1)} %get-tuple-element.116, bf16[896,256]{1,0:T(8,128)(2,1)S(1)} %select_convert_fusion.13), kind=kOutput, calls=%fused_computation.85 | convolution fusion | flops 411959296 | bytes 7110656 | tf_op jit(solution)/shard_map/dot_general | solution.py:94
  55.5 1.0 %add_convert_fusion = bf16[896,1792]{1,0:T(8,128)(2,1)S(1)} fusion(f32[896,1792]{1,0:T(8,128)S(1)} %get-tuple-element.141, f32[896,1792]{1,0:T(8,128)S(1)} %fusion.54, bf16[128,896]{1,0:T(8,128)(2,1)S(1)} %get-tuple-element.113, bf16[128,896]{1,0:T(8,128)(2,1)S(1)} %get-tuple-element.112, bf16[896,256]{1,0:T(8,128)(2,1)S(1)} %select_convert_fusion.13), kind=kOutput, calls=%fused_computation | convolution fusion | flops 416776192 | bytes 16744448 | tf_op jit(solution)/shard_map/dot_general | solution.py:94
  57.0 1.1 %fusion.46 = f32[1792,256]{1,0:T(8,128)S(1)} fusion(bf16[896,896]{1,0:T(8,128)(2,1)S(1)} %get-tuple-element.67, bf16[896,896]{1,0:T(8,128)(2,1)S(1)} %get-tuple-element.66, bf16[896,128]{1,0:T(8,128)(2,1)S(1)} %fusion.48, bf16[896,128]{1,0:T(8,128)(2,1)S(1)} %get-tuple-element.60), kind=kOutput, calls=%fused_computation.49 | convolution fusion | flops 829423616 | bytes 5505024 | tf_op jit(solution)/shard_map/dot_general | solution.py:190
  58.2 0.7 collective-permute-start.10
  58.9 2.7 %collective-permute-start.11 = (f32[224,128]{1,0:T(8,128)S(1)}, f32[224,128]{1,0:T(8,128)S(1)}, u32[]{:S(2)}, u32[]{:S(2)}) collective-permute-start(f32[224,128]{1,0:T(8,128)S(1)} %get-tuple-element.109), channel_id=1, source_target_pairs={{0,1},{1,0},{2,3},{3,2},{4,5},{5,4},{6,7},{7,6},{8,9},{9,8},{10,11... | collective-permute-start | bytes 344072 | tf_op jit(solution)/shard_map/ppermute | solution.py:75
  61.7 0.7 collective-permute-start.12
  62.3 1.5 %collective-permute-start.13 = (f32[224,128]{1,0:T(8,128)S(1)}, f32[224,128]{1,0:T(8,128)S(1)}, u32[]{:S(2)}, u32[]{:S(2)}) collective-permute-start(f32[224,128]{1,0:T(8,128)S(1)} %get-tuple-element.108), channel_id=1, source_target_pairs={{0,4},{4,0},{8,12},{12,8},{16,20},{20,16},{24,28},{28,24},{1,5},{5... | collective-permute-start | bytes 344072 | tf_op jit(solution)/shard_map/ppermute | solution.py:75
  63.8 3.3 %collective-permute-done.11 = f32[224,128]{1,0:T(8,128)S(1)} collective-permute-done((f32[224,128]{1,0:T(8,128)S(1)}, f32[224,128]{1,0:T(8,128)S(1)}, u32[]{:S(2)}, u32[]{:S(2)}) %collective-permute-start.11) | collective-permute-done | bytes 114720 | tf_op jit(solution)/shard_map/ppermute | solution.py:75
  67.4 1.1 %fusion.45 = f32[1792,256]{1,0:T(8,128)S(1)} fusion(bf16[896,896]{1,0:T(8,128)(2,1)S(1)} %get-tuple-element.67, bf16[896,896]{1,0:T(8,128)(2,1)S(1)} %get-tuple-element.66, bf16[896,128]{1,0:T(8,128)(2,1)S(1)} %fusion.49, bf16[896,128]{1,0:T(8,128)(2,1)S(1)} %get-tuple-element.58), kind=kOutput, calls=%fused_computation.48 | convolution fusion | flops 829423616 | bytes 5505024 | tf_op jit(solution)/shard_map/dot_general | solution.py:190
  68.6 0.7 collective-permute-start.14
  69.3 2.7 %collective-permute-start.15 = (f32[224,128]{1,0:T(8,128)S(1)}, f32[224,128]{1,0:T(8,128)S(1)}, u32[]{:S(2)}, u32[]{:S(2)}) collective-permute-start(f32[224,128]{1,0:T(8,128)S(1)} %get-tuple-element.103), channel_id=1, source_target_pairs={{0,1},{1,0},{2,3},{3,2},{4,5},{5,4},{6,7},{7,6},{8,9},{9,8},{10,11... | collective-permute-start | bytes 344072 | tf_op jit(solution)/shard_map/ppermute | solution.py:75
  72.0 0.7 collective-permute-start.16
  72.7 2.6 %collective-permute-start.17 = (f32[224,128]{1,0:T(8,128)S(1)}, f32[224,128]{1,0:T(8,128)S(1)}, u32[]{:S(2)}, u32[]{:S(2)}) collective-permute-start(f32[224,128]{1,0:T(8,128)S(1)} %get-tuple-element.102), channel_id=1, source_target_pairs={{0,4},{4,0},{8,12},{12,8},{16,20},{20,16},{24,28},{28,24},{1,5},{5... | collective-permute-start | bytes 344072 | tf_op jit(solution)/shard_map/ppermute | solution.py:75
  75.3 2.6 %collective-permute-done.15 = f32[224,128]{1,0:T(8,128)S(1)} collective-permute-done((f32[224,128]{1,0:T(8,128)S(1)}, f32[224,128]{1,0:T(8,128)S(1)}, u32[]{:S(2)}, u32[]{:S(2)}) %collective-permute-start.15) | collective-permute-done | bytes 114720 | tf_op jit(solution)/shard_map/ppermute | solution.py:75
  78.2 1.1 %fusion.44 = f32[1792,256]{1,0:T(8,128)S(1)} fusion(bf16[896,896]{1,0:T(8,128)(2,1)S(1)} %get-tuple-element.67, bf16[896,896]{1,0:T(8,128)(2,1)S(1)} %get-tuple-element.66, bf16[896,128]{1,0:T(8,128)(2,1)S(1)} %fusion.50, bf16[896,128]{1,0:T(8,128)(2,1)S(1)} %get-tuple-element.56), kind=kOutput, calls=%fused_computation.47 | convolution fusion | flops 829423616 | bytes 5505024 | tf_op jit(solution)/shard_map/dot_general | solution.py:190
  79.5 0.7 collective-permute-start.18
  80.1 2.3 %collective-permute-start.19 = (f32[224,128]{1,0:T(8,128)S(1)}, f32[224,128]{1,0:T(8,128)S(1)}, u32[]{:S(2)}, u32[]{:S(2)}) collective-permute-start(f32[224,128]{1,0:T(8,128)S(1)} %get-tuple-element.97), channel_id=1, source_target_pairs={{0,1},{1,0},{2,3},{3,2},{4,5},{5,4},{6,7},{7,6},{8,9},{9,8},{10,11... | collective-permute-start | bytes 344072 | tf_op jit(solution)/shard_map/ppermute | solution.py:75
  82.4 0.7 collective-permute-start.20
  83.1 3.3 %collective-permute-start.21 = (f32[224,128]{1,0:T(8,128)S(1)}, f32[224,128]{1,0:T(8,128)S(1)}, u32[]{:S(2)}, u32[]{:S(2)}) collective-permute-start(f32[224,128]{1,0:T(8,128)S(1)} %get-tuple-element.96), channel_id=1, source_target_pairs={{0,4},{4,0},{8,12},{12,8},{16,20},{20,16},{24,28},{28,24},{1,5},{5... | collective-permute-start | bytes 344072 | tf_op jit(solution)/shard_map/ppermute | solution.py:75
  86.4 1.0 %add_add_fusion = f32[1,1,896,128]{3,2,1,0:T(8,128)} fusion(f32[1,1,224,128]{3,2,1,0:T(8,128)S(1)} %bitcast.45, f32[1,1,224,128]{3,2,1,0:T(8,128)S(1)} %bitcast.47, f32[1,1,224,128]{3,2,1,0:T(8,128)S(1)} %bitcast.43, f32[1,1,224,128]{3,2,1,0:T(8,128)S(1)} %bitcast.41, f32[1,1,224,128]{3,2,1,0:T(8,128)S(1)} %bitcast.53, f32[1,1,224,128]{3,2,1,0:T(8,128)S(1)} %bitcast.55, ...), kind=kLoop, calls=%fused_computation.112 | loop fusion | flops 3211264 | bytes 2293760 | tf_op jit(solution)/shard_map/add | solution.py:167
  87.4 1.3 %collective-permute-done.19 = f32[224,128]{1,0:T(8,128)S(1)} collective-permute-done((f32[224,128]{1,0:T(8,128)S(1)}, f32[224,128]{1,0:T(8,128)S(1)}, u32[]{:S(2)}, u32[]{:S(2)}) %collective-permute-start.19) | collective-permute-done | bytes 114720 | tf_op jit(solution)/shard_map/ppermute | solution.py:75
  88.8 0.9 maximum_subtract_fusion.6
  (58 shorter events, 3.0 us)
Async XLA Ops:
  0.6 17.1 %copy-start = (f32[1,1,640,896]{3,2,1,0:T(8,128)S(1)}, f32[1,1,640,896]{3,2,1,0:T(8,128)}, u32[]{:S(2)}) copy-start(f32[1,1,640,896]{3,2,1,0:T(8,128)} %param.7) | copy-start | bytes 6881284
  4.8 23.3 %collective-permute-start = (f32[224,128]{1,0:T(8,128)}, f32[224,128]{1,0:T(8,128)S(1)}, u32[]{:S(2)}, u32[]{:S(2)}) collective-permute-start(f32[224,128]{1,0:T(8,128)} %get-tuple-element.132), channel_id=1, source_target_pairs={{4,8},{8,4},{12,16},{16,12},{20,24},{24,20},{5,9},{9,5},{13,17},{1... | collective-permute-start | bytes 344072 | tf_op jit(solution)/shard_map/ppermute | solution.py:66
  5.4 22.6 %collective-permute-start.1 = (f32[224,128]{1,0:T(8,128)}, f32[224,128]{1,0:T(8,128)S(1)}, u32[]{:S(2)}, u32[]{:S(2)}) collective-permute-start(f32[224,128]{1,0:T(8,128)} %get-tuple-element.130), channel_id=1, source_target_pairs={{0,4},{4,0},{8,12},{12,8},{16,20},{20,16},{24,28},{28,24},{1,5},{5... | collective-permute-start | bytes 344072 | tf_op jit(solution)/shard_map/ppermute | solution.py:66
  9.9 29.5 %collective-permute-start.5 = (f32[128,896]{1,0:T(8,128)}, f32[128,896]{1,0:T(8,128)S(1)}, u32[]{:S(2)}, u32[]{:S(2)}) collective-permute-start(f32[128,896]{1,0:T(8,128)} %get-tuple-element.39), channel_id=1, source_target_pairs={{0,16},{4,20},{8,24},{12,28},{16,0},{20,4},{24,8},{28,12},{1,17},{... | collective-permute-start | bytes 1376264 | tf_op jit(solution)/shard_map/ppermute | solution.py:22
  12.4 27.5 %collective-permute-start.4 = (f32[128,896]{1,0:T(8,128)}, f32[128,896]{1,0:T(8,128)S(1)}, u32[]{:S(2)}, u32[]{:S(2)}) collective-permute-start(f32[128,896]{1,0:T(8,128)} %get-tuple-element.38), channel_id=1, source_target_pairs={{0,24},{4,28},{8,0},{12,4},{16,8},{20,12},{24,16},{28,20},{1,25},{... | collective-permute-start | bytes 1376264 | tf_op jit(solution)/shard_map/ppermute | solution.py:22
  25.2 2.8 %copy-start.2 = (f32[224,128]{1,0:T(8,128)S(1)}, f32[224,128]{1,0:T(8,128)}, u32[]{:S(2)}) copy-start(f32[224,128]{1,0:T(8,128)} %get-tuple-element.30) | copy-start | bytes 344068
  25.2 12.7 %copy-start.1 = (f32[1,1,896,128]{3,2,1,0:T(8,128)S(1)}, f32[1,1,896,128]{3,2,1,0:T(8,128)}, u32[]{:S(2)}) copy-start(f32[1,1,896,128]{3,2,1,0:T(8,128)} %param.6) | copy-start | bytes 1376260
  28.0 5.3 %collective-permute-start.2 = (f32[224,128]{1,0:T(8,128)S(1)}, f32[224,128]{1,0:T(8,128)S(1)}, u32[]{:S(2)}, u32[]{:S(2)}) collective-permute-start(f32[224,128]{1,0:T(8,128)S(1)} %copy-done.2), channel_id=1, source_target_pairs={{1,2},{2,1},{5,6},{6,5},{9,10},{10,9},{13,14},{14,13},{17,18},{18,... | collective-permute-start | bytes 344072 | tf_op jit(solution)/shard_map/ppermute | solution.py:69
  28.7 9.2 %collective-permute-start.3 = (f32[224,128]{1,0:T(8,128)S(1)}, f32[224,128]{1,0:T(8,128)S(1)}, u32[]{:S(2)}, u32[]{:S(2)}) collective-permute-start(f32[224,128]{1,0:T(8,128)S(1)} %get-tuple-element.31), channel_id=1, source_target_pairs={{0,1},{1,0},{2,3},{3,2},{4,5},{5,4},{6,7},{7,6},{8,9},{9,8},{10,11... | collective-permute-start | bytes 344072 | tf_op jit(solution)/shard_map/ppermute | solution.py:69
  41.9 14.8 %collective-permute-start.6 = (f32[224,128]{1,0:T(8,128)S(1)}, f32[224,128]{1,0:T(8,128)S(1)}, u32[]{:S(2)}, u32[]{:S(2)}) collective-permute-start(f32[224,128]{1,0:T(8,128)S(1)} %get-tuple-element.125), channel_id=1, source_target_pairs={{1,2},{2,1},{5,6},{6,5},{9,10},{10,9},{13,14},{14,13},{17,18},{18,... | collective-permute-start | bytes 344072 | tf_op jit(solution)/shard_map/ppermute | solution.py:75
  42.6 14.1 %collective-permute-start.7 = (f32[224,128]{1,0:T(8,128)S(1)}, f32[224,128]{1,0:T(8,128)S(1)}, u32[]{:S(2)}, u32[]{:S(2)}) collective-permute-start(f32[224,128]{1,0:T(8,128)S(1)} %get-tuple-element.123), channel_id=1, source_target_pairs={{0,1},{1,0},{2,3},{3,2},{4,5},{5,4},{6,7},{7,6},{8,9},{9,8},{10,11... | collective-permute-start | bytes 344072 | tf_op jit(solution)/shard_map/ppermute | solution.py:75
  45.6 11.1 %collective-permute-start.8 = (f32[224,128]{1,0:T(8,128)S(1)}, f32[224,128]{1,0:T(8,128)S(1)}, u32[]{:S(2)}, u32[]{:S(2)}) collective-permute-start(f32[224,128]{1,0:T(8,128)S(1)} %get-tuple-element.124), channel_id=1, source_target_pairs={{4,8},{8,4},{12,16},{16,12},{20,24},{24,20},{5,9},{9,5},{13,17},{1... | collective-permute-start | bytes 344072 | tf_op jit(solution)/shard_map/ppermute | solution.py:75
  46.5 10.3 %collective-permute-start.9 = (f32[224,128]{1,0:T(8,128)S(1)}, f32[224,128]{1,0:T(8,128)S(1)}, u32[]{:S(2)}, u32[]{:S(2)}) collective-permute-start(f32[224,128]{1,0:T(8,128)S(1)} %get-tuple-element.122), channel_id=1, source_target_pairs={{0,4},{4,0},{8,12},{12,8},{16,20},{20,16},{24,28},{28,24},{1,5},{5... | collective-permute-start | bytes 344072 | tf_op jit(solution)/shard_map/ppermute | solution.py:75
  58.2 5.6 %collective-permute-start.10 = (f32[224,128]{1,0:T(8,128)S(1)}, f32[224,128]{1,0:T(8,128)S(1)}, u32[]{:S(2)}, u32[]{:S(2)}) collective-permute-start(f32[224,128]{1,0:T(8,128)S(1)} %get-tuple-element.111), channel_id=1, source_target_pairs={{1,2},{2,1},{5,6},{6,5},{9,10},{10,9},{13,14},{14,13},{17,18},{18,... | collective-permute-start | bytes 344072 | tf_op jit(solution)/shard_map/ppermute | solution.py:75
  58.9 8.2 %collective-permute-start.11 = (f32[224,128]{1,0:T(8,128)S(1)}, f32[224,128]{1,0:T(8,128)S(1)}, u32[]{:S(2)}, u32[]{:S(2)}) collective-permute-start(f32[224,128]{1,0:T(8,128)S(1)} %get-tuple-element.109), channel_id=1, source_target_pairs={{0,1},{1,0},{2,3},{3,2},{4,5},{5,4},{6,7},{7,6},{8,9},{9,8},{10,11... | collective-permute-start | bytes 344072 | tf_op jit(solution)/shard_map/ppermute | solution.py:75
  61.7 5.4 %collective-permute-start.12 = (f32[224,128]{1,0:T(8,128)S(1)}, f32[224,128]{1,0:T(8,128)S(1)}, u32[]{:S(2)}, u32[]{:S(2)}) collective-permute-start(f32[224,128]{1,0:T(8,128)S(1)} %get-tuple-element.110), channel_id=1, source_target_pairs={{4,8},{8,4},{12,16},{16,12},{20,24},{24,20},{5,9},{9,5},{13,17},{1... | collective-permute-start | bytes 344072 | tf_op jit(solution)/shard_map/ppermute | solution.py:75
  62.3 4.8 %collective-permute-start.13 = (f32[224,128]{1,0:T(8,128)S(1)}, f32[224,128]{1,0:T(8,128)S(1)}, u32[]{:S(2)}, u32[]{:S(2)}) collective-permute-start(f32[224,128]{1,0:T(8,128)S(1)} %get-tuple-element.108), channel_id=1, source_target_pairs={{0,4},{4,0},{8,12},{12,8},{16,20},{20,16},{24,28},{28,24},{1,5},{5... | collective-permute-start | bytes 344072 | tf_op jit(solution)/shard_map/ppermute | solution.py:75
  68.6 6.7 %collective-permute-start.14 = (f32[224,128]{1,0:T(8,128)S(1)}, f32[224,128]{1,0:T(8,128)S(1)}, u32[]{:S(2)}, u32[]{:S(2)}) collective-permute-start(f32[224,128]{1,0:T(8,128)S(1)} %get-tuple-element.105), channel_id=1, source_target_pairs={{1,2},{2,1},{5,6},{6,5},{9,10},{10,9},{13,14},{14,13},{17,18},{18,... | collective-permute-start | bytes 344072 | tf_op jit(solution)/shard_map/ppermute | solution.py:75
  69.3 8.6 %collective-permute-start.15 = (f32[224,128]{1,0:T(8,128)S(1)}, f32[224,128]{1,0:T(8,128)S(1)}, u32[]{:S(2)}, u32[]{:S(2)}) collective-permute-start(f32[224,128]{1,0:T(8,128)S(1)} %get-tuple-element.103), channel_id=1, source_target_pairs={{0,1},{1,0},{2,3},{3,2},{4,5},{5,4},{6,7},{7,6},{8,9},{9,8},{10,11... | collective-permute-start | bytes 344072 | tf_op jit(solution)/shard_map/ppermute | solution.py:75
  72.0 5.9 %collective-permute-start.16 = (f32[224,128]{1,0:T(8,128)S(1)}, f32[224,128]{1,0:T(8,128)S(1)}, u32[]{:S(2)}, u32[]{:S(2)}) collective-permute-start(f32[224,128]{1,0:T(8,128)S(1)} %get-tuple-element.104), channel_id=1, source_target_pairs={{4,8},{8,4},{12,16},{16,12},{20,24},{24,20},{5,9},{9,5},{13,17},{1... | collective-permute-start | bytes 344072 | tf_op jit(solution)/shard_map/ppermute | solution.py:75
  72.7 5.3 %collective-permute-start.17 = (f32[224,128]{1,0:T(8,128)S(1)}, f32[224,128]{1,0:T(8,128)S(1)}, u32[]{:S(2)}, u32[]{:S(2)}) collective-permute-start(f32[224,128]{1,0:T(8,128)S(1)} %get-tuple-element.102), channel_id=1, source_target_pairs={{0,4},{4,0},{8,12},{12,8},{16,20},{20,16},{24,28},{28,24},{1,5},{5... | collective-permute-start | bytes 344072 | tf_op jit(solution)/shard_map/ppermute | solution.py:75
  79.5 7.9 %collective-permute-start.18 = (f32[224,128]{1,0:T(8,128)S(1)}, f32[224,128]{1,0:T(8,128)S(1)}, u32[]{:S(2)}, u32[]{:S(2)}) collective-permute-start(f32[224,128]{1,0:T(8,128)S(1)} %get-tuple-element.99), channel_id=1, source_target_pairs={{1,2},{2,1},{5,6},{6,5},{9,10},{10,9},{13,14},{14,13},{17,18},{18,... | collective-permute-start | bytes 344072 | tf_op jit(solution)/shard_map/ppermute | solution.py:75
  80.1 8.6 %collective-permute-start.19 = (f32[224,128]{1,0:T(8,128)S(1)}, f32[224,128]{1,0:T(8,128)S(1)}, u32[]{:S(2)}, u32[]{:S(2)}) collective-permute-start(f32[224,128]{1,0:T(8,128)S(1)} %get-tuple-element.97), channel_id=1, source_target_pairs={{0,1},{1,0},{2,3},{3,2},{4,5},{5,4},{6,7},{7,6},{8,9},{9,8},{10,11... | collective-permute-start | bytes 344072 | tf_op jit(solution)/shard_map/ppermute | solution.py:75
  82.4 6.3 %collective-permute-start.20 = (f32[224,128]{1,0:T(8,128)S(1)}, f32[224,128]{1,0:T(8,128)S(1)}, u32[]{:S(2)}, u32[]{:S(2)}) collective-permute-start(f32[224,128]{1,0:T(8,128)S(1)} %get-tuple-element.98), channel_id=1, source_target_pairs={{4,8},{8,4},{12,16},{16,12},{20,24},{24,20},{5,9},{9,5},{13,17},{1... | collective-permute-start | bytes 344072 | tf_op jit(solution)/shard_map/ppermute | solution.py:75
  83.1 5.6 %collective-permute-start.21 = (f32[224,128]{1,0:T(8,128)S(1)}, f32[224,128]{1,0:T(8,128)S(1)}, u32[]{:S(2)}, u32[]{:S(2)}) collective-permute-start(f32[224,128]{1,0:T(8,128)S(1)} %get-tuple-element.96), channel_id=1, source_target_pairs={{0,4},{4,0},{8,12},{12,8},{16,20},{20,16},{24,28},{28,24},{1,5},{5... | collective-permute-start | bytes 344072 | tf_op jit(solution)/shard_map/ppermute | solution.py:75
